TPU v7x, 32 devices: a whole 2x2x4 slice. The times are simulated.
32 devices in a mesh: dp: 2 (over x), mp: 16 (over z, y, core).
Axes of the slice: x: 2, y: 2, z: 4, core: 2. Of those that a mesh axis runs over, the one named last changes fastest.
Arguments:
- node_features: bfloat16 [512, 6144], P('mp', 'dp'), may hold values from -6 to 6
- weights_one: bfloat16 [1024, 512], replicated, may hold values from -0.25 to 0.25
- weights_two: bfloat16 [1024, 512], replicated, may hold values from -0.25 to 0.25
- neighbor_owner: int32 [6144, 8], P('dp'), may hold values from 0 to 15, all different within a row; in each aligned block of 192 rows (0 to 191, 192 to 383, ...) at most 144 rows name the same one
- neighbor_row: int32 [6144, 8], P('dp'), may hold values from 0 to 191
- neighbor_count: int32 [6144], P('dp'), may hold values from 4 to 8
- cotangent: bfloat16 [6144, 512], P(('dp', 'mp')), may hold values from -0.076171875 to 0.076171875
Outputs:
- node_output: bfloat16 [6144, 512], P(('dp', 'mp'))
- weight_grads: float32 [2048, 512], P(('dp', 'mp'))
Inputs may be any that keep to these rules, and one draw needn't show every extreme that they name: `neighbor_owner`: each row names 8 different owners; among the rows of one device (aligned blocks of 192 rows) no owner is named more than 144 times, and in some block one owner exactly 144 times. Slots k >= neighbor_count[r] are padding and carry no edge.
All inputs are finite; a program needn't handle non-finite values.
Results may differ from a plain program's by a relative error of at most 0.0052.
Values may be sent and summed in bfloat16 or wider, within the bound.
No kernel may reach another device: no remote copies, remote signals or barrier semaphores. Data moves between devices by JAX's collectives and lax.ppermute only.
A program may use at most 64 MiB of HBM per device.

v0:
```python
import jax
import jax.numpy as jnp
from jax import lax
from jax.sharding import PartitionSpec as P


def column_mean(table, indices, live, inverse):
    total = jnp.zeros((table.shape[0], indices.shape[1]), jnp.float32)
    for slot_index in range(indices.shape[0]):
        picked = jnp.take(table, indices[slot_index], axis=1)
        kept = jnp.where(live[slot_index][None, :], picked, jnp.zeros_like(picked))
        total = total + kept.astype(jnp.float32)
    return (total * inverse[None, :]).astype(jnp.bfloat16)


def silu_slope(values):
    sigmoid = jax.nn.sigmoid(values)
    return sigmoid * (1.0 + values * (1.0 - sigmoid))


def contract(left, right, left_dim, right_dim):
    return lax.dot_general(
        left, right, (((left_dim,), (right_dim,)), ((), ())), preferred_element_type=jnp.float32
    )


def shards(
    node_features, weights_one, weights_two, neighbor_owner, neighbor_row, neighbor_count, cotangent
):
    devices = lax.axis_size("mp")
    own_index = lax.axis_index("mp")
    node_dev = cotangent.shape[0]
    all_nodes = neighbor_owner.shape[0]
    fanout = neighbor_owner.shape[1]
    feat_width = weights_one.shape[0] // 2
    hidden = weights_one.shape[1]
    capacity = 3 * node_dev * fanout // (2 * devices)
    owner_slots = neighbor_owner.T
    row_slots = neighbor_row.T
    global_ids = owner_slots * node_dev + row_slots
    live_all = lax.broadcasted_iota(jnp.int32, (fanout, all_nodes), 0) < neighbor_count[None, :]
    inverse_all = 1.0 / neighbor_count.astype(jnp.float32)
    agg_one_cols = column_mean(node_features, global_ids, live_all, inverse_all)
    own_feats, own_agg_one = (
        lax.all_to_all(node_features, "mp", split_axis=1, concat_axis=0, tiled=True),
        lax.all_to_all(agg_one_cols, "mp", split_axis=1, concat_axis=0, tiled=True),
    )
    pre_one = contract(weights_one[:feat_width], own_feats, 0, 0) + contract(
        weights_one[feat_width:], own_agg_one, 0, 0
    )
    hidden_one = jax.nn.silu(pre_one).astype(jnp.bfloat16)
    start_row = own_index * node_dev
    own_owner = lax.dynamic_slice_in_dim(owner_slots, start_row, node_dev, 1)
    own_live = lax.dynamic_slice_in_dim(live_all, start_row, node_dev, 1)
    own_inverse = lax.dynamic_slice_in_dim(inverse_all, start_row, node_dev, 0)
    owner_major = own_owner.reshape(-1)
    owner_hits = (owner_major[None, :] == lax.broadcasted_iota(jnp.int32, (devices, 1), 0)).astype(
        jnp.int32
    )
    ranks = jnp.sum(jnp.cumsum(owner_hits, axis=1) * owner_hits, axis=0) - 1
    slot_ids = owner_major * capacity + ranks
    source_owner = (
        owner_slots.reshape(fanout, devices, node_dev)
        .transpose(1, 0, 2)
        .reshape(devices, fanout * node_dev)
    )
    source_row = (
        row_slots.reshape(fanout, devices, node_dev)
        .transpose(1, 0, 2)
        .reshape(devices, fanout * node_dev)
    )
    asked = (source_owner == own_index).astype(jnp.int32)
    target = jnp.where(asked == 1, jnp.cumsum(asked, axis=1) - 1, capacity)
    sources = lax.broadcasted_iota(jnp.int32, target.shape, 0)
    requested = (
        jnp.zeros((devices, capacity), jnp.int32).at[sources, target].set(source_row, mode="drop")
    )
    requested_flat = requested.reshape(-1)
    outgoing = jnp.take(hidden_one, requested_flat, axis=1)
    incoming = lax.all_to_all(outgoing, "mp", split_axis=1, concat_axis=1, tiled=True)
    fetched = jnp.take(incoming, slot_ids, axis=1).reshape(hidden, fanout, node_dev)
    total = jnp.zeros((hidden, node_dev), jnp.float32)
    for slot_index in range(fanout):
        picked = fetched[:, slot_index]
        kept = jnp.where(own_live[slot_index][None, :], picked, jnp.zeros_like(picked))
        total = total + kept.astype(jnp.float32)
    agg_two = (total * own_inverse[None, :]).astype(jnp.bfloat16)
    self_two = weights_two[:hidden]
    neigh_two = weights_two[hidden:]
    node_output = (
        contract(hidden_one, self_two, 0, 0) + contract(agg_two, neigh_two, 0, 0)
    ).astype(jnp.bfloat16)
    down_self = contract(self_two, cotangent, 1, 1)
    down_neigh = (contract(neigh_two, cotangent, 1, 1) * own_inverse[None, :]).astype(jnp.bfloat16)
    spread = jnp.tile(down_neigh, (1, fanout))
    keep_flat = own_live.reshape(-1)
    send_ids = jnp.where(keep_flat, slot_ids, devices * capacity)
    outgoing_grad = (
        jnp.zeros((hidden, devices * capacity), jnp.bfloat16)
        .at[:, send_ids]
        .set(spread, mode="drop")
    )
    incoming_grad = lax.all_to_all(outgoing_grad, "mp", split_axis=1, concat_axis=1, tiled=True)
    neighbor_sum = (
        jnp.zeros((hidden, node_dev), jnp.float32)
        .at[:, requested_flat]
        .add(incoming_grad.astype(jnp.float32))
    )
    grad_hidden = down_self + neighbor_sum
    grad_pre = (grad_hidden * silu_slope(pre_one)).astype(jnp.bfloat16)
    terms = jnp.concatenate(
        [
            contract(own_feats, grad_pre, 1, 1),
            contract(own_agg_one, grad_pre, 1, 1),
            contract(hidden_one, cotangent, 1, 0),
            contract(agg_two, cotangent, 1, 0),
        ],
        axis=0,
    )
    weight_grads = lax.psum_scatter(terms, ("dp", "mp"), scatter_dimension=0, tiled=True)
    return (node_output, weight_grads)


def solution(mesh):
    in_specs = (
        P("mp", "dp"),
        P(),
        P(),
        P("dp", None),
        P("dp", None),
        P("dp"),
        P(("dp", "mp"), None),
    )
    out_specs = (P(("dp", "mp"), None), P(("dp", "mp"), None))
    return jax.shard_map(shards, mesh=mesh, in_specs=in_specs, out_specs=out_specs, check_vma=False)
```

profile of v0, /device:TPU:0, one launch (start us, length us, event | category | flops | bytes accessed | tf_op | source)
XLA Modules:
  0.0 531.8 jit_solution(14688060896775258228)
XLA Ops:
  7.2 1.3 all_to_all.40
  8.5 0.8 copy.32
  9.3 7.4 %all-to-all-start = ((bf16[32,16,192]{2,0,1:T(8,128)(2,1)}), bf16[32,16,192]{2,0,1:T(8,128)(2,1)S(1)}, u32[]{:S(2)}, u32[]{:S(2)}) async-start(bf16[32,16,192]{2,0,1:T(8,128)(2,1)} %copy.32), calls=%async_computation | async-start | bytes 524288 | tf_op jit(solution)/shard_map/all_to_all | solution.py:45
  16.7 0.7 convert_divide_fusion
  17.4 0.7 iota_compare_fusion.1
  18.2 1.3 copy.33
  20.7 4.5 reduce-window.16
  26.3 4.5 reduce-window.14
  32.4 90.2 %scatter_custom_fusion.2 = s32[2304]{0:T(1024)S(1)} fusion(s32[24576]{0:T(1024)S(1)} %reshape.391, s32[24576]{0:T(1024)S(1)} %reshape.393, s32[]{:T(128)} %constant.29.clone.1), kind=kCustom, calls=%fused_computation.132 | custom fusion | bytes 9220
  122.6 0.7 reshape.287
  124.3 1.3 tile.4
  125.6 9.5 %scatter_custom_fusion = bf16[512,2304]{0,1:T(8,128)(2,1)} fusion(s32[1536]{0:T(1024)S(1)} %get-tuple-element.19, bf16[1536,512]{1,0:T(8,128)(2,1)} %bitcast.171, bf16[]{:T(256)} %constant.27.clone.1), kind=kCustom, calls=%fused_computation.23 | custom fusion | bytes 2359808 | tf_op jit(solution)/shard_map/scatter | solution.py:101
  135.1 0.7 copy-done.6
  135.8 6.0 %all-to-all-start.3 = ((bf16[512,16,144]{0,2,1:T(8,128)(2,1)}), bf16[512,16,144]{0,2,1:T(8,128)(2,1)S(1)}, u32[]{:S(2)}, u32[]{:S(2)}) async-start(bf16[512,16,144]{0,2,1:T(8,128)(2,1)} %bitcast.166), calls=%async_computation.3 | async-start | bytes 4718592 | tf_op jit(solution)/shard_map/all_to_all | solution.py:103
  141.8 0.7 fusion.39
  143.1 11.4 %gather_fusion.9 = bf16[3072,32]{1,0:T(8,128)(2,1)} fusion(bf16[32,3072]{0,1:T(8,128)(2,1)S(1)} %copy.33, s32[3072]{0:T(1024)S(1)} %fusion.32), kind=kCustom, calls=%fused_computation.7.clone | custom fusion | bytes 405504 | tf_op jit(solution)/shard_map/jit(_take)/gather | solution.py:10
  154.5 1.4 copy.48
  155.9 1.3 fusion.31
  157.2 12.5 %gather_fusion.8 = bf16[3072,32]{1,0:T(8,128)(2,1)} fusion(bf16[32,3072]{0,1:T(8,128)(2,1)S(1)} %copy.33, s32[3072]{0:T(1024)} %fusion.31), kind=kCustom, calls=%fused_computation.6.clone | custom fusion | bytes 405504 | tf_op jit(solution)/shard_map/jit(_take)/gather | solution.py:10
  169.7 2.1 copy.46
  171.8 1.3 fusion.30
  173.1 12.5 %gather_fusion.7 = bf16[3072,32]{1,0:T(8,128)(2,1)} fusion(bf16[32,3072]{0,1:T(8,128)(2,1)S(1)} %copy.33, s32[3072]{0:T(1024)} %fusion.30), kind=kCustom, calls=%fused_computation.5.clone | custom fusion | bytes 405504 | tf_op jit(solution)/shard_map/jit(_take)/gather | solution.py:10
  185.5 2.1 copy.44
  187.6 1.3 fusion.29
  188.9 12.5 %gather_fusion.6 = bf16[3072,32]{1,0:T(8,128)(2,1)} fusion(bf16[32,3072]{0,1:T(8,128)(2,1)S(1)} %copy.33, s32[3072]{0:T(1024)} %fusion.29), kind=kCustom, calls=%fused_computation.4.clone | custom fusion | bytes 405504 | tf_op jit(solution)/shard_map/jit(_take)/gather | solution.py:10
  201.4 2.1 copy.42
  203.4 1.3 fusion.28
  204.7 12.5 %gather_fusion.5 = bf16[3072,32]{1,0:T(8,128)(2,1)} fusion(bf16[32,3072]{0,1:T(8,128)(2,1)S(1)} %copy.33, s32[3072]{0:T(1024)} %fusion.28), kind=kCustom, calls=%fused_computation.3.clone | custom fusion | bytes 405504 | tf_op jit(solution)/shard_map/jit(_take)/gather | solution.py:10
  217.2 2.0 copy.40
  219.3 1.3 fusion.27
  220.6 12.5 %gather_fusion.4 = bf16[3072,32]{1,0:T(8,128)(2,1)} fusion(bf16[32,3072]{0,1:T(8,128)(2,1)S(1)} %copy.33, s32[3072]{0:T(1024)} %fusion.27), kind=kCustom, calls=%fused_computation.2.clone | custom fusion | bytes 405504 | tf_op jit(solution)/shard_map/jit(_take)/gather | solution.py:10
  233.0 2.1 copy.38
  235.1 1.3 fusion.26
  236.4 12.5 %gather_fusion.3 = bf16[3072,32]{1,0:T(8,128)(2,1)} fusion(bf16[32,3072]{0,1:T(8,128)(2,1)S(1)} %copy.33, s32[3072]{0:T(1024)} %fusion.26), kind=kCustom, calls=%fused_computation.1.clone | custom fusion | bytes 405504 | tf_op jit(solution)/shard_map/jit(_take)/gather | solution.py:10
  248.9 2.1 copy.36
  250.9 1.3 fusion.25
  252.2 12.5 %gather_fusion.2 = bf16[3072,32]{1,0:T(8,128)(2,1)} fusion(bf16[32,3072]{0,1:T(8,128)(2,1)S(1)} %copy.33, s32[3072]{0:T(1024)} %fusion.25), kind=kCustom, calls=%fused_computation.clone | custom fusion | bytes 405504 | tf_op jit(solution)/shard_map/jit(_take)/gather | solution.py:10
  264.7 1.4 copy.34
  266.1 1.3 slice_reduce_fusion.9
  267.4 0.8 compare_and_fusion.1
  268.2 0.7 compare_and_fusion.7
  269.0 0.7 compare_and_fusion.3
  269.7 0.7 compare_and_fusion.5
  270.4 1.9 multiply_convert_fusion.3
  272.7 0.8 copy.49
  273.5 2.1 fusion.11
  275.6 6.0 %all-to-all-start.1 = ((bf16[32,16,192]{2,0,1:T(8,128)(2,1)}), bf16[32,16,192]{2,0,1:T(8,128)(2,1)S(1)}, u32[]{:S(2)}, u32[]{:S(2)}) async-start(bf16[32,16,192]{2,0,1:T(8,128)(2,1)} %copy.49), calls=%async_computation.1 | async-start | bytes 524288 | tf_op jit(solution)/shard_map/all_to_all | solution.py:46
  281.7 2.1 fusion.7
  283.7 18.7 %scatter_custom_fusion.1 = f32[512,192]{0,1:T(8,128)} fusion(f32[512,192]{0,1:T(8,128)} %fusion.11, s32[2304]{0:T(1024)S(1)} %fusion.33, bf16[512,2304]{0,1:T(8,128)(2,1)S(1)} %bitcast.165), kind=kCustom, calls=%fused_computation.14 | custom fusion | flops 2359296 | bytes 2752512 | tf_op jit(solution)/shard_map/scatter-add | solution.py:107
  302.5 1.8 multiply_convert_fusion
  304.3 6.9 %gather_fusion = bf16[2304,512]{1,0:T(8,128)(2,1)S(1)} fusion(bf16[512,192]{0,1:T(8,128)(2,1)S(1)} %get-tuple-element.26, s32[3072]{0:T(1024)S(1)} %pad_clamp_fusion), kind=kCustom, calls=%fused_computation.8 | custom fusion | bytes 4727808 | tf_op jit(solution)/shard_map/jit(_take)/gather | solution.py:79
  311.2 1.7 broadcast_select_fusion
  312.9 6.3 %all-to-all-start.2 = ((bf16[512,16,144]{0,2,1:T(8,128)(2,1)}), bf16[512,16,144]{0,2,1:T(8,128)(2,1)S(1)}, u32[]{:S(2)}, u32[]{:S(2)}) async-start(bf16[512,16,144]{0,2,1:T(8,128)(2,1)} %broadcast_select_fusion), calls=%async_computation.2 | async-start | bytes 4718592 | tf_op jit(solution)/shard_map/all_to_all | solution.py:80
  319.5 1.1 dynamic-slice_reduce_fusion.7
  320.7 1.3 fusion.41
  322.0 1.3 fusion.40
  323.2 1.3 convolution_bitcast_fusion
  324.5 40.3 %all-to-all-done.2 = bf16[512,16,144]{0,2,1:T(8,128)(2,1)S(1)} async-done(((bf16[512,16,144]{0,2,1:T(8,128)(2,1)}), bf16[512,16,144]{0,2,1:T(8,128)(2,1)S(1)}, u32[]{:S(2)}, u32[]{:S(2)}) %all-to-all-start.2) | async-done | bytes 2359328 | tf_op jit(solution)/shard_map/all_to_all | solution.py:80
  364.8 5.4 %gather_fusion.1 = bf16[1536,512]{1,0:T(8,128)(2,1)} fusion(bf16[512,2304]{0,1:T(8,128)(2,1)S(1)} %bitcast.164, s32[2048]{0:T(1024)S(1)} %pad_clamp_fusion.1), kind=kCustom, calls=%fused_computation.9 | custom fusion | bytes 3151872 | tf_op jit(solution)/shard_map/jit(_take)/gather | solution.py:81
  370.2 1.7 broadcast_select_fusion.1
  373.8 2.4 pad_maximum_fusion
  376.2 1.2 copy-done.5
  377.7 1.0 fusion.4
  378.6 146.3 %reduce-scatter.2.cloned.1.call-done = f32[64,512]{1,0:T(8,128)} async-done(((f32[2048,512]{1,0:T(8,128)}), f32[64,512]{1,0:T(8,128)}) %reduce-scatter.2.cloned.1.call-update) | async-done | bytes 131088 | tf_op jit(solution)/shard_map/reduce_scatter | solution.py:120
  (95 shorter events, 8.1 us)
Async XLA Ops:
  7.2 116.8 %copy-start = (bf16[192,512]{1,0:T(8,128)(2,1)S(1)}, bf16[192,512]{1,0:T(8,128)(2,1)}, u32[]{:S(2)}) copy-start(bf16[192,512]{1,0:T(8,128)(2,1)} %param.15) | copy-start | bytes 589828
  7.2 12.4 %copy-start.12 = (s32[3072,8]{0,1:T(8,128)S(1)}, s32[3072,8]{0,1:T(8,128)}, u32[]{:S(2)}) copy-start(s32[3072,8]{0,1:T(8,128)} %param.12) | copy-start | bytes 294916
  8.5 17.5 %copy-start.22 = (s32[2]{0:T(128)S(1)}, s32[2]{0:T(128)}, u32[]{:S(2)}) copy-start(s32[2]{0:T(128)} %constant.56) | copy-start | bytes 28
  8.5 17.6 %copy-start.21 = (s32[2]{0:T(128)S(1)}, s32[2]{0:T(128)}, u32[]{:S(2)}) copy-start(s32[2]{0:T(128)} %constant.53) | copy-start | bytes 28
  9.3 125.8 %all-to-all-start = ((bf16[32,16,192]{2,0,1:T(8,128)(2,1)}), bf16[32,16,192]{2,0,1:T(8,128)(2,1)S(1)}, u32[]{:S(2)}, u32[]{:S(2)}) async-start(bf16[32,16,192]{2,0,1:T(8,128)(2,1)} %copy.32), calls=%async_computation | async-start | bytes 524288 | tf_op jit(solution)/shard_map/all_to_all | solution.py:45
  17.4 2.6 copy-start.18
  18.2 1.7 copy-start.11
  18.2 13.9 %copy-start.13 = (s32[3072,8]{0,1:T(8,128)S(1)}, s32[3072,8]{0,1:T(8,128)}, u32[]{:S(2)}) copy-start(s32[3072,8]{0,1:T(8,128)} %param.13) | copy-start | bytes 294916
  19.7 0.6 copy-start.15
  20.0 104.0 %copy-start.4 = (bf16[1024,512]{1,0:T(8,128)(2,1)S(1)}, bf16[1024,512]{1,0:T(8,128)(2,1)}, u32[]{:S(2)}) copy-start(bf16[1024,512]{1,0:T(8,128)(2,1)} %param.11) | copy-start | bytes 3145732
  135.1 0.7 copy-start.6
  135.8 139.8 %all-to-all-start.3 = ((bf16[512,16,144]{0,2,1:T(8,128)(2,1)}), bf16[512,16,144]{0,2,1:T(8,128)(2,1)S(1)}, u32[]{:S(2)}, u32[]{:S(2)}) async-start(bf16[512,16,144]{0,2,1:T(8,128)(2,1)} %bitcast.166), calls=%async_computation.3 | async-start | bytes 4718592 | tf_op jit(solution)/shard_map/all_to_all | solution.py:103
  142.5 0.6 copy-start.14
  264.7 8.7 %copy-start.17 = (s32[16,144]{1,0:T(8,128)S(1)}, s32[16,144]{1,0:T(8,128)}, u32[]{:S(2)}) copy-start(s32[16,144]{1,0:T(8,128)} %reshape.287) | copy-start | bytes 27652
  267.4 14.2 %copy-start.7 = (bf16[32,16,192]{2,0,1:T(8,128)(2,1)S(1)}, bf16[32,16,192]{2,0,1:T(8,128)(2,1)}, u32[]{:S(2)}) copy-start(bf16[32,16,192]{2,0,1:T(8,128)(2,1)} %copy-done.6) | copy-start | bytes 589828
  275.6 26.9 %all-to-all-start.1 = ((bf16[32,16,192]{2,0,1:T(8,128)(2,1)}), bf16[32,16,192]{2,0,1:T(8,128)(2,1)S(1)}, u32[]{:S(2)}, u32[]{:S(2)}) async-start(bf16[32,16,192]{2,0,1:T(8,128)(2,1)} %copy.49), calls=%async_computation.1 | async-start | bytes 524288 | tf_op jit(solution)/shard_map/all_to_all | solution.py:46
  302.5 1.8 copy-start.9
  312.9 6.6 %copy-start.19 = (s32[12,128]{1,0:T(8,128)S(1)}, s32[12,128]{1,0:T(8,128)}, u32[]{:S(2)}) copy-start(s32[12,128]{1,0:T(8,128)} %get-tuple-element.35) | copy-start | bytes 18436
  312.9 7.7 %copy-start.20 = (s32[1536]{0:T(1024)S(1)}, s32[1536]{0:T(1024)}, u32[]{:S(2)}) copy-start(s32[1536]{0:T(1024)} %get-tuple-element.20) | copy-start | bytes 18436
  312.9 7.8 %copy-start.16 = (s32[8,192]{1,0:T(8,128)S(1)}, s32[8,192]{1,0:T(8,128)}, u32[]{:S(2)}) copy-start(s32[8,192]{1,0:T(8,128)} %copy-done.15) | copy-start | bytes 18436
  312.9 9.1 %copy-start.10 = (bf16[32,16,192]{2,0,1:T(8,128)(2,1)S(1)}, bf16[32,16,192]{2,0,1:T(8,128)(2,1)}, u32[]{:S(2)}) copy-start(bf16[32,16,192]{2,0,1:T(8,128)(2,1)} %copy-done.9) | copy-start | bytes 589828
  312.9 52.0 %all-to-all-start.2 = ((bf16[512,16,144]{0,2,1:T(8,128)(2,1)}), bf16[512,16,144]{0,2,1:T(8,128)(2,1)S(1)}, u32[]{:S(2)}, u32[]{:S(2)}) async-start(bf16[512,16,144]{0,2,1:T(8,128)(2,1)} %broadcast_select_fusion), calls=%async_computation.2 | async-start | bytes 4718592 | tf_op jit(solution)/shard_map/all_to_all | solution.py:80
  319.2 4.1 copy-start.8
  319.2 205.8 %reduce-scatter.2.cloned.1.call-start = ((), (), s32[]{:S(2)}) async-start(), calls=%async_computation.5 | async-start | bytes 4325376 | tf_op jit(solution)/shard_map/reduce_scatter | solution.py:120
  371.9 1.2 copy-start.1
  371.9 1.5 copy-start.2
  372.0 1.8 copy-start.3
  376.2 1.2 copy-start.5
Sparse Core Ops, SparseCore 0:
  376.3 148.6 reduce-scatter.1
where the time goes:
time: 535 us; the launch traced here: 532 us
  local copies, waits for them, and re-layouts  241 us (45%)
  waiting for transfers between devices  187 us (35%)
  other arithmetic  51.6 us (10%)
  starting transfers between devices  25.9 us (5%)
  between operations  14.6 us (3%)
  matrix products  11.7 us (2%)
    reduce_scatter x1, waiting for transfers between devices, shards(): lax.psum_scatter(terms, ('dp', 'mp'), scatter_dimension=0, tiled=True)  146 us
    gather x16, local copies, waits for them, and re-layouts, column_mean(): picked = jnp.take(table, indices[slot_index], axis=1)  114 us
    unnamed x49, local copies, waits for them, and re-layouts  95.2 us
    all_to_all x1, waiting for transfers between devices, shards(): lax.all_to_all(outgoing, 'mp', split_axis=1, concat_axis=1, tiled=True)  40.3 us
    scatter-add x1, other arithmetic, shards(): neighbor_sum = jnp.zeros((hidden, node_dev), jnp.float32).at[:, requested...  18.7 us
    dot_general x10, matrix products, contract(): lax.dot_general(left, right, (((left_dim,), (right_dim,)), ((), ())), pre...  11.7 us
  transfers between devices with their start and end apart: 5, of which 2 were waited for; matrix products, arithmetic and copies ran while one was open for 52% of the time, Pallas kernels for 0%

commit v1 on v0

v1 whole, which is shorter than its diff:
```python
import jax
import jax.numpy as jnp
from jax import lax
from jax.sharding import PartitionSpec as P


def column_mean(table, indices, live, inverse):
    total = jnp.zeros((table.shape[0], indices.shape[1]), jnp.float32)
    for slot_index in range(indices.shape[0]):
        picked = jnp.take(table, indices[slot_index], axis=1)
        kept = jnp.where(live[slot_index][None, :], picked, jnp.zeros_like(picked))
        total = total + kept.astype(jnp.float32)
    return (total * inverse[None, :]).astype(jnp.bfloat16)


def silu_slope(values):
    sigmoid = jax.nn.sigmoid(values)
    return sigmoid * (1.0 + values * (1.0 - sigmoid))


def contract(left, right, left_dim, right_dim):
    return lax.dot_general(
        left, right, (((left_dim,), (right_dim,)), ((), ())), preferred_element_type=jnp.float32
    )


def shards(
    node_features, weights_one, weights_two, neighbor_owner, neighbor_row, neighbor_count, cotangent
):
    devices = lax.axis_size("mp")
    own_index = lax.axis_index("mp")
    node_dev = cotangent.shape[0]
    all_nodes = neighbor_owner.shape[0]
    fanout = neighbor_owner.shape[1]
    feat_width = weights_one.shape[0] // 2
    hidden = weights_one.shape[1]
    capacity = 3 * node_dev * fanout // (2 * devices)
    live = lax.broadcasted_iota(jnp.int32, (all_nodes, fanout), 1) < neighbor_count[:, None]
    inverse_all = 1.0 / neighbor_count.astype(jnp.float32)

    owner_ids = lax.broadcasted_iota(jnp.int32, (devices, 1, 1), 0)
    match = (neighbor_owner[None, :, :] == owner_ids) & live[None, :, :]
    rowsel = jnp.max(jnp.where(match, neighbor_row[None, :, :], -1), axis=2)
    has = rowsel >= 0

    with jax.named_scope("layer_one_mean"):
        if all_nodes * all_nodes <= 4096 * 4096:
            row_ids = lax.broadcasted_iota(jnp.int32, (1, node_dev, 1), 1)
            adjacency = (rowsel[:, None, :] == row_ids).astype(jnp.bfloat16)
            adjacency = adjacency.reshape(devices * node_dev, all_nodes)
            summed = contract(node_features, adjacency, 1, 0)
            agg_one_cols = (summed * inverse_all[None, :]).astype(jnp.bfloat16)
        else:
            owner_slots = neighbor_owner.T
            global_ids = owner_slots * node_dev + neighbor_row.T
            agg_one_cols = column_mean(node_features, global_ids, live.T, inverse_all)

    own_feats, own_agg_one = (
        lax.all_to_all(node_features, "mp", split_axis=1, concat_axis=0, tiled=True),
        lax.all_to_all(agg_one_cols, "mp", split_axis=1, concat_axis=0, tiled=True),
    )
    pre_one = contract(weights_one[:feat_width], own_feats, 0, 0) + contract(
        weights_one[feat_width:], own_agg_one, 0, 0
    )
    hidden_one = jax.nn.silu(pre_one).astype(jnp.bfloat16)

    with jax.named_scope("slot_tables"):
        blocks = has.reshape(devices * devices, node_dev).astype(jnp.bfloat16)
        before = (
            lax.broadcasted_iota(jnp.int32, (node_dev, node_dev), 0)
            < lax.broadcasted_iota(jnp.int32, (node_dev, node_dev), 1)
        ).astype(jnp.bfloat16)
        ranks = contract(blocks, before, 1, 0).astype(jnp.int32).reshape(devices, devices, node_dev)
        has_blocks = has.reshape(devices, devices, node_dev)
        rows_blocks = rowsel.reshape(devices, devices, node_dev)
        cap_ids = lax.broadcasted_iota(jnp.int32, (1, capacity, 1), 1)
        own_rank = lax.dynamic_index_in_dim(ranks, own_index, 1, keepdims=False)
        own_has = lax.dynamic_index_in_dim(has_blocks, own_index, 1, keepdims=False)
        gathered = ((own_rank[:, None, :] == cap_ids) & own_has[:, None, :]).astype(jnp.bfloat16)
        gathered = gathered.reshape(devices * capacity, node_dev)
        req_rank = lax.dynamic_index_in_dim(ranks, own_index, 0, keepdims=False)
        req_has = lax.dynamic_index_in_dim(has_blocks, own_index, 0, keepdims=False)
        req_rows = lax.dynamic_index_in_dim(rows_blocks, own_index, 0, keepdims=False)
        pick = ((req_rank[:, None, :] == cap_ids) & req_has[:, None, :]).astype(jnp.bfloat16)
        row_ids = lax.broadcasted_iota(jnp.int32, (1, 1, node_dev), 2)
        which = (req_rows[:, :, None] == row_ids).astype(jnp.bfloat16)
        asked = lax.dot_general(
            pick, which, (((2,), (1,)), ((0,), (0,))), preferred_element_type=jnp.float32
        )
        asked = asked.astype(jnp.bfloat16).reshape(devices * capacity, node_dev)

    own_inverse = lax.dynamic_slice_in_dim(inverse_all, own_index * node_dev, node_dev, 0)
    outgoing = contract(hidden_one, asked, 1, 1).astype(jnp.bfloat16)
    incoming = lax.all_to_all(outgoing, "mp", split_axis=1, concat_axis=1, tiled=True)
    total = contract(incoming, gathered, 1, 0)
    agg_two = (total * own_inverse[None, :]).astype(jnp.bfloat16)
    self_two = weights_two[:hidden]
    neigh_two = weights_two[hidden:]
    node_output = (
        contract(hidden_one, self_two, 0, 0) + contract(agg_two, neigh_two, 0, 0)
    ).astype(jnp.bfloat16)
    down_self = contract(self_two, cotangent, 1, 1)
    down_neigh = (contract(neigh_two, cotangent, 1, 1) * own_inverse[None, :]).astype(jnp.bfloat16)
    outgoing_grad = contract(down_neigh, gathered, 1, 1).astype(jnp.bfloat16)
    incoming_grad = lax.all_to_all(outgoing_grad, "mp", split_axis=1, concat_axis=1, tiled=True)
    neighbor_sum = contract(incoming_grad, asked, 1, 0)
    grad_hidden = down_self + neighbor_sum
    grad_pre = (grad_hidden * silu_slope(pre_one)).astype(jnp.bfloat16)
    terms = jnp.concatenate(
        [
            contract(own_feats, grad_pre, 1, 1),
            contract(own_agg_one, grad_pre, 1, 1),
            contract(hidden_one, cotangent, 1, 0),
            contract(agg_two, cotangent, 1, 0),
        ],
        axis=0,
    )
    weight_grads = lax.psum_scatter(terms, ("dp", "mp"), scatter_dimension=0, tiled=True)
    return (node_output, weight_grads)


def solution(mesh):
    in_specs = (
        P("mp", "dp"),
        P(),
        P(),
        P("dp", None),
        P("dp", None),
        P("dp"),
        P(("dp", "mp"), None),
    )
    out_specs = (P(("dp", "mp"), None), P(("dp", "mp"), None))
    return jax.shard_map(shards, mesh=mesh, in_specs=in_specs, out_specs=out_specs, check_vma=False)
```

time: 535 us -> 326 us (0.61)
  local copies, waits for them, and re-layouts: 241 us -> 12.7 us
  waiting for transfers between devices: 187 us -> 227 us
  other arithmetic: 51.6 us -> 15.9 us
  matrix products: 11.7 us -> 25.9 us
    gather x18 -> x0, local copies, waits for them, and re-layouts: 126 us -> none  [the longest x16 114 us: column_mean(): picked = jnp.take(table, indices[slot_index], axis=1)]
    unnamed x49 -> x20, local copies, waits for them, and re-layouts: 95.2 us -> 1.25 us
    all_to_all x1, waiting for transfers between devices: 0.01 us -> 35.1 us  [shards(): lax.all_to_all(outgoing_grad, 'mp', split_axis=1, concat_axis=1, tiled=True)]
    scatter-add x1 -> x0, other arithmetic: 18.7 us -> none  [shards(): neighbor_sum = jnp.zeros((hidden, node_dev), jnp.float32).at[:, requested...]
    dot_general x10 -> x15, matrix products: 11.7 us -> 24.6 us  [contract(): lax.dot_general(left, right, (((left_dim,), (right_dim,)), ((), ())), pre...]
    scatter x2 -> x0, local copies, waits for them, and re-layouts: 10.1 us -> none  [the longest x1 9.47 us: shards(): outgoing_grad = jnp.zeros((hidden, devices * capacity), jnp.bfloat16).at[...]
    eq x1, other arithmetic: 0.02 us -> 9.7 us  [shards(): adjacency = (rowsel[:, None, :] == row_ids).astype(jnp.bfloat16)]
    another operation x4 -> x0, other arithmetic: 9.42 us -> none
  transfers between devices with their start and end apart: 5 -> 5, of which waited for: 2 -> 4; matrix products, arithmetic and copies ran while one was open for 52% -> 14% of each run, Pallas kernels for 0% -> 0%
where the time goes in v1:
time: 326 us; the launch traced here: 325 us
  waiting for transfers between devices  227 us (70%)
  starting transfers between devices  29.5 us (9%)
  matrix products  25.9 us (8%)
  other arithmetic  15.9 us (5%)
  between operations  14.4 us (4%)
  local copies, waits for them, and re-layouts  12.7 us (4%)
    reduce_scatter x1, waiting for transfers between devices, shards(): lax.psum_scatter(terms, ('dp', 'mp'), scatter_dimension=0, tiled=True)  147 us
    all_to_all x1, waiting for transfers between devices, shards(): lax.all_to_all(outgoing, 'mp', split_axis=1, concat_axis=1, tiled=True)  40.4 us
    all_to_all x1, waiting for transfers between devices, shards(): lax.all_to_all(outgoing_grad, 'mp', split_axis=1, concat_axis=1, tiled=True)  35.1 us
    dot_general x15, matrix products, contract(): lax.dot_general(left, right, (((left_dim,), (right_dim,)), ((), ())), pre...  24.6 us
    all_to_all x1, starting transfers between devices, shards(): lax.all_to_all(outgoing, 'mp', split_axis=1, concat_axis=1, tiled=True)  12.3 us
    eq x1, other arithmetic, shards(): adjacency = (rowsel[:, None, :] == row_ids).astype(jnp.bfloat16)  9.7 us
    all_to_all x1, starting transfers between devices, shards(): lax.all_to_all(node_features, 'mp', split_axis=1, concat_axis=0, tiled=True)  7.39 us
  transfers between devices with their start and end apart: 5, of which 4 were waited for; matrix products, arithmetic and copies ran while one was open for 14% of the time, Pallas kernels for 0%

profile of v1, /device:TPU:0, one launch (start us, length us, event | category | flops | bytes accessed | tf_op | source)
XLA Modules:
  0.0 325.1 jit_solution(16609977738096543799)
XLA Ops:
  7.2 0.0 copy-start
  7.2 1.3 all_to_all.40
  8.5 0.8 copy.27
  9.3 7.4 %all-to-all-start = ((bf16[32,16,192]{2,0,1:T(8,128)(2,1)}), bf16[32,16,192]{2,0,1:T(8,128)(2,1)S(1)}, u32[]{:S(2)}, u32[]{:S(2)}) async-start(bf16[32,16,192]{2,0,1:T(8,128)(2,1)} %copy.27), calls=%async_computation | async-start | bytes 524288 | tf_op jit(solution)/shard_map/all_to_all | solution.py:59
  16.7 0.7 iota_compare_fusion.9
  17.4 0.7 convert_divide_fusion
  18.1 0.1 eq.95
  18.2 1.8 select_reduce_fusion
  20.0 0.0 copy-start.7
  20.0 9.7 %bitcast_compare_fusion = pred[3072,3072]{1,0:T(32,128)(4,1)} fusion(s32[3072]{0:T(1024)S(1)} %eq.95, s32[16,3072]{1,0:T(8,128)S(1)} %select_reduce_fusion), kind=kLoop, calls=%fused_computation | loop fusion | flops 9437184 | bytes 9646080 | tf_op jit(solution)/shard_map/layer_one_mean/eq | solution.py:49
  29.7 0.2 ge.17
  29.9 0.0 copy-done.7
  29.9 8.5 %fusion.1 = bf16[32,3072]{1,0:T(8,128)(2,1)S(1)} fusion(pred[3072,3072]{1,0:T(32,128)(4,1)} %bitcast_compare_fusion, bf16[32,3072]{1,0:T(8,128)(2,1)S(1)} %copy-done.7, f32[3072]{0:T(1024)S(1)} %convert_divide_fusion), kind=kOutput, calls=%fused_computation.6 | convolution fusion | flops 604176384 | bytes 9842688 | tf_op jit(solution)/shard_map/layer_one_mean/dot_general | solution.py:22
  38.4 0.4 convolution_convert_fusion.2
  38.9 0.1 reduce_max.12
  39.0 0.0 copy-start.1
  39.0 0.3 all_to_all.44
  39.3 0.8 copy.28
  40.1 0.1 copy.29
  40.2 0.0 copy-start.6
  40.3 0.0 all-to-all-done
  40.4 6.1 %all-to-all-start.1 = ((bf16[32,16,192]{2,0,1:T(8,128)(2,1)}), bf16[32,16,192]{2,0,1:T(8,128)(2,1)}, u32[]{:S(2)}, u32[]{:S(2)}) async-start(bf16[32,16,192]{2,0,1:T(8,128)(2,1)} %copy.28), calls=%async_computation.1 | async-start | bytes 524288 | tf_op jit(solution)/shard_map/all_to_all | solution.py:60
  46.5 0.1 dynamic_slice.27
  46.6 0.1 eq.112
  46.7 0.0 copy-done.1
  46.7 0.0 copy-done.6
  46.7 0.5 fusion.8
  47.2 0.0 copy-done
  47.2 2.2 convolution_convert_fusion
  49.4 2.5 copy.31
  51.9 4.6 %all-to-all-done.1 = bf16[32,16,192]{2,0,1:T(8,128)(2,1)} async-done(((bf16[32,16,192]{2,0,1:T(8,128)(2,1)}), bf16[32,16,192]{2,0,1:T(8,128)(2,1)}, u32[]{:S(2)}, u32[]{:S(2)}) %all-to-all-start.1) | async-done | bytes 196640 | tf_op jit(solution)/shard_map/all_to_all | solution.py:60
  56.5 3.7 %all-to-all-start.3 = ((bf16[512,16,144]{0,2,1:T(8,128)(2,1)}), bf16[512,16,144]{0,2,1:T(8,128)(2,1)S(1)}, u32[]{:S(2)}, u32[]{:S(2)}) async-start(bf16[512,16,144]{0,2,1:T(8,128)(2,1)} %bitcast.16), calls=%async_computation.3 | async-start | bytes 4718592 | tf_op jit(solution)/shard_map/all_to_all | solution.py:105
  60.3 0.0 copy-start.2
  60.3 0.8 dynamic-slice_bitcast_fusion
  61.1 1.3 fusion.11
  62.5 0.0 copy-start.8
  62.5 0.0 copy-done.2
  62.5 0.3 fusion.33
  62.8 1.3 fusion.18
  64.1 0.0 copy-done.8
  64.1 2.4 convolution_convert_fusion.1
  66.5 4.3 %copy.30 = bf16[512,2304]{0,1:T(8,128)(2,1)} copy(bf16[512,2304]{1,0:T(8,128)(2,1)} %convolution_convert_fusion.1) | data formatting | bytes 4718592 | tf_op jit(solution)/shard_map/convert_element_type | solution.py:93
  70.8 35.1 %all-to-all-done.3 = bf16[512,16,144]{0,2,1:T(8,128)(2,1)S(1)} async-done(((bf16[512,16,144]{0,2,1:T(8,128)(2,1)}), bf16[512,16,144]{0,2,1:T(8,128)(2,1)S(1)}, u32[]{:S(2)}, u32[]{:S(2)}) %all-to-all-start.3) | async-done | bytes 2359328 | tf_op jit(solution)/shard_map/all_to_all | solution.py:105
  105.9 12.3 %all-to-all-start.2 = ((bf16[512,16,144]{0,2,1:T(8,128)(2,1)}), bf16[512,16,144]{0,2,1:T(8,128)(2,1)}, u32[]{:S(2)}, u32[]{:S(2)}) async-start(bf16[512,16,144]{0,2,1:T(8,128)(2,1)} %bitcast.12), calls=%async_computation.2 | async-start | bytes 4718592 | tf_op jit(solution)/shard_map/all_to_all | solution.py:94
  118.2 0.0 reduce-scatter.2.cloned.1.call-start
  118.2 1.4 fusion.42
  119.6 0.0 copy-start.3
  119.6 2.0 convolution_bitcast_fusion.1
  121.6 0.0 copy-done.3
  121.6 0.4 fusion.29
  122.0 1.2 fusion.43
  123.2 0.3 convolution_bitcast_fusion
  123.5 40.4 %all-to-all-done.2 = bf16[512,16,144]{0,2,1:T(8,128)(2,1)} async-done(((bf16[512,16,144]{0,2,1:T(8,128)(2,1)}), bf16[512,16,144]{0,2,1:T(8,128)(2,1)}, u32[]{:S(2)}, u32[]{:S(2)}) %all-to-all-start.2) | async-done | bytes 2359328 | tf_op jit(solution)/shard_map/all_to_all | solution.py:94
  163.9 0.0 copy-start.5
  163.9 2.6 fusion.26
  166.5 0.3 fusion.44
  166.9 0.0 copy-done.5
  166.9 2.4 pad_maximum_fusion
  169.3 0.0 copy-start.4
  169.3 0.0 reduce-scatter.2.cloned.1.call-update
  169.3 1.2 copy-done.4
  170.5 0.3 fusion.39
  170.8 1.0 fusion.30
  171.7 146.5 %reduce-scatter.2.cloned.1.call-done = f32[64,512]{1,0:T(8,128)} async-done(((f32[2048,512]{1,0:T(8,128)}), f32[64,512]{1,0:T(8,128)}) %reduce-scatter.2.cloned.1.call-update) | async-done | bytes 131088 | tf_op jit(solution)/shard_map/reduce_scatter | solution.py:118
  (9 shorter events, 0.2 us)
Async XLA Ops:
  7.2 40.0 %copy-start = (bf16[192,512]{1,0:T(8,128)(2,1)S(1)}, bf16[192,512]{1,0:T(8,128)(2,1)}, u32[]{:S(2)}) copy-start(bf16[192,512]{1,0:T(8,128)(2,1)} %param.13) | copy-start | bytes 589828
  9.3 31.1 %all-to-all-start = ((bf16[32,16,192]{2,0,1:T(8,128)(2,1)}), bf16[32,16,192]{2,0,1:T(8,128)(2,1)S(1)}, u32[]{:S(2)}, u32[]{:S(2)}) async-start(bf16[32,16,192]{2,0,1:T(8,128)(2,1)} %copy.27), calls=%async_computation | async-start | bytes 524288 | tf_op jit(solution)/shard_map/all_to_all | solution.py:59
  20.0 9.9 %copy-start.7 = (bf16[32,3072]{1,0:T(8,128)(2,1)S(1)}, bf16[32,3072]{1,0:T(8,128)(2,1)}, u32[]{:S(2)}) copy-start(bf16[32,3072]{1,0:T(8,128)(2,1)} %param.7) | copy-start | bytes 589828
  39.0 7.7 %copy-start.1 = (s32[16,16,192]{2,1,0:T(8,128)}, s32[16,16,192]{2,1,0:T(8,128)S(1)}, u32[]{:S(2)}) copy-start(s32[16,16,192]{2,1,0:T(8,128)S(1)} %reduce_max.12) | copy-start | bytes 589828
  40.2 6.4 %copy-start.6 = (s32[256,192]{1,0:T(8,128)}, s32[256,192]{1,0:T(8,128)S(1)}, u32[]{:S(2)}) copy-start(s32[256,192]{1,0:T(8,128)S(1)} %copy.29) | copy-start | bytes 589828
  40.4 16.2 %all-to-all-start.1 = ((bf16[32,16,192]{2,0,1:T(8,128)(2,1)}), bf16[32,16,192]{2,0,1:T(8,128)(2,1)}, u32[]{:S(2)}, u32[]{:S(2)}) async-start(bf16[32,16,192]{2,0,1:T(8,128)(2,1)} %copy.28), calls=%async_computation.1 | async-start | bytes 524288 | tf_op jit(solution)/shard_map/all_to_all | solution.py:60
  56.5 49.3 %all-to-all-start.3 = ((bf16[512,16,144]{0,2,1:T(8,128)(2,1)}), bf16[512,16,144]{0,2,1:T(8,128)(2,1)S(1)}, u32[]{:S(2)}, u32[]{:S(2)}) async-start(bf16[512,16,144]{0,2,1:T(8,128)(2,1)} %bitcast.16), calls=%async_computation.3 | async-start | bytes 4718592 | tf_op jit(solution)/shard_map/all_to_all | solution.py:105
  60.3 2.2 copy-start.2
  62.5 1.7 copy-start.8
  105.9 58.0 %all-to-all-start.2 = ((bf16[512,16,144]{0,2,1:T(8,128)(2,1)}), bf16[512,16,144]{0,2,1:T(8,128)(2,1)}, u32[]{:S(2)}, u32[]{:S(2)}) async-start(bf16[512,16,144]{0,2,1:T(8,128)(2,1)} %bitcast.12), calls=%async_computation.2 | async-start | bytes 4718592 | tf_op jit(solution)/shard_map/all_to_all | solution.py:94
  118.2 200.1 %reduce-scatter.2.cloned.1.call-start = ((), (), s32[]{:S(2)}) async-start(), calls=%async_computation.5 | async-start | bytes 4325376 | tf_op jit(solution)/shard_map/reduce_scatter | solution.py:118
  119.6 2.0 copy-start.3
  163.9 3.0 copy-start.5
  169.3 1.2 copy-start.4
Sparse Core Ops, SparseCore 0:
  169.4 148.7 reduce-scatter.1

commit v2 on v1

--- a/solution.py
+++ b/solution.py
@@ -22,6 +22,29 @@
     return lax.dot_general(
         left, right, (((left_dim,), (right_dim,)), ((), ())), preferred_element_type=jnp.float32
     )
+
+
+def swap(values, axis, mask):
+    size = lax.axis_size(axis)
+    return lax.ppermute(values, axis, [(j, j ^ mask) for j in range(size)])
+
+
+def halving_scatter(terms, order):
+    n_mp = lax.axis_size("mp")
+    top = n_mp.bit_length() - 1
+    place = lax.axis_index("dp") * n_mp + lax.axis_index("mp")
+    rows = terms.shape[0] // (2 * n_mp)
+    bits = list(range(top, -1, -1))
+    values = terms.reshape((2,) * (top + 1) + (rows, terms.shape[1]))
+    for bit in order:
+        position = bits.index(bit)
+        mine = (place >> bit) & 1
+        keep = lax.dynamic_index_in_dim(values, mine, position, keepdims=False)
+        send = lax.dynamic_index_in_dim(values, 1 - mine, position, keepdims=False)
+        got = swap(send, "dp", 1) if bit == top else swap(send, "mp", 1 << bit)
+        values = keep + got
+        bits.pop(position)
+    return values.reshape(rows, terms.shape[1])
 
 
 def shards(
@@ -115,7 +138,11 @@
         ],
         axis=0,
     )
-    weight_grads = lax.psum_scatter(terms, ("dp", "mp"), scatter_dimension=0, tiled=True)
+    with jax.named_scope("weight_grad_sum"):
+        if lax.axis_size("dp") == 2 and devices == 16:
+            weight_grads = halving_scatter(terms, [0, 4, 1, 3, 2])
+        else:
+            weight_grads = lax.psum_scatter(terms, ("dp", "mp"), scatter_dimension=0, tiled=True)
     return (node_output, weight_grads)
 
 

time: 326 us -> 238 us (0.73)
  waiting for transfers between devices: 227 us -> 133 us
  starting transfers between devices: 29.5 us -> 43.4 us
  between operations: 14.4 us -> 1.13 us
    reduce_scatter x1 -> x0, waiting for transfers between devices: 147 us -> none  [shards(): lax.psum_scatter(terms, ('dp', 'mp'), scatter_dimension=0, tiled=True)]
    ppermute x0 -> x5, waiting for transfers between devices: none -> 52.8 us  [swap(): return lax.ppermute(values, axis, [(j, j ^ mask) for j in range(size)])]
    ppermute x0 -> x5, starting transfers between devices: none -> 13.9 us  [swap(): return lax.ppermute(values, axis, [(j, j ^ mask) for j in range(size)])]
    add x0 -> x5, other arithmetic: none -> 4.99 us  [halving_scatter(): values = keep + got]
  transfers between devices with their start and end apart: 5 -> 9, of which waited for: 4 -> 8; matrix products, arithmetic and copies ran while one was open for 14% -> 20% of each run, Pallas kernels for 0% -> 0%
where the time goes in v2:
time: 238 us; the launch traced here: 237 us
  waiting for transfers between devices  133 us (56%)
  starting transfers between devices  43.4 us (18%)
  matrix products  26.9 us (11%)
  other arithmetic  18.9 us (8%)
  local copies, waits for them, and re-layouts  13.9 us (6%)
    ppermute x5, waiting for transfers between devices, swap(): return lax.ppermute(values, axis, [(j, j ^ mask) for j in range(size)])  52.8 us
    all_to_all x1, waiting for transfers between devices, shards(): lax.all_to_all(outgoing, 'mp', split_axis=1, concat_axis=1, tiled=True)  40.4 us
    all_to_all x1, waiting for transfers between devices, shards(): lax.all_to_all(outgoing_grad, 'mp', split_axis=1, concat_axis=1, tiled=True)  35.1 us
    dot_general x15, matrix products, contract(): lax.dot_general(left, right, (((left_dim,), (right_dim,)), ((), ())), pre...  25.6 us
    ppermute x5, starting transfers between devices, swap(): return lax.ppermute(values, axis, [(j, j ^ mask) for j in range(size)])  13.9 us
    all_to_all x1, starting transfers between devices, shards(): lax.all_to_all(outgoing, 'mp', split_axis=1, concat_axis=1, tiled=True)  12.3 us
    eq x1, other arithmetic, shards(): adjacency = (rowsel[:, None, :] == row_ids).astype(jnp.bfloat16)  9.72 us
    all_to_all x1, starting transfers between devices, shards(): lax.all_to_all(node_features, 'mp', split_axis=1, concat_axis=0, tiled=True)  7.39 us
  transfers between devices with their start and end apart: 9, of which 8 were waited for; matrix products, arithmetic and copies ran while one was open for 20% of the time, Pallas kernels for 0%

profile of v2, /device:TPU:0, one launch (start us, length us, event | category | flops | bytes accessed | tf_op | source)
XLA Modules:
  0.0 237.1 jit_solution(4608742141640779869)
XLA Ops:
  0.6 0.0 copy-start
  0.6 1.3 all_to_all.40
  1.9 0.8 copy.27
  2.7 7.4 %all-to-all-start = ((bf16[32,16,192]{2,0,1:T(8,128)(2,1)}), bf16[32,16,192]{2,0,1:T(8,128)(2,1)S(1)}, u32[]{:S(2)}, u32[]{:S(2)}) async-start(bf16[32,16,192]{2,0,1:T(8,128)(2,1)} %copy.27), calls=%async_computation | async-start | bytes 524288 | tf_op jit(solution)/shard_map/all_to_all | solution.py:82
  10.1 0.7 iota_compare_fusion.9
  10.9 0.7 convert_divide_fusion
  11.6 0.1 eq.95
  11.6 1.8 select_reduce_fusion
  13.5 0.0 copy-start.9
  13.5 9.7 %bitcast_compare_fusion = pred[3072,3072]{1,0:T(32,128)(4,1)} fusion(s32[3072]{0:T(1024)S(1)} %eq.95, s32[16,3072]{1,0:T(8,128)S(1)} %select_reduce_fusion), kind=kLoop, calls=%fused_computation | loop fusion | flops 9437184 | bytes 9646080 | tf_op jit(solution)/shard_map/layer_one_mean/eq | solution.py:72
  23.2 0.2 ge.17
  23.4 8.5 %fusion.1 = bf16[32,3072]{1,0:T(8,128)(2,1)S(1)} fusion(pred[3072,3072]{1,0:T(32,128)(4,1)} %bitcast_compare_fusion, bf16[32,3072]{1,0:T(8,128)(2,1)S(1)} %copy-done.9, f32[3072]{0:T(1024)S(1)} %convert_divide_fusion), kind=kOutput, calls=%fused_computation.6 | convolution fusion | flops 604176384 | bytes 9842688 | tf_op jit(solution)/shard_map/layer_one_mean/dot_general | solution.py:22
  31.9 0.4 convolution_convert_fusion.2
  32.3 0.1 reduce_max.12
  32.5 0.3 all_to_all.44
  32.8 0.8 copy.28
  33.6 0.1 copy.29
  33.8 6.1 %all-to-all-start.1 = ((bf16[32,16,192]{2,0,1:T(8,128)(2,1)}), bf16[32,16,192]{2,0,1:T(8,128)(2,1)}, u32[]{:S(2)}, u32[]{:S(2)}) async-start(bf16[32,16,192]{2,0,1:T(8,128)(2,1)} %copy.28), calls=%async_computation.1 | async-start | bytes 524288 | tf_op jit(solution)/shard_map/all_to_all | solution.py:83
  39.9 0.0 copy-start.10
  40.0 0.1 dynamic_slice.62
  40.0 0.1 eq.112
  40.2 0.5 fusion.8
  40.6 2.2 convolution_convert_fusion
  42.9 2.5 %copy.31 = bf16[512,2304]{0,1:T(8,128)(2,1)} copy(bf16[512,2304]{1,0:T(8,128)(2,1)S(1)} %convolution_convert_fusion) | data formatting | bytes 4718592 | tf_op jit(solution)/shard_map/convert_element_type | solution.py:127
  45.4 4.6 %all-to-all-done.1 = bf16[32,16,192]{2,0,1:T(8,128)(2,1)} async-done(((bf16[32,16,192]{2,0,1:T(8,128)(2,1)}), bf16[32,16,192]{2,0,1:T(8,128)(2,1)}, u32[]{:S(2)}, u32[]{:S(2)}) %all-to-all-start.1) | async-done | bytes 196640 | tf_op jit(solution)/shard_map/all_to_all | solution.py:83
  50.0 3.7 %all-to-all-start.3 = ((bf16[512,16,144]{0,2,1:T(8,128)(2,1)}), bf16[512,16,144]{0,2,1:T(8,128)(2,1)S(1)}, u32[]{:S(2)}, u32[]{:S(2)}) async-start(bf16[512,16,144]{0,2,1:T(8,128)(2,1)} %bitcast.16), calls=%async_computation.3 | async-start | bytes 4718592 | tf_op jit(solution)/shard_map/all_to_all | solution.py:128
  53.7 0.0 copy-start.3
  53.8 0.8 dynamic-slice_bitcast_fusion.5
  54.6 1.3 fusion.11
  55.9 0.3 fusion.33
  56.2 1.3 fusion.18
  57.6 2.3 convolution_convert_fusion.1
  59.9 4.3 %copy.30 = bf16[512,2304]{0,1:T(8,128)(2,1)} copy(bf16[512,2304]{1,0:T(8,128)(2,1)} %convolution_convert_fusion.1) | data formatting | bytes 4718592 | tf_op jit(solution)/shard_map/convert_element_type | solution.py:116
  64.2 35.1 %all-to-all-done.3 = bf16[512,16,144]{0,2,1:T(8,128)(2,1)S(1)} async-done(((bf16[512,16,144]{0,2,1:T(8,128)(2,1)}), bf16[512,16,144]{0,2,1:T(8,128)(2,1)S(1)}, u32[]{:S(2)}, u32[]{:S(2)}) %all-to-all-start.3) | async-done | bytes 2359328 | tf_op jit(solution)/shard_map/all_to_all | solution.py:128
  99.3 12.3 %all-to-all-start.2 = ((bf16[512,16,144]{0,2,1:T(8,128)(2,1)}), bf16[512,16,144]{0,2,1:T(8,128)(2,1)}, u32[]{:S(2)}, u32[]{:S(2)}) async-start(bf16[512,16,144]{0,2,1:T(8,128)(2,1)} %bitcast.12), calls=%async_computation.2 | async-start | bytes 4718592 | tf_op jit(solution)/shard_map/all_to_all | solution.py:117
  111.6 1.3 fusion.42
  113.0 2.0 convolution_bitcast_fusion.1
  115.0 0.0 copy-start.11
  115.1 0.4 fusion.29
  115.4 1.2 fusion.43
  116.7 0.3 convolution_bitcast_fusion
  117.0 40.4 %all-to-all-done.2 = bf16[512,16,144]{0,2,1:T(8,128)(2,1)} async-done(((bf16[512,16,144]{0,2,1:T(8,128)(2,1)}), bf16[512,16,144]{0,2,1:T(8,128)(2,1)}, u32[]{:S(2)}, u32[]{:S(2)}) %all-to-all-start.2) | async-done | bytes 2359328 | tf_op jit(solution)/shard_map/all_to_all | solution.py:117
  157.4 2.6 %fusion.26 = bf16[512,192]{0,1:T(8,128)(2,1)S(1)} fusion(bf16[512,16,144]{0,2,1:T(8,128)(2,1)} %all-to-all-done.2, s32[16,192]{1,0:T(8,128)S(1)} %bitcast.94, pred[16,192]{1,0:T(8,128)(4,1)S(1)} %bitcast.96, f32[192]{0:T(256)S(1)} %copy-done.13), kind=kOutput, calls=%fused_computation.37 | convolution fusion | flops 454066176 | bytes 2572032 | tf_op jit(solution)/shard_map/dot_general | solution.py:22
  160.0 0.3 fusion.44
  160.3 0.4 pad_maximum_fusion
  160.8 1.9 copy-done.1
  162.7 0.3 dynamic-slice_bitcast_fusion
  163.0 0.8 collective-permute-start
  163.8 3.9 %collective-permute-done = f32[2,2,2,2,64,512]{5,4,3,2,1,0:T(8,128)} collective-permute-done((f32[2,2,2,2,64,512]{5,4,3,2,1,0:T(8,128)S(1)}, f32[2,2,2,2,64,512]{5,4,3,2,1,0:T(8,128)}, u32[]{:S(2)}, u32[]{:S(2)}) %collective-permute-start) | collective-permute-done | bytes 2097184 | tf_op jit(solution)/shard_map/weight_grad_sum/ppermute | solution.py:29
  167.7 2.8 %bitcast_add_fusion = f32[2,2,2,2,64,512]{5,4,3,2,1,0:T(8,128)S(1)} fusion(f32[2,2,2,2,64,512]{5,4,3,2,1,0:T(8,128)} %collective-permute-done, f32[2,2,2,2,2,64,512]{6,5,4,3,2,1,0:T(8,128)} %bitcast.88, s32[]{:T(128)S(6)} %select_n.56), kind=kLoop, calls=%fused_computation.16 | loop fusion | flops 524288 | bytes 6291460 | tf_op jit(solution)/shard_map/weight_grad_sum/add | solution.py:45
  170.5 0.1 dynamic-slice_bitcast_fusion.1
  170.6 1.6 collective-permute-start.1
  172.2 24.0 %collective-permute-done.1 = f32[2,2,2,64,512]{4,3,2,1,0:T(8,128)} collective-permute-done((f32[2,2,2,64,512]{4,3,2,1,0:T(8,128)S(1)}, f32[2,2,2,64,512]{4,3,2,1,0:T(8,128)}, u32[]{:S(2)}, u32[]{:S(2)}) %collective-permute-start.1) | collective-permute-done | bytes 1048608 | tf_op jit(solution)/shard_map/weight_grad_sum/ppermute | solution.py:29
  196.2 1.4 bitcast_add_fusion.1
  197.7 3.8 %collective-permute-start.2 = (f32[2,2,64,512]{3,2,1,0:T(8,128)S(1)}, f32[2,2,64,512]{3,2,1,0:T(8,128)S(1)}, u32[]{:S(2)}, u32[]{:S(2)}) collective-permute-start(f32[2,2,64,512]{3,2,1,0:T(8,128)S(1)} %dynamic-slice_bitcast_fusion.2), channel_id=1, source_target_pairs={{0,2},{1,3},{2,0},{3,1},{4,6},{5,7},{6,4},{7,5},{8,10},{9,11},{10,... | collective-permute-start | bytes 1572872 | tf_op jit(solution)/shard_map/weight_grad_sum/ppermute | solution.py:29
  201.5 11.6 %collective-permute-done.2 = f32[2,2,64,512]{3,2,1,0:T(8,128)S(1)} collective-permute-done((f32[2,2,64,512]{3,2,1,0:T(8,128)S(1)}, f32[2,2,64,512]{3,2,1,0:T(8,128)S(1)}, u32[]{:S(2)}, u32[]{:S(2)}) %collective-permute-start.2) | collective-permute-done | bytes 524320 | tf_op jit(solution)/shard_map/weight_grad_sum/ppermute | solution.py:29
  213.1 0.1 bitcast_add_fusion.2
  213.3 7.6 %collective-permute-start.3 = (f32[2,64,512]{2,1,0:T(8,128)S(1)}, f32[2,64,512]{2,1,0:T(8,128)S(1)}, u32[]{:S(2)}, u32[]{:S(2)}) collective-permute-start(f32[2,64,512]{2,1,0:T(8,128)S(1)} %dynamic-slice_bitcast_fusion.3), channel_id=1, source_target_pairs={{0,8},{1,9},{2,10},{3,11},{4,12},{5,13},{6,14},{7,15},{8,0},{9,1},... | collective-permute-start | bytes 786440 | tf_op jit(solution)/shard_map/weight_grad_sum/ppermute | solution.py:29
  220.9 1.3 fusion.39
  222.2 9.2 %collective-permute-done.3 = f32[2,64,512]{2,1,0:T(8,128)S(1)} collective-permute-done((f32[2,64,512]{2,1,0:T(8,128)S(1)}, f32[2,64,512]{2,1,0:T(8,128)S(1)}, u32[]{:S(2)}, u32[]{:S(2)}) %collective-permute-start.3) | collective-permute-done | bytes 262176 | tf_op jit(solution)/shard_map/weight_grad_sum/ppermute | solution.py:29
  231.4 0.1 collective-permute-start.4
  231.5 1.0 fusion.30
  232.5 4.0 %collective-permute-done.4 = f32[64,512]{1,0:T(8,128)S(1)} collective-permute-done((f32[64,512]{1,0:T(8,128)S(1)}, f32[64,512]{1,0:T(8,128)S(1)}, u32[]{:S(2)}, u32[]{:S(2)}) %collective-permute-start.4) | collective-permute-done | bytes 131104 | tf_op jit(solution)/shard_map/weight_grad_sum/ppermute | solution.py:29
  236.5 0.7 bitcast_add_fusion.4
  (38 shorter events, 0.3 us)
Async XLA Ops:
  0.6 40.0 %copy-start = (bf16[192,512]{1,0:T(8,128)(2,1)S(1)}, bf16[192,512]{1,0:T(8,128)(2,1)}, u32[]{:S(2)}) copy-start(bf16[192,512]{1,0:T(8,128)(2,1)} %param.13) | copy-start | bytes 589828
  2.7 31.1 %all-to-all-start = ((bf16[32,16,192]{2,0,1:T(8,128)(2,1)}), bf16[32,16,192]{2,0,1:T(8,128)(2,1)S(1)}, u32[]{:S(2)}, u32[]{:S(2)}) async-start(bf16[32,16,192]{2,0,1:T(8,128)(2,1)} %copy.27), calls=%async_computation | async-start | bytes 524288 | tf_op jit(solution)/shard_map/all_to_all | solution.py:82
  13.5 9.9 %copy-start.9 = (bf16[32,3072]{1,0:T(8,128)(2,1)S(1)}, bf16[32,3072]{1,0:T(8,128)(2,1)}, u32[]{:S(2)}) copy-start(bf16[32,3072]{1,0:T(8,128)(2,1)} %param.7) | copy-start | bytes 589828
  32.5 7.7 %copy-start.2 = (s32[16,16,192]{2,1,0:T(8,128)}, s32[16,16,192]{2,1,0:T(8,128)S(1)}, u32[]{:S(2)}) copy-start(s32[16,16,192]{2,1,0:T(8,128)S(1)} %reduce_max.12) | copy-start | bytes 589828
  33.7 6.4 %copy-start.8 = (s32[256,192]{1,0:T(8,128)}, s32[256,192]{1,0:T(8,128)S(1)}, u32[]{:S(2)}) copy-start(s32[256,192]{1,0:T(8,128)S(1)} %copy.29) | copy-start | bytes 589828
  33.8 16.2 %all-to-all-start.1 = ((bf16[32,16,192]{2,0,1:T(8,128)(2,1)}), bf16[32,16,192]{2,0,1:T(8,128)(2,1)}, u32[]{:S(2)}, u32[]{:S(2)}) async-start(bf16[32,16,192]{2,0,1:T(8,128)(2,1)} %copy.28), calls=%async_computation.1 | async-start | bytes 524288 | tf_op jit(solution)/shard_map/all_to_all | solution.py:83
  39.9 5.4 %copy-start.10 = (pred[16,1,192]{2,0,1:T(8,128)(4,1)}, pred[16,1,192]{2,0,1:T(8,128)(4,1)S(1)}, u32[]{:S(2)}) copy-start(pred[16,1,192]{2,0,1:T(8,128)(4,1)S(1)} %copy.37) | copy-start | bytes 9220
  40.0 5.3 %copy-start.12 = (f32[192]{0:T(256)}, f32[192]{0:T(256)S(1)}, u32[]{:S(2)}) copy-start(f32[192]{0:T(256)S(1)} %dynamic_slice.62) | copy-start | bytes 2308
  50.0 49.3 %all-to-all-start.3 = ((bf16[512,16,144]{0,2,1:T(8,128)(2,1)}), bf16[512,16,144]{0,2,1:T(8,128)(2,1)S(1)}, u32[]{:S(2)}, u32[]{:S(2)}) async-start(bf16[512,16,144]{0,2,1:T(8,128)(2,1)} %bitcast.16), calls=%async_computation.3 | async-start | bytes 4718592 | tf_op jit(solution)/shard_map/all_to_all | solution.py:128
  53.7 2.2 copy-start.3
  55.9 1.7 copy-start.14
  57.6 57.5 %copy-start.7 = (f32[512,192]{0,1:T(8,128)}, f32[512,192]{0,1:T(8,128)S(1)}, u32[]{:S(2)}) copy-start(f32[512,192]{0,1:T(8,128)S(1)} %fusion.18) | copy-start | bytes 1179652
  99.3 58.0 %all-to-all-start.2 = ((bf16[512,16,144]{0,2,1:T(8,128)(2,1)}), bf16[512,16,144]{0,2,1:T(8,128)(2,1)}, u32[]{:S(2)}, u32[]{:S(2)}) async-start(bf16[512,16,144]{0,2,1:T(8,128)(2,1)} %bitcast.12), calls=%async_computation.2 | async-start | bytes 4718592 | tf_op jit(solution)/shard_map/all_to_all | solution.py:117
  113.0 2.0 copy-start.4
  115.0 42.3 %copy-start.11 = (pred[16,1,192]{2,0,1:T(8,128)(4,1)S(1)}, pred[16,1,192]{2,0,1:T(8,128)(4,1)}, u32[]{:S(2)}) copy-start(pred[16,1,192]{2,0,1:T(8,128)(4,1)} %copy-done.10) | copy-start | bytes 9220
  115.0 42.3 %copy-start.13 = (f32[192]{0:T(256)S(1)}, f32[192]{0:T(256)}, u32[]{:S(2)}) copy-start(f32[192]{0:T(256)} %copy-done.12) | copy-start | bytes 2308
  157.4 3.0 %copy-start.6 = (f32[512,512]{1,0:T(8,128)S(1)}, f32[512,512]{1,0:T(8,128)}, u32[]{:S(2)}) copy-start(f32[512,512]{1,0:T(8,128)} %fusion.42) | copy-start | bytes 3145732
  160.8 1.9 copy-start.1
  163.0 4.8 %collective-permute-start = (f32[2,2,2,2,64,512]{5,4,3,2,1,0:T(8,128)S(1)}, f32[2,2,2,2,64,512]{5,4,3,2,1,0:T(8,128)}, u32[]{:S(2)}, u32[]{:S(2)}) collective-permute-start(f32[2,2,2,2,64,512]{5,4,3,2,1,0:T(8,128)S(1)} %dynamic-slice_bitcast_fusion), channel_id=1, source_target_pairs={{0,1},{1,0},{2,3},{3,2},{4,5},{5,4},{6,7},{7,6},{8,9},{9,8},{10,11... | collective-permute-start | bytes 6291464 | tf_op jit(solution)/shard_map/weight_grad_sum/ppermute | solution.py:29
  170.6 25.6 %collective-permute-start.1 = (f32[2,2,2,64,512]{4,3,2,1,0:T(8,128)S(1)}, f32[2,2,2,64,512]{4,3,2,1,0:T(8,128)}, u32[]{:S(2)}, u32[]{:S(2)}) collective-permute-start(f32[2,2,2,64,512]{4,3,2,1,0:T(8,128)S(1)} %dynamic-slice_bitcast_fusion.1), channel_id=1, source_target_pairs={{0,16},{16,0},{1,17},{17,1},{2,18},{18,2},{3,19},{19,3},{4,20},{20... | collective-permute-start | bytes 3145736 | tf_op jit(solution)/shard_map/weight_grad_sum/ppermute | solution.py:29
  197.6 23.2 %copy-start.5 = (bf16[1024,512]{1,0:T(8,128)(2,1)S(1)}, bf16[1024,512]{1,0:T(8,128)(2,1)}, u32[]{:S(2)}) copy-start(bf16[1024,512]{1,0:T(8,128)(2,1)} %param.9) | copy-start | bytes 3145732
  197.7 15.4 %collective-permute-start.2 = (f32[2,2,64,512]{3,2,1,0:T(8,128)S(1)}, f32[2,2,64,512]{3,2,1,0:T(8,128)S(1)}, u32[]{:S(2)}, u32[]{:S(2)}) collective-permute-start(f32[2,2,64,512]{3,2,1,0:T(8,128)S(1)} %dynamic-slice_bitcast_fusion.2), channel_id=1, source_target_pairs={{0,2},{1,3},{2,0},{3,1},{4,6},{5,7},{6,4},{7,5},{8,10},{9,11},{10,... | collective-permute-start | bytes 1572872 | tf_op jit(solution)/shard_map/weight_grad_sum/ppermute | solution.py:29
  213.3 18.1 %collective-permute-start.3 = (f32[2,64,512]{2,1,0:T(8,128)S(1)}, f32[2,64,512]{2,1,0:T(8,128)S(1)}, u32[]{:S(2)}, u32[]{:S(2)}) collective-permute-start(f32[2,64,512]{2,1,0:T(8,128)S(1)} %dynamic-slice_bitcast_fusion.3), channel_id=1, source_target_pairs={{0,8},{1,9},{2,10},{3,11},{4,12},{5,13},{6,14},{7,15},{8,0},{9,1},... | collective-permute-start | bytes 786440 | tf_op jit(solution)/shard_map/weight_grad_sum/ppermute | solution.py:29
  231.4 5.0 %collective-permute-start.4 = (f32[64,512]{1,0:T(8,128)S(1)}, f32[64,512]{1,0:T(8,128)S(1)}, u32[]{:S(2)}, u32[]{:S(2)}) collective-permute-start(f32[64,512]{1,0:T(8,128)S(1)} %dynamic-slice_bitcast_fusion.4), channel_id=1, source_target_pairs={{0,4},{1,5},{2,6},{3,7},{4,0},{5,1},{6,2},{7,3},{8,12},{9,13},{10,... | collective-permute-start | bytes 393224 | tf_op jit(solution)/shard_map/weight_grad_sum/ppermute | solution.py:29

commit v3 on v2

v3 whole, which is shorter than its diff:
```python
import jax
import jax.numpy as jnp
from jax import lax
from jax.sharding import PartitionSpec as P


def column_mean(table, indices, live, inverse):
    total = jnp.zeros((table.shape[0], indices.shape[1]), jnp.float32)
    for slot_index in range(indices.shape[0]):
        picked = jnp.take(table, indices[slot_index], axis=1)
        kept = jnp.where(live[slot_index][None, :], picked, jnp.zeros_like(picked))
        total = total + kept.astype(jnp.float32)
    return (total * inverse[None, :]).astype(jnp.bfloat16)


def silu_slope(values):
    sigmoid = jax.nn.sigmoid(values)
    return sigmoid * (1.0 + values * (1.0 - sigmoid))


def contract(left, right, left_dim, right_dim):
    return lax.dot_general(
        left, right, (((left_dim,), (right_dim,)), ((), ())), preferred_element_type=jnp.float32
    )


def swap(values, axis, mask):
    size = lax.axis_size(axis)
    return lax.ppermute(values, axis, [(j, j ^ mask) for j in range(size)])


def halving_scatter(terms, order):
    n_mp = lax.axis_size("mp")
    top = n_mp.bit_length() - 1
    place = lax.axis_index("dp") * n_mp + lax.axis_index("mp")
    rows = terms.shape[0] // (2 * n_mp)
    bits = list(range(top, -1, -1))
    values = terms.reshape((2,) * (top + 1) + (rows, terms.shape[1]))
    for bit in order:
        position = bits.index(bit)
        mine = (place >> bit) & 1
        keep = lax.dynamic_index_in_dim(values, mine, position, keepdims=False)
        send = lax.dynamic_index_in_dim(values, 1 - mine, position, keepdims=False)
        got = swap(send, "dp", 1) if bit == top else swap(send, "mp", 1 << bit)
        values = keep + got
        bits.pop(position)
    return values.reshape(rows, terms.shape[1])


def doubling_gather(rows, order):
    own = lax.axis_index("mp")
    current = rows
    for step, bit in enumerate(order):
        got = swap(current, "mp", 1 << bit)
        low = jnp.where((own >> bit) & 1 == 0, current, got)
        high = jnp.where((own >> bit) & 1 == 0, got, current)
        current = jnp.stack([low, high], axis=step)
    return current.reshape(-1, rows.shape[-1])


def shards(
    node_features, weights_one, weights_two, neighbor_owner, neighbor_row, neighbor_count, cotangent
):
    devices = lax.axis_size("mp")
    own_index = lax.axis_index("mp")
    node_dev = cotangent.shape[0]
    all_nodes = neighbor_owner.shape[0]
    fanout = neighbor_owner.shape[1]
    feat_width = weights_one.shape[0] // 2
    hidden = weights_one.shape[1]
    live = lax.broadcasted_iota(jnp.int32, (all_nodes, fanout), 1) < neighbor_count[:, None]
    inverse_all = 1.0 / neighbor_count.astype(jnp.float32)

    owner_ids = lax.broadcasted_iota(jnp.int32, (devices, 1, 1), 0)
    match = (neighbor_owner[None, :, :] == owner_ids) & live[None, :, :]
    rowsel = jnp.max(jnp.where(match, neighbor_row[None, :, :], -1), axis=2)

    with jax.named_scope("layer_one_mean"):
        if all_nodes * all_nodes <= 4096 * 4096:
            row_ids = lax.broadcasted_iota(jnp.int32, (1, node_dev, 1), 1)
            adjacency = (rowsel[:, None, :] == row_ids).astype(jnp.bfloat16)
            adjacency = adjacency.reshape(devices * node_dev, all_nodes)
            summed = contract(node_features, adjacency, 1, 0)
            agg_one_cols = (summed * inverse_all[None, :]).astype(jnp.bfloat16)
        else:
            owner_slots = neighbor_owner.T
            global_ids = owner_slots * node_dev + neighbor_row.T
            agg_one_cols = column_mean(node_features, global_ids, live.T, inverse_all)

    own_feats, own_agg_one = (
        lax.all_to_all(node_features, "mp", split_axis=1, concat_axis=0, tiled=True),
        lax.all_to_all(agg_one_cols, "mp", split_axis=1, concat_axis=0, tiled=True),
    )
    self_two = weights_two[:hidden]
    neigh_two = weights_two[hidden:]
    own_inverse = lax.dynamic_slice_in_dim(inverse_all, own_index * node_dev, node_dev, 0)
    order = list(range(devices.bit_length() - 2, -1, -1))

    with jax.named_scope("neighbor_tables"):
        row_ids = lax.broadcasted_iota(jnp.int32, (1, node_dev, 1), 1)
        own_sel = lax.dynamic_slice_in_dim(rowsel, own_index * node_dev, node_dev, 1)
        own_edges = (own_sel[:, None, :] == row_ids).astype(jnp.bfloat16)
        own_edges = own_edges.reshape(devices * node_dev, node_dev)
        mine_sel = lax.dynamic_index_in_dim(rowsel, own_index, 0, keepdims=False)
        named_by = (mine_sel[:, None] == row_ids.reshape(1, node_dev)).astype(jnp.bfloat16)

    down_neigh = (contract(cotangent, neigh_two, 1, 1) * own_inverse[:, None]).astype(jnp.bfloat16)
    down_all = doubling_gather(down_neigh, order)

    pre_one = contract(own_feats, weights_one[:feat_width], 0, 0) + contract(
        own_agg_one, weights_one[feat_width:], 0, 0
    )
    hidden_one = jax.nn.silu(pre_one).astype(jnp.bfloat16)
    hidden_all = doubling_gather(hidden_one, order)
    total = contract(own_edges, hidden_all, 0, 0)
    agg_two = (total * own_inverse[:, None]).astype(jnp.bfloat16)
    node_output = (
        contract(hidden_one, self_two, 1, 0) + contract(agg_two, neigh_two, 1, 0)
    ).astype(jnp.bfloat16)
    down_self = contract(cotangent, self_two, 1, 1)
    neighbor_sum = contract(named_by, down_all, 0, 0)
    grad_hidden = down_self + neighbor_sum
    grad_pre = (grad_hidden * silu_slope(pre_one)).astype(jnp.bfloat16)
    terms = jnp.concatenate(
        [
            contract(own_feats, grad_pre, 1, 0),
            contract(own_agg_one, grad_pre, 1, 0),
            contract(hidden_one, cotangent, 0, 0),
            contract(agg_two, cotangent, 0, 0),
        ],
        axis=0,
    )
    with jax.named_scope("weight_grad_sum"):
        if lax.axis_size("dp") == 2 and devices == 16:
            weight_grads = halving_scatter(terms, [0, 4, 1, 3, 2])
        else:
            weight_grads = lax.psum_scatter(terms, ("dp", "mp"), scatter_dimension=0, tiled=True)
    return (node_output, weight_grads)


def solution(mesh):
    in_specs = (
        P("mp", "dp"),
        P(),
        P(),
        P("dp", None),
        P("dp", None),
        P("dp"),
        P(("dp", "mp"), None),
    )
    out_specs = (P(("dp", "mp"), None), P(("dp", "mp"), None))
    return jax.shard_map(shards, mesh=mesh, in_specs=in_specs, out_specs=out_specs, check_vma=False)
```

time: 238 us -> 197 us (0.83)
  waiting for transfers between devices: 133 us -> 111 us
  starting transfers between devices: 43.4 us -> 31.8 us
  matrix products: 26.9 us -> 18.8 us
  other arithmetic: 18.9 us -> 24.7 us
  local copies, waits for them, and re-layouts: 13.9 us -> 8.59 us
    all_to_all x2 -> x0, waiting for transfers between devices: 75.5 us -> none  [the longest x1 40.4 us: shards(): lax.all_to_all(outgoing, 'mp', split_axis=1, concat_axis=1, tiled=True)]
    ppermute x5 -> x13, waiting for transfers between devices: 52.8 us -> 105 us  [swap(): return lax.ppermute(values, axis, [(j, j ^ mask) for j in range(size)])]
    all_to_all x2 -> x0, starting transfers between devices: 16 us -> none  [the longest x1 12.3 us: shards(): lax.all_to_all(outgoing, 'mp', split_axis=1, concat_axis=1, tiled=True)]
    convert_element_type x3 -> x0, local copies, waits for them, and re-layouts: 6.86 us -> none  [the longest x1 4.27 us: shards(): outgoing = contract(hidden_one, asked, 1, 1).astype(jnp.bfloat16)]
    dot_general x15 -> x13, matrix products: 25.6 us -> 18.8 us  [contract(): lax.dot_general(left, right, (((left_dim,), (right_dim,)), ((), ())), pre...]
    another operation x0 -> x15, other arithmetic: none -> 5.92 us  [doubling_gather(): current = jnp.stack([low, high], axis=step)]
    ppermute x5 -> x13, starting transfers between devices: 13.9 us -> 18.4 us  [swap(): return lax.ppermute(values, axis, [(j, j ^ mask) for j in range(size)])]
  transfers between devices with their start and end apart: 9 -> 15, of which waited for: 8 -> 12; matrix products, arithmetic and copies ran while one was open for 20% -> 18% of each run, Pallas kernels for 0% -> 0%
where the time goes in v3:
time: 197 us; the launch traced here: 196 us
  waiting for transfers between devices  111 us (56%)
  starting transfers between devices  31.8 us (16%)
  other arithmetic  24.7 us (13%)
  matrix products  18.8 us (10%)
  local copies, waits for them, and re-layouts  8.59 us (4%)
    ppermute x13, waiting for transfers between devices, swap(): return lax.ppermute(values, axis, [(j, j ^ mask) for j in range(size)])  105 us
    dot_general x13, matrix products, contract(): lax.dot_general(left, right, (((left_dim,), (right_dim,)), ((), ())), pre...  18.8 us
    ppermute x13, starting transfers between devices, swap(): return lax.ppermute(values, axis, [(j, j ^ mask) for j in range(size)])  18.4 us
    eq x1, other arithmetic, shards(): adjacency = (rowsel[:, None, :] == row_ids).astype(jnp.bfloat16)  9.7 us
    all_to_all x1, starting transfers between devices, shards(): lax.all_to_all(node_features, 'mp', split_axis=1, concat_axis=0, tiled=True)  7.39 us
    all_to_all x1, starting transfers between devices, shards(): lax.all_to_all(agg_one_cols, 'mp', split_axis=1, concat_axis=0, tiled=True)  6 us
    all_to_all x1, waiting for transfers between devices, shards(): lax.all_to_all(agg_one_cols, 'mp', split_axis=1, concat_axis=0, tiled=True)  5.95 us
    another operation x15, other arithmetic, doubling_gather(): current = jnp.stack([low, high], axis=step)  5.92 us
  transfers between devices with their start and end apart: 15, of which 12 were waited for; matrix products, arithmetic and copies ran while one was open for 18% of the time, Pallas kernels for 0%

profile of v3, /device:TPU:0, one launch (start us, length us, event | category | flops | bytes accessed | tf_op | source)
XLA Modules:
  0.0 196.3 jit_solution(13458386725401083699)
XLA Ops:
  0.6 1.3 all_to_all.28
  1.9 0.8 copy.17
  2.7 7.4 %all-to-all-start = ((bf16[32,16,192]{2,0,1:T(8,128)(2,1)}), bf16[32,16,192]{2,0,1:T(8,128)(2,1)S(1)}, u32[]{:S(2)}, u32[]{:S(2)}) async-start(bf16[32,16,192]{2,0,1:T(8,128)(2,1)} %copy.17), calls=%async_computation | async-start | bytes 524288 | tf_op jit(solution)/shard_map/all_to_all | solution.py:91
  10.1 0.7 convert_divide_fusion
  10.8 0.7 iota_compare_fusion.10
  11.7 1.8 select_reduce_fusion
  13.5 9.7 %bitcast_compare_fusion = pred[3072,3072]{1,0:T(32,128)(4,1)} fusion(s32[3072]{0:T(1024)S(1)} %eq.101, s32[16,3072]{1,0:T(8,128)S(1)} %select_reduce_fusion), kind=kLoop, calls=%fused_computation | loop fusion | flops 9437184 | bytes 9646080 | tf_op jit(solution)/shard_map/layer_one_mean/eq | solution.py:81
  23.2 8.6 %fusion.1 = bf16[32,3072]{1,0:T(8,128)(2,1)S(1)} fusion(pred[3072,3072]{1,0:T(32,128)(4,1)} %bitcast_compare_fusion, bf16[32,3072]{1,0:T(8,128)(2,1)S(1)} %copy-done.6, f32[3072]{0:T(1024)S(1)} %convert_divide_fusion), kind=kOutput, calls=%fused_computation.4 | convolution fusion | flops 604176384 | bytes 9842688 | tf_op jit(solution)/shard_map/layer_one_mean/dot_general | solution.py:22
  31.9 0.5 all_to_all.32
  32.4 0.8 copy.18
  33.2 6.0 %all-to-all-start.1 = ((bf16[32,16,192]{2,0,1:T(8,128)(2,1)}), bf16[32,16,192]{2,0,1:T(8,128)(2,1)S(1)}, u32[]{:S(2)}, u32[]{:S(2)}) async-start(bf16[32,16,192]{2,0,1:T(8,128)(2,1)} %copy.18), calls=%async_computation.1 | async-start | bytes 524288 | tf_op jit(solution)/shard_map/all_to_all | solution.py:92
  39.2 0.3 fusion.10
  39.5 2.9 %collective-permute-start.4 = (bf16[192,512]{1,0:T(8,128)(2,1)S(1)}, bf16[192,512]{1,0:T(8,128)(2,1)S(1)}, u32[]{:S(2)}, u32[]{:S(2)}) collective-permute-start(bf16[192,512]{1,0:T(8,128)(2,1)S(1)} %fusion.10), channel_id=1, source_target_pairs={{0,8},{1,9},{2,10},{3,11},{4,12},{5,13},{6,14},{7,15},{8,0},{9,1},... | collective-permute-start | bytes 589832 | tf_op jit(solution)/shard_map/ppermute | solution.py:29
  42.4 1.3 fusion.12
  43.7 5.9 %all-to-all-done.1 = bf16[32,16,192]{2,0,1:T(8,128)(2,1)S(1)} async-done(((bf16[32,16,192]{2,0,1:T(8,128)(2,1)}), bf16[32,16,192]{2,0,1:T(8,128)(2,1)S(1)}, u32[]{:S(2)}, u32[]{:S(2)}) %all-to-all-start.1) | async-done | bytes 196640 | tf_op jit(solution)/shard_map/all_to_all | solution.py:92
  49.7 2.1 %multiply_convert_fusion = (bf16[192,512]{1,0:T(8,128)(2,1)S(1)}, f32[192,512]{1,0:T(8,128)}) fusion(f32[192,512]{1,0:T(8,128)S(1)} %fusion.12, bf16[512,192]{1,0:T(8,128)(2,1)S(1)} %bitcast.94, bf16[1024,512]{1,0:T(8,128)(2,1)} %param.8), kind=kOutput, calls=%fused_computation.58 | convolution fusion | flops 101253120 | bytes 1703936 | tf_op jit(solution)/shard_map/dot_general | solution.py:22
  51.8 5.1 %collective-permute-start = (bf16[192,512]{1,0:T(8,128)(2,1)S(1)}, bf16[192,512]{1,0:T(8,128)(2,1)S(1)}, u32[]{:S(2)}, u32[]{:S(2)}) collective-permute-start(bf16[192,512]{1,0:T(8,128)(2,1)S(1)} %get-tuple-element.18), channel_id=1, source_target_pairs={{0,8},{1,9},{2,10},{3,11},{4,12},{5,13},{6,14},{7,15},{8,0},{9,1},... | collective-permute-start | bytes 589832 | tf_op jit(solution)/shard_map/ppermute | solution.py:29
  56.9 0.5 collective-permute-done.4
  57.4 8.3 %collective-permute-done = bf16[192,512]{1,0:T(8,128)(2,1)S(1)} collective-permute-done((bf16[192,512]{1,0:T(8,128)(2,1)S(1)}, bf16[192,512]{1,0:T(8,128)(2,1)S(1)}, u32[]{:S(2)}, u32[]{:S(2)}) %collective-permute-start) | collective-permute-done | bytes 196640 | tf_op jit(solution)/shard_map/ppermute | solution.py:29
  65.8 0.4 collective-permute-start.5
  66.2 9.9 %collective-permute-done.5 = bf16[2,192,512]{2,1,0:T(8,128)(2,1)} collective-permute-done((bf16[2,192,512]{2,1,0:T(8,128)(2,1)S(1)}, bf16[2,192,512]{2,1,0:T(8,128)(2,1)}, u32[]{:S(2)}, u32[]{:S(2)}) %collective-permute-start.5) | collective-permute-done | bytes 393248 | tf_op jit(solution)/shard_map/ppermute | solution.py:29
  76.1 1.1 select_bitcast_fusion.9
  77.2 1.0 pad_maximum_fusion.6
  78.1 2.2 %collective-permute-start.6 = (bf16[2,2,192,512]{3,2,0,1:T(8,128)(2,1)}, bf16[2,2,192,512]{3,2,0,1:T(8,128)(2,1)}, u32[]{:S(2)}, u32[]{:S(2)}) collective-permute-start(bf16[2,2,192,512]{3,2,0,1:T(8,128)(2,1)} %pad_maximum_fusion.6), channel_id=1, source_target_pairs={{0,2},{1,3},{2,0},{3,1},{4,6},{5,7},{6,4},{7,5},{8,10},{9,11},{10,... | collective-permute-start | bytes 2359304 | tf_op jit(solution)/shard_map/ppermute | solution.py:29
  80.3 0.4 collective-permute-start.1
  80.7 0.8 constant_dynamic-slice_fusion.1
  81.5 9.8 %collective-permute-done.1 = bf16[2,192,512]{2,1,0:T(8,128)(2,1)} collective-permute-done((bf16[2,192,512]{2,1,0:T(8,128)(2,1)S(1)}, bf16[2,192,512]{2,1,0:T(8,128)(2,1)}, u32[]{:S(2)}, u32[]{:S(2)}) %collective-permute-start.1) | collective-permute-done | bytes 393248 | tf_op jit(solution)/shard_map/ppermute | solution.py:29
  91.2 1.1 select_bitcast_fusion.11
  92.3 6.0 %collective-permute-done.6 = bf16[2,2,192,512]{3,2,0,1:T(8,128)(2,1)} collective-permute-done((bf16[2,2,192,512]{3,2,0,1:T(8,128)(2,1)}, bf16[2,2,192,512]{3,2,0,1:T(8,128)(2,1)}, u32[]{:S(2)}, u32[]{:S(2)}) %collective-permute-start.6) | collective-permute-done | bytes 786464 | tf_op jit(solution)/shard_map/ppermute | solution.py:29
  98.3 1.2 select_bitcast_fusion.5
  99.9 1.8 collective-permute-start.2
  101.7 0.3 fusion.16
  102.0 0.5 iota_compare_fusion.1
  102.5 0.9 constant_dynamic-slice_fusion
  103.4 16.5 %collective-permute-done.2 = bf16[2,2,192,512]{3,2,0,1:T(8,128)(2,1)S(1)} collective-permute-done((bf16[2,2,192,512]{3,2,0,1:T(8,128)(2,1)S(1)}, bf16[2,2,192,512]{3,2,0,1:T(8,128)(2,1)S(1)}, u32[]{:S(2)}, u32[]{:S(2)}) %collective-permute-start.2) | collective-permute-done | bytes 786464 | tf_op jit(solution)/shard_map/ppermute | solution.py:29
  120.2 0.3 fusion.21
  120.6 0.2 select_bitcast_fusion.1
  120.8 0.3 pad_maximum_fusion.2
  121.1 0.3 copy.20
  121.4 0.7 copy-done.7
  122.1 1.6 fusion.7
  123.7 0.3 convolution_bitcast_fusion
  124.0 0.3 fusion.20
  124.5 0.3 pad_maximum_fusion.1
  124.8 0.3 copy.19
  125.0 1.1 fusion.8
  126.2 0.3 fusion.22
  126.5 0.4 pad_maximum_fusion
  127.0 0.3 dynamic-slice_bitcast_fusion
  127.3 1.7 copy-done.1
  128.9 0.5 collective-permute-start.8
  129.4 3.9 %collective-permute-done.8 = f32[2,2,2,2,64,512]{5,4,3,2,1,0:T(8,128)} collective-permute-done((f32[2,2,2,2,64,512]{5,4,3,2,1,0:T(8,128)S(1)}, f32[2,2,2,2,64,512]{5,4,3,2,1,0:T(8,128)}, u32[]{:S(2)}, u32[]{:S(2)}) %collective-permute-start.8) | collective-permute-done | bytes 2097184 | tf_op jit(solution)/shard_map/weight_grad_sum/ppermute | solution.py:29
  133.3 2.8 %bitcast_add_fusion = f32[2,2,2,2,64,512]{5,4,3,2,1,0:T(8,128)S(1)} fusion(f32[2,2,2,2,64,512]{5,4,3,2,1,0:T(8,128)} %collective-permute-done.8, f32[2,2,2,2,2,64,512]{6,5,4,3,2,1,0:T(8,128)} %bitcast.89, s32[]{:T(128)S(6)} %select_n.150), kind=kLoop, calls=%fused_computation.10 | loop fusion | flops 524288 | bytes 6291460 | tf_op jit(solution)/shard_map/weight_grad_sum/add | solution.py:45
  136.2 1.6 collective-permute-start.9
  137.8 24.0 %collective-permute-done.9 = f32[2,2,2,64,512]{4,3,2,1,0:T(8,128)} collective-permute-done((f32[2,2,2,64,512]{4,3,2,1,0:T(8,128)S(1)}, f32[2,2,2,64,512]{4,3,2,1,0:T(8,128)}, u32[]{:S(2)}, u32[]{:S(2)}) %collective-permute-start.9) | collective-permute-done | bytes 1048608 | tf_op jit(solution)/shard_map/weight_grad_sum/ppermute | solution.py:29
  161.8 1.4 bitcast_add_fusion.1
  163.3 1.8 collective-permute-start.10
  165.1 11.6 %collective-permute-done.10 = f32[2,2,64,512]{3,2,1,0:T(8,128)S(1)} collective-permute-done((f32[2,2,64,512]{3,2,1,0:T(8,128)S(1)}, f32[2,2,64,512]{3,2,1,0:T(8,128)S(1)}, u32[]{:S(2)}, u32[]{:S(2)}) %collective-permute-start.10) | collective-permute-done | bytes 524320 | tf_op jit(solution)/shard_map/weight_grad_sum/ppermute | solution.py:29
  176.9 1.6 collective-permute-start.11
  178.5 0.3 fusion.18
  178.8 11.3 %collective-permute-done.11 = f32[2,64,512]{2,1,0:T(8,128)S(1)} collective-permute-done((f32[2,64,512]{2,1,0:T(8,128)S(1)}, f32[2,64,512]{2,1,0:T(8,128)S(1)}, u32[]{:S(2)}, u32[]{:S(2)}) %collective-permute-start.11) | collective-permute-done | bytes 262176 | tf_op jit(solution)/shard_map/weight_grad_sum/ppermute | solution.py:29
  190.2 1.9 fusion.9
  192.1 3.5 %collective-permute-done.12 = f32[64,512]{1,0:T(8,128)S(1)} collective-permute-done((f32[64,512]{1,0:T(8,128)S(1)}, f32[64,512]{1,0:T(8,128)S(1)}, u32[]{:S(2)}, u32[]{:S(2)}) %collective-permute-start.12) | collective-permute-done | bytes 131104 | tf_op jit(solution)/shard_map/weight_grad_sum/ppermute | solution.py:29
  195.7 0.7 bitcast_add_fusion.4
  (37 shorter events, 1.5 us)
Async XLA Ops:
  0.6 38.5 %copy-start = (bf16[192,512]{1,0:T(8,128)(2,1)S(1)}, bf16[192,512]{1,0:T(8,128)(2,1)}, u32[]{:S(2)}) copy-start(bf16[192,512]{1,0:T(8,128)(2,1)} %param.13) | copy-start | bytes 589828
  2.7 30.4 %all-to-all-start = ((bf16[32,16,192]{2,0,1:T(8,128)(2,1)}), bf16[32,16,192]{2,0,1:T(8,128)(2,1)S(1)}, u32[]{:S(2)}, u32[]{:S(2)}) async-start(bf16[32,16,192]{2,0,1:T(8,128)(2,1)} %copy.17), calls=%async_computation | async-start | bytes 524288 | tf_op jit(solution)/shard_map/all_to_all | solution.py:91
  13.5 9.7 %copy-start.4 = (s32[16,3072]{1,0:T(8,128)}, s32[16,3072]{1,0:T(8,128)S(1)}, u32[]{:S(2)}) copy-start(s32[16,3072]{1,0:T(8,128)S(1)} %select_reduce_fusion) | copy-start | bytes 589828
  13.5 9.7 %copy-start.6 = (bf16[32,3072]{1,0:T(8,128)(2,1)S(1)}, bf16[32,3072]{1,0:T(8,128)(2,1)}, u32[]{:S(2)}) copy-start(bf16[32,3072]{1,0:T(8,128)(2,1)} %param.7) | copy-start | bytes 589828
  23.2 15.9 %copy-start.2 = (bf16[1024,512]{1,0:T(8,128)(2,1)S(1)}, bf16[1024,512]{1,0:T(8,128)(2,1)}, u32[]{:S(2)}) copy-start(bf16[1024,512]{1,0:T(8,128)(2,1)} %param.9) | copy-start | bytes 3145732
  33.2 16.5 %all-to-all-start.1 = ((bf16[32,16,192]{2,0,1:T(8,128)(2,1)}), bf16[32,16,192]{2,0,1:T(8,128)(2,1)S(1)}, u32[]{:S(2)}, u32[]{:S(2)}) async-start(bf16[32,16,192]{2,0,1:T(8,128)(2,1)} %copy.18), calls=%async_computation.1 | async-start | bytes 524288 | tf_op jit(solution)/shard_map/all_to_all | solution.py:92
  39.5 17.9 %collective-permute-start.4 = (bf16[192,512]{1,0:T(8,128)(2,1)S(1)}, bf16[192,512]{1,0:T(8,128)(2,1)S(1)}, u32[]{:S(2)}, u32[]{:S(2)}) collective-permute-start(bf16[192,512]{1,0:T(8,128)(2,1)S(1)} %fusion.10), channel_id=1, source_target_pairs={{0,8},{1,9},{2,10},{3,11},{4,12},{5,13},{6,14},{7,15},{8,0},{9,1},... | collective-permute-start | bytes 589832 | tf_op jit(solution)/shard_map/ppermute | solution.py:29
  51.8 13.9 %collective-permute-start = (bf16[192,512]{1,0:T(8,128)(2,1)S(1)}, bf16[192,512]{1,0:T(8,128)(2,1)S(1)}, u32[]{:S(2)}, u32[]{:S(2)}) collective-permute-start(bf16[192,512]{1,0:T(8,128)(2,1)S(1)} %get-tuple-element.18), channel_id=1, source_target_pairs={{0,8},{1,9},{2,10},{3,11},{4,12},{5,13},{6,14},{7,15},{8,0},{9,1},... | collective-permute-start | bytes 589832 | tf_op jit(solution)/shard_map/ppermute | solution.py:29
  65.8 10.3 %collective-permute-start.5 = (bf16[2,192,512]{2,1,0:T(8,128)(2,1)S(1)}, bf16[2,192,512]{2,1,0:T(8,128)(2,1)}, u32[]{:S(2)}, u32[]{:S(2)}) collective-permute-start(bf16[2,192,512]{2,1,0:T(8,128)(2,1)S(1)} %pad_maximum_fusion.8), channel_id=1, source_target_pairs={{0,4},{1,5},{2,6},{3,7},{4,0},{5,1},{6,2},{7,3},{8,12},{9,13},{10,... | collective-permute-start | bytes 1179656 | tf_op jit(solution)/shard_map/ppermute | solution.py:29
  78.1 20.2 %collective-permute-start.6 = (bf16[2,2,192,512]{3,2,0,1:T(8,128)(2,1)}, bf16[2,2,192,512]{3,2,0,1:T(8,128)(2,1)}, u32[]{:S(2)}, u32[]{:S(2)}) collective-permute-start(bf16[2,2,192,512]{3,2,0,1:T(8,128)(2,1)} %pad_maximum_fusion.6), channel_id=1, source_target_pairs={{0,2},{1,3},{2,0},{3,1},{4,6},{5,7},{6,4},{7,5},{8,10},{9,11},{10,... | collective-permute-start | bytes 2359304 | tf_op jit(solution)/shard_map/ppermute | solution.py:29
  80.3 10.9 %collective-permute-start.1 = (bf16[2,192,512]{2,1,0:T(8,128)(2,1)S(1)}, bf16[2,192,512]{2,1,0:T(8,128)(2,1)}, u32[]{:S(2)}, u32[]{:S(2)}) collective-permute-start(bf16[2,192,512]{2,1,0:T(8,128)(2,1)S(1)} %pad_maximum_fusion.7), channel_id=1, source_target_pairs={{0,4},{1,5},{2,6},{3,7},{4,0},{5,1},{6,2},{7,3},{8,12},{9,13},{10,... | collective-permute-start | bytes 1179656 | tf_op jit(solution)/shard_map/ppermute | solution.py:29
  99.7 20.8 %collective-permute-start.7 = (bf16[2,2,2,192,512]{4,3,0,1,2:T(8,128)(2,1)S(1)}, bf16[2,2,2,192,512]{4,3,0,1,2:T(8,128)(2,1)S(1)}, u32[]{:S(2)}, u32[]{:S(2)}) collective-permute-start(bf16[2,2,2,192,512]{4,3,0,1,2:T(8,128)(2,1)S(1)} %pad_maximum_fusion.4), channel_id=1, source_target_pairs={{0,1},{1,0},{2,3},{3,2},{4,5},{5,4},{6,7},{7,6},{8,9},{9,8},{10,11... | collective-permute-start | bytes 4718600 | tf_op jit(solution)/shard_map/ppermute | solution.py:29
  99.9 20.0 %collective-permute-start.2 = (bf16[2,2,192,512]{3,2,0,1:T(8,128)(2,1)S(1)}, bf16[2,2,192,512]{3,2,0,1:T(8,128)(2,1)S(1)}, u32[]{:S(2)}, u32[]{:S(2)}) collective-permute-start(bf16[2,2,192,512]{3,2,0,1:T(8,128)(2,1)S(1)} %pad_maximum_fusion.5), channel_id=1, source_target_pairs={{0,2},{1,3},{2,0},{3,1},{4,6},{5,7},{6,4},{7,5},{8,10},{9,11},{10,... | collective-permute-start | bytes 2359304 | tf_op jit(solution)/shard_map/ppermute | solution.py:29
  120.1 4.1 %collective-permute-start.3 = (bf16[2,2,2,192,512]{4,3,0,1,2:T(8,128)(2,1)S(1)}, bf16[2,2,2,192,512]{4,3,0,1,2:T(8,128)(2,1)S(1)}, u32[]{:S(2)}, u32[]{:S(2)}) collective-permute-start(bf16[2,2,2,192,512]{4,3,0,1,2:T(8,128)(2,1)S(1)} %pad_maximum_fusion.3), channel_id=1, source_target_pairs={{0,1},{1,0},{2,3},{3,2},{4,5},{5,4},{6,7},{7,6},{8,9},{9,8},{10,11... | collective-permute-start | bytes 4718600 | tf_op jit(solution)/shard_map/ppermute | solution.py:29
  121.1 1.0 copy-start.7
  126.2 1.1 copy-start.5
  127.0 2.0 copy-start.1
  128.9 4.4 %collective-permute-start.8 = (f32[2,2,2,2,64,512]{5,4,3,2,1,0:T(8,128)S(1)}, f32[2,2,2,2,64,512]{5,4,3,2,1,0:T(8,128)}, u32[]{:S(2)}, u32[]{:S(2)}) collective-permute-start(f32[2,2,2,2,64,512]{5,4,3,2,1,0:T(8,128)S(1)} %dynamic-slice_bitcast_fusion), channel_id=1, source_target_pairs={{0,1},{1,0},{2,3},{3,2},{4,5},{5,4},{6,7},{7,6},{8,9},{9,8},{10,11... | collective-permute-start | bytes 6291464 | tf_op jit(solution)/shard_map/weight_grad_sum/ppermute | solution.py:29
  136.2 25.6 %collective-permute-start.9 = (f32[2,2,2,64,512]{4,3,2,1,0:T(8,128)S(1)}, f32[2,2,2,64,512]{4,3,2,1,0:T(8,128)}, u32[]{:S(2)}, u32[]{:S(2)}) collective-permute-start(f32[2,2,2,64,512]{4,3,2,1,0:T(8,128)S(1)} %dynamic-slice_bitcast_fusion.1), channel_id=1, source_target_pairs={{0,16},{16,0},{1,17},{17,1},{2,18},{18,2},{3,19},{19,3},{4,20},{20... | collective-permute-start | bytes 3145736 | tf_op jit(solution)/shard_map/weight_grad_sum/ppermute | solution.py:29
  163.2 15.3 %copy-start.3 = (bf16[1024,512]{1,0:T(8,128)(2,1)S(1)}, bf16[1024,512]{1,0:T(8,128)(2,1)}, u32[]{:S(2)}) copy-start(bf16[1024,512]{1,0:T(8,128)(2,1)} %param.9) | copy-start | bytes 3145732
  163.3 13.5 %collective-permute-start.10 = (f32[2,2,64,512]{3,2,1,0:T(8,128)S(1)}, f32[2,2,64,512]{3,2,1,0:T(8,128)S(1)}, u32[]{:S(2)}, u32[]{:S(2)}) collective-permute-start(f32[2,2,64,512]{3,2,1,0:T(8,128)S(1)} %dynamic-slice_bitcast_fusion.2), channel_id=1, source_target_pairs={{0,2},{1,3},{2,0},{3,1},{4,6},{5,7},{6,4},{7,5},{8,10},{9,11},{10,... | collective-permute-start | bytes 1572872 | tf_op jit(solution)/shard_map/weight_grad_sum/ppermute | solution.py:29
  176.9 13.2 %collective-permute-start.11 = (f32[2,64,512]{2,1,0:T(8,128)S(1)}, f32[2,64,512]{2,1,0:T(8,128)S(1)}, u32[]{:S(2)}, u32[]{:S(2)}) collective-permute-start(f32[2,64,512]{2,1,0:T(8,128)S(1)} %dynamic-slice_bitcast_fusion.3), channel_id=1, source_target_pairs={{0,8},{1,9},{2,10},{3,11},{4,12},{5,13},{6,14},{7,15},{8,0},{9,1},... | collective-permute-start | bytes 786440 | tf_op jit(solution)/shard_map/weight_grad_sum/ppermute | solution.py:29
  190.2 5.5 %collective-permute-start.12 = (f32[64,512]{1,0:T(8,128)S(1)}, f32[64,512]{1,0:T(8,128)S(1)}, u32[]{:S(2)}, u32[]{:S(2)}) collective-permute-start(f32[64,512]{1,0:T(8,128)S(1)} %dynamic-slice_bitcast_fusion.4), channel_id=1, source_target_pairs={{0,4},{1,5},{2,6},{3,7},{4,0},{5,1},{6,2},{7,3},{8,12},{9,13},{10,... | collective-permute-start | bytes 393224 | tf_op jit(solution)/shard_map/weight_grad_sum/ppermute | solution.py:29

commit v4 on v3

--- a/solution.py
+++ b/solution.py
@@ -132,7 +132,14 @@
     )
     with jax.named_scope("weight_grad_sum"):
         if lax.axis_size("dp") == 2 and devices == 16:
-            weight_grads = halving_scatter(terms, [0, 4, 1, 3, 2])
+            half = terms.shape[1] // 2
+            weight_grads = jnp.concatenate(
+                [
+                    halving_scatter(terms[:, :half], [0, 4, 1, 3, 2]),
+                    halving_scatter(terms[:, half:], [0, 1, 4, 2, 3]),
+                ],
+                axis=1,
+            )
         else:
             weight_grads = lax.psum_scatter(terms, ("dp", "mp"), scatter_dimension=0, tiled=True)
     return (node_output, weight_grads)

time: 197 us -> 174 us (0.88)
  waiting for transfers between devices: 111 us -> 83.3 us
  starting transfers between devices: 31.8 us -> 35.5 us
  local copies, waits for them, and re-layouts: 8.59 us -> 11.4 us
    ppermute x13 -> x18, waiting for transfers between devices: 105 us -> 76.9 us  [swap(): return lax.ppermute(values, axis, [(j, j ^ mask) for j in range(size)])]
    ppermute x13 -> x18, starting transfers between devices: 18.4 us -> 22.1 us  [swap(): return lax.ppermute(values, axis, [(j, j ^ mask) for j in range(size)])]
    add x5 -> x10, other arithmetic: 4.99 us -> 3.09 us  [halving_scatter(): values = keep + got]
  transfers between devices with their start and end apart: 15 -> 20, of which waited for: 12 -> 16; matrix products, arithmetic and copies ran while one was open for 18% -> 22% of each run, Pallas kernels for 0% -> 0%
where the time goes in v4:
time: 174 us; the launch traced here: 173 us
  waiting for transfers between devices  83.3 us (48%)
  starting transfers between devices  35.5 us (20%)
  other arithmetic  24.5 us (14%)
  matrix products  17.5 us (10%)
  local copies, waits for them, and re-layouts  11.4 us (7%)
    ppermute x18, waiting for transfers between devices, swap(): return lax.ppermute(values, axis, [(j, j ^ mask) for j in range(size)])  76.9 us
    ppermute x18, starting transfers between devices, swap(): return lax.ppermute(values, axis, [(j, j ^ mask) for j in range(size)])  22.1 us
    dot_general x13, matrix products, contract(): lax.dot_general(left, right, (((left_dim,), (right_dim,)), ((), ())), pre...  17.5 us
    eq x1, other arithmetic, shards(): adjacency = (rowsel[:, None, :] == row_ids).astype(jnp.bfloat16)  9.69 us
    all_to_all x1, starting transfers between devices, shards(): lax.all_to_all(node_features, 'mp', split_axis=1, concat_axis=0, tiled=True)  7.39 us
    another operation x15, other arithmetic, doubling_gather(): current = jnp.stack([low, high], axis=step)  6.93 us
    all_to_all x1, waiting for transfers between devices, shards(): lax.all_to_all(agg_one_cols, 'mp', split_axis=1, concat_axis=0, tiled=True)  6.37 us
    all_to_all x1, starting transfers between devices, shards(): lax.all_to_all(agg_one_cols, 'mp', split_axis=1, concat_axis=0, tiled=True)  6 us
  transfers between devices with their start and end apart: 20, of which 16 were waited for; matrix products, arithmetic and copies ran while one was open for 22% of the time, Pallas kernels for 0%

profile of v4, /device:TPU:0, one launch (start us, length us, event | category | flops | bytes accessed | tf_op | source)
XLA Modules:
  0.0 173.3 jit_solution(4753998514691794708)
XLA Ops:
  0.6 1.3 all_to_all.28
  1.9 0.8 copy.19
  2.7 7.4 %all-to-all-start = ((bf16[32,16,192]{2,0,1:T(8,128)(2,1)}), bf16[32,16,192]{2,0,1:T(8,128)(2,1)S(1)}, u32[]{:S(2)}, u32[]{:S(2)}) async-start(bf16[32,16,192]{2,0,1:T(8,128)(2,1)} %copy.19), calls=%async_computation | async-start | bytes 524288 | tf_op jit(solution)/shard_map/all_to_all | solution.py:91
  10.1 0.7 convert_divide_fusion
  10.8 0.7 iota_compare_fusion.10
  11.7 1.8 %select_reduce_fusion = s32[16,3072]{1,0:T(8,128)S(1)} fusion(s32[3072,8]{0,1:T(8,128)} %param.11, s32[3072,8]{0,1:T(8,128)} %param.10, pred[3072,8]{0,1:T(8,128)(4,1)S(1)} %iota_compare_fusion.10), kind=kLoop, calls=%fused_computation.17 | loop fusion | flops 1523712 | bytes 417792 | tf_op jit(solution)/shard_map/reduce_max | solution.py:76
  13.5 9.7 %bitcast_compare_fusion = pred[3072,3072]{1,0:T(32,128)(4,1)} fusion(s32[3072]{0:T(1024)S(1)} %eq.101, s32[16,3072]{1,0:T(8,128)S(1)} %select_reduce_fusion), kind=kLoop, calls=%fused_computation | loop fusion | flops 9437184 | bytes 9646080 | tf_op jit(solution)/shard_map/layer_one_mean/eq | solution.py:81
  23.2 8.6 %fusion.1 = bf16[32,3072]{1,0:T(8,128)(2,1)S(1)} fusion(pred[3072,3072]{1,0:T(32,128)(4,1)} %bitcast_compare_fusion, bf16[32,3072]{1,0:T(8,128)(2,1)S(1)} %copy-done.9, f32[3072]{0:T(1024)S(1)} %convert_divide_fusion), kind=kOutput, calls=%fused_computation.4 | convolution fusion | flops 604176384 | bytes 9842688 | tf_op jit(solution)/shard_map/layer_one_mean/dot_general | solution.py:22
  31.9 0.5 all_to_all.32
  32.4 0.8 copy.20
  33.2 6.0 %all-to-all-start.1 = ((bf16[32,16,192]{2,0,1:T(8,128)(2,1)}), bf16[32,16,192]{2,0,1:T(8,128)(2,1)S(1)}, u32[]{:S(2)}, u32[]{:S(2)}) async-start(bf16[32,16,192]{2,0,1:T(8,128)(2,1)} %copy.20), calls=%async_computation.1 | async-start | bytes 524288 | tf_op jit(solution)/shard_map/all_to_all | solution.py:92
  39.2 1.0 fusion.10
  40.2 2.8 %collective-permute-start.4 = (bf16[192,512]{1,0:T(8,128)(2,1)}, bf16[192,512]{1,0:T(8,128)(2,1)}, u32[]{:S(2)}, u32[]{:S(2)}) collective-permute-start(bf16[192,512]{1,0:T(8,128)(2,1)} %fusion.10), channel_id=1, source_target_pairs={{0,8},{1,9},{2,10},{3,11},{4,12},{5,13},{6,14},{7,15},{8,0},{9,1},... | collective-permute-start | bytes 589832 | tf_op jit(solution)/shard_map/ppermute | solution.py:29
  43.3 6.4 %all-to-all-done.1 = bf16[32,16,192]{2,0,1:T(8,128)(2,1)S(1)} async-done(((bf16[32,16,192]{2,0,1:T(8,128)(2,1)}), bf16[32,16,192]{2,0,1:T(8,128)(2,1)S(1)}, u32[]{:S(2)}, u32[]{:S(2)}) %all-to-all-start.1) | async-done | bytes 196640 | tf_op jit(solution)/shard_map/all_to_all | solution.py:92
  49.7 1.1 multiply_convert_fusion
  50.7 5.1 %collective-permute-start = (bf16[192,512]{1,0:T(8,128)(2,1)S(1)}, bf16[192,512]{1,0:T(8,128)(2,1)S(1)}, u32[]{:S(2)}, u32[]{:S(2)}) collective-permute-start(bf16[192,512]{1,0:T(8,128)(2,1)S(1)} %get-tuple-element.22), channel_id=1, source_target_pairs={{0,8},{1,9},{2,10},{3,11},{4,12},{5,13},{6,14},{7,15},{8,0},{9,1},... | collective-permute-start | bytes 589832 | tf_op jit(solution)/shard_map/ppermute | solution.py:29
  55.8 6.2 %collective-permute-done.4 = bf16[192,512]{1,0:T(8,128)(2,1)} collective-permute-done((bf16[192,512]{1,0:T(8,128)(2,1)}, bf16[192,512]{1,0:T(8,128)(2,1)}, u32[]{:S(2)}, u32[]{:S(2)}) %collective-permute-start.4) | collective-permute-done | bytes 196640 | tf_op jit(solution)/shard_map/ppermute | solution.py:29
  62.0 3.6 %collective-permute-done = bf16[192,512]{1,0:T(8,128)(2,1)S(1)} collective-permute-done((bf16[192,512]{1,0:T(8,128)(2,1)S(1)}, bf16[192,512]{1,0:T(8,128)(2,1)S(1)}, u32[]{:S(2)}, u32[]{:S(2)}) %collective-permute-start) | collective-permute-done | bytes 196640 | tf_op jit(solution)/shard_map/ppermute | solution.py:29
  65.7 1.1 select_bitcast_fusion.13
  66.9 10.7 %collective-permute-done.5 = bf16[2,192,512]{2,1,0:T(8,128)(2,1)} collective-permute-done((bf16[2,192,512]{2,1,0:T(8,128)(2,1)S(1)}, bf16[2,192,512]{2,1,0:T(8,128)(2,1)}, u32[]{:S(2)}, u32[]{:S(2)}) %collective-permute-start.5) | collective-permute-done | bytes 393248 | tf_op jit(solution)/shard_map/ppermute | solution.py:29
  77.6 1.1 select_bitcast_fusion.9
  78.7 1.0 pad_maximum_fusion.6
  79.6 1.9 %collective-permute-start.6 = (bf16[2,2,192,512]{3,2,0,1:T(8,128)(2,1)}, bf16[2,2,192,512]{3,2,0,1:T(8,128)(2,1)}, u32[]{:S(2)}, u32[]{:S(2)}) collective-permute-start(bf16[2,2,192,512]{3,2,0,1:T(8,128)(2,1)} %pad_maximum_fusion.6), channel_id=1, source_target_pairs={{0,2},{1,3},{2,0},{3,1},{4,6},{5,7},{6,4},{7,5},{8,10},{9,11},{10,... | collective-permute-start | bytes 2359304 | tf_op jit(solution)/shard_map/ppermute | solution.py:29
  81.6 0.4 collective-permute-start.1
  82.0 0.8 constant_dynamic-slice_fusion.3
  82.8 9.0 %collective-permute-done.1 = bf16[2,192,512]{2,1,0:T(8,128)(2,1)} collective-permute-done((bf16[2,192,512]{2,1,0:T(8,128)(2,1)S(1)}, bf16[2,192,512]{2,1,0:T(8,128)(2,1)}, u32[]{:S(2)}, u32[]{:S(2)}) %collective-permute-start.1) | collective-permute-done | bytes 393248 | tf_op jit(solution)/shard_map/ppermute | solution.py:29
  91.8 1.1 select_bitcast_fusion.11
  92.8 6.0 %collective-permute-done.6 = bf16[2,2,192,512]{3,2,0,1:T(8,128)(2,1)} collective-permute-done((bf16[2,2,192,512]{3,2,0,1:T(8,128)(2,1)}, bf16[2,2,192,512]{3,2,0,1:T(8,128)(2,1)}, u32[]{:S(2)}, u32[]{:S(2)}) %collective-permute-start.6) | collective-permute-done | bytes 786464 | tf_op jit(solution)/shard_map/ppermute | solution.py:29
  98.9 1.2 select_bitcast_fusion.5
  100.4 1.8 %collective-permute-start.2 = (bf16[2,2,192,512]{3,2,0,1:T(8,128)(2,1)S(1)}, bf16[2,2,192,512]{3,2,0,1:T(8,128)(2,1)S(1)}, u32[]{:S(2)}, u32[]{:S(2)}) collective-permute-start(bf16[2,2,192,512]{3,2,0,1:T(8,128)(2,1)S(1)} %pad_maximum_fusion.5), channel_id=1, source_target_pairs={{0,2},{1,3},{2,0},{3,1},{4,6},{5,7},{6,4},{7,5},{8,10},{9,11},{10,... | collective-permute-start | bytes 2359304 | tf_op jit(solution)/shard_map/ppermute | solution.py:29
  102.5 0.5 iota_compare_fusion.1
  103.0 0.9 constant_dynamic-slice_fusion.2
  103.9 16.5 %collective-permute-done.2 = bf16[2,2,192,512]{3,2,0,1:T(8,128)(2,1)S(1)} collective-permute-done((bf16[2,2,192,512]{3,2,0,1:T(8,128)(2,1)S(1)}, bf16[2,2,192,512]{3,2,0,1:T(8,128)(2,1)S(1)}, u32[]{:S(2)}, u32[]{:S(2)}) %collective-permute-start.2) | collective-permute-done | bytes 786464 | tf_op jit(solution)/shard_map/ppermute | solution.py:29
  120.8 0.3 fusion.22
  121.9 0.7 copy-done.10
  122.6 1.6 fusion.7
  125.6 1.1 fusion.8
  126.7 0.7 copy-done.6
  127.7 0.4 pad_maximum_fusion
  128.2 0.3 fusion.20
  128.5 1.3 copy-done.1
  129.9 1.1 dynamic-slice_bitcast_fusion
  131.0 0.5 collective-permute-start.8
  131.6 1.0 copy.27
  132.7 1.3 fusion.18
  134.1 1.4 bitcast_add_fusion.1
  135.5 1.6 collective-permute-start.9
  137.1 1.5 bitcast_add_fusion
  138.6 1.8 %collective-permute-start.14 = (f32[2,2,2,64,256]{4,3,2,1,0:T(8,128)S(1)}, f32[2,2,2,64,256]{4,3,2,1,0:T(8,128)S(1)}, u32[]{:S(2)}, u32[]{:S(2)}) collective-permute-start(f32[2,2,2,64,256]{4,3,2,1,0:T(8,128)S(1)} %dynamic-slice_bitcast_fusion.1), channel_id=1, source_target_pairs={{0,2},{1,3},{2,0},{3,1},{4,6},{5,7},{6,4},{7,5},{8,10},{9,11},{10,... | collective-permute-start | bytes 1572872 | tf_op jit(solution)/shard_map/weight_grad_sum/ppermute | solution.py:29
  140.4 1.0 fusion.9
  141.4 8.5 %collective-permute-done.9 = f32[2,2,2,64,256]{4,3,2,1,0:T(8,128)S(1)} collective-permute-done((f32[2,2,2,64,256]{4,3,2,1,0:T(8,128)S(1)}, f32[2,2,2,64,256]{4,3,2,1,0:T(8,128)S(1)}, u32[]{:S(2)}, u32[]{:S(2)}) %collective-permute-start.9) | collective-permute-done | bytes 524320 | tf_op jit(solution)/shard_map/weight_grad_sum/ppermute | solution.py:29
  150.0 1.8 %collective-permute-start.10 = (f32[2,2,64,256]{3,2,1,0:T(8,128)S(1)}, f32[2,2,64,256]{3,2,1,0:T(8,128)S(1)}, u32[]{:S(2)}, u32[]{:S(2)}) collective-permute-start(f32[2,2,64,256]{3,2,1,0:T(8,128)S(1)} %dynamic-slice_bitcast_fusion.4), channel_id=1, source_target_pairs={{0,2},{1,3},{2,0},{3,1},{4,6},{5,7},{6,4},{7,5},{8,10},{9,11},{10,... | collective-permute-start | bytes 786440 | tf_op jit(solution)/shard_map/weight_grad_sum/ppermute | solution.py:29
  151.8 1.2 collective-permute-done.14
  153.1 0.4 collective-permute-start.15
  153.4 4.8 %collective-permute-done.10 = f32[2,2,64,256]{3,2,1,0:T(8,128)S(1)} collective-permute-done((f32[2,2,64,256]{3,2,1,0:T(8,128)S(1)}, f32[2,2,64,256]{3,2,1,0:T(8,128)S(1)}, u32[]{:S(2)}, u32[]{:S(2)}) %collective-permute-start.10) | collective-permute-done | bytes 262176 | tf_op jit(solution)/shard_map/weight_grad_sum/ppermute | solution.py:29
  158.3 1.0 collective-permute-start.11
  159.4 1.0 collective-permute-done.15
  160.4 0.7 collective-permute-start.16
  161.1 5.6 %collective-permute-done.11 = f32[2,64,256]{2,1,0:T(8,128)S(1)} collective-permute-done((f32[2,64,256]{2,1,0:T(8,128)S(1)}, f32[2,64,256]{2,1,0:T(8,128)S(1)}, u32[]{:S(2)}, u32[]{:S(2)}) %collective-permute-start.11) | collective-permute-done | bytes 131104 | tf_op jit(solution)/shard_map/weight_grad_sum/ppermute | solution.py:29
  166.8 0.4 collective-permute-done.16
  167.2 2.1 %collective-permute-start.17 = (f32[64,256]{1,0:T(8,128)S(1)}, f32[64,256]{1,0:T(8,128)S(1)}, u32[]{:S(2)}, u32[]{:S(2)}) collective-permute-start(f32[64,256]{1,0:T(8,128)S(1)} %dynamic-slice_bitcast_fusion.7), channel_id=1, source_target_pairs={{0,8},{1,9},{2,10},{3,11},{4,12},{5,13},{6,14},{7,15},{8,0},{9,1},... | collective-permute-start | bytes 196616 | tf_op jit(solution)/shard_map/weight_grad_sum/ppermute | solution.py:29
  169.3 2.1 %collective-permute-done.12 = f32[64,256]{1,0:T(8,128)S(1)} collective-permute-done((f32[64,256]{1,0:T(8,128)S(1)}, f32[64,256]{1,0:T(8,128)S(1)}, u32[]{:S(2)}, u32[]{:S(2)}) %collective-permute-start.12) | collective-permute-done | bytes 65568 | tf_op jit(solution)/shard_map/weight_grad_sum/ppermute | solution.py:29
  171.4 1.1 collective-permute-done.17
  172.6 0.7 pad_maximum_fusion.9
  (66 shorter events, 4.8 us)
Async XLA Ops:
  0.6 38.5 %copy-start = (bf16[192,512]{1,0:T(8,128)(2,1)S(1)}, bf16[192,512]{1,0:T(8,128)(2,1)}, u32[]{:S(2)}) copy-start(bf16[192,512]{1,0:T(8,128)(2,1)} %param.13) | copy-start | bytes 589828
  2.7 30.4 %all-to-all-start = ((bf16[32,16,192]{2,0,1:T(8,128)(2,1)}), bf16[32,16,192]{2,0,1:T(8,128)(2,1)S(1)}, u32[]{:S(2)}, u32[]{:S(2)}) async-start(bf16[32,16,192]{2,0,1:T(8,128)(2,1)} %copy.19), calls=%async_computation | async-start | bytes 524288 | tf_op jit(solution)/shard_map/all_to_all | solution.py:91
  13.5 9.7 %copy-start.5 = (s32[16,3072]{1,0:T(8,128)}, s32[16,3072]{1,0:T(8,128)S(1)}, u32[]{:S(2)}) copy-start(s32[16,3072]{1,0:T(8,128)S(1)} %select_reduce_fusion) | copy-start | bytes 589828
  13.5 9.7 %copy-start.9 = (bf16[32,3072]{1,0:T(8,128)(2,1)S(1)}, bf16[32,3072]{1,0:T(8,128)(2,1)}, u32[]{:S(2)}) copy-start(bf16[32,3072]{1,0:T(8,128)(2,1)} %param.7) | copy-start | bytes 589828
  23.2 16.0 %copy-start.3 = (bf16[1024,512]{1,0:T(8,128)(2,1)S(1)}, bf16[1024,512]{1,0:T(8,128)(2,1)}, u32[]{:S(2)}) copy-start(bf16[1024,512]{1,0:T(8,128)(2,1)} %param.9) | copy-start | bytes 3145732
  31.9 11.2 %copy-start.8 = (bf16[1024,512]{1,0:T(8,128)(2,1)S(1)}, bf16[1024,512]{1,0:T(8,128)(2,1)}, u32[]{:S(2)}) copy-start(bf16[1024,512]{1,0:T(8,128)(2,1)} %param.8) | copy-start | bytes 3145732
  33.2 16.5 %all-to-all-start.1 = ((bf16[32,16,192]{2,0,1:T(8,128)(2,1)}), bf16[32,16,192]{2,0,1:T(8,128)(2,1)S(1)}, u32[]{:S(2)}, u32[]{:S(2)}) async-start(bf16[32,16,192]{2,0,1:T(8,128)(2,1)} %copy.20), calls=%async_computation.1 | async-start | bytes 524288 | tf_op jit(solution)/shard_map/all_to_all | solution.py:92
  40.2 21.8 %collective-permute-start.4 = (bf16[192,512]{1,0:T(8,128)(2,1)}, bf16[192,512]{1,0:T(8,128)(2,1)}, u32[]{:S(2)}, u32[]{:S(2)}) collective-permute-start(bf16[192,512]{1,0:T(8,128)(2,1)} %fusion.10), channel_id=1, source_target_pairs={{0,8},{1,9},{2,10},{3,11},{4,12},{5,13},{6,14},{7,15},{8,0},{9,1},... | collective-permute-start | bytes 589832 | tf_op jit(solution)/shard_map/ppermute | solution.py:29
  50.7 14.9 %collective-permute-start = (bf16[192,512]{1,0:T(8,128)(2,1)S(1)}, bf16[192,512]{1,0:T(8,128)(2,1)S(1)}, u32[]{:S(2)}, u32[]{:S(2)}) collective-permute-start(bf16[192,512]{1,0:T(8,128)(2,1)S(1)} %get-tuple-element.22), channel_id=1, source_target_pairs={{0,8},{1,9},{2,10},{3,11},{4,12},{5,13},{6,14},{7,15},{8,0},{9,1},... | collective-permute-start | bytes 589832 | tf_op jit(solution)/shard_map/ppermute | solution.py:29
  66.8 10.8 %collective-permute-start.5 = (bf16[2,192,512]{2,1,0:T(8,128)(2,1)S(1)}, bf16[2,192,512]{2,1,0:T(8,128)(2,1)}, u32[]{:S(2)}, u32[]{:S(2)}) collective-permute-start(bf16[2,192,512]{2,1,0:T(8,128)(2,1)S(1)} %pad_maximum_fusion.8), channel_id=1, source_target_pairs={{0,4},{1,5},{2,6},{3,7},{4,0},{5,1},{6,2},{7,3},{8,12},{9,13},{10,... | collective-permute-start | bytes 1179656 | tf_op jit(solution)/shard_map/ppermute | solution.py:29
  79.6 19.2 %collective-permute-start.6 = (bf16[2,2,192,512]{3,2,0,1:T(8,128)(2,1)}, bf16[2,2,192,512]{3,2,0,1:T(8,128)(2,1)}, u32[]{:S(2)}, u32[]{:S(2)}) collective-permute-start(bf16[2,2,192,512]{3,2,0,1:T(8,128)(2,1)} %pad_maximum_fusion.6), channel_id=1, source_target_pairs={{0,2},{1,3},{2,0},{3,1},{4,6},{5,7},{6,4},{7,5},{8,10},{9,11},{10,... | collective-permute-start | bytes 2359304 | tf_op jit(solution)/shard_map/ppermute | solution.py:29
  81.6 10.2 %collective-permute-start.1 = (bf16[2,192,512]{2,1,0:T(8,128)(2,1)S(1)}, bf16[2,192,512]{2,1,0:T(8,128)(2,1)}, u32[]{:S(2)}, u32[]{:S(2)}) collective-permute-start(bf16[2,192,512]{2,1,0:T(8,128)(2,1)S(1)} %pad_maximum_fusion.7), channel_id=1, source_target_pairs={{0,4},{1,5},{2,6},{3,7},{4,0},{5,1},{6,2},{7,3},{8,12},{9,13},{10,... | collective-permute-start | bytes 1179656 | tf_op jit(solution)/shard_map/ppermute | solution.py:29
  100.2 20.8 %collective-permute-start.7 = (bf16[2,2,2,192,512]{4,3,0,1,2:T(8,128)(2,1)S(1)}, bf16[2,2,2,192,512]{4,3,0,1,2:T(8,128)(2,1)S(1)}, u32[]{:S(2)}, u32[]{:S(2)}) collective-permute-start(bf16[2,2,2,192,512]{4,3,0,1,2:T(8,128)(2,1)S(1)} %pad_maximum_fusion.4), channel_id=1, source_target_pairs={{0,1},{1,0},{2,3},{3,2},{4,5},{5,4},{6,7},{7,6},{8,9},{9,8},{10,11... | collective-permute-start | bytes 4718600 | tf_op jit(solution)/shard_map/ppermute | solution.py:29
  100.4 20.0 %collective-permute-start.2 = (bf16[2,2,192,512]{3,2,0,1:T(8,128)(2,1)S(1)}, bf16[2,2,192,512]{3,2,0,1:T(8,128)(2,1)S(1)}, u32[]{:S(2)}, u32[]{:S(2)}) collective-permute-start(bf16[2,2,192,512]{3,2,0,1:T(8,128)(2,1)S(1)} %pad_maximum_fusion.5), channel_id=1, source_target_pairs={{0,2},{1,3},{2,0},{3,1},{4,6},{5,7},{6,4},{7,5},{8,10},{9,11},{10,... | collective-permute-start | bytes 2359304 | tf_op jit(solution)/shard_map/ppermute | solution.py:29
  120.7 4.1 %collective-permute-start.3 = (bf16[2,2,2,192,512]{4,3,0,1,2:T(8,128)(2,1)S(1)}, bf16[2,2,2,192,512]{4,3,0,1,2:T(8,128)(2,1)S(1)}, u32[]{:S(2)}, u32[]{:S(2)}) collective-permute-start(bf16[2,2,2,192,512]{4,3,0,1,2:T(8,128)(2,1)S(1)} %pad_maximum_fusion.3), channel_id=1, source_target_pairs={{0,1},{1,0},{2,3},{3,2},{4,5},{5,4},{6,7},{7,6},{8,9},{9,8},{10,11... | collective-permute-start | bytes 4718600 | tf_op jit(solution)/shard_map/ppermute | solution.py:29
  121.6 1.0 copy-start.10
  126.7 0.7 copy-start.6
  128.5 1.4 copy-start.1
  131.0 3.1 %collective-permute-start.8 = (f32[2,2,2,2,64,256]{5,4,3,2,1,0:T(8,128)}, f32[2,2,2,2,64,256]{5,4,3,2,1,0:T(8,128)}, u32[]{:S(2)}, u32[]{:S(2)}) collective-permute-start(f32[2,2,2,2,64,256]{5,4,3,2,1,0:T(8,128)} %dynamic-slice_bitcast_fusion), channel_id=1, source_target_pairs={{0,1},{1,0},{2,3},{3,2},{4,5},{5,4},{6,7},{7,6},{8,9},{9,8},{10,11... | collective-permute-start | bytes 3145736 | tf_op jit(solution)/shard_map/weight_grad_sum/ppermute | solution.py:29
  131.6 2.5 %copy-start.2 = (f32[2048,256]{1,0:T(8,128)S(1)}, f32[2048,256]{1,0:T(8,128)}, u32[]{:S(2)}) copy-start(f32[2048,256]{1,0:T(8,128)} %copy-done.1) | copy-start | bytes 6291460
  132.7 4.4 %collective-permute-start.13 = (f32[2,2,2,2,64,256]{5,4,2,1,0,3:T(8,128)}, f32[2,2,2,2,64,256]{5,4,2,1,0,3:T(8,128)}, u32[]{:S(2)}, u32[]{:S(2)}) collective-permute-start(f32[2,2,2,2,64,256]{5,4,2,1,0,3:T(8,128)} %bitcast.109), channel_id=1, source_target_pairs={{0,1},{1,0},{2,3},{3,2},{4,5},{5,4},{6,7},{7,6},{8,9},{9,8},{10,11... | collective-permute-start | bytes 3145736 | tf_op jit(solution)/shard_map/weight_grad_sum/ppermute | solution.py:29
  135.5 14.3 %collective-permute-start.9 = (f32[2,2,2,64,256]{4,3,2,1,0:T(8,128)S(1)}, f32[2,2,2,64,256]{4,3,2,1,0:T(8,128)S(1)}, u32[]{:S(2)}, u32[]{:S(2)}) collective-permute-start(f32[2,2,2,64,256]{4,3,2,1,0:T(8,128)S(1)} %dynamic-slice_bitcast_fusion.2), channel_id=1, source_target_pairs={{0,16},{16,0},{1,17},{17,1},{2,18},{18,2},{3,19},{19,3},{4,20},{20... | collective-permute-start | bytes 1572872 | tf_op jit(solution)/shard_map/weight_grad_sum/ppermute | solution.py:29
  137.1 3.3 %copy-start.4 = (bf16[1024,512]{1,0:T(8,128)(2,1)S(1)}, bf16[1024,512]{1,0:T(8,128)(2,1)}, u32[]{:S(2)}) copy-start(bf16[1024,512]{1,0:T(8,128)(2,1)} %param.9) | copy-start | bytes 3145732
  137.1 3.3 %copy-start.7 = (bf16[192,512]{1,0:T(8,128)(2,1)S(1)}, bf16[192,512]{1,0:T(8,128)(2,1)}, u32[]{:S(2)}) copy-start(bf16[192,512]{1,0:T(8,128)(2,1)} %copy-done.6) | copy-start | bytes 589828
  138.6 14.4 %collective-permute-start.14 = (f32[2,2,2,64,256]{4,3,2,1,0:T(8,128)S(1)}, f32[2,2,2,64,256]{4,3,2,1,0:T(8,128)S(1)}, u32[]{:S(2)}, u32[]{:S(2)}) collective-permute-start(f32[2,2,2,64,256]{4,3,2,1,0:T(8,128)S(1)} %dynamic-slice_bitcast_fusion.1), channel_id=1, source_target_pairs={{0,2},{1,3},{2,0},{3,1},{4,6},{5,7},{6,4},{7,5},{8,10},{9,11},{10,... | collective-permute-start | bytes 1572872 | tf_op jit(solution)/shard_map/weight_grad_sum/ppermute | solution.py:29
  150.0 8.3 %collective-permute-start.10 = (f32[2,2,64,256]{3,2,1,0:T(8,128)S(1)}, f32[2,2,64,256]{3,2,1,0:T(8,128)S(1)}, u32[]{:S(2)}, u32[]{:S(2)}) collective-permute-start(f32[2,2,64,256]{3,2,1,0:T(8,128)S(1)} %dynamic-slice_bitcast_fusion.4), channel_id=1, source_target_pairs={{0,2},{1,3},{2,0},{3,1},{4,6},{5,7},{6,4},{7,5},{8,10},{9,11},{10,... | collective-permute-start | bytes 786440 | tf_op jit(solution)/shard_map/weight_grad_sum/ppermute | solution.py:29
  153.1 7.3 %collective-permute-start.15 = (f32[2,2,64,256]{3,2,1,0:T(8,128)S(1)}, f32[2,2,64,256]{3,2,1,0:T(8,128)S(1)}, u32[]{:S(2)}, u32[]{:S(2)}) collective-permute-start(f32[2,2,64,256]{3,2,1,0:T(8,128)S(1)} %dynamic-slice_bitcast_fusion.3), channel_id=1, source_target_pairs={{0,16},{16,0},{1,17},{17,1},{2,18},{18,2},{3,19},{19,3},{4,20},{20... | collective-permute-start | bytes 786440 | tf_op jit(solution)/shard_map/weight_grad_sum/ppermute | solution.py:29
  158.3 8.4 %collective-permute-start.11 = (f32[2,64,256]{2,1,0:T(8,128)S(1)}, f32[2,64,256]{2,1,0:T(8,128)S(1)}, u32[]{:S(2)}, u32[]{:S(2)}) collective-permute-start(f32[2,64,256]{2,1,0:T(8,128)S(1)} %dynamic-slice_bitcast_fusion.6), channel_id=1, source_target_pairs={{0,8},{1,9},{2,10},{3,11},{4,12},{5,13},{6,14},{7,15},{8,0},{9,1},... | collective-permute-start | bytes 393224 | tf_op jit(solution)/shard_map/weight_grad_sum/ppermute | solution.py:29
  160.4 6.8 %collective-permute-start.16 = (f32[2,64,256]{2,1,0:T(8,128)S(1)}, f32[2,64,256]{2,1,0:T(8,128)S(1)}, u32[]{:S(2)}, u32[]{:S(2)}) collective-permute-start(f32[2,64,256]{2,1,0:T(8,128)S(1)} %dynamic-slice_bitcast_fusion.5), channel_id=1, source_target_pairs={{0,4},{1,5},{2,6},{3,7},{4,0},{5,1},{6,2},{7,3},{8,12},{9,13},{10,... | collective-permute-start | bytes 393224 | tf_op jit(solution)/shard_map/weight_grad_sum/ppermute | solution.py:29
  166.8 4.7 %collective-permute-start.12 = (f32[64,256]{1,0:T(8,128)S(1)}, f32[64,256]{1,0:T(8,128)S(1)}, u32[]{:S(2)}, u32[]{:S(2)}) collective-permute-start(f32[64,256]{1,0:T(8,128)S(1)} %dynamic-slice_bitcast_fusion.8), channel_id=1, source_target_pairs={{0,4},{1,5},{2,6},{3,7},{4,0},{5,1},{6,2},{7,3},{8,12},{9,13},{10,... | collective-permute-start | bytes 196616 | tf_op jit(solution)/shard_map/weight_grad_sum/ppermute | solution.py:29
  167.2 5.3 %collective-permute-start.17 = (f32[64,256]{1,0:T(8,128)S(1)}, f32[64,256]{1,0:T(8,128)S(1)}, u32[]{:S(2)}, u32[]{:S(2)}) collective-permute-start(f32[64,256]{1,0:T(8,128)S(1)} %dynamic-slice_bitcast_fusion.7), channel_id=1, source_target_pairs={{0,8},{1,9},{2,10},{3,11},{4,12},{5,13},{6,14},{7,15},{8,0},{9,1},... | collective-permute-start | bytes 196616 | tf_op jit(solution)/shard_map/weight_grad_sum/ppermute | solution.py:29

commit v5 on v4

--- a/solution.py
+++ b/solution.py
@@ -54,8 +54,17 @@
         got = swap(current, "mp", 1 << bit)
         low = jnp.where((own >> bit) & 1 == 0, current, got)
         high = jnp.where((own >> bit) & 1 == 0, got, current)
-        current = jnp.stack([low, high], axis=step)
+        current = jnp.stack([low, high], axis=sum(1 for done in order[:step] if done > bit))
     return current.reshape(-1, rows.shape[-1])
+
+
+def split_gather(rows, order, other):
+    if other == order:
+        return doubling_gather(rows, order)
+    half = rows.shape[1] // 2
+    return jnp.concatenate(
+        [doubling_gather(rows[:, :half], order), doubling_gather(rows[:, half:], other)], axis=1
+    )
 
 
 def shards(
@@ -95,6 +104,7 @@
     neigh_two = weights_two[hidden:]
     own_inverse = lax.dynamic_slice_in_dim(inverse_all, own_index * node_dev, node_dev, 0)
     order = list(range(devices.bit_length() - 2, -1, -1))
+    other = [1] + [bit for bit in order if bit != 1] if devices == 16 else order
 
     with jax.named_scope("neighbor_tables"):
         row_ids = lax.broadcasted_iota(jnp.int32, (1, node_dev, 1), 1)
@@ -105,13 +115,13 @@
         named_by = (mine_sel[:, None] == row_ids.reshape(1, node_dev)).astype(jnp.bfloat16)
 
     down_neigh = (contract(cotangent, neigh_two, 1, 1) * own_inverse[:, None]).astype(jnp.bfloat16)
-    down_all = doubling_gather(down_neigh, order)
+    down_all = split_gather(down_neigh, order, other)
 
     pre_one = contract(own_feats, weights_one[:feat_width], 0, 0) + contract(
         own_agg_one, weights_one[feat_width:], 0, 0
     )
     hidden_one = jax.nn.silu(pre_one).astype(jnp.bfloat16)
-    hidden_all = doubling_gather(hidden_one, order)
+    hidden_all = split_gather(hidden_one, order, other)
     total = contract(own_edges, hidden_all, 0, 0)
     agg_two = (total * own_inverse[:, None]).astype(jnp.bfloat16)
     node_output = (

time: 174 us -> 150 us (0.86)
  waiting for transfers between devices: 83.3 us -> 68.1 us
  other arithmetic: 24.5 us -> 19.8 us
  local copies, waits for them, and re-layouts: 11.4 us -> 9.17 us
  starting transfers between devices: 35.5 us -> 33.6 us
    ppermute x18 -> x26, waiting for transfers between devices: 76.9 us -> 57.5 us  [swap(): return lax.ppermute(values, axis, [(j, j ^ mask) for j in range(size)])]
    all_to_all x1, waiting for transfers between devices: 6.37 us -> 10.6 us  [shards(): lax.all_to_all(agg_one_cols, 'mp', split_axis=1, concat_axis=0, tiled=True)]
    another operation x15 -> x28, other arithmetic: 6.93 us -> 2.92 us  [doubling_gather(): jnp.stack([low, high], axis=sum((1 for done in order[:step] if done > bit)))]
    all_to_all x1, starting transfers between devices: 6 us -> 3.75 us  [shards(): lax.all_to_all(agg_one_cols, 'mp', split_axis=1, concat_axis=0, tiled=True)]
    ppermute x18 -> x26, starting transfers between devices: 22.1 us -> 22.5 us  [swap(): return lax.ppermute(values, axis, [(j, j ^ mask) for j in range(size)])]
  transfers between devices with their start and end apart: 20 -> 28, of which waited for: 16 -> 16; matrix products, arithmetic and copies ran while one was open for 22% -> 25% of each run, Pallas kernels for 0% -> 0%
where the time goes in v5:
time: 150 us; the launch traced here: 149 us
  waiting for transfers between devices  68.1 us (45%)
  starting transfers between devices  33.6 us (22%)
  other arithmetic  19.8 us (13%)
  matrix products  17.2 us (11%)
  local copies, waits for them, and re-layouts  9.17 us (6%)
    ppermute x26, waiting for transfers between devices, swap(): return lax.ppermute(values, axis, [(j, j ^ mask) for j in range(size)])  57.5 us
    ppermute x26, starting transfers between devices, swap(): return lax.ppermute(values, axis, [(j, j ^ mask) for j in range(size)])  22.5 us
    dot_general x13, matrix products, contract(): lax.dot_general(left, right, (((left_dim,), (right_dim,)), ((), ())), pre...  17.2 us
    all_to_all x1, waiting for transfers between devices, shards(): lax.all_to_all(agg_one_cols, 'mp', split_axis=1, concat_axis=0, tiled=True)  10.6 us
    eq x1, other arithmetic, shards(): adjacency = (rowsel[:, None, :] == row_ids).astype(jnp.bfloat16)  9.69 us
    all_to_all x1, starting transfers between devices, shards(): lax.all_to_all(node_features, 'mp', split_axis=1, concat_axis=0, tiled=True)  7.39 us
    all_to_all x1, starting transfers between devices, shards(): lax.all_to_all(agg_one_cols, 'mp', split_axis=1, concat_axis=0, tiled=True)  3.75 us
    add x10, other arithmetic, halving_scatter(): values = keep + got  3.09 us
  transfers between devices with their start and end apart: 28, of which 16 were waited for; matrix products, arithmetic and copies ran while one was open for 25% of the time, Pallas kernels for 0%

profile of v5, /device:TPU:0, one launch (start us, length us, event | category | flops | bytes accessed | tf_op | source)
XLA Modules:
  0.0 149.3 jit_solution(13323972847738344084)
XLA Ops:
  0.7 1.3 all_to_all.28
  2.0 0.8 copy.29
  2.8 7.4 %all-to-all-start = ((bf16[32,16,192]{2,0,1:T(8,128)(2,1)}), bf16[32,16,192]{2,0,1:T(8,128)(2,1)S(1)}, u32[]{:S(2)}, u32[]{:S(2)}) async-start(bf16[32,16,192]{2,0,1:T(8,128)(2,1)} %copy.29), calls=%async_computation | async-start | bytes 524288 | tf_op jit(solution)/shard_map/all_to_all | solution.py:100
  10.2 0.7 convert_divide_fusion
  11.0 1.4 fusion.21
  12.4 2.0 %collective-permute-start.12 = (bf16[192,256]{1,0:T(8,128)(2,1)S(1)}, bf16[192,256]{1,0:T(8,128)(2,1)S(1)}, u32[]{:S(2)}, u32[]{:S(2)}) collective-permute-start(bf16[192,256]{1,0:T(8,128)(2,1)S(1)} %get-tuple-element.41), channel_id=1, source_target_pairs={{0,2},{1,3},{2,0},{3,1},{4,6},{5,7},{6,4},{7,5},{8,10},{9,11},{10,... | collective-permute-start | bytes 294920 | tf_op jit(solution)/shard_map/ppermute | solution.py:29
  14.4 2.4 %collective-permute-start.8 = (bf16[192,256]{1,0:T(8,128)(2,1)S(1)}, bf16[192,256]{1,0:T(8,128)(2,1)S(1)}, u32[]{:S(2)}, u32[]{:S(2)}) collective-permute-start(bf16[192,256]{1,0:T(8,128)(2,1)S(1)} %get-tuple-element.40), channel_id=1, source_target_pairs={{0,8},{1,9},{2,10},{3,11},{4,12},{5,13},{6,14},{7,15},{8,0},{9,1},... | collective-permute-start | bytes 294920 | tf_op jit(solution)/shard_map/ppermute | solution.py:29
  16.9 0.8 select_reduce_fusion
  17.7 9.7 %bitcast_compare_fusion = pred[3072,3072]{1,0:T(32,128)(4,1)} fusion(s32[3072]{0:T(1024)S(1)} %eq.54, s32[16,3072]{1,0:T(8,128)S(1)} %select_reduce_fusion), kind=kLoop, calls=%fused_computation | loop fusion | flops 9437184 | bytes 9646080 | tf_op jit(solution)/shard_map/layer_one_mean/eq | solution.py:90
  27.4 8.7 %fusion.1 = bf16[32,3072]{1,0:T(8,128)(2,1)S(1)} fusion(pred[3072,3072]{1,0:T(32,128)(4,1)} %bitcast_compare_fusion, bf16[32,3072]{1,0:T(8,128)(2,1)S(1)} %copy-done.9, f32[3072]{0:T(1024)S(1)} %convert_divide_fusion), kind=kOutput, calls=%fused_computation.4 | convolution fusion | flops 604176384 | bytes 9842688 | tf_op jit(solution)/shard_map/layer_one_mean/dot_general | solution.py:22
  36.1 0.3 all_to_all.32
  36.5 0.8 copy.30
  37.3 1.5 %collective-permute-start.9 = (bf16[2,192,256]{2,1,0:T(8,128)(2,1)S(1)}, bf16[2,192,256]{2,1,0:T(8,128)(2,1)S(1)}, u32[]{:S(2)}, u32[]{:S(2)}) collective-permute-start(bf16[2,192,256]{2,1,0:T(8,128)(2,1)S(1)} %pad_maximum_fusion.15), channel_id=1, source_target_pairs={{0,4},{1,5},{2,6},{3,7},{4,0},{5,1},{6,2},{7,3},{8,12},{9,13},{10,... | collective-permute-start | bytes 589832 | tf_op jit(solution)/shard_map/ppermute | solution.py:29
  38.9 1.4 bitcast_compare_fusion.1
  40.3 0.6 collective-permute-start.13
  41.0 3.8 %all-to-all-start.1 = ((bf16[32,16,192]{2,0,1:T(8,128)(2,1)}), bf16[32,16,192]{2,0,1:T(8,128)(2,1)S(1)}, u32[]{:S(2)}, u32[]{:S(2)}) async-start(bf16[32,16,192]{2,0,1:T(8,128)(2,1)} %copy.30), calls=%async_computation.1 | async-start | bytes 524288 | tf_op jit(solution)/shard_map/all_to_all | solution.py:101
  45.1 10.6 %all-to-all-done.1 = bf16[32,16,192]{2,0,1:T(8,128)(2,1)S(1)} async-done(((bf16[32,16,192]{2,0,1:T(8,128)(2,1)}), bf16[32,16,192]{2,0,1:T(8,128)(2,1)S(1)}, u32[]{:S(2)}, u32[]{:S(2)}) %all-to-all-start.1) | async-done | bytes 196640 | tf_op jit(solution)/shard_map/all_to_all | solution.py:101
  55.7 0.4 multiply_convert_fusion
  56.0 1.2 collective-permute-start
  57.3 0.6 collective-permute-start.4
  57.9 1.5 collective-permute-start.10
  59.4 5.3 %collective-permute-done = bf16[192,256]{1,0:T(8,128)(2,1)S(1)} collective-permute-done((bf16[192,256]{1,0:T(8,128)(2,1)S(1)}, bf16[192,256]{1,0:T(8,128)(2,1)S(1)}, u32[]{:S(2)}, u32[]{:S(2)}) %collective-permute-start) | collective-permute-done | bytes 98336 | tf_op jit(solution)/shard_map/ppermute | solution.py:29
  64.9 0.3 fusion.36
  65.2 1.5 %collective-permute-start.5 = (bf16[2,192,256]{2,1,0:T(8,128)(2,1)S(1)}, bf16[2,192,256]{2,1,0:T(8,128)(2,1)S(1)}, u32[]{:S(2)}, u32[]{:S(2)}) collective-permute-start(bf16[2,192,256]{2,1,0:T(8,128)(2,1)S(1)} %pad_maximum_fusion.14), channel_id=1, source_target_pairs={{0,8},{1,9},{2,10},{3,11},{4,12},{5,13},{6,14},{7,15},{8,0},{9,1},... | collective-permute-start | bytes 589832 | tf_op jit(solution)/shard_map/ppermute | solution.py:29
  66.8 6.9 %collective-permute-done.1 = bf16[2,192,256]{2,1,0:T(8,128)(2,1)S(1)} collective-permute-done((bf16[2,192,256]{2,1,0:T(8,128)(2,1)S(1)}, bf16[2,192,256]{2,1,0:T(8,128)(2,1)S(1)}, u32[]{:S(2)}, u32[]{:S(2)}) %collective-permute-start.1) | collective-permute-done | bytes 196640 | tf_op jit(solution)/shard_map/ppermute | solution.py:29
  73.7 1.7 %collective-permute-start.2 = (bf16[2,2,192,256]{3,2,0,1:T(8,128)(2,1)S(1)}, bf16[2,2,192,256]{3,2,0,1:T(8,128)(2,1)S(1)}, u32[]{:S(2)}, u32[]{:S(2)}) collective-permute-start(bf16[2,2,192,256]{3,2,0,1:T(8,128)(2,1)S(1)} %pad_maximum_fusion.9), channel_id=1, source_target_pairs={{0,2},{1,3},{2,0},{3,1},{4,6},{5,7},{6,4},{7,5},{8,10},{9,11},{10,... | collective-permute-start | bytes 1179656 | tf_op jit(solution)/shard_map/ppermute | solution.py:29
  75.5 1.9 %collective-permute-done.5 = bf16[2,192,256]{2,1,0:T(8,128)(2,1)S(1)} collective-permute-done((bf16[2,192,256]{2,1,0:T(8,128)(2,1)S(1)}, bf16[2,192,256]{2,1,0:T(8,128)(2,1)S(1)}, u32[]{:S(2)}, u32[]{:S(2)}) %collective-permute-start.5) | collective-permute-done | bytes 196640 | tf_op jit(solution)/shard_map/ppermute | solution.py:29
  77.3 1.0 select_bitcast_fusion.17
  78.5 2.1 %collective-permute-start.6 = (bf16[2,2,192,256]{3,2,1,0:T(8,128)(2,1)S(1)}, bf16[2,2,192,256]{3,2,1,0:T(8,128)(2,1)S(1)}, u32[]{:S(2)}, u32[]{:S(2)}) collective-permute-start(bf16[2,2,192,256]{3,2,1,0:T(8,128)(2,1)S(1)} %pad_maximum_fusion.10), channel_id=1, source_target_pairs={{0,4},{1,5},{2,6},{3,7},{4,0},{5,1},{6,2},{7,3},{8,12},{9,13},{10,... | collective-permute-start | bytes 1179656 | tf_op jit(solution)/shard_map/ppermute | solution.py:29
  80.6 3.5 %collective-permute-done.2 = bf16[2,2,192,256]{3,2,0,1:T(8,128)(2,1)S(1)} collective-permute-done((bf16[2,2,192,256]{3,2,0,1:T(8,128)(2,1)S(1)}, bf16[2,2,192,256]{3,2,0,1:T(8,128)(2,1)S(1)}, u32[]{:S(2)}, u32[]{:S(2)}) %collective-permute-start.2) | collective-permute-done | bytes 393248 | tf_op jit(solution)/shard_map/ppermute | solution.py:29
  84.3 6.1 %collective-permute-done.14 = bf16[2,2,192,256]{3,2,1,0:T(8,128)(2,1)S(1)} collective-permute-done((bf16[2,2,192,256]{3,2,1,0:T(8,128)(2,1)S(1)}, bf16[2,2,192,256]{3,2,1,0:T(8,128)(2,1)S(1)}, u32[]{:S(2)}, u32[]{:S(2)}) %collective-permute-start.14) | collective-permute-done | bytes 393248 | tf_op jit(solution)/shard_map/ppermute | solution.py:29
  90.8 0.6 collective-permute-start.3
  91.4 5.8 %collective-permute-done.6 = bf16[2,2,192,256]{3,2,1,0:T(8,128)(2,1)S(1)} collective-permute-done((bf16[2,2,192,256]{3,2,1,0:T(8,128)(2,1)S(1)}, bf16[2,2,192,256]{3,2,1,0:T(8,128)(2,1)S(1)}, u32[]{:S(2)}, u32[]{:S(2)}) %collective-permute-start.6) | collective-permute-done | bytes 393248 | tf_op jit(solution)/shard_map/ppermute | solution.py:29
  98.5 1.6 %fusion.6 = f32[192,512]{1,0:T(8,128)S(1)} fusion(bf16[3072,256]{1,0:T(8,128)(2,1)S(1)} %bitcast.150, bf16[3072,256]{1,0:T(8,128)(2,1)S(1)} %bitcast.148, s32[3072]{0:T(1024)S(1)} %bitcast.154), kind=kOutput, calls=%fused_computation.9 | convolution fusion | flops 610861056 | bytes 3551232 | tf_op jit(solution)/shard_map/dot_general | solution.py:22
  100.1 0.4 fusion.19
  100.5 0.3 convolution_bitcast_fusion
  101.5 1.0 copy-done.5
  102.5 1.1 fusion.16
  103.6 0.3 fusion.37
  104.0 0.4 pad_maximum_fusion
  104.4 0.3 fusion.32
  104.8 1.3 copy-done.1
  106.1 1.1 dynamic-slice_bitcast_fusion
  107.2 0.5 collective-permute-start.16
  107.9 1.1 copy.43
  108.9 1.3 fusion.28
  110.3 1.4 bitcast_add_fusion.1
  111.7 1.5 %collective-permute-start.17 = (f32[2,2,2,64,256]{4,3,2,1,0:T(8,128)S(1)}, f32[2,2,2,64,256]{4,3,2,1,0:T(8,128)S(1)}, u32[]{:S(2)}, u32[]{:S(2)}) collective-permute-start(f32[2,2,2,64,256]{4,3,2,1,0:T(8,128)S(1)} %dynamic-slice_bitcast_fusion.2), channel_id=1, source_target_pairs={{0,16},{16,0},{1,17},{17,1},{2,18},{18,2},{3,19},{19,3},{4,20},{20... | collective-permute-start | bytes 1572872 | tf_op jit(solution)/shard_map/weight_grad_sum/ppermute | solution.py:29
  113.3 1.5 bitcast_add_fusion
  114.8 1.6 %collective-permute-start.22 = (f32[2,2,2,64,256]{4,3,2,1,0:T(8,128)S(1)}, f32[2,2,2,64,256]{4,3,2,1,0:T(8,128)S(1)}, u32[]{:S(2)}, u32[]{:S(2)}) collective-permute-start(f32[2,2,2,64,256]{4,3,2,1,0:T(8,128)S(1)} %dynamic-slice_bitcast_fusion.1), channel_id=1, source_target_pairs={{0,2},{1,3},{2,0},{3,1},{4,6},{5,7},{6,4},{7,5},{8,10},{9,11},{10,... | collective-permute-start | bytes 1572872 | tf_op jit(solution)/shard_map/weight_grad_sum/ppermute | solution.py:29
  116.4 1.0 fusion.20
  117.3 8.7 %collective-permute-done.17 = f32[2,2,2,64,256]{4,3,2,1,0:T(8,128)S(1)} collective-permute-done((f32[2,2,2,64,256]{4,3,2,1,0:T(8,128)S(1)}, f32[2,2,2,64,256]{4,3,2,1,0:T(8,128)S(1)}, u32[]{:S(2)}, u32[]{:S(2)}) %collective-permute-start.17) | collective-permute-done | bytes 524320 | tf_op jit(solution)/shard_map/weight_grad_sum/ppermute | solution.py:29
  126.2 1.6 %collective-permute-start.18 = (f32[2,2,64,256]{3,2,1,0:T(8,128)S(1)}, f32[2,2,64,256]{3,2,1,0:T(8,128)S(1)}, u32[]{:S(2)}, u32[]{:S(2)}) collective-permute-start(f32[2,2,64,256]{3,2,1,0:T(8,128)S(1)} %dynamic-slice_bitcast_fusion.4), channel_id=1, source_target_pairs={{0,2},{1,3},{2,0},{3,1},{4,6},{5,7},{6,4},{7,5},{8,10},{9,11},{10,... | collective-permute-start | bytes 786440 | tf_op jit(solution)/shard_map/weight_grad_sum/ppermute | solution.py:29
  127.7 1.4 collective-permute-done.22
  129.3 0.3 collective-permute-start.23
  129.6 4.9 %collective-permute-done.18 = f32[2,2,64,256]{3,2,1,0:T(8,128)S(1)} collective-permute-done((f32[2,2,64,256]{3,2,1,0:T(8,128)S(1)}, f32[2,2,64,256]{3,2,1,0:T(8,128)S(1)}, u32[]{:S(2)}, u32[]{:S(2)}) %collective-permute-start.18) | collective-permute-done | bytes 262176 | tf_op jit(solution)/shard_map/weight_grad_sum/ppermute | solution.py:29
  134.8 1.8 %collective-permute-done.23 = f32[2,2,64,256]{3,2,1,0:T(8,128)S(1)} collective-permute-done((f32[2,2,64,256]{3,2,1,0:T(8,128)S(1)}, f32[2,2,64,256]{3,2,1,0:T(8,128)S(1)}, u32[]{:S(2)}, u32[]{:S(2)}) %collective-permute-start.23) | collective-permute-done | bytes 262176 | tf_op jit(solution)/shard_map/weight_grad_sum/ppermute | solution.py:29
  136.6 0.4 collective-permute-start.24
  137.0 5.6 %collective-permute-done.19 = f32[2,64,256]{2,1,0:T(8,128)S(1)} collective-permute-done((f32[2,64,256]{2,1,0:T(8,128)S(1)}, f32[2,64,256]{2,1,0:T(8,128)S(1)}, u32[]{:S(2)}, u32[]{:S(2)}) %collective-permute-start.19) | collective-permute-done | bytes 131104 | tf_op jit(solution)/shard_map/weight_grad_sum/ppermute | solution.py:29
  142.7 0.6 collective-permute-done.24
  143.3 0.3 collective-permute-start.25
  143.7 3.5 %collective-permute-done.20 = f32[64,256]{1,0:T(8,128)S(1)} collective-permute-done((f32[64,256]{1,0:T(8,128)S(1)}, f32[64,256]{1,0:T(8,128)S(1)}, u32[]{:S(2)}, u32[]{:S(2)}) %collective-permute-start.20) | collective-permute-done | bytes 65568 | tf_op jit(solution)/shard_map/weight_grad_sum/ppermute | solution.py:29
  147.2 1.4 collective-permute-done.25
  148.6 0.7 pad_maximum_fusion.17
  (103 shorter events, 4.7 us)
Async XLA Ops:
  0.6 10.4 %copy-start = (bf16[192,512]{1,0:T(8,128)(2,1)S(1)}, bf16[192,512]{1,0:T(8,128)(2,1)}, u32[]{:S(2)}) copy-start(bf16[192,512]{1,0:T(8,128)(2,1)} %param.13) | copy-start | bytes 589828
  0.6 16.1 %copy-start.12 = (s32[3072]{0:T(1024)S(1)}, s32[3072]{0:T(1024)}, u32[]{:S(2)}) copy-start(s32[3072]{0:T(1024)} %param.12) | copy-start | bytes 36868
  0.7 16.2 %copy-start.11 = (s32[3072,8]{0,1:T(8,128)S(1)}, s32[3072,8]{0,1:T(8,128)}, u32[]{:S(2)}) copy-start(s32[3072,8]{0,1:T(8,128)} %param.10) | copy-start | bytes 294916
  0.7 16.2 %copy-start.10 = (s32[3072,8]{0,1:T(8,128)S(1)}, s32[3072,8]{0,1:T(8,128)}, u32[]{:S(2)}) copy-start(s32[3072,8]{0,1:T(8,128)} %param.11) | copy-start | bytes 294916
  2.8 38.2 %all-to-all-start = ((bf16[32,16,192]{2,0,1:T(8,128)(2,1)}), bf16[32,16,192]{2,0,1:T(8,128)(2,1)S(1)}, u32[]{:S(2)}, u32[]{:S(2)}) async-start(bf16[32,16,192]{2,0,1:T(8,128)(2,1)} %copy.29), calls=%async_computation | async-start | bytes 524288 | tf_op jit(solution)/shard_map/all_to_all | solution.py:100
  12.4 24.9 %collective-permute-start.12 = (bf16[192,256]{1,0:T(8,128)(2,1)S(1)}, bf16[192,256]{1,0:T(8,128)(2,1)S(1)}, u32[]{:S(2)}, u32[]{:S(2)}) collective-permute-start(bf16[192,256]{1,0:T(8,128)(2,1)S(1)} %get-tuple-element.41), channel_id=1, source_target_pairs={{0,2},{1,3},{2,0},{3,1},{4,6},{5,7},{6,4},{7,5},{8,10},{9,11},{10,... | collective-permute-start | bytes 294920 | tf_op jit(solution)/shard_map/ppermute | solution.py:29
  14.4 22.9 %collective-permute-start.8 = (bf16[192,256]{1,0:T(8,128)(2,1)S(1)}, bf16[192,256]{1,0:T(8,128)(2,1)S(1)}, u32[]{:S(2)}, u32[]{:S(2)}) collective-permute-start(bf16[192,256]{1,0:T(8,128)(2,1)S(1)} %get-tuple-element.40), channel_id=1, source_target_pairs={{0,8},{1,9},{2,10},{3,11},{4,12},{5,13},{6,14},{7,15},{8,0},{9,1},... | collective-permute-start | bytes 294920 | tf_op jit(solution)/shard_map/ppermute | solution.py:29
  17.7 9.7 %copy-start.9 = (bf16[32,3072]{1,0:T(8,128)(2,1)S(1)}, bf16[32,3072]{1,0:T(8,128)(2,1)}, u32[]{:S(2)}) copy-start(bf16[32,3072]{1,0:T(8,128)(2,1)} %param.7) | copy-start | bytes 589828
  36.5 8.3 %copy-start.8 = (bf16[1024,512]{1,0:T(8,128)(2,1)S(1)}, bf16[1024,512]{1,0:T(8,128)(2,1)}, u32[]{:S(2)}) copy-start(bf16[1024,512]{1,0:T(8,128)(2,1)} %param.8) | copy-start | bytes 3145732
  37.3 7.4 %collective-permute-start.9 = (bf16[2,192,256]{2,1,0:T(8,128)(2,1)S(1)}, bf16[2,192,256]{2,1,0:T(8,128)(2,1)S(1)}, u32[]{:S(2)}, u32[]{:S(2)}) collective-permute-start(bf16[2,192,256]{2,1,0:T(8,128)(2,1)S(1)} %pad_maximum_fusion.15), channel_id=1, source_target_pairs={{0,4},{1,5},{2,6},{3,7},{4,0},{5,1},{6,2},{7,3},{8,12},{9,13},{10,... | collective-permute-start | bytes 589832 | tf_op jit(solution)/shard_map/ppermute | solution.py:29
  40.3 35.1 %collective-permute-start.13 = (bf16[2,192,256]{2,1,0:T(8,128)(2,1)S(1)}, bf16[2,192,256]{2,1,0:T(8,128)(2,1)}, u32[]{:S(2)}, u32[]{:S(2)}) collective-permute-start(bf16[2,192,256]{2,1,0:T(8,128)(2,1)S(1)} %pad_maximum_fusion.16), channel_id=1, source_target_pairs={{0,8},{1,9},{2,10},{3,11},{4,12},{5,13},{6,14},{7,15},{8,0},{9,1},... | collective-permute-start | bytes 589832 | tf_op jit(solution)/shard_map/ppermute | solution.py:29
  41.0 14.7 %all-to-all-start.1 = ((bf16[32,16,192]{2,0,1:T(8,128)(2,1)}), bf16[32,16,192]{2,0,1:T(8,128)(2,1)S(1)}, u32[]{:S(2)}, u32[]{:S(2)}) async-start(bf16[32,16,192]{2,0,1:T(8,128)(2,1)} %copy.30), calls=%async_computation.1 | async-start | bytes 524288 | tf_op jit(solution)/shard_map/all_to_all | solution.py:101
  56.0 8.7 %collective-permute-start = (bf16[192,256]{1,0:T(8,128)(2,1)S(1)}, bf16[192,256]{1,0:T(8,128)(2,1)S(1)}, u32[]{:S(2)}, u32[]{:S(2)}) collective-permute-start(bf16[192,256]{1,0:T(8,128)(2,1)S(1)} %get-tuple-element.44), channel_id=1, source_target_pairs={{0,8},{1,9},{2,10},{3,11},{4,12},{5,13},{6,14},{7,15},{8,0},{9,1},... | collective-permute-start | bytes 294920 | tf_op jit(solution)/shard_map/ppermute | solution.py:29
  57.3 7.5 %collective-permute-start.4 = (bf16[192,256]{1,0:T(8,128)(2,1)S(1)}, bf16[192,256]{1,0:T(8,128)(2,1)S(1)}, u32[]{:S(2)}, u32[]{:S(2)}) collective-permute-start(bf16[192,256]{1,0:T(8,128)(2,1)S(1)} %get-tuple-element.45), channel_id=1, source_target_pairs={{0,2},{1,3},{2,0},{3,1},{4,6},{5,7},{6,4},{7,5},{8,10},{9,11},{10,... | collective-permute-start | bytes 294920 | tf_op jit(solution)/shard_map/ppermute | solution.py:29
  57.9 22.6 %collective-permute-start.10 = (bf16[2,2,192,256]{3,2,0,1:T(8,128)(2,1)S(1)}, bf16[2,2,192,256]{3,2,0,1:T(8,128)(2,1)S(1)}, u32[]{:S(2)}, u32[]{:S(2)}) collective-permute-start(bf16[2,2,192,256]{3,2,0,1:T(8,128)(2,1)S(1)} %pad_maximum_fusion.11), channel_id=1, source_target_pairs={{0,2},{1,3},{2,0},{3,1},{4,6},{5,7},{6,4},{7,5},{8,10},{9,11},{10,... | collective-permute-start | bytes 1179656 | tf_op jit(solution)/shard_map/ppermute | solution.py:29
  64.8 8.9 %collective-permute-start.1 = (bf16[2,192,256]{2,1,0:T(8,128)(2,1)S(1)}, bf16[2,192,256]{2,1,0:T(8,128)(2,1)S(1)}, u32[]{:S(2)}, u32[]{:S(2)}) collective-permute-start(bf16[2,192,256]{2,1,0:T(8,128)(2,1)S(1)} %pad_maximum_fusion.13), channel_id=1, source_target_pairs={{0,4},{1,5},{2,6},{3,7},{4,0},{5,1},{6,2},{7,3},{8,12},{9,13},{10,... | collective-permute-start | bytes 589832 | tf_op jit(solution)/shard_map/ppermute | solution.py:29
  65.2 12.1 %collective-permute-start.5 = (bf16[2,192,256]{2,1,0:T(8,128)(2,1)S(1)}, bf16[2,192,256]{2,1,0:T(8,128)(2,1)S(1)}, u32[]{:S(2)}, u32[]{:S(2)}) collective-permute-start(bf16[2,192,256]{2,1,0:T(8,128)(2,1)S(1)} %pad_maximum_fusion.14), channel_id=1, source_target_pairs={{0,8},{1,9},{2,10},{3,11},{4,12},{5,13},{6,14},{7,15},{8,0},{9,1},... | collective-permute-start | bytes 589832 | tf_op jit(solution)/shard_map/ppermute | solution.py:29
  73.7 10.3 %collective-permute-start.2 = (bf16[2,2,192,256]{3,2,0,1:T(8,128)(2,1)S(1)}, bf16[2,2,192,256]{3,2,0,1:T(8,128)(2,1)S(1)}, u32[]{:S(2)}, u32[]{:S(2)}) collective-permute-start(bf16[2,2,192,256]{3,2,0,1:T(8,128)(2,1)S(1)} %pad_maximum_fusion.9), channel_id=1, source_target_pairs={{0,2},{1,3},{2,0},{3,1},{4,6},{5,7},{6,4},{7,5},{8,10},{9,11},{10,... | collective-permute-start | bytes 1179656 | tf_op jit(solution)/shard_map/ppermute | solution.py:29
  78.4 12.1 %collective-permute-start.14 = (bf16[2,2,192,256]{3,2,1,0:T(8,128)(2,1)S(1)}, bf16[2,2,192,256]{3,2,1,0:T(8,128)(2,1)S(1)}, u32[]{:S(2)}, u32[]{:S(2)}) collective-permute-start(bf16[2,2,192,256]{3,2,1,0:T(8,128)(2,1)S(1)} %pad_maximum_fusion.12), channel_id=1, source_target_pairs={{0,4},{1,5},{2,6},{3,7},{4,0},{5,1},{6,2},{7,3},{8,12},{9,13},{10,... | collective-permute-start | bytes 1179656 | tf_op jit(solution)/shard_map/ppermute | solution.py:29
  78.5 18.6 %collective-permute-start.6 = (bf16[2,2,192,256]{3,2,1,0:T(8,128)(2,1)S(1)}, bf16[2,2,192,256]{3,2,1,0:T(8,128)(2,1)S(1)}, u32[]{:S(2)}, u32[]{:S(2)}) collective-permute-start(bf16[2,2,192,256]{3,2,1,0:T(8,128)(2,1)S(1)} %pad_maximum_fusion.10), channel_id=1, source_target_pairs={{0,4},{1,5},{2,6},{3,7},{4,0},{5,1},{6,2},{7,3},{8,12},{9,13},{10,... | collective-permute-start | bytes 1179656 | tf_op jit(solution)/shard_map/ppermute | solution.py:29
  84.3 13.1 %collective-permute-start.11 = (bf16[2,2,2,192,256]{4,3,0,1,2:T(8,128)(2,1)S(1)}, bf16[2,2,2,192,256]{4,3,0,1,2:T(8,128)(2,1)S(1)}, u32[]{:S(2)}, u32[]{:S(2)}) collective-permute-start(bf16[2,2,2,192,256]{4,3,0,1,2:T(8,128)(2,1)S(1)} %pad_maximum_fusion.7), channel_id=1, source_target_pairs={{0,1},{1,0},{2,3},{3,2},{4,5},{5,4},{6,7},{7,6},{8,9},{9,8},{10,11... | collective-permute-start | bytes 2359304 | tf_op jit(solution)/shard_map/ppermute | solution.py:29
  90.6 7.1 %collective-permute-start.15 = (bf16[2,2,2,192,256]{4,3,2,0,1:T(8,128)(2,1)S(1)}, bf16[2,2,2,192,256]{4,3,2,0,1:T(8,128)(2,1)S(1)}, u32[]{:S(2)}, u32[]{:S(2)}) collective-permute-start(bf16[2,2,2,192,256]{4,3,2,0,1:T(8,128)(2,1)S(1)} %pad_maximum_fusion.8), channel_id=1, source_target_pairs={{0,1},{1,0},{2,3},{3,2},{4,5},{5,4},{6,7},{7,6},{8,9},{9,8},{10,11... | collective-permute-start | bytes 2359304 | tf_op jit(solution)/shard_map/ppermute | solution.py:29
  90.8 7.3 %collective-permute-start.3 = (bf16[2,2,2,192,256]{4,3,0,1,2:T(8,128)(2,1)S(1)}, bf16[2,2,2,192,256]{4,3,0,1,2:T(8,128)(2,1)S(1)}, u32[]{:S(2)}, u32[]{:S(2)}) collective-permute-start(bf16[2,2,2,192,256]{4,3,0,1,2:T(8,128)(2,1)S(1)} %pad_maximum_fusion.5), channel_id=1, source_target_pairs={{0,1},{1,0},{2,3},{3,2},{4,5},{5,4},{6,7},{7,6},{8,9},{9,8},{10,11... | collective-permute-start | bytes 2359304 | tf_op jit(solution)/shard_map/ppermute | solution.py:29
  97.2 3.8 %collective-permute-start.7 = (bf16[2,2,2,192,256]{4,3,2,0,1:T(8,128)(2,1)S(1)}, bf16[2,2,2,192,256]{4,3,2,0,1:T(8,128)(2,1)S(1)}, u32[]{:S(2)}, u32[]{:S(2)}) collective-permute-start(bf16[2,2,2,192,256]{4,3,2,0,1:T(8,128)(2,1)S(1)} %pad_maximum_fusion.6), channel_id=1, source_target_pairs={{0,1},{1,0},{2,3},{3,2},{4,5},{5,4},{6,7},{7,6},{8,9},{9,8},{10,11... | collective-permute-start | bytes 2359304 | tf_op jit(solution)/shard_map/ppermute | solution.py:29
  98.5 1.6 %copy-start.3 = (bf16[1024,512]{1,0:T(8,128)(2,1)S(1)}, bf16[1024,512]{1,0:T(8,128)(2,1)}, u32[]{:S(2)}) copy-start(bf16[1024,512]{1,0:T(8,128)(2,1)} %param.9) | copy-start | bytes 3145732
  101.4 1.1 copy-start.5
  103.6 0.8 copy-start.6
  104.8 1.3 copy-start.1
  107.2 3.1 %collective-permute-start.16 = (f32[2,2,2,2,64,256]{5,4,3,2,1,0:T(8,128)}, f32[2,2,2,2,64,256]{5,4,3,2,1,0:T(8,128)}, u32[]{:S(2)}, u32[]{:S(2)}) collective-permute-start(f32[2,2,2,2,64,256]{5,4,3,2,1,0:T(8,128)} %dynamic-slice_bitcast_fusion), channel_id=1, source_target_pairs={{0,1},{1,0},{2,3},{3,2},{4,5},{5,4},{6,7},{7,6},{8,9},{9,8},{10,11... | collective-permute-start | bytes 3145736 | tf_op jit(solution)/shard_map/weight_grad_sum/ppermute | solution.py:29
  107.9 2.5 %copy-start.2 = (f32[2048,256]{1,0:T(8,128)S(1)}, f32[2048,256]{1,0:T(8,128)}, u32[]{:S(2)}) copy-start(f32[2048,256]{1,0:T(8,128)} %copy-done.1) | copy-start | bytes 6291460
  108.9 4.4 %collective-permute-start.21 = (f32[2,2,2,2,64,256]{5,4,2,1,0,3:T(8,128)}, f32[2,2,2,2,64,256]{5,4,2,1,0,3:T(8,128)}, u32[]{:S(2)}, u32[]{:S(2)}) collective-permute-start(f32[2,2,2,2,64,256]{5,4,2,1,0,3:T(8,128)} %bitcast.142), channel_id=1, source_target_pairs={{0,1},{1,0},{2,3},{3,2},{4,5},{5,4},{6,7},{7,6},{8,9},{9,8},{10,11... | collective-permute-start | bytes 3145736 | tf_op jit(solution)/shard_map/weight_grad_sum/ppermute | solution.py:29
  111.7 14.3 %collective-permute-start.17 = (f32[2,2,2,64,256]{4,3,2,1,0:T(8,128)S(1)}, f32[2,2,2,64,256]{4,3,2,1,0:T(8,128)S(1)}, u32[]{:S(2)}, u32[]{:S(2)}) collective-permute-start(f32[2,2,2,64,256]{4,3,2,1,0:T(8,128)S(1)} %dynamic-slice_bitcast_fusion.2), channel_id=1, source_target_pairs={{0,16},{16,0},{1,17},{17,1},{2,18},{18,2},{3,19},{19,3},{4,20},{20... | collective-permute-start | bytes 1572872 | tf_op jit(solution)/shard_map/weight_grad_sum/ppermute | solution.py:29
  113.3 3.1 %copy-start.4 = (bf16[1024,512]{1,0:T(8,128)(2,1)S(1)}, bf16[1024,512]{1,0:T(8,128)(2,1)}, u32[]{:S(2)}) copy-start(bf16[1024,512]{1,0:T(8,128)(2,1)} %param.9) | copy-start | bytes 3145732
  113.3 3.1 %copy-start.7 = (bf16[192,512]{1,0:T(8,128)(2,1)S(1)}, bf16[192,512]{1,0:T(8,128)(2,1)}, u32[]{:S(2)}) copy-start(bf16[192,512]{1,0:T(8,128)(2,1)} %copy-done.6) | copy-start | bytes 589828
  114.8 14.4 %collective-permute-start.22 = (f32[2,2,2,64,256]{4,3,2,1,0:T(8,128)S(1)}, f32[2,2,2,64,256]{4,3,2,1,0:T(8,128)S(1)}, u32[]{:S(2)}, u32[]{:S(2)}) collective-permute-start(f32[2,2,2,64,256]{4,3,2,1,0:T(8,128)S(1)} %dynamic-slice_bitcast_fusion.1), channel_id=1, source_target_pairs={{0,2},{1,3},{2,0},{3,1},{4,6},{5,7},{6,4},{7,5},{8,10},{9,11},{10,... | collective-permute-start | bytes 1572872 | tf_op jit(solution)/shard_map/weight_grad_sum/ppermute | solution.py:29
  126.2 8.3 %collective-permute-start.18 = (f32[2,2,64,256]{3,2,1,0:T(8,128)S(1)}, f32[2,2,64,256]{3,2,1,0:T(8,128)S(1)}, u32[]{:S(2)}, u32[]{:S(2)}) collective-permute-start(f32[2,2,64,256]{3,2,1,0:T(8,128)S(1)} %dynamic-slice_bitcast_fusion.4), channel_id=1, source_target_pairs={{0,2},{1,3},{2,0},{3,1},{4,6},{5,7},{6,4},{7,5},{8,10},{9,11},{10,... | collective-permute-start | bytes 786440 | tf_op jit(solution)/shard_map/weight_grad_sum/ppermute | solution.py:29
  129.3 7.3 %collective-permute-start.23 = (f32[2,2,64,256]{3,2,1,0:T(8,128)S(1)}, f32[2,2,64,256]{3,2,1,0:T(8,128)S(1)}, u32[]{:S(2)}, u32[]{:S(2)}) collective-permute-start(f32[2,2,64,256]{3,2,1,0:T(8,128)S(1)} %dynamic-slice_bitcast_fusion.3), channel_id=1, source_target_pairs={{0,16},{16,0},{1,17},{17,1},{2,18},{18,2},{3,19},{19,3},{4,20},{20... | collective-permute-start | bytes 786440 | tf_op jit(solution)/shard_map/weight_grad_sum/ppermute | solution.py:29
  134.5 8.1 %collective-permute-start.19 = (f32[2,64,256]{2,1,0:T(8,128)S(1)}, f32[2,64,256]{2,1,0:T(8,128)S(1)}, u32[]{:S(2)}, u32[]{:S(2)}) collective-permute-start(f32[2,64,256]{2,1,0:T(8,128)S(1)} %dynamic-slice_bitcast_fusion.6), channel_id=1, source_target_pairs={{0,8},{1,9},{2,10},{3,11},{4,12},{5,13},{6,14},{7,15},{8,0},{9,1},... | collective-permute-start | bytes 393224 | tf_op jit(solution)/shard_map/weight_grad_sum/ppermute | solution.py:29
  136.6 6.7 %collective-permute-start.24 = (f32[2,64,256]{2,1,0:T(8,128)S(1)}, f32[2,64,256]{2,1,0:T(8,128)S(1)}, u32[]{:S(2)}, u32[]{:S(2)}) collective-permute-start(f32[2,64,256]{2,1,0:T(8,128)S(1)} %dynamic-slice_bitcast_fusion.5), channel_id=1, source_target_pairs={{0,4},{1,5},{2,6},{3,7},{4,0},{5,1},{6,2},{7,3},{8,12},{9,13},{10,... | collective-permute-start | bytes 393224 | tf_op jit(solution)/shard_map/weight_grad_sum/ppermute | solution.py:29
  142.7 4.5 %collective-permute-start.20 = (f32[64,256]{1,0:T(8,128)S(1)}, f32[64,256]{1,0:T(8,128)S(1)}, u32[]{:S(2)}, u32[]{:S(2)}) collective-permute-start(f32[64,256]{1,0:T(8,128)S(1)} %dynamic-slice_bitcast_fusion.8), channel_id=1, source_target_pairs={{0,4},{1,5},{2,6},{3,7},{4,0},{5,1},{6,2},{7,3},{8,12},{9,13},{10,... | collective-permute-start | bytes 196616 | tf_op jit(solution)/shard_map/weight_grad_sum/ppermute | solution.py:29
  143.3 5.2 %collective-permute-start.25 = (f32[64,256]{1,0:T(8,128)S(1)}, f32[64,256]{1,0:T(8,128)S(1)}, u32[]{:S(2)}, u32[]{:S(2)}) collective-permute-start(f32[64,256]{1,0:T(8,128)S(1)} %dynamic-slice_bitcast_fusion.7), channel_id=1, source_target_pairs={{0,8},{1,9},{2,10},{3,11},{4,12},{5,13},{6,14},{7,15},{8,0},{9,1},... | collective-permute-start | bytes 196616 | tf_op jit(solution)/shard_map/weight_grad_sum/ppermute | solution.py:29

commit v6 on v5

--- a/solution.py
+++ b/solution.py
@@ -67,6 +67,25 @@
     )
 
 
+def last_block_sum(block):
+    mp_index = lax.axis_index("mp")
+    rows = block.shape[0] // 8
+    values = block.reshape(2, 2, 2, rows, block.shape[1])
+    bits = [2, 1, 0]
+    for bit in [0, 1, 2]:
+        position = bits.index(bit)
+        mine = (mp_index >> bit) & 1
+        keep = lax.dynamic_index_in_dim(values, mine, position, keepdims=False)
+        send = lax.dynamic_index_in_dim(values, 1 - mine, position, keepdims=False)
+        values = keep + swap(send, "mp", 1 << bit)
+        bits.pop(position)
+    values = values.reshape(rows, block.shape[1])
+    values = values + swap(values, "mp", 8)
+    values = values + swap(values, "dp", 1)
+    lands = (lax.axis_index("dp") == 1) & (mp_index >= 8)
+    return jnp.where(lands, values, jnp.zeros_like(values))
+
+
 def shards(
     node_features, weights_one, weights_two, neighbor_owner, neighbor_row, neighbor_count, cotangent
 ):
@@ -131,17 +150,15 @@
     neighbor_sum = contract(named_by, down_all, 0, 0)
     grad_hidden = down_self + neighbor_sum
     grad_pre = (grad_hidden * silu_slope(pre_one)).astype(jnp.bfloat16)
-    terms = jnp.concatenate(
-        [
-            contract(own_feats, grad_pre, 1, 0),
-            contract(own_agg_one, grad_pre, 1, 0),
-            contract(hidden_one, cotangent, 0, 0),
-            contract(agg_two, cotangent, 0, 0),
-        ],
-        axis=0,
-    )
+    early_terms = [
+        contract(own_feats, grad_pre, 1, 0),
+        contract(own_agg_one, grad_pre, 1, 0),
+        contract(hidden_one, cotangent, 0, 0),
+    ]
+    last_term = contract(agg_two, cotangent, 0, 0)
     with jax.named_scope("weight_grad_sum"):
         if lax.axis_size("dp") == 2 and devices == 16:
+            terms = jnp.concatenate(early_terms + [jnp.zeros_like(last_term)], axis=0)
             half = terms.shape[1] // 2
             weight_grads = jnp.concatenate(
                 [
@@ -150,7 +167,9 @@
                 ],
                 axis=1,
             )
+            weight_grads = weight_grads + last_block_sum(last_term)
         else:
+            terms = jnp.concatenate(early_terms + [last_term], axis=0)
             weight_grads = lax.psum_scatter(terms, ("dp", "mp"), scatter_dimension=0, tiled=True)
     return (node_output, weight_grads)
 

time: 150 us -> 157 us (1.047)
  starting transfers between devices: 33.6 us -> 52.9 us
  waiting for transfers between devices: 68.1 us -> 52.7 us
  matrix products: 17.2 us -> 19.3 us
    ppermute x26 -> x31, starting transfers between devices: 22.5 us -> 39.1 us  [swap(): return lax.ppermute(values, axis, [(j, j ^ mask) for j in range(size)])]
    ppermute x26 -> x31, waiting for transfers between devices: 57.5 us -> 44.2 us  [swap(): return lax.ppermute(values, axis, [(j, j ^ mask) for j in range(size)])]
    all_to_all x1, starting transfers between devices: 3.75 us -> 6.49 us  [shards(): lax.all_to_all(agg_one_cols, 'mp', split_axis=1, concat_axis=0, tiled=True)]
    all_to_all x1, waiting for transfers between devices: 10.6 us -> 8.51 us  [shards(): lax.all_to_all(agg_one_cols, 'mp', split_axis=1, concat_axis=0, tiled=True)]
    dot_general x13, matrix products: 17.2 us -> 19.3 us  [contract(): lax.dot_general(left, right, (((left_dim,), (right_dim,)), ((), ())), pre...]
    add x0 -> x5, other arithmetic: none -> 1.92 us  [the longest x3 1.2 us: last_block_sum(): values = keep + swap(send, 'mp', 1 << bit)]
  transfers between devices with their start and end apart: 28 -> 33, of which waited for: 16 -> 14; matrix products, arithmetic and copies ran while one was open for 25% -> 28% of each run, Pallas kernels for 0% -> 0%
where the time goes in v6:
time: 157 us; the launch traced here: 156 us
  starting transfers between devices  52.9 us (34%)
  waiting for transfers between devices  52.7 us (34%)
  other arithmetic  19.7 us (13%)
  matrix products  19.3 us (12%)
  local copies, waits for them, and re-layouts  10 us (6%)
    ppermute x31, waiting for transfers between devices, swap(): return lax.ppermute(values, axis, [(j, j ^ mask) for j in range(size)])  44.2 us
    ppermute x31, starting transfers between devices, swap(): return lax.ppermute(values, axis, [(j, j ^ mask) for j in range(size)])  39.1 us
    dot_general x13, matrix products, contract(): lax.dot_general(left, right, (((left_dim,), (right_dim,)), ((), ())), pre...  19.3 us
    eq x1, other arithmetic, shards(): adjacency = (rowsel[:, None, :] == row_ids).astype(jnp.bfloat16)  9.72 us
    all_to_all x1, waiting for transfers between devices, shards(): lax.all_to_all(agg_one_cols, 'mp', split_axis=1, concat_axis=0, tiled=True)  8.51 us
    all_to_all x1, starting transfers between devices, shards(): lax.all_to_all(node_features, 'mp', split_axis=1, concat_axis=0, tiled=True)  7.39 us
    all_to_all x1, starting transfers between devices, shards(): lax.all_to_all(agg_one_cols, 'mp', split_axis=1, concat_axis=0, tiled=True)  6.49 us
  transfers between devices with their start and end apart: 33, of which 14 were waited for; matrix products, arithmetic and copies ran while one was open for 28% of the time, Pallas kernels for 0%

profile of v6, /device:TPU:0, one launch (start us, length us, event | category | flops | bytes accessed | tf_op | source)
XLA Modules:
  0.0 156.0 jit_solution(10851760950087555694)
XLA Ops:
  0.7 1.3 all_to_all.28
  2.0 0.8 copy.29
  2.8 7.4 %all-to-all-start = ((bf16[32,16,192]{2,0,1:T(8,128)(2,1)}), bf16[32,16,192]{2,0,1:T(8,128)(2,1)S(1)}, u32[]{:S(2)}, u32[]{:S(2)}) async-start(bf16[32,16,192]{2,0,1:T(8,128)(2,1)} %copy.29), calls=%async_computation | async-start | bytes 524288 | tf_op jit(solution)/shard_map/all_to_all | solution.py:119
  10.2 0.7 convert_divide_fusion
  11.0 1.4 fusion.21
  12.4 2.0 %collective-permute-start.12 = (bf16[192,256]{1,0:T(8,128)(2,1)S(1)}, bf16[192,256]{1,0:T(8,128)(2,1)S(1)}, u32[]{:S(2)}, u32[]{:S(2)}) collective-permute-start(bf16[192,256]{1,0:T(8,128)(2,1)S(1)} %get-tuple-element.41), channel_id=1, source_target_pairs={{0,2},{1,3},{2,0},{3,1},{4,6},{5,7},{6,4},{7,5},{8,10},{9,11},{10,... | collective-permute-start | bytes 294920 | tf_op jit(solution)/shard_map/ppermute | solution.py:29
  14.4 2.4 %collective-permute-start.8 = (bf16[192,256]{1,0:T(8,128)(2,1)S(1)}, bf16[192,256]{1,0:T(8,128)(2,1)S(1)}, u32[]{:S(2)}, u32[]{:S(2)}) collective-permute-start(bf16[192,256]{1,0:T(8,128)(2,1)S(1)} %get-tuple-element.40), channel_id=1, source_target_pairs={{0,8},{1,9},{2,10},{3,11},{4,12},{5,13},{6,14},{7,15},{8,0},{9,1},... | collective-permute-start | bytes 294920 | tf_op jit(solution)/shard_map/ppermute | solution.py:29
  16.9 0.8 select_reduce_fusion
  17.7 9.7 %bitcast_compare_fusion = pred[3072,3072]{1,0:T(32,128)(4,1)} fusion(s32[3072]{0:T(1024)S(1)} %eq.56, s32[16,3072]{1,0:T(8,128)S(1)} %select_reduce_fusion), kind=kLoop, calls=%fused_computation | loop fusion | flops 9437184 | bytes 9646080 | tf_op jit(solution)/shard_map/layer_one_mean/eq | solution.py:109
  27.4 8.7 %fusion.1 = bf16[32,3072]{1,0:T(8,128)(2,1)S(1)} fusion(pred[3072,3072]{1,0:T(32,128)(4,1)} %bitcast_compare_fusion, bf16[32,3072]{1,0:T(8,128)(2,1)S(1)} %copy-done.8, f32[3072]{0:T(1024)S(1)} %convert_divide_fusion), kind=kOutput, calls=%fused_computation.4 | convolution fusion | flops 604176384 | bytes 9842688 | tf_op jit(solution)/shard_map/layer_one_mean/dot_general | solution.py:22
  36.1 0.6 constant_dynamic-slice_fusion.2
  37.1 0.8 copy.30
  37.9 1.5 collective-permute-start.9
  39.5 1.4 bitcast_compare_fusion.1
  41.0 0.6 collective-permute-start.13
  41.6 3.4 %collective-permute-done.9 = bf16[2,192,256]{2,1,0:T(8,128)(2,1)S(1)} collective-permute-done((bf16[2,192,256]{2,1,0:T(8,128)(2,1)S(1)}, bf16[2,192,256]{2,1,0:T(8,128)(2,1)S(1)}, u32[]{:S(2)}, u32[]{:S(2)}) %collective-permute-start.9) | collective-permute-done | bytes 196640 | tf_op jit(solution)/shard_map/ppermute | solution.py:29
  45.1 0.5 collective-permute-start.10
  45.6 6.5 %all-to-all-start.1 = ((bf16[32,16,192]{2,0,1:T(8,128)(2,1)}), bf16[32,16,192]{2,0,1:T(8,128)(2,1)S(1)}, u32[]{:S(2)}, u32[]{:S(2)}) async-start(bf16[32,16,192]{2,0,1:T(8,128)(2,1)} %copy.30), calls=%async_computation.1 | async-start | bytes 524288 | tf_op jit(solution)/shard_map/all_to_all | solution.py:120
  52.3 1.3 fusion.23
  53.6 8.5 %all-to-all-done.1 = bf16[32,16,192]{2,0,1:T(8,128)(2,1)S(1)} async-done(((bf16[32,16,192]{2,0,1:T(8,128)(2,1)}), bf16[32,16,192]{2,0,1:T(8,128)(2,1)S(1)}, u32[]{:S(2)}, u32[]{:S(2)}) %all-to-all-start.1) | async-done | bytes 196640 | tf_op jit(solution)/shard_map/all_to_all | solution.py:120
  62.1 1.4 multiply_convert_fusion
  63.5 1.1 collective-permute-start
  64.7 1.7 %collective-permute-start.14 = (bf16[2,2,192,256]{3,2,1,0:T(8,128)(2,1)S(1)}, bf16[2,2,192,256]{3,2,1,0:T(8,128)(2,1)S(1)}, u32[]{:S(2)}, u32[]{:S(2)}) collective-permute-start(bf16[2,2,192,256]{3,2,1,0:T(8,128)(2,1)S(1)} %pad_maximum_fusion.11), channel_id=1, source_target_pairs={{0,4},{1,5},{2,6},{3,7},{4,0},{5,1},{6,2},{7,3},{8,12},{9,13},{10,... | collective-permute-start | bytes 1179656 | tf_op jit(solution)/shard_map/ppermute | solution.py:29
  66.4 4.8 %collective-permute-done = bf16[192,256]{1,0:T(8,128)(2,1)S(1)} collective-permute-done((bf16[192,256]{1,0:T(8,128)(2,1)S(1)}, bf16[192,256]{1,0:T(8,128)(2,1)S(1)}, u32[]{:S(2)}, u32[]{:S(2)}) %collective-permute-start) | collective-permute-done | bytes 98336 | tf_op jit(solution)/shard_map/ppermute | solution.py:29
  71.4 2.1 %collective-permute-start.5 = (bf16[2,192,256]{2,1,0:T(8,128)(2,1)S(1)}, bf16[2,192,256]{2,1,0:T(8,128)(2,1)S(1)}, u32[]{:S(2)}, u32[]{:S(2)}) collective-permute-start(bf16[2,192,256]{2,1,0:T(8,128)(2,1)S(1)} %pad_maximum_fusion.13), channel_id=1, source_target_pairs={{0,8},{1,9},{2,10},{3,11},{4,12},{5,13},{6,14},{7,15},{8,0},{9,1},... | collective-permute-start | bytes 589832 | tf_op jit(solution)/shard_map/ppermute | solution.py:29
  73.8 12.0 %collective-permute-done.1 = bf16[2,192,256]{2,1,0:T(8,128)(2,1)S(1)} collective-permute-done((bf16[2,192,256]{2,1,0:T(8,128)(2,1)S(1)}, bf16[2,192,256]{2,1,0:T(8,128)(2,1)S(1)}, u32[]{:S(2)}, u32[]{:S(2)}) %collective-permute-start.1) | collective-permute-done | bytes 196640 | tf_op jit(solution)/shard_map/ppermute | solution.py:29
  86.0 0.9 collective-permute-start.2
  87.0 0.9 collective-permute-start.6
  87.8 1.1 select_bitcast_fusion.11
  89.2 0.5 collective-permute-start.15
  89.8 6.3 %collective-permute-done.2 = bf16[2,2,192,256]{3,2,0,1:T(8,128)(2,1)S(1)} collective-permute-done((bf16[2,2,192,256]{3,2,0,1:T(8,128)(2,1)S(1)}, bf16[2,2,192,256]{3,2,0,1:T(8,128)(2,1)S(1)}, u32[]{:S(2)}, u32[]{:S(2)}) %collective-permute-start.2) | collective-permute-done | bytes 393248 | tf_op jit(solution)/shard_map/ppermute | solution.py:29
  96.5 0.5 collective-permute-start.7
  97.8 0.6 copy-done.12
  98.4 1.6 fusion.6
  100.0 0.4 fusion.19
  101.6 1.2 dynamic-slice_bitcast_fusion
  104.0 1.0 copy-done.5
  105.0 1.1 fusion.16
  106.1 0.7 copy-done.6
  107.1 0.8 dynamic-slice_bitcast_fusion.1
  108.1 1.3 fusion.28
  109.7 0.4 collective-permute-start.21
  110.2 1.1 bitcast_add_fusion.2
  111.4 1.5 collective-permute-start.27
  113.0 1.4 bitcast_add_fusion.1
  114.4 1.5 collective-permute-start.17
  115.9 4.1 %collective-permute-done.27 = f32[2,64,512]{2,1,0:T(8,128)S(1)} collective-permute-done((f32[2,64,512]{2,1,0:T(8,128)S(1)}, f32[2,64,512]{2,1,0:T(8,128)S(1)}, u32[]{:S(2)}, u32[]{:S(2)}) %collective-permute-start.27) | collective-permute-done | bytes 262176 | tf_op jit(solution)/shard_map/weight_grad_sum/ppermute | solution.py:29
  120.1 1.8 %collective-permute-start.28 = (f32[64,512]{1,0:T(8,128)S(1)}, f32[64,512]{1,0:T(8,128)S(1)}, u32[]{:S(2)}, u32[]{:S(2)}) collective-permute-start(f32[64,512]{1,0:T(8,128)S(1)} %dynamic-slice_bitcast_fusion.7), channel_id=1, source_target_pairs={{0,4},{1,5},{2,6},{3,7},{4,0},{5,1},{6,2},{7,3},{8,12},{9,13},{10,... | collective-permute-start | bytes 393224 | tf_op jit(solution)/shard_map/weight_grad_sum/ppermute | solution.py:29
  122.1 1.4 collective-permute-start.22
  123.5 1.6 %collective-permute-done.28 = f32[64,512]{1,0:T(8,128)S(1)} collective-permute-done((f32[64,512]{1,0:T(8,128)S(1)}, f32[64,512]{1,0:T(8,128)S(1)}, u32[]{:S(2)}, u32[]{:S(2)}) %collective-permute-start.28) | collective-permute-done | bytes 131104 | tf_op jit(solution)/shard_map/weight_grad_sum/ppermute | solution.py:29
  125.1 2.6 %collective-permute-start.29 = (f32[64,512]{1,0:T(8,128)S(1)}, f32[64,512]{1,0:T(8,128)S(1)}, u32[]{:S(2)}, u32[]{:S(2)}) collective-permute-start(f32[64,512]{1,0:T(8,128)S(1)} %bitcast_add_fusion.8), channel_id=1, source_target_pairs={{0,8},{1,9},{2,10},{3,11},{4,12},{5,13},{6,14},{7,15},{8,0},{9,1},... | collective-permute-start | bytes 393224 | tf_op jit(solution)/shard_map/weight_grad_sum/ppermute | solution.py:29
  127.8 1.0 fusion.20
  128.7 4.3 %collective-permute-done.29 = f32[64,512]{1,0:T(8,128)S(1)} collective-permute-done((f32[64,512]{1,0:T(8,128)S(1)}, f32[64,512]{1,0:T(8,128)S(1)}, u32[]{:S(2)}, u32[]{:S(2)}) %collective-permute-start.29) | collective-permute-done | bytes 131104 | tf_op jit(solution)/shard_map/weight_grad_sum/ppermute | solution.py:29
  133.0 1.5 collective-permute-start.30
  134.7 1.2 collective-permute-start.18
  136.1 2.5 %collective-permute-start.23 = (f32[2,2,64,256]{3,2,1,0:T(8,128)S(1)}, f32[2,2,64,256]{3,2,1,0:T(8,128)S(1)}, u32[]{:S(2)}, u32[]{:S(2)}) collective-permute-start(f32[2,2,64,256]{3,2,1,0:T(8,128)S(1)} %dynamic-slice_bitcast_fusion.5), channel_id=1, source_target_pairs={{0,16},{16,0},{1,17},{17,1},{2,18},{18,2},{3,19},{19,3},{4,20},{20... | collective-permute-start | bytes 786440 | tf_op jit(solution)/shard_map/weight_grad_sum/ppermute | solution.py:29
  138.6 2.5 %collective-permute-done.18 = f32[2,2,64,256]{3,2,1,0:T(8,128)S(1)} collective-permute-done((f32[2,2,64,256]{3,2,1,0:T(8,128)S(1)}, f32[2,2,64,256]{3,2,1,0:T(8,128)S(1)}, u32[]{:S(2)}, u32[]{:S(2)}) %collective-permute-start.18) | collective-permute-done | bytes 262176 | tf_op jit(solution)/shard_map/weight_grad_sum/ppermute | solution.py:29
  141.2 2.2 %collective-permute-start.19 = (f32[2,64,256]{2,1,0:T(8,128)S(1)}, f32[2,64,256]{2,1,0:T(8,128)S(1)}, u32[]{:S(2)}, u32[]{:S(2)}) collective-permute-start(f32[2,64,256]{2,1,0:T(8,128)S(1)} %dynamic-slice_bitcast_fusion.9), channel_id=1, source_target_pairs={{0,8},{1,9},{2,10},{3,11},{4,12},{5,13},{6,14},{7,15},{8,0},{9,1},... | collective-permute-start | bytes 393224 | tf_op jit(solution)/shard_map/weight_grad_sum/ppermute | solution.py:29
  143.4 2.3 %collective-permute-start.24 = (f32[2,64,256]{2,1,0:T(8,128)S(1)}, f32[2,64,256]{2,1,0:T(8,128)S(1)}, u32[]{:S(2)}, u32[]{:S(2)}) collective-permute-start(f32[2,64,256]{2,1,0:T(8,128)S(1)} %dynamic-slice_bitcast_fusion.8), channel_id=1, source_target_pairs={{0,4},{1,5},{2,6},{3,7},{4,0},{5,1},{6,2},{7,3},{8,12},{9,13},{10,... | collective-permute-start | bytes 393224 | tf_op jit(solution)/shard_map/weight_grad_sum/ppermute | solution.py:29
  145.7 1.9 %collective-permute-done.19 = f32[2,64,256]{2,1,0:T(8,128)S(1)} collective-permute-done((f32[2,64,256]{2,1,0:T(8,128)S(1)}, f32[2,64,256]{2,1,0:T(8,128)S(1)}, u32[]{:S(2)}, u32[]{:S(2)}) %collective-permute-start.19) | collective-permute-done | bytes 131104 | tf_op jit(solution)/shard_map/weight_grad_sum/ppermute | solution.py:29
  147.7 2.3 %collective-permute-start.20 = (f32[64,256]{1,0:T(8,128)S(1)}, f32[64,256]{1,0:T(8,128)S(1)}, u32[]{:S(2)}, u32[]{:S(2)}) collective-permute-start(f32[64,256]{1,0:T(8,128)S(1)} %dynamic-slice_bitcast_fusion.11), channel_id=1, source_target_pairs={{0,4},{1,5},{2,6},{3,7},{4,0},{5,1},{6,2},{7,3},{8,12},{9,13},{10,... | collective-permute-start | bytes 196616 | tf_op jit(solution)/shard_map/weight_grad_sum/ppermute | solution.py:29
  150.0 2.6 %collective-permute-start.25 = (f32[64,256]{1,0:T(8,128)S(1)}, f32[64,256]{1,0:T(8,128)S(1)}, u32[]{:S(2)}, u32[]{:S(2)}) collective-permute-start(f32[64,256]{1,0:T(8,128)S(1)} %dynamic-slice_bitcast_fusion.10), channel_id=1, source_target_pairs={{0,8},{1,9},{2,10},{3,11},{4,12},{5,13},{6,14},{7,15},{8,0},{9,1},... | collective-permute-start | bytes 196616 | tf_op jit(solution)/shard_map/weight_grad_sum/ppermute | solution.py:29
  152.6 2.6 %collective-permute-done.25 = f32[64,256]{1,0:T(8,128)S(1)} collective-permute-done((f32[64,256]{1,0:T(8,128)S(1)}, f32[64,256]{1,0:T(8,128)S(1)}, u32[]{:S(2)}, u32[]{:S(2)}) %collective-permute-start.25) | collective-permute-done | bytes 65568 | tf_op jit(solution)/shard_map/weight_grad_sum/ppermute | solution.py:29
  155.3 0.7 maximum_add_fusion
  (123 shorter events, 7.0 us)
Async XLA Ops:
  0.6 10.4 %copy-start = (bf16[192,512]{1,0:T(8,128)(2,1)S(1)}, bf16[192,512]{1,0:T(8,128)(2,1)}, u32[]{:S(2)}) copy-start(bf16[192,512]{1,0:T(8,128)(2,1)} %param.13) | copy-start | bytes 589828
  0.6 16.1 %copy-start.11 = (s32[3072]{0:T(1024)S(1)}, s32[3072]{0:T(1024)}, u32[]{:S(2)}) copy-start(s32[3072]{0:T(1024)} %param.12) | copy-start | bytes 36868
  0.7 16.2 %copy-start.10 = (s32[3072,8]{0,1:T(8,128)S(1)}, s32[3072,8]{0,1:T(8,128)}, u32[]{:S(2)}) copy-start(s32[3072,8]{0,1:T(8,128)} %param.10) | copy-start | bytes 294916
  0.7 16.2 %copy-start.9 = (s32[3072,8]{0,1:T(8,128)S(1)}, s32[3072,8]{0,1:T(8,128)}, u32[]{:S(2)}) copy-start(s32[3072,8]{0,1:T(8,128)} %param.11) | copy-start | bytes 294916
  2.8 42.8 %all-to-all-start = ((bf16[32,16,192]{2,0,1:T(8,128)(2,1)}), bf16[32,16,192]{2,0,1:T(8,128)(2,1)S(1)}, u32[]{:S(2)}, u32[]{:S(2)}) async-start(bf16[32,16,192]{2,0,1:T(8,128)(2,1)} %copy.29), calls=%async_computation | async-start | bytes 524288 | tf_op jit(solution)/shard_map/all_to_all | solution.py:119
  12.4 25.4 %collective-permute-start.12 = (bf16[192,256]{1,0:T(8,128)(2,1)S(1)}, bf16[192,256]{1,0:T(8,128)(2,1)S(1)}, u32[]{:S(2)}, u32[]{:S(2)}) collective-permute-start(bf16[192,256]{1,0:T(8,128)(2,1)S(1)} %get-tuple-element.41), channel_id=1, source_target_pairs={{0,2},{1,3},{2,0},{3,1},{4,6},{5,7},{6,4},{7,5},{8,10},{9,11},{10,... | collective-permute-start | bytes 294920 | tf_op jit(solution)/shard_map/ppermute | solution.py:29
  14.4 23.5 %collective-permute-start.8 = (bf16[192,256]{1,0:T(8,128)(2,1)S(1)}, bf16[192,256]{1,0:T(8,128)(2,1)S(1)}, u32[]{:S(2)}, u32[]{:S(2)}) collective-permute-start(bf16[192,256]{1,0:T(8,128)(2,1)S(1)} %get-tuple-element.40), channel_id=1, source_target_pairs={{0,8},{1,9},{2,10},{3,11},{4,12},{5,13},{6,14},{7,15},{8,0},{9,1},... | collective-permute-start | bytes 294920 | tf_op jit(solution)/shard_map/ppermute | solution.py:29
  17.7 9.7 %copy-start.8 = (bf16[32,3072]{1,0:T(8,128)(2,1)S(1)}, bf16[32,3072]{1,0:T(8,128)(2,1)}, u32[]{:S(2)}) copy-start(bf16[32,3072]{1,0:T(8,128)(2,1)} %param.7) | copy-start | bytes 589828
  37.9 7.1 %collective-permute-start.9 = (bf16[2,192,256]{2,1,0:T(8,128)(2,1)S(1)}, bf16[2,192,256]{2,1,0:T(8,128)(2,1)S(1)}, u32[]{:S(2)}, u32[]{:S(2)}) collective-permute-start(bf16[2,192,256]{2,1,0:T(8,128)(2,1)S(1)} %pad_maximum_fusion.14), channel_id=1, source_target_pairs={{0,4},{1,5},{2,6},{3,7},{4,0},{5,1},{6,2},{7,3},{8,12},{9,13},{10,... | collective-permute-start | bytes 589832 | tf_op jit(solution)/shard_map/ppermute | solution.py:29
  41.0 11.3 %collective-permute-start.13 = (bf16[2,192,256]{2,1,0:T(8,128)(2,1)S(1)}, bf16[2,192,256]{2,1,0:T(8,128)(2,1)S(1)}, u32[]{:S(2)}, u32[]{:S(2)}) collective-permute-start(bf16[2,192,256]{2,1,0:T(8,128)(2,1)S(1)} %pad_maximum_fusion.15), channel_id=1, source_target_pairs={{0,8},{1,9},{2,10},{3,11},{4,12},{5,13},{6,14},{7,15},{8,0},{9,1},... | collective-permute-start | bytes 589832 | tf_op jit(solution)/shard_map/ppermute | solution.py:29
  45.1 42.7 %collective-permute-start.10 = (bf16[2,2,192,256]{3,2,0,1:T(8,128)(2,1)S(1)}, bf16[2,2,192,256]{3,2,0,1:T(8,128)(2,1)}, u32[]{:S(2)}, u32[]{:S(2)}) collective-permute-start(bf16[2,2,192,256]{3,2,0,1:T(8,128)(2,1)S(1)} %pad_maximum_fusion.10), channel_id=1, source_target_pairs={{0,2},{1,3},{2,0},{3,1},{4,6},{5,7},{6,4},{7,5},{8,10},{9,11},{10,... | collective-permute-start | bytes 1179656 | tf_op jit(solution)/shard_map/ppermute | solution.py:29
  45.6 16.5 %all-to-all-start.1 = ((bf16[32,16,192]{2,0,1:T(8,128)(2,1)}), bf16[32,16,192]{2,0,1:T(8,128)(2,1)S(1)}, u32[]{:S(2)}, u32[]{:S(2)}) async-start(bf16[32,16,192]{2,0,1:T(8,128)(2,1)} %copy.30), calls=%async_computation.1 | async-start | bytes 524288 | tf_op jit(solution)/shard_map/all_to_all | solution.py:120
  63.5 7.7 %collective-permute-start = (bf16[192,256]{1,0:T(8,128)(2,1)S(1)}, bf16[192,256]{1,0:T(8,128)(2,1)S(1)}, u32[]{:S(2)}, u32[]{:S(2)}) collective-permute-start(bf16[192,256]{1,0:T(8,128)(2,1)S(1)} %get-tuple-element.44), channel_id=1, source_target_pairs={{0,8},{1,9},{2,10},{3,11},{4,12},{5,13},{6,14},{7,15},{8,0},{9,1},... | collective-permute-start | bytes 294920 | tf_op jit(solution)/shard_map/ppermute | solution.py:29
  64.7 6.6 %collective-permute-start.4 = (bf16[192,256]{1,0:T(8,128)(2,1)S(1)}, bf16[192,256]{1,0:T(8,128)(2,1)S(1)}, u32[]{:S(2)}, u32[]{:S(2)}) collective-permute-start(bf16[192,256]{1,0:T(8,128)(2,1)S(1)} %get-tuple-element.45), channel_id=1, source_target_pairs={{0,2},{1,3},{2,0},{3,1},{4,6},{5,7},{6,4},{7,5},{8,10},{9,11},{10,... | collective-permute-start | bytes 294920 | tf_op jit(solution)/shard_map/ppermute | solution.py:29
  64.7 24.4 %collective-permute-start.14 = (bf16[2,2,192,256]{3,2,1,0:T(8,128)(2,1)S(1)}, bf16[2,2,192,256]{3,2,1,0:T(8,128)(2,1)S(1)}, u32[]{:S(2)}, u32[]{:S(2)}) collective-permute-start(bf16[2,2,192,256]{3,2,1,0:T(8,128)(2,1)S(1)} %pad_maximum_fusion.11), channel_id=1, source_target_pairs={{0,4},{1,5},{2,6},{3,7},{4,0},{5,1},{6,2},{7,3},{8,12},{9,13},{10,... | collective-permute-start | bytes 1179656 | tf_op jit(solution)/shard_map/ppermute | solution.py:29
  71.3 14.5 %collective-permute-start.1 = (bf16[2,192,256]{2,1,0:T(8,128)(2,1)S(1)}, bf16[2,192,256]{2,1,0:T(8,128)(2,1)S(1)}, u32[]{:S(2)}, u32[]{:S(2)}) collective-permute-start(bf16[2,192,256]{2,1,0:T(8,128)(2,1)S(1)} %pad_maximum_fusion.12), channel_id=1, source_target_pairs={{0,4},{1,5},{2,6},{3,7},{4,0},{5,1},{6,2},{7,3},{8,12},{9,13},{10,... | collective-permute-start | bytes 589832 | tf_op jit(solution)/shard_map/ppermute | solution.py:29
  71.4 14.4 %collective-permute-start.5 = (bf16[2,192,256]{2,1,0:T(8,128)(2,1)S(1)}, bf16[2,192,256]{2,1,0:T(8,128)(2,1)S(1)}, u32[]{:S(2)}, u32[]{:S(2)}) collective-permute-start(bf16[2,192,256]{2,1,0:T(8,128)(2,1)S(1)} %pad_maximum_fusion.13), channel_id=1, source_target_pairs={{0,8},{1,9},{2,10},{3,11},{4,12},{5,13},{6,14},{7,15},{8,0},{9,1},... | collective-permute-start | bytes 589832 | tf_op jit(solution)/shard_map/ppermute | solution.py:29
  86.0 10.1 %collective-permute-start.2 = (bf16[2,2,192,256]{3,2,0,1:T(8,128)(2,1)S(1)}, bf16[2,2,192,256]{3,2,0,1:T(8,128)(2,1)S(1)}, u32[]{:S(2)}, u32[]{:S(2)}) collective-permute-start(bf16[2,2,192,256]{3,2,0,1:T(8,128)(2,1)S(1)} %pad_maximum_fusion.8), channel_id=1, source_target_pairs={{0,2},{1,3},{2,0},{3,1},{4,6},{5,7},{6,4},{7,5},{8,10},{9,11},{10,... | collective-permute-start | bytes 1179656 | tf_op jit(solution)/shard_map/ppermute | solution.py:29
  87.0 9.3 %collective-permute-start.6 = (bf16[2,2,192,256]{3,2,1,0:T(8,128)(2,1)S(1)}, bf16[2,2,192,256]{3,2,1,0:T(8,128)(2,1)S(1)}, u32[]{:S(2)}, u32[]{:S(2)}) collective-permute-start(bf16[2,2,192,256]{3,2,1,0:T(8,128)(2,1)S(1)} %pad_maximum_fusion.9), channel_id=1, source_target_pairs={{0,4},{1,5},{2,6},{3,7},{4,0},{5,1},{6,2},{7,3},{8,12},{9,13},{10,... | collective-permute-start | bytes 1179656 | tf_op jit(solution)/shard_map/ppermute | solution.py:29
  89.0 8.0 %collective-permute-start.11 = (bf16[2,2,2,192,256]{4,3,0,1,2:T(8,128)(2,1)S(1)}, bf16[2,2,2,192,256]{4,3,0,1,2:T(8,128)(2,1)S(1)}, u32[]{:S(2)}, u32[]{:S(2)}) collective-permute-start(bf16[2,2,2,192,256]{4,3,0,1,2:T(8,128)(2,1)S(1)} %pad_maximum_fusion.6), channel_id=1, source_target_pairs={{0,1},{1,0},{2,3},{3,2},{4,5},{5,4},{6,7},{7,6},{8,9},{9,8},{10,11... | collective-permute-start | bytes 2359304 | tf_op jit(solution)/shard_map/ppermute | solution.py:29
  89.2 8.2 %collective-permute-start.15 = (bf16[2,2,2,192,256]{4,3,2,0,1:T(8,128)(2,1)S(1)}, bf16[2,2,2,192,256]{4,3,2,0,1:T(8,128)(2,1)S(1)}, u32[]{:S(2)}, u32[]{:S(2)}) collective-permute-start(bf16[2,2,2,192,256]{4,3,2,0,1:T(8,128)(2,1)S(1)} %pad_maximum_fusion.7), channel_id=1, source_target_pairs={{0,1},{1,0},{2,3},{3,2},{4,5},{5,4},{6,7},{7,6},{8,9},{9,8},{10,11... | collective-permute-start | bytes 2359304 | tf_op jit(solution)/shard_map/ppermute | solution.py:29
  96.2 6.6 %collective-permute-start.3 = (bf16[2,2,2,192,256]{4,3,0,1,2:T(8,128)(2,1)S(1)}, bf16[2,2,2,192,256]{4,3,0,1,2:T(8,128)(2,1)S(1)}, u32[]{:S(2)}, u32[]{:S(2)}) collective-permute-start(bf16[2,2,2,192,256]{4,3,0,1,2:T(8,128)(2,1)S(1)} %pad_maximum_fusion.4), channel_id=1, source_target_pairs={{0,1},{1,0},{2,3},{3,2},{4,5},{5,4},{6,7},{7,6},{8,9},{9,8},{10,11... | collective-permute-start | bytes 2359304 | tf_op jit(solution)/shard_map/ppermute | solution.py:29
  96.5 7.1 %collective-permute-start.7 = (bf16[2,2,2,192,256]{4,3,2,0,1:T(8,128)(2,1)S(1)}, bf16[2,2,2,192,256]{4,3,2,0,1:T(8,128)(2,1)S(1)}, u32[]{:S(2)}, u32[]{:S(2)}) collective-permute-start(bf16[2,2,2,192,256]{4,3,2,0,1:T(8,128)(2,1)S(1)} %pad_maximum_fusion.5), channel_id=1, source_target_pairs={{0,1},{1,0},{2,3},{3,2},{4,5},{5,4},{6,7},{7,6},{8,9},{9,8},{10,11... | collective-permute-start | bytes 2359304 | tf_op jit(solution)/shard_map/ppermute | solution.py:29
  97.7 0.7 copy-start.12
  98.4 1.6 %copy-start.3 = (bf16[1024,512]{1,0:T(8,128)(2,1)S(1)}, bf16[1024,512]{1,0:T(8,128)(2,1)}, u32[]{:S(2)}) copy-start(bf16[1024,512]{1,0:T(8,128)(2,1)} %param.9) | copy-start | bytes 3145732
  101.6 1.7 %copy-start.1 = (f32[2048,256]{1,0:T(8,128)}, f32[2048,256]{1,0:T(8,128)S(1)}, u32[]{:S(2)}) copy-start(f32[2048,256]{1,0:T(8,128)S(1)} %get-tuple-element.2) | copy-start | bytes 6291460
  102.8 10.1 %collective-permute-start.16 = (f32[2,2,2,2,64,256]{5,4,3,2,1,0:T(8,128)}, f32[2,2,2,2,64,256]{5,4,3,2,1,0:T(8,128)}, u32[]{:S(2)}, u32[]{:S(2)}) collective-permute-start(f32[2,2,2,2,64,256]{5,4,3,2,1,0:T(8,128)} %dynamic-slice_bitcast_fusion), channel_id=1, source_target_pairs={{0,1},{1,0},{2,3},{3,2},{4,5},{5,4},{6,7},{7,6},{8,9},{9,8},{10,11... | collective-permute-start | bytes 3145736 | tf_op jit(solution)/shard_map/weight_grad_sum/ppermute | solution.py:29
  103.9 1.1 copy-start.5
  106.1 0.7 copy-start.6
  108.0 2.3 %collective-permute-start.26 = (f32[2,2,64,512]{3,2,1,0:T(8,128)}, f32[2,2,64,512]{3,2,1,0:T(8,128)}, u32[]{:S(2)}, u32[]{:S(2)}) collective-permute-start(f32[2,2,64,512]{3,2,1,0:T(8,128)} %dynamic-slice_bitcast_fusion.1), channel_id=1, source_target_pairs={{0,1},{1,0},{2,3},{3,2},{4,5},{5,4},{6,7},{7,6},{8,9},{9,8},{10,11... | collective-permute-start | bytes 1572872 | tf_op jit(solution)/shard_map/weight_grad_sum/ppermute | solution.py:29
  109.6 3.3 %copy-start.2 = (f32[2048,256]{1,0:T(8,128)S(1)}, f32[2048,256]{1,0:T(8,128)}, u32[]{:S(2)}) copy-start(f32[2048,256]{1,0:T(8,128)} %copy-done.1) | copy-start | bytes 6291460
  109.7 12.2 %collective-permute-start.21 = (f32[2,2,2,2,64,256]{5,4,2,1,0,3:T(8,128)S(1)}, f32[2,2,2,2,64,256]{5,4,2,1,0,3:T(8,128)S(1)}, u32[]{:S(2)}, u32[]{:S(2)}) collective-permute-start(f32[2,2,2,2,64,256]{5,4,2,1,0,3:T(8,128)S(1)} %bitcast.167), channel_id=1, source_target_pairs={{0,1},{1,0},{2,3},{3,2},{4,5},{5,4},{6,7},{7,6},{8,9},{9,8},{10,11... | collective-permute-start | bytes 3145736 | tf_op jit(solution)/shard_map/weight_grad_sum/ppermute | solution.py:29
  111.4 8.6 %collective-permute-start.27 = (f32[2,64,512]{2,1,0:T(8,128)S(1)}, f32[2,64,512]{2,1,0:T(8,128)S(1)}, u32[]{:S(2)}, u32[]{:S(2)}) collective-permute-start(f32[2,64,512]{2,1,0:T(8,128)S(1)} %dynamic-slice_bitcast_fusion.4), channel_id=1, source_target_pairs={{0,2},{1,3},{2,0},{3,1},{4,6},{5,7},{6,4},{7,5},{8,10},{9,11},{10,... | collective-permute-start | bytes 786440 | tf_op jit(solution)/shard_map/weight_grad_sum/ppermute | solution.py:29
  114.4 20.2 %collective-permute-start.17 = (f32[2,2,2,64,256]{4,3,2,1,0:T(8,128)S(1)}, f32[2,2,2,64,256]{4,3,2,1,0:T(8,128)S(1)}, u32[]{:S(2)}, u32[]{:S(2)}) collective-permute-start(f32[2,2,2,64,256]{4,3,2,1,0:T(8,128)S(1)} %dynamic-slice_bitcast_fusion.3), channel_id=1, source_target_pairs={{0,16},{16,0},{1,17},{17,1},{2,18},{18,2},{3,19},{19,3},{4,20},{20... | collective-permute-start | bytes 1572872 | tf_op jit(solution)/shard_map/weight_grad_sum/ppermute | solution.py:29
  120.1 5.0 %collective-permute-start.28 = (f32[64,512]{1,0:T(8,128)S(1)}, f32[64,512]{1,0:T(8,128)S(1)}, u32[]{:S(2)}, u32[]{:S(2)}) collective-permute-start(f32[64,512]{1,0:T(8,128)S(1)} %dynamic-slice_bitcast_fusion.7), channel_id=1, source_target_pairs={{0,4},{1,5},{2,6},{3,7},{4,0},{5,1},{6,2},{7,3},{8,12},{9,13},{10,... | collective-permute-start | bytes 393224 | tf_op jit(solution)/shard_map/weight_grad_sum/ppermute | solution.py:29
  121.9 5.9 %copy-start.4 = (bf16[1024,512]{1,0:T(8,128)(2,1)S(1)}, bf16[1024,512]{1,0:T(8,128)(2,1)}, u32[]{:S(2)}) copy-start(bf16[1024,512]{1,0:T(8,128)(2,1)} %param.9) | copy-start | bytes 3145732
  121.9 5.9 %copy-start.7 = (bf16[192,512]{1,0:T(8,128)(2,1)S(1)}, bf16[192,512]{1,0:T(8,128)(2,1)}, u32[]{:S(2)}) copy-start(bf16[192,512]{1,0:T(8,128)(2,1)} %copy-done.6) | copy-start | bytes 589828
  122.1 13.9 %collective-permute-start.22 = (f32[2,2,2,64,256]{4,3,2,1,0:T(8,128)S(1)}, f32[2,2,2,64,256]{4,3,2,1,0:T(8,128)S(1)}, u32[]{:S(2)}, u32[]{:S(2)}) collective-permute-start(f32[2,2,2,64,256]{4,3,2,1,0:T(8,128)S(1)} %dynamic-slice_bitcast_fusion.2), channel_id=1, source_target_pairs={{0,2},{1,3},{2,0},{3,1},{4,6},{5,7},{6,4},{7,5},{8,10},{9,11},{10,... | collective-permute-start | bytes 1572872 | tf_op jit(solution)/shard_map/weight_grad_sum/ppermute | solution.py:29
  125.1 7.8 %collective-permute-start.29 = (f32[64,512]{1,0:T(8,128)S(1)}, f32[64,512]{1,0:T(8,128)S(1)}, u32[]{:S(2)}, u32[]{:S(2)}) collective-permute-start(f32[64,512]{1,0:T(8,128)S(1)} %bitcast_add_fusion.8), channel_id=1, source_target_pairs={{0,8},{1,9},{2,10},{3,11},{4,12},{5,13},{6,14},{7,15},{8,0},{9,1},... | collective-permute-start | bytes 393224 | tf_op jit(solution)/shard_map/weight_grad_sum/ppermute | solution.py:29
  133.0 22.3 %collective-permute-start.30 = (f32[64,512]{1,0:T(8,128)S(1)}, f32[64,512]{1,0:T(8,128)S(1)}, u32[]{:S(2)}, u32[]{:S(2)}) collective-permute-start(f32[64,512]{1,0:T(8,128)S(1)} %add.191), channel_id=1, source_target_pairs={{0,16},{16,0},{1,17},{17,1},{2,18},{18,2},{3,19},{19,3},{4,20},{20... | collective-permute-start | bytes 393224 | tf_op jit(solution)/shard_map/weight_grad_sum/ppermute | solution.py:29
  134.7 6.4 %collective-permute-start.18 = (f32[2,2,64,256]{3,2,1,0:T(8,128)S(1)}, f32[2,2,64,256]{3,2,1,0:T(8,128)S(1)}, u32[]{:S(2)}, u32[]{:S(2)}) collective-permute-start(f32[2,2,64,256]{3,2,1,0:T(8,128)S(1)} %dynamic-slice_bitcast_fusion.6), channel_id=1, source_target_pairs={{0,2},{1,3},{2,0},{3,1},{4,6},{5,7},{6,4},{7,5},{8,10},{9,11},{10,... | collective-permute-start | bytes 786440 | tf_op jit(solution)/shard_map/weight_grad_sum/ppermute | solution.py:29
  136.1 7.3 %collective-permute-start.23 = (f32[2,2,64,256]{3,2,1,0:T(8,128)S(1)}, f32[2,2,64,256]{3,2,1,0:T(8,128)S(1)}, u32[]{:S(2)}, u32[]{:S(2)}) collective-permute-start(f32[2,2,64,256]{3,2,1,0:T(8,128)S(1)} %dynamic-slice_bitcast_fusion.5), channel_id=1, source_target_pairs={{0,16},{16,0},{1,17},{17,1},{2,18},{18,2},{3,19},{19,3},{4,20},{20... | collective-permute-start | bytes 786440 | tf_op jit(solution)/shard_map/weight_grad_sum/ppermute | solution.py:29
  141.2 6.5 %collective-permute-start.19 = (f32[2,64,256]{2,1,0:T(8,128)S(1)}, f32[2,64,256]{2,1,0:T(8,128)S(1)}, u32[]{:S(2)}, u32[]{:S(2)}) collective-permute-start(f32[2,64,256]{2,1,0:T(8,128)S(1)} %dynamic-slice_bitcast_fusion.9), channel_id=1, source_target_pairs={{0,8},{1,9},{2,10},{3,11},{4,12},{5,13},{6,14},{7,15},{8,0},{9,1},... | collective-permute-start | bytes 393224 | tf_op jit(solution)/shard_map/weight_grad_sum/ppermute | solution.py:29
  143.4 6.6 %collective-permute-start.24 = (f32[2,64,256]{2,1,0:T(8,128)S(1)}, f32[2,64,256]{2,1,0:T(8,128)S(1)}, u32[]{:S(2)}, u32[]{:S(2)}) collective-permute-start(f32[2,64,256]{2,1,0:T(8,128)S(1)} %dynamic-slice_bitcast_fusion.8), channel_id=1, source_target_pairs={{0,4},{1,5},{2,6},{3,7},{4,0},{5,1},{6,2},{7,3},{8,12},{9,13},{10,... | collective-permute-start | bytes 393224 | tf_op jit(solution)/shard_map/weight_grad_sum/ppermute | solution.py:29
  147.7 4.9 %collective-permute-start.20 = (f32[64,256]{1,0:T(8,128)S(1)}, f32[64,256]{1,0:T(8,128)S(1)}, u32[]{:S(2)}, u32[]{:S(2)}) collective-permute-start(f32[64,256]{1,0:T(8,128)S(1)} %dynamic-slice_bitcast_fusion.11), channel_id=1, source_target_pairs={{0,4},{1,5},{2,6},{3,7},{4,0},{5,1},{6,2},{7,3},{8,12},{9,13},{10,... | collective-permute-start | bytes 196616 | tf_op jit(solution)/shard_map/weight_grad_sum/ppermute | solution.py:29
  150.0 5.2 %collective-permute-start.25 = (f32[64,256]{1,0:T(8,128)S(1)}, f32[64,256]{1,0:T(8,128)S(1)}, u32[]{:S(2)}, u32[]{:S(2)}) collective-permute-start(f32[64,256]{1,0:T(8,128)S(1)} %dynamic-slice_bitcast_fusion.10), channel_id=1, source_target_pairs={{0,8},{1,9},{2,10},{3,11},{4,12},{5,13},{6,14},{7,15},{8,0},{9,1},... | collective-permute-start | bytes 196616 | tf_op jit(solution)/shard_map/weight_grad_sum/ppermute | solution.py:29

commit v7 on v5

--- a/solution.py
+++ b/solution.py
@@ -96,10 +96,9 @@
             global_ids = owner_slots * node_dev + neighbor_row.T
             agg_one_cols = column_mean(node_features, global_ids, live.T, inverse_all)
 
-    own_feats, own_agg_one = (
-        lax.all_to_all(node_features, "mp", split_axis=1, concat_axis=0, tiled=True),
-        lax.all_to_all(agg_one_cols, "mp", split_axis=1, concat_axis=0, tiled=True),
-    )
+    both = jnp.stack([node_features, agg_one_cols], axis=0)
+    both = lax.all_to_all(both, "mp", split_axis=2, concat_axis=1, tiled=True)
+    own_feats, own_agg_one = both[0], both[1]
     self_two = weights_two[:hidden]
     neigh_two = weights_two[hidden:]
     own_inverse = lax.dynamic_slice_in_dim(inverse_all, own_index * node_dev, node_dev, 0)

time: 150 us -> 151 us (level)
  local copies, waits for them, and re-layouts: 9.17 us -> 13.5 us
  starting transfers between devices: 33.6 us -> 30.5 us
  other arithmetic: 19.8 us -> 22.2 us
  waiting for transfers between devices: 68.1 us -> 65.9 us
    all_to_all x2 -> x1, waiting for transfers between devices: 10.6 us -> 0.01 us  [shards(): both = lax.all_to_all(both, 'mp', split_axis=2, concat_axis=1, tiled=True)]
    ppermute x26, waiting for transfers between devices: 57.5 us -> 65.8 us  [swap(): return lax.ppermute(values, axis, [(j, j ^ mask) for j in range(size)])]
    all_to_all x2 -> x1, starting transfers between devices: 11.1 us -> 7.39 us  [shards(): both = lax.all_to_all(both, 'mp', split_axis=2, concat_axis=1, tiled=True)]
    unnamed x26 -> x24, local copies, waits for them, and re-layouts: 2.41 us -> 6.03 us
    another operation x0 -> x1, local copies, waits for them, and re-layouts: none -> 2.04 us  [shards(): both = jnp.stack([node_features, agg_one_cols], axis=0)]
    all_to_all x4 -> x1, local copies, waits for them, and re-layouts: 3.18 us -> 1.76 us  [shards(): both = lax.all_to_all(both, 'mp', split_axis=2, concat_axis=1, tiled=True)]
  transfers between devices with their start and end apart: 28 -> 27, of which waited for: 16 -> 18; matrix products, arithmetic and copies ran while one was open for 25% -> 13% of each run, Pallas kernels for 0% -> 0%
where the time goes in v7:
time: 151 us
  waiting for transfers between devices  65.9 us (44%)
  starting transfers between devices  30.5 us (20%)
  other arithmetic  22.2 us (15%)
  matrix products  17.1 us (11%)
  local copies, waits for them, and re-layouts  13.5 us (9%)
    ppermute x26, waiting for transfers between devices, swap(): return lax.ppermute(values, axis, [(j, j ^ mask) for j in range(size)])  65.8 us
    ppermute x26, starting transfers between devices, swap(): return lax.ppermute(values, axis, [(j, j ^ mask) for j in range(size)])  23.1 us
    dot_general x13, matrix products, contract(): lax.dot_general(left, right, (((left_dim,), (right_dim,)), ((), ())), pre...  17.1 us
    eq x1, other arithmetic, shards(): adjacency = (rowsel[:, None, :] == row_ids).astype(jnp.bfloat16)  9.69 us
    all_to_all x1, starting transfers between devices, shards(): both = lax.all_to_all(both, 'mp', split_axis=2, concat_axis=1, tiled=True)  7.39 us
    unnamed x24, local copies, waits for them, and re-layouts  6.03 us
    another operation x28, other arithmetic, doubling_gather(): jnp.stack([low, high], axis=sum((1 for done in order[:step] if done > bit)))  3.59 us
    add x10, other arithmetic, halving_scatter(): values = keep + got  3.09 us
  transfers between devices with their start and end apart: 27, of which 18 were waited for; matrix products, arithmetic and copies ran while one was open for 13% of the time, Pallas kernels for 0%

profile of v7, /device:TPU:0, one launch (start us, length us, event | category | flops | bytes accessed | tf_op | source)
XLA Modules:
  0.0 150.6 jit_solution(3410312135040896838)
XLA Ops:
  0.6 0.8 iota_compare_fusion.3
  1.4 0.7 convert_divide_fusion
  2.2 1.8 %select_reduce_fusion = s32[16,3072]{1,0:T(8,128)S(1)} fusion(s32[3072,8]{0,1:T(8,128)} %param.11, s32[3072,8]{0,1:T(8,128)} %param.10, pred[3072,8]{0,1:T(8,128)(4,1)S(1)} %iota_compare_fusion.3), kind=kLoop, calls=%fused_computation.20 | loop fusion | flops 1523712 | bytes 417792 | tf_op jit(solution)/shard_map/reduce_max | solution.py:85
  4.0 9.7 %bitcast_compare_fusion = pred[3072,3072]{1,0:T(32,128)(4,1)} fusion(s32[3072]{0:T(1024)S(1)} %eq.54, s32[16,3072]{1,0:T(8,128)S(1)} %select_reduce_fusion), kind=kLoop, calls=%fused_computation | loop fusion | flops 9437184 | bytes 9646080 | tf_op jit(solution)/shard_map/layer_one_mean/eq | solution.py:90
  13.7 8.5 %fusion.1 = bf16[1,32,3072]{2,1,0:T(8,128)(2,1)S(1)} fusion(pred[3072,3072]{1,0:T(32,128)(4,1)} %bitcast_compare_fusion, bf16[32,3072]{1,0:T(8,128)(2,1)S(1)} %copy-done.10, f32[3072]{0:T(1024)S(1)} %convert_divide_fusion), kind=kOutput, calls=%fused_computation.4 | convolution fusion | flops 604176384 | bytes 9842688 | tf_op jit(solution)/shard_map/layer_one_mean/dot_general | solution.py:22
  22.3 2.0 %copy.42 = bf16[2,32,3072]{1,0,2:T(2,128)(2,1)S(1)} copy(bf16[2,32,3072]{2,1,0:T(8,128)(2,1)S(1)} %pad_maximum_fusion.9) | data formatting | bytes 786432 | tf_op jit(solution)/shard_map/stack | solution.py:99
  24.4 2.2 %reshape.61 = bf16[16,2,6144]{2,1,0:T(2,128)(2,1)} reshape(bf16[3072,2,32]{2,1,0:T(2,128)(2,1)S(1)} %bitcast.147) | data formatting | bytes 786432
  26.6 7.4 %all-to-all-start = ((bf16[16,2,6144]{2,1,0:T(2,128)(2,1)}), bf16[16,2,6144]{2,1,0:T(2,128)(2,1)S(1)}, u32[]{:S(2)}, u32[]{:S(2)}) async-start(bf16[16,2,6144]{2,1,0:T(2,128)(2,1)} %reshape.61), calls=%async_computation | async-start | bytes 786432 | tf_op jit(solution)/shard_map/all_to_all | solution.py:100
  34.1 0.3 fusion.21
  34.4 2.0 %collective-permute-start.12 = (bf16[192,256]{1,0:T(8,128)(2,1)S(1)}, bf16[192,256]{1,0:T(8,128)(2,1)S(1)}, u32[]{:S(2)}, u32[]{:S(2)}) collective-permute-start(bf16[192,256]{1,0:T(8,128)(2,1)S(1)} %get-tuple-element.43), channel_id=1, source_target_pairs={{0,2},{1,3},{2,0},{3,1},{4,6},{5,7},{6,4},{7,5},{8,10},{9,11},{10,... | collective-permute-start | bytes 294920 | tf_op jit(solution)/shard_map/ppermute | solution.py:29
  36.4 2.4 %collective-permute-start.8 = (bf16[192,256]{1,0:T(8,128)(2,1)S(1)}, bf16[192,256]{1,0:T(8,128)(2,1)S(1)}, u32[]{:S(2)}, u32[]{:S(2)}) collective-permute-start(bf16[192,256]{1,0:T(8,128)(2,1)S(1)} %get-tuple-element.42), channel_id=1, source_target_pairs={{0,8},{1,9},{2,10},{3,11},{4,12},{5,13},{6,14},{7,15},{8,0},{9,1},... | collective-permute-start | bytes 294920 | tf_op jit(solution)/shard_map/ppermute | solution.py:29
  38.8 3.0 %collective-permute-done.12 = bf16[192,256]{1,0:T(8,128)(2,1)S(1)} collective-permute-done((bf16[192,256]{1,0:T(8,128)(2,1)S(1)}, bf16[192,256]{1,0:T(8,128)(2,1)S(1)}, u32[]{:S(2)}, u32[]{:S(2)}) %collective-permute-start.12) | collective-permute-done | bytes 98336 | tf_op jit(solution)/shard_map/ppermute | solution.py:29
  41.9 8.8 %collective-permute-done.8 = bf16[192,256]{1,0:T(8,128)(2,1)S(1)} collective-permute-done((bf16[192,256]{1,0:T(8,128)(2,1)S(1)}, bf16[192,256]{1,0:T(8,128)(2,1)S(1)}, u32[]{:S(2)}, u32[]{:S(2)}) %collective-permute-start.8) | collective-permute-done | bytes 98336 | tf_op jit(solution)/shard_map/ppermute | solution.py:29
  50.9 1.4 bitcast_compare_fusion.1
  52.3 0.7 pad_maximum_fusion.17
  53.0 2.0 %collective-permute-start.13 = (bf16[2,192,256]{2,1,0:T(8,128)(2,1)}, bf16[2,192,256]{2,1,0:T(8,128)(2,1)}, u32[]{:S(2)}, u32[]{:S(2)}) collective-permute-start(bf16[2,192,256]{2,1,0:T(8,128)(2,1)} %pad_maximum_fusion.17), channel_id=1, source_target_pairs={{0,8},{1,9},{2,10},{3,11},{4,12},{5,13},{6,14},{7,15},{8,0},{9,1},... | collective-permute-start | bytes 589832 | tf_op jit(solution)/shard_map/ppermute | solution.py:29
  55.0 3.5 %collective-permute-done.9 = bf16[2,192,256]{2,1,0:T(8,128)(2,1)S(1)} collective-permute-done((bf16[2,192,256]{2,1,0:T(8,128)(2,1)S(1)}, bf16[2,192,256]{2,1,0:T(8,128)(2,1)S(1)}, u32[]{:S(2)}, u32[]{:S(2)}) %collective-permute-start.9) | collective-permute-done | bytes 196640 | tf_op jit(solution)/shard_map/ppermute | solution.py:29
  58.5 0.8 reshape.62
  59.3 1.8 %copy.43 = bf16[2,32,16,192]{3,1,2,0:T(8,128)(2,1)S(1)} copy(bf16[2,32,16,192]{1,0,3,2:T(2,128)(2,1)S(1)} %bitcast.148) | data formatting | bytes 786432 | tf_op jit(solution)/shard_map/all_to_all | solution.py:100
  61.1 1.4 fusion.23
  62.5 0.4 multiply_convert_fusion
  63.0 1.5 %collective-permute-start.4 = (bf16[192,256]{1,0:T(8,128)(2,1)S(1)}, bf16[192,256]{1,0:T(8,128)(2,1)S(1)}, u32[]{:S(2)}, u32[]{:S(2)}) collective-permute-start(bf16[192,256]{1,0:T(8,128)(2,1)S(1)} %get-tuple-element.47), channel_id=1, source_target_pairs={{0,2},{1,3},{2,0},{3,1},{4,6},{5,7},{6,4},{7,5},{8,10},{9,11},{10,... | collective-permute-start | bytes 294920 | tf_op jit(solution)/shard_map/ppermute | solution.py:29
  64.5 0.6 collective-permute-start.10
  65.2 3.8 %collective-permute-done = bf16[192,256]{1,0:T(8,128)(2,1)S(1)} collective-permute-done((bf16[192,256]{1,0:T(8,128)(2,1)S(1)}, bf16[192,256]{1,0:T(8,128)(2,1)S(1)}, u32[]{:S(2)}, u32[]{:S(2)}) %collective-permute-start) | collective-permute-done | bytes 98336 | tf_op jit(solution)/shard_map/ppermute | solution.py:29
  69.1 2.2 %collective-permute-start.1 = (bf16[2,192,256]{2,1,0:T(8,128)(2,1)S(1)}, bf16[2,192,256]{2,1,0:T(8,128)(2,1)S(1)}, u32[]{:S(2)}, u32[]{:S(2)}) collective-permute-start(bf16[2,192,256]{2,1,0:T(8,128)(2,1)S(1)} %pad_maximum_fusion.14), channel_id=1, source_target_pairs={{0,4},{1,5},{2,6},{3,7},{4,0},{5,1},{6,2},{7,3},{8,12},{9,13},{10,... | collective-permute-start | bytes 589832 | tf_op jit(solution)/shard_map/ppermute | solution.py:29
  71.6 0.6 collective-permute-start.5
  72.2 6.4 %collective-permute-done.1 = bf16[2,192,256]{2,1,0:T(8,128)(2,1)S(1)} collective-permute-done((bf16[2,192,256]{2,1,0:T(8,128)(2,1)S(1)}, bf16[2,192,256]{2,1,0:T(8,128)(2,1)S(1)}, u32[]{:S(2)}, u32[]{:S(2)}) %collective-permute-start.1) | collective-permute-done | bytes 196640 | tf_op jit(solution)/shard_map/ppermute | solution.py:29
  78.7 1.5 %collective-permute-start.2 = (bf16[2,2,192,256]{3,2,0,1:T(8,128)(2,1)S(1)}, bf16[2,2,192,256]{3,2,0,1:T(8,128)(2,1)S(1)}, u32[]{:S(2)}, u32[]{:S(2)}) collective-permute-start(bf16[2,2,192,256]{3,2,0,1:T(8,128)(2,1)S(1)} %pad_maximum_fusion.10), channel_id=1, source_target_pairs={{0,2},{1,3},{2,0},{3,1},{4,6},{5,7},{6,4},{7,5},{8,10},{9,11},{10,... | collective-permute-start | bytes 1179656 | tf_op jit(solution)/shard_map/ppermute | solution.py:29
  80.3 0.7 collective-permute-done.5
  81.0 1.0 select_bitcast_fusion.17
  82.1 2.1 %collective-permute-start.6 = (bf16[2,2,192,256]{3,2,1,0:T(8,128)(2,1)S(1)}, bf16[2,2,192,256]{3,2,1,0:T(8,128)(2,1)S(1)}, u32[]{:S(2)}, u32[]{:S(2)}) collective-permute-start(bf16[2,2,192,256]{3,2,1,0:T(8,128)(2,1)S(1)} %pad_maximum_fusion.11), channel_id=1, source_target_pairs={{0,4},{1,5},{2,6},{3,7},{4,0},{5,1},{6,2},{7,3},{8,12},{9,13},{10,... | collective-permute-start | bytes 1179656 | tf_op jit(solution)/shard_map/ppermute | solution.py:29
  84.2 2.4 %collective-permute-done.2 = bf16[2,2,192,256]{3,2,0,1:T(8,128)(2,1)S(1)} collective-permute-done((bf16[2,2,192,256]{3,2,0,1:T(8,128)(2,1)S(1)}, bf16[2,2,192,256]{3,2,0,1:T(8,128)(2,1)S(1)}, u32[]{:S(2)}, u32[]{:S(2)}) %collective-permute-start.2) | collective-permute-done | bytes 393248 | tf_op jit(solution)/shard_map/ppermute | solution.py:29
  86.9 6.7 %collective-permute-done.14 = bf16[2,2,192,256]{3,2,1,0:T(8,128)(2,1)S(1)} collective-permute-done((bf16[2,2,192,256]{3,2,1,0:T(8,128)(2,1)S(1)}, bf16[2,2,192,256]{3,2,1,0:T(8,128)(2,1)S(1)}, u32[]{:S(2)}, u32[]{:S(2)}) %collective-permute-start.14) | collective-permute-done | bytes 393248 | tf_op jit(solution)/shard_map/ppermute | solution.py:29
  93.9 0.6 collective-permute-start.3
  94.4 3.4 %collective-permute-done.6 = bf16[2,2,192,256]{3,2,1,0:T(8,128)(2,1)S(1)} collective-permute-done((bf16[2,2,192,256]{3,2,1,0:T(8,128)(2,1)S(1)}, bf16[2,2,192,256]{3,2,1,0:T(8,128)(2,1)S(1)}, u32[]{:S(2)}, u32[]{:S(2)}) %collective-permute-start.6) | collective-permute-done | bytes 393248 | tf_op jit(solution)/shard_map/ppermute | solution.py:29
  99.3 1.6 %fusion.6 = f32[192,512]{1,0:T(8,128)S(1)} fusion(bf16[3072,256]{1,0:T(8,128)(2,1)S(1)} %bitcast.154, bf16[3072,256]{1,0:T(8,128)(2,1)S(1)} %bitcast.152, s32[3072]{0:T(1024)S(1)} %bitcast.159), kind=kOutput, calls=%fused_computation.9 | convolution fusion | flops 610861056 | bytes 3551232 | tf_op jit(solution)/shard_map/dot_general | solution.py:22
  100.9 0.4 fusion.19
  102.3 1.0 copy-done.6
  103.3 1.1 fusion.16
  104.4 0.7 copy-done.7
  105.1 0.3 fusion.39
  105.4 0.4 pad_maximum_fusion
  105.8 0.3 fusion.32
  106.2 1.3 copy-done.1
  107.5 1.1 dynamic-slice_bitcast_fusion
  108.6 0.5 collective-permute-start.16
  109.3 1.0 copy.56
  110.3 1.3 fusion.28
  111.7 1.4 bitcast_add_fusion.1
  113.2 1.6 %collective-permute-start.17 = (f32[2,2,2,64,256]{4,3,2,1,0:T(8,128)S(1)}, f32[2,2,2,64,256]{4,3,2,1,0:T(8,128)S(1)}, u32[]{:S(2)}, u32[]{:S(2)}) collective-permute-start(f32[2,2,2,64,256]{4,3,2,1,0:T(8,128)S(1)} %dynamic-slice_bitcast_fusion.2), channel_id=1, source_target_pairs={{0,16},{16,0},{1,17},{17,1},{2,18},{18,2},{3,19},{19,3},{4,20},{20... | collective-permute-start | bytes 1572872 | tf_op jit(solution)/shard_map/weight_grad_sum/ppermute | solution.py:29
  114.7 1.5 bitcast_add_fusion
  116.2 1.5 %collective-permute-start.22 = (f32[2,2,2,64,256]{4,3,2,1,0:T(8,128)S(1)}, f32[2,2,2,64,256]{4,3,2,1,0:T(8,128)S(1)}, u32[]{:S(2)}, u32[]{:S(2)}) collective-permute-start(f32[2,2,2,64,256]{4,3,2,1,0:T(8,128)S(1)} %dynamic-slice_bitcast_fusion.1), channel_id=1, source_target_pairs={{0,2},{1,3},{2,0},{3,1},{4,6},{5,7},{6,4},{7,5},{8,10},{9,11},{10,... | collective-permute-start | bytes 1572872 | tf_op jit(solution)/shard_map/weight_grad_sum/ppermute | solution.py:29
  117.8 1.0 fusion.20
  118.7 8.8 %collective-permute-done.17 = f32[2,2,2,64,256]{4,3,2,1,0:T(8,128)S(1)} collective-permute-done((f32[2,2,2,64,256]{4,3,2,1,0:T(8,128)S(1)}, f32[2,2,2,64,256]{4,3,2,1,0:T(8,128)S(1)}, u32[]{:S(2)}, u32[]{:S(2)}) %collective-permute-start.17) | collective-permute-done | bytes 524320 | tf_op jit(solution)/shard_map/weight_grad_sum/ppermute | solution.py:29
  127.6 1.5 %collective-permute-start.18 = (f32[2,2,64,256]{3,2,1,0:T(8,128)S(1)}, f32[2,2,64,256]{3,2,1,0:T(8,128)S(1)}, u32[]{:S(2)}, u32[]{:S(2)}) collective-permute-start(f32[2,2,64,256]{3,2,1,0:T(8,128)S(1)} %dynamic-slice_bitcast_fusion.4), channel_id=1, source_target_pairs={{0,2},{1,3},{2,0},{3,1},{4,6},{5,7},{6,4},{7,5},{8,10},{9,11},{10,... | collective-permute-start | bytes 786440 | tf_op jit(solution)/shard_map/weight_grad_sum/ppermute | solution.py:29
  129.1 1.5 collective-permute-done.22
  131.0 4.9 %collective-permute-done.18 = f32[2,2,64,256]{3,2,1,0:T(8,128)S(1)} collective-permute-done((f32[2,2,64,256]{3,2,1,0:T(8,128)S(1)}, f32[2,2,64,256]{3,2,1,0:T(8,128)S(1)}, u32[]{:S(2)}, u32[]{:S(2)}) %collective-permute-start.18) | collective-permute-done | bytes 262176 | tf_op jit(solution)/shard_map/weight_grad_sum/ppermute | solution.py:29
  136.0 2.0 %collective-permute-done.23 = f32[2,2,64,256]{3,2,1,0:T(8,128)S(1)} collective-permute-done((f32[2,2,64,256]{3,2,1,0:T(8,128)S(1)}, f32[2,2,64,256]{3,2,1,0:T(8,128)S(1)}, u32[]{:S(2)}, u32[]{:S(2)}) %collective-permute-start.23) | collective-permute-done | bytes 262176 | tf_op jit(solution)/shard_map/weight_grad_sum/ppermute | solution.py:29
  138.1 5.6 %collective-permute-done.19 = f32[2,64,256]{2,1,0:T(8,128)S(1)} collective-permute-done((f32[2,64,256]{2,1,0:T(8,128)S(1)}, f32[2,64,256]{2,1,0:T(8,128)S(1)}, u32[]{:S(2)}, u32[]{:S(2)}) %collective-permute-start.19) | collective-permute-done | bytes 131104 | tf_op jit(solution)/shard_map/weight_grad_sum/ppermute | solution.py:29
  143.9 0.7 collective-permute-done.24
  144.6 1.7 %collective-permute-start.25 = (f32[64,256]{1,0:T(8,128)S(1)}, f32[64,256]{1,0:T(8,128)S(1)}, u32[]{:S(2)}, u32[]{:S(2)}) collective-permute-start(f32[64,256]{1,0:T(8,128)S(1)} %dynamic-slice_bitcast_fusion.7), channel_id=1, source_target_pairs={{0,8},{1,9},{2,10},{3,11},{4,12},{5,13},{6,14},{7,15},{8,0},{9,1},... | collective-permute-start | bytes 196616 | tf_op jit(solution)/shard_map/weight_grad_sum/ppermute | solution.py:29
  146.3 1.9 %collective-permute-done.20 = f32[64,256]{1,0:T(8,128)S(1)} collective-permute-done((f32[64,256]{1,0:T(8,128)S(1)}, f32[64,256]{1,0:T(8,128)S(1)}, u32[]{:S(2)}, u32[]{:S(2)}) %collective-permute-start.20) | collective-permute-done | bytes 65568 | tf_op jit(solution)/shard_map/weight_grad_sum/ppermute | solution.py:29
  148.2 1.7 %collective-permute-done.25 = f32[64,256]{1,0:T(8,128)S(1)} collective-permute-done((f32[64,256]{1,0:T(8,128)S(1)}, f32[64,256]{1,0:T(8,128)S(1)}, u32[]{:S(2)}, u32[]{:S(2)}) %collective-permute-start.25) | collective-permute-done | bytes 65568 | tf_op jit(solution)/shard_map/weight_grad_sum/ppermute | solution.py:29
  149.9 0.7 pad_maximum_fusion.18
  (99 shorter events, 5.5 us)
Async XLA Ops:
  0.6 33.5 %copy-start = (bf16[192,512]{1,0:T(8,128)(2,1)S(1)}, bf16[192,512]{1,0:T(8,128)(2,1)}, u32[]{:S(2)}) copy-start(bf16[192,512]{1,0:T(8,128)(2,1)} %param.13) | copy-start | bytes 589828
  4.0 9.7 %copy-start.10 = (bf16[32,3072]{1,0:T(8,128)(2,1)S(1)}, bf16[32,3072]{1,0:T(8,128)(2,1)}, u32[]{:S(2)}) copy-start(bf16[32,3072]{1,0:T(8,128)(2,1)} %param.7) | copy-start | bytes 589828
  22.3 11.8 %copy-start.3 = (bf16[1024,512]{1,0:T(8,128)(2,1)S(1)}, bf16[1024,512]{1,0:T(8,128)(2,1)}, u32[]{:S(2)}) copy-start(bf16[1024,512]{1,0:T(8,128)(2,1)} %param.9) | copy-start | bytes 3145732
  26.6 31.9 %all-to-all-start = ((bf16[16,2,6144]{2,1,0:T(2,128)(2,1)}), bf16[16,2,6144]{2,1,0:T(2,128)(2,1)S(1)}, u32[]{:S(2)}, u32[]{:S(2)}) async-start(bf16[16,2,6144]{2,1,0:T(2,128)(2,1)} %reshape.61), calls=%async_computation | async-start | bytes 786432 | tf_op jit(solution)/shard_map/all_to_all | solution.py:100
  34.4 7.4 %collective-permute-start.12 = (bf16[192,256]{1,0:T(8,128)(2,1)S(1)}, bf16[192,256]{1,0:T(8,128)(2,1)S(1)}, u32[]{:S(2)}, u32[]{:S(2)}) collective-permute-start(bf16[192,256]{1,0:T(8,128)(2,1)S(1)} %get-tuple-element.43), channel_id=1, source_target_pairs={{0,2},{1,3},{2,0},{3,1},{4,6},{5,7},{6,4},{7,5},{8,10},{9,11},{10,... | collective-permute-start | bytes 294920 | tf_op jit(solution)/shard_map/ppermute | solution.py:29
  36.4 14.2 %collective-permute-start.8 = (bf16[192,256]{1,0:T(8,128)(2,1)S(1)}, bf16[192,256]{1,0:T(8,128)(2,1)S(1)}, u32[]{:S(2)}, u32[]{:S(2)}) collective-permute-start(bf16[192,256]{1,0:T(8,128)(2,1)S(1)} %get-tuple-element.42), channel_id=1, source_target_pairs={{0,8},{1,9},{2,10},{3,11},{4,12},{5,13},{6,14},{7,15},{8,0},{9,1},... | collective-permute-start | bytes 294920 | tf_op jit(solution)/shard_map/ppermute | solution.py:29
  50.7 7.7 %collective-permute-start.9 = (bf16[2,192,256]{2,1,0:T(8,128)(2,1)S(1)}, bf16[2,192,256]{2,1,0:T(8,128)(2,1)S(1)}, u32[]{:S(2)}, u32[]{:S(2)}) collective-permute-start(bf16[2,192,256]{2,1,0:T(8,128)(2,1)S(1)} %pad_maximum_fusion.16), channel_id=1, source_target_pairs={{0,4},{1,5},{2,6},{3,7},{4,0},{5,1},{6,2},{7,3},{8,12},{9,13},{10,... | collective-permute-start | bytes 589832 | tf_op jit(solution)/shard_map/ppermute | solution.py:29
  53.0 27.3 %collective-permute-start.13 = (bf16[2,192,256]{2,1,0:T(8,128)(2,1)}, bf16[2,192,256]{2,1,0:T(8,128)(2,1)}, u32[]{:S(2)}, u32[]{:S(2)}) collective-permute-start(bf16[2,192,256]{2,1,0:T(8,128)(2,1)} %pad_maximum_fusion.17), channel_id=1, source_target_pairs={{0,8},{1,9},{2,10},{3,11},{4,12},{5,13},{6,14},{7,15},{8,0},{9,1},... | collective-permute-start | bytes 589832 | tf_op jit(solution)/shard_map/ppermute | solution.py:29
  61.0 1.5 copy-start.9
  62.9 6.1 %collective-permute-start = (bf16[192,256]{1,0:T(8,128)(2,1)S(1)}, bf16[192,256]{1,0:T(8,128)(2,1)S(1)}, u32[]{:S(2)}, u32[]{:S(2)}) collective-permute-start(bf16[192,256]{1,0:T(8,128)(2,1)S(1)} %get-tuple-element.46), channel_id=1, source_target_pairs={{0,8},{1,9},{2,10},{3,11},{4,12},{5,13},{6,14},{7,15},{8,0},{9,1},... | collective-permute-start | bytes 294920 | tf_op jit(solution)/shard_map/ppermute | solution.py:29
  63.0 6.0 %collective-permute-start.4 = (bf16[192,256]{1,0:T(8,128)(2,1)S(1)}, bf16[192,256]{1,0:T(8,128)(2,1)S(1)}, u32[]{:S(2)}, u32[]{:S(2)}) collective-permute-start(bf16[192,256]{1,0:T(8,128)(2,1)S(1)} %get-tuple-element.47), channel_id=1, source_target_pairs={{0,2},{1,3},{2,0},{3,1},{4,6},{5,7},{6,4},{7,5},{8,10},{9,11},{10,... | collective-permute-start | bytes 294920 | tf_op jit(solution)/shard_map/ppermute | solution.py:29
  64.5 19.7 %collective-permute-start.10 = (bf16[2,2,192,256]{3,2,0,1:T(8,128)(2,1)S(1)}, bf16[2,2,192,256]{3,2,0,1:T(8,128)(2,1)S(1)}, u32[]{:S(2)}, u32[]{:S(2)}) collective-permute-start(bf16[2,2,192,256]{3,2,0,1:T(8,128)(2,1)S(1)} %pad_maximum_fusion.12), channel_id=1, source_target_pairs={{0,2},{1,3},{2,0},{3,1},{4,6},{5,7},{6,4},{7,5},{8,10},{9,11},{10,... | collective-permute-start | bytes 1179656 | tf_op jit(solution)/shard_map/ppermute | solution.py:29
  69.1 9.6 %collective-permute-start.1 = (bf16[2,192,256]{2,1,0:T(8,128)(2,1)S(1)}, bf16[2,192,256]{2,1,0:T(8,128)(2,1)S(1)}, u32[]{:S(2)}, u32[]{:S(2)}) collective-permute-start(bf16[2,192,256]{2,1,0:T(8,128)(2,1)S(1)} %pad_maximum_fusion.14), channel_id=1, source_target_pairs={{0,4},{1,5},{2,6},{3,7},{4,0},{5,1},{6,2},{7,3},{8,12},{9,13},{10,... | collective-permute-start | bytes 589832 | tf_op jit(solution)/shard_map/ppermute | solution.py:29
  71.6 9.4 %collective-permute-start.5 = (bf16[2,192,256]{2,1,0:T(8,128)(2,1)S(1)}, bf16[2,192,256]{2,1,0:T(8,128)(2,1)S(1)}, u32[]{:S(2)}, u32[]{:S(2)}) collective-permute-start(bf16[2,192,256]{2,1,0:T(8,128)(2,1)S(1)} %pad_maximum_fusion.15), channel_id=1, source_target_pairs={{0,8},{1,9},{2,10},{3,11},{4,12},{5,13},{6,14},{7,15},{8,0},{9,1},... | collective-permute-start | bytes 589832 | tf_op jit(solution)/shard_map/ppermute | solution.py:29
  78.7 7.8 %collective-permute-start.2 = (bf16[2,2,192,256]{3,2,0,1:T(8,128)(2,1)S(1)}, bf16[2,2,192,256]{3,2,0,1:T(8,128)(2,1)S(1)}, u32[]{:S(2)}, u32[]{:S(2)}) collective-permute-start(bf16[2,2,192,256]{3,2,0,1:T(8,128)(2,1)S(1)} %pad_maximum_fusion.10), channel_id=1, source_target_pairs={{0,2},{1,3},{2,0},{3,1},{4,6},{5,7},{6,4},{7,5},{8,10},{9,11},{10,... | collective-permute-start | bytes 1179656 | tf_op jit(solution)/shard_map/ppermute | solution.py:29
  82.0 11.6 %collective-permute-start.14 = (bf16[2,2,192,256]{3,2,1,0:T(8,128)(2,1)S(1)}, bf16[2,2,192,256]{3,2,1,0:T(8,128)(2,1)S(1)}, u32[]{:S(2)}, u32[]{:S(2)}) collective-permute-start(bf16[2,2,192,256]{3,2,1,0:T(8,128)(2,1)S(1)} %pad_maximum_fusion.13), channel_id=1, source_target_pairs={{0,4},{1,5},{2,6},{3,7},{4,0},{5,1},{6,2},{7,3},{8,12},{9,13},{10,... | collective-permute-start | bytes 1179656 | tf_op jit(solution)/shard_map/ppermute | solution.py:29
  82.1 15.7 %collective-permute-start.6 = (bf16[2,2,192,256]{3,2,1,0:T(8,128)(2,1)S(1)}, bf16[2,2,192,256]{3,2,1,0:T(8,128)(2,1)S(1)}, u32[]{:S(2)}, u32[]{:S(2)}) collective-permute-start(bf16[2,2,192,256]{3,2,1,0:T(8,128)(2,1)S(1)} %pad_maximum_fusion.11), channel_id=1, source_target_pairs={{0,4},{1,5},{2,6},{3,7},{4,0},{5,1},{6,2},{7,3},{8,12},{9,13},{10,... | collective-permute-start | bytes 1179656 | tf_op jit(solution)/shard_map/ppermute | solution.py:29
  86.8 11.2 %collective-permute-start.11 = (bf16[2,2,2,192,256]{4,3,0,1,2:T(8,128)(2,1)S(1)}, bf16[2,2,2,192,256]{4,3,0,1,2:T(8,128)(2,1)S(1)}, u32[]{:S(2)}, u32[]{:S(2)}) collective-permute-start(bf16[2,2,2,192,256]{4,3,0,1,2:T(8,128)(2,1)S(1)} %pad_maximum_fusion.7), channel_id=1, source_target_pairs={{0,1},{1,0},{2,3},{3,2},{4,5},{5,4},{6,7},{7,6},{8,9},{9,8},{10,11... | collective-permute-start | bytes 2359304 | tf_op jit(solution)/shard_map/ppermute | solution.py:29
  93.7 4.7 %collective-permute-start.15 = (bf16[2,2,2,192,256]{4,3,2,0,1:T(8,128)(2,1)S(1)}, bf16[2,2,2,192,256]{4,3,2,0,1:T(8,128)(2,1)S(1)}, u32[]{:S(2)}, u32[]{:S(2)}) collective-permute-start(bf16[2,2,2,192,256]{4,3,2,0,1:T(8,128)(2,1)S(1)} %pad_maximum_fusion.8), channel_id=1, source_target_pairs={{0,1},{1,0},{2,3},{3,2},{4,5},{5,4},{6,7},{7,6},{8,9},{9,8},{10,11... | collective-permute-start | bytes 2359304 | tf_op jit(solution)/shard_map/ppermute | solution.py:29
  93.9 5.0 %collective-permute-start.3 = (bf16[2,2,2,192,256]{4,3,0,1,2:T(8,128)(2,1)S(1)}, bf16[2,2,2,192,256]{4,3,0,1,2:T(8,128)(2,1)S(1)}, u32[]{:S(2)}, u32[]{:S(2)}) collective-permute-start(bf16[2,2,2,192,256]{4,3,0,1,2:T(8,128)(2,1)S(1)} %pad_maximum_fusion.5), channel_id=1, source_target_pairs={{0,1},{1,0},{2,3},{3,2},{4,5},{5,4},{6,7},{7,6},{8,9},{9,8},{10,11... | collective-permute-start | bytes 2359304 | tf_op jit(solution)/shard_map/ppermute | solution.py:29
  97.9 3.9 %collective-permute-start.7 = (bf16[2,2,2,192,256]{4,3,2,0,1:T(8,128)(2,1)S(1)}, bf16[2,2,2,192,256]{4,3,2,0,1:T(8,128)(2,1)S(1)}, u32[]{:S(2)}, u32[]{:S(2)}) collective-permute-start(bf16[2,2,2,192,256]{4,3,2,0,1:T(8,128)(2,1)S(1)} %pad_maximum_fusion.6), channel_id=1, source_target_pairs={{0,1},{1,0},{2,3},{3,2},{4,5},{5,4},{6,7},{7,6},{8,9},{9,8},{10,11... | collective-permute-start | bytes 2359304 | tf_op jit(solution)/shard_map/ppermute | solution.py:29
  99.3 1.6 %copy-start.4 = (bf16[1024,512]{1,0:T(8,128)(2,1)S(1)}, bf16[1024,512]{1,0:T(8,128)(2,1)}, u32[]{:S(2)}) copy-start(bf16[1024,512]{1,0:T(8,128)(2,1)} %param.9) | copy-start | bytes 3145732
  102.1 1.1 copy-start.6
  104.4 0.7 copy-start.7
  106.2 1.3 copy-start.1
  108.6 3.1 %collective-permute-start.16 = (f32[2,2,2,2,64,256]{5,4,3,2,1,0:T(8,128)}, f32[2,2,2,2,64,256]{5,4,3,2,1,0:T(8,128)}, u32[]{:S(2)}, u32[]{:S(2)}) collective-permute-start(f32[2,2,2,2,64,256]{5,4,3,2,1,0:T(8,128)} %dynamic-slice_bitcast_fusion), channel_id=1, source_target_pairs={{0,1},{1,0},{2,3},{3,2},{4,5},{5,4},{6,7},{7,6},{8,9},{9,8},{10,11... | collective-permute-start | bytes 3145736 | tf_op jit(solution)/shard_map/weight_grad_sum/ppermute | solution.py:29
  109.3 2.5 %copy-start.2 = (f32[2048,256]{1,0:T(8,128)S(1)}, f32[2048,256]{1,0:T(8,128)}, u32[]{:S(2)}) copy-start(f32[2048,256]{1,0:T(8,128)} %copy-done.1) | copy-start | bytes 6291460
  110.3 4.4 %collective-permute-start.21 = (f32[2,2,2,2,64,256]{5,4,2,1,0,3:T(8,128)}, f32[2,2,2,2,64,256]{5,4,2,1,0,3:T(8,128)}, u32[]{:S(2)}, u32[]{:S(2)}) collective-permute-start(f32[2,2,2,2,64,256]{5,4,2,1,0,3:T(8,128)} %bitcast.143), channel_id=1, source_target_pairs={{0,1},{1,0},{2,3},{3,2},{4,5},{5,4},{6,7},{7,6},{8,9},{9,8},{10,11... | collective-permute-start | bytes 3145736 | tf_op jit(solution)/shard_map/weight_grad_sum/ppermute | solution.py:29
  113.2 14.3 %collective-permute-start.17 = (f32[2,2,2,64,256]{4,3,2,1,0:T(8,128)S(1)}, f32[2,2,2,64,256]{4,3,2,1,0:T(8,128)S(1)}, u32[]{:S(2)}, u32[]{:S(2)}) collective-permute-start(f32[2,2,2,64,256]{4,3,2,1,0:T(8,128)S(1)} %dynamic-slice_bitcast_fusion.2), channel_id=1, source_target_pairs={{0,16},{16,0},{1,17},{17,1},{2,18},{18,2},{3,19},{19,3},{4,20},{20... | collective-permute-start | bytes 1572872 | tf_op jit(solution)/shard_map/weight_grad_sum/ppermute | solution.py:29
  114.7 3.1 %copy-start.5 = (bf16[1024,512]{1,0:T(8,128)(2,1)S(1)}, bf16[1024,512]{1,0:T(8,128)(2,1)}, u32[]{:S(2)}) copy-start(bf16[1024,512]{1,0:T(8,128)(2,1)} %param.9) | copy-start | bytes 3145732
  114.7 3.1 %copy-start.8 = (bf16[192,512]{1,0:T(8,128)(2,1)S(1)}, bf16[192,512]{1,0:T(8,128)(2,1)}, u32[]{:S(2)}) copy-start(bf16[192,512]{1,0:T(8,128)(2,1)} %copy-done.7) | copy-start | bytes 589828
  116.2 14.4 %collective-permute-start.22 = (f32[2,2,2,64,256]{4,3,2,1,0:T(8,128)S(1)}, f32[2,2,2,64,256]{4,3,2,1,0:T(8,128)S(1)}, u32[]{:S(2)}, u32[]{:S(2)}) collective-permute-start(f32[2,2,2,64,256]{4,3,2,1,0:T(8,128)S(1)} %dynamic-slice_bitcast_fusion.1), channel_id=1, source_target_pairs={{0,2},{1,3},{2,0},{3,1},{4,6},{5,7},{6,4},{7,5},{8,10},{9,11},{10,... | collective-permute-start | bytes 1572872 | tf_op jit(solution)/shard_map/weight_grad_sum/ppermute | solution.py:29
  127.6 8.3 %collective-permute-start.18 = (f32[2,2,64,256]{3,2,1,0:T(8,128)S(1)}, f32[2,2,64,256]{3,2,1,0:T(8,128)S(1)}, u32[]{:S(2)}, u32[]{:S(2)}) collective-permute-start(f32[2,2,64,256]{3,2,1,0:T(8,128)S(1)} %dynamic-slice_bitcast_fusion.4), channel_id=1, source_target_pairs={{0,2},{1,3},{2,0},{3,1},{4,6},{5,7},{6,4},{7,5},{8,10},{9,11},{10,... | collective-permute-start | bytes 786440 | tf_op jit(solution)/shard_map/weight_grad_sum/ppermute | solution.py:29
  130.7 7.3 %collective-permute-start.23 = (f32[2,2,64,256]{3,2,1,0:T(8,128)S(1)}, f32[2,2,64,256]{3,2,1,0:T(8,128)S(1)}, u32[]{:S(2)}, u32[]{:S(2)}) collective-permute-start(f32[2,2,64,256]{3,2,1,0:T(8,128)S(1)} %dynamic-slice_bitcast_fusion.3), channel_id=1, source_target_pairs={{0,16},{16,0},{1,17},{17,1},{2,18},{18,2},{3,19},{19,3},{4,20},{20... | collective-permute-start | bytes 786440 | tf_op jit(solution)/shard_map/weight_grad_sum/ppermute | solution.py:29
  136.0 7.8 %collective-permute-start.19 = (f32[2,64,256]{2,1,0:T(8,128)S(1)}, f32[2,64,256]{2,1,0:T(8,128)S(1)}, u32[]{:S(2)}, u32[]{:S(2)}) collective-permute-start(f32[2,64,256]{2,1,0:T(8,128)S(1)} %dynamic-slice_bitcast_fusion.6), channel_id=1, source_target_pairs={{0,8},{1,9},{2,10},{3,11},{4,12},{5,13},{6,14},{7,15},{8,0},{9,1},... | collective-permute-start | bytes 393224 | tf_op jit(solution)/shard_map/weight_grad_sum/ppermute | solution.py:29
  138.1 6.5 %collective-permute-start.24 = (f32[2,64,256]{2,1,0:T(8,128)S(1)}, f32[2,64,256]{2,1,0:T(8,128)S(1)}, u32[]{:S(2)}, u32[]{:S(2)}) collective-permute-start(f32[2,64,256]{2,1,0:T(8,128)S(1)} %dynamic-slice_bitcast_fusion.5), channel_id=1, source_target_pairs={{0,4},{1,5},{2,6},{3,7},{4,0},{5,1},{6,2},{7,3},{8,12},{9,13},{10,... | collective-permute-start | bytes 393224 | tf_op jit(solution)/shard_map/weight_grad_sum/ppermute | solution.py:29
  143.8 4.4 %collective-permute-start.20 = (f32[64,256]{1,0:T(8,128)S(1)}, f32[64,256]{1,0:T(8,128)S(1)}, u32[]{:S(2)}, u32[]{:S(2)}) collective-permute-start(f32[64,256]{1,0:T(8,128)S(1)} %dynamic-slice_bitcast_fusion.8), channel_id=1, source_target_pairs={{0,4},{1,5},{2,6},{3,7},{4,0},{5,1},{6,2},{7,3},{8,12},{9,13},{10,... | collective-permute-start | bytes 196616 | tf_op jit(solution)/shard_map/weight_grad_sum/ppermute | solution.py:29
  144.6 5.2 %collective-permute-start.25 = (f32[64,256]{1,0:T(8,128)S(1)}, f32[64,256]{1,0:T(8,128)S(1)}, u32[]{:S(2)}, u32[]{:S(2)}) collective-permute-start(f32[64,256]{1,0:T(8,128)S(1)} %dynamic-slice_bitcast_fusion.7), channel_id=1, source_target_pairs={{0,8},{1,9},{2,10},{3,11},{4,12},{5,13},{6,14},{7,15},{8,0},{9,1},... | collective-permute-start | bytes 196616 | tf_op jit(solution)/shard_map/weight_grad_sum/ppermute | solution.py:29

commit v8 on v5

--- a/solution.py
+++ b/solution.py
@@ -142,11 +142,12 @@
     )
     with jax.named_scope("weight_grad_sum"):
         if lax.axis_size("dp") == 2 and devices == 16:
-            half = terms.shape[1] // 2
+            cut = [0, 3 * terms.shape[1] // 8, 6 * terms.shape[1] // 8, terms.shape[1]]
+            orders = [[0, 4, 1, 2, 3], [0, 1, 2, 4, 3], [0, 2, 4, 1, 3]]
             weight_grads = jnp.concatenate(
                 [
-                    halving_scatter(terms[:, :half], [0, 4, 1, 3, 2]),
-                    halving_scatter(terms[:, half:], [0, 1, 4, 2, 3]),
+                    halving_scatter(terms[:, cut[i]:cut[i + 1]], orders[i])
+                    for i in range(3)
                 ],
                 axis=1,
             )

time: 150 us -> 169 us (1.13)
  waiting for transfers between devices: 68.1 us -> 85.3 us
  starting transfers between devices: 33.6 us -> 40.8 us
  local copies, waits for them, and re-layouts: 9.17 us -> 5.64 us
  other arithmetic: 19.8 us -> 16.7 us
    ppermute x26 -> x31, waiting for transfers between devices: 57.5 us -> 78.6 us  [swap(): return lax.ppermute(values, axis, [(j, j ^ mask) for j in range(size)])]
    ppermute x26 -> x31, starting transfers between devices: 22.5 us -> 27.8 us  [swap(): return lax.ppermute(values, axis, [(j, j ^ mask) for j in range(size)])]
    all_to_all x1, waiting for transfers between devices: 10.6 us -> 6.71 us  [shards(): lax.all_to_all(agg_one_cols, 'mp', split_axis=1, concat_axis=0, tiled=True)]
    add x10 -> x15, other arithmetic: 3.09 us -> 0.69 us  [halving_scatter(): values = keep + got]
    unnamed x26 -> x12, local copies, waits for them, and re-layouts: 2.41 us -> 0.04 us
    all_to_all x1, starting transfers between devices: 3.75 us -> 5.58 us  [shards(): lax.all_to_all(agg_one_cols, 'mp', split_axis=1, concat_axis=0, tiled=True)]
  transfers between devices with their start and end apart: 28 -> 33, of which waited for: 16 -> 18; matrix products, arithmetic and copies ran while one was open for 25% -> 21% of each run, Pallas kernels for 0% -> 0%
where the time goes in v8:
time: 169 us; the launch traced here: 168 us
  waiting for transfers between devices  85.3 us (50%)
  starting transfers between devices  40.8 us (24%)
  matrix products  18.3 us (11%)
  other arithmetic  16.7 us (10%)
  local copies, waits for them, and re-layouts  5.64 us (3%)
    ppermute x31, waiting for transfers between devices, swap(): return lax.ppermute(values, axis, [(j, j ^ mask) for j in range(size)])  78.6 us
    ppermute x31, starting transfers between devices, swap(): return lax.ppermute(values, axis, [(j, j ^ mask) for j in range(size)])  27.8 us
    dot_general x13, matrix products, contract(): lax.dot_general(left, right, (((left_dim,), (right_dim,)), ((), ())), pre...  18.3 us
    eq x1, other arithmetic, shards(): adjacency = (rowsel[:, None, :] == row_ids).astype(jnp.bfloat16)  9.7 us
    all_to_all x1, starting transfers between devices, shards(): lax.all_to_all(node_features, 'mp', split_axis=1, concat_axis=0, tiled=True)  7.39 us
    all_to_all x1, waiting for transfers between devices, shards(): lax.all_to_all(agg_one_cols, 'mp', split_axis=1, concat_axis=0, tiled=True)  6.71 us
    all_to_all x1, starting transfers between devices, shards(): lax.all_to_all(agg_one_cols, 'mp', split_axis=1, concat_axis=0, tiled=True)  5.58 us
  transfers between devices with their start and end apart: 33, of which 18 were waited for; matrix products, arithmetic and copies ran while one was open for 21% of the time, Pallas kernels for 0%

profile of v8, /device:TPU:0, one launch (start us, length us, event | category | flops | bytes accessed | tf_op | source)
XLA Modules:
  0.0 168.0 jit_solution(17158408318765990527)
XLA Ops:
  0.7 1.3 all_to_all.28
  2.0 0.8 copy.31
  2.8 7.4 %all-to-all-start = ((bf16[32,16,192]{2,0,1:T(8,128)(2,1)}), bf16[32,16,192]{2,0,1:T(8,128)(2,1)S(1)}, u32[]{:S(2)}, u32[]{:S(2)}) async-start(bf16[32,16,192]{2,0,1:T(8,128)(2,1)} %copy.31), calls=%async_computation | async-start | bytes 524288 | tf_op jit(solution)/shard_map/all_to_all | solution.py:100
  10.2 0.7 convert_divide_fusion
  11.0 1.4 fusion.21
  12.4 2.9 %collective-permute-start.8 = (bf16[192,256]{1,0:T(8,128)(2,1)S(1)}, bf16[192,256]{1,0:T(8,128)(2,1)S(1)}, u32[]{:S(2)}, u32[]{:S(2)}) collective-permute-start(bf16[192,256]{1,0:T(8,128)(2,1)S(1)} %get-tuple-element.42), channel_id=1, source_target_pairs={{0,8},{1,9},{2,10},{3,11},{4,12},{5,13},{6,14},{7,15},{8,0},{9,1},... | collective-permute-start | bytes 294920 | tf_op jit(solution)/shard_map/ppermute | solution.py:29
  15.3 1.5 collective-permute-start.12
  16.9 0.8 select_reduce_fusion
  17.7 9.7 %bitcast_compare_fusion = pred[3072,3072]{1,0:T(32,128)(4,1)} fusion(s32[3072]{0:T(1024)S(1)} %eq.54, s32[16,3072]{1,0:T(8,128)S(1)} %select_reduce_fusion), kind=kLoop, calls=%fused_computation | loop fusion | flops 9437184 | bytes 9646080 | tf_op jit(solution)/shard_map/layer_one_mean/eq | solution.py:90
  27.4 8.7 %fusion.1 = bf16[32,3072]{1,0:T(8,128)(2,1)S(1)} fusion(pred[3072,3072]{1,0:T(32,128)(4,1)} %bitcast_compare_fusion, bf16[32,3072]{1,0:T(8,128)(2,1)S(1)} %copy-done.2, f32[3072]{0:T(1024)S(1)} %convert_divide_fusion), kind=kOutput, calls=%fused_computation.4 | convolution fusion | flops 604176384 | bytes 9842688 | tf_op jit(solution)/shard_map/layer_one_mean/dot_general | solution.py:22
  36.2 1.5 collective-permute-start.9
  37.9 0.3 all_to_all.32
  38.2 0.8 copy.32
  38.9 0.5 bitcast_compare_fusion.1
  39.5 0.6 collective-permute-start.13
  40.1 3.1 %collective-permute-done.9 = bf16[2,192,256]{2,1,0:T(8,128)(2,1)S(1)} collective-permute-done((bf16[2,192,256]{2,1,0:T(8,128)(2,1)S(1)}, bf16[2,192,256]{2,1,0:T(8,128)(2,1)S(1)}, u32[]{:S(2)}, u32[]{:S(2)}) %collective-permute-start.9) | collective-permute-done | bytes 196640 | tf_op jit(solution)/shard_map/ppermute | solution.py:29
  43.2 5.6 %all-to-all-start.1 = ((bf16[32,16,192]{2,0,1:T(8,128)(2,1)}), bf16[32,16,192]{2,0,1:T(8,128)(2,1)S(1)}, u32[]{:S(2)}, u32[]{:S(2)}) async-start(bf16[32,16,192]{2,0,1:T(8,128)(2,1)} %copy.32), calls=%async_computation.1 | async-start | bytes 524288 | tf_op jit(solution)/shard_map/all_to_all | solution.py:101
  48.9 2.0 %collective-permute-start.10 = (bf16[2,2,192,256]{3,2,0,1:T(8,128)(2,1)S(1)}, bf16[2,2,192,256]{3,2,0,1:T(8,128)(2,1)S(1)}, u32[]{:S(2)}, u32[]{:S(2)}) collective-permute-start(bf16[2,2,192,256]{3,2,0,1:T(8,128)(2,1)S(1)} %pad_maximum_fusion.12), channel_id=1, source_target_pairs={{0,2},{1,3},{2,0},{3,1},{4,6},{5,7},{6,4},{7,5},{8,10},{9,11},{10,... | collective-permute-start | bytes 1179656 | tf_op jit(solution)/shard_map/ppermute | solution.py:29
  50.8 1.3 fusion.23
  52.2 6.7 %all-to-all-done.1 = bf16[32,16,192]{2,0,1:T(8,128)(2,1)S(1)} async-done(((bf16[32,16,192]{2,0,1:T(8,128)(2,1)}), bf16[32,16,192]{2,0,1:T(8,128)(2,1)S(1)}, u32[]{:S(2)}, u32[]{:S(2)}) %all-to-all-start.1) | async-done | bytes 196640 | tf_op jit(solution)/shard_map/all_to_all | solution.py:101
  58.9 1.4 multiply_convert_fusion
  60.3 1.1 collective-permute-start
  61.4 0.3 fusion.36
  61.8 6.1 %collective-permute-done = bf16[192,256]{1,0:T(8,128)(2,1)S(1)} collective-permute-done((bf16[192,256]{1,0:T(8,128)(2,1)S(1)}, bf16[192,256]{1,0:T(8,128)(2,1)S(1)}, u32[]{:S(2)}, u32[]{:S(2)}) %collective-permute-start) | collective-permute-done | bytes 98336 | tf_op jit(solution)/shard_map/ppermute | solution.py:29
  68.4 2.1 %collective-permute-start.1 = (bf16[2,192,256]{2,1,0:T(8,128)(2,1)S(1)}, bf16[2,192,256]{2,1,0:T(8,128)(2,1)S(1)}, u32[]{:S(2)}, u32[]{:S(2)}) collective-permute-start(bf16[2,192,256]{2,1,0:T(8,128)(2,1)S(1)} %pad_maximum_fusion.14), channel_id=1, source_target_pairs={{0,4},{1,5},{2,6},{3,7},{4,0},{5,1},{6,2},{7,3},{8,12},{9,13},{10,... | collective-permute-start | bytes 589832 | tf_op jit(solution)/shard_map/ppermute | solution.py:29
  70.5 8.3 %collective-permute-done.5 = bf16[2,192,256]{2,1,0:T(8,128)(2,1)S(1)} collective-permute-done((bf16[2,192,256]{2,1,0:T(8,128)(2,1)S(1)}, bf16[2,192,256]{2,1,0:T(8,128)(2,1)S(1)}, u32[]{:S(2)}, u32[]{:S(2)}) %collective-permute-start.5) | collective-permute-done | bytes 196640 | tf_op jit(solution)/shard_map/ppermute | solution.py:29
  78.8 1.0 select_bitcast_fusion.17
  79.9 2.1 %collective-permute-start.14 = (bf16[2,2,192,256]{3,2,1,0:T(8,128)(2,1)S(1)}, bf16[2,2,192,256]{3,2,1,0:T(8,128)(2,1)S(1)}, u32[]{:S(2)}, u32[]{:S(2)}) collective-permute-start(bf16[2,2,192,256]{3,2,1,0:T(8,128)(2,1)S(1)} %pad_maximum_fusion.13), channel_id=1, source_target_pairs={{0,4},{1,5},{2,6},{3,7},{4,0},{5,1},{6,2},{7,3},{8,12},{9,13},{10,... | collective-permute-start | bytes 1179656 | tf_op jit(solution)/shard_map/ppermute | solution.py:29
  82.1 1.0 collective-permute-start.2
  83.1 8.8 %collective-permute-done.6 = bf16[2,2,192,256]{3,2,1,0:T(8,128)(2,1)S(1)} collective-permute-done((bf16[2,2,192,256]{3,2,1,0:T(8,128)(2,1)S(1)}, bf16[2,2,192,256]{3,2,1,0:T(8,128)(2,1)S(1)}, u32[]{:S(2)}, u32[]{:S(2)}) %collective-permute-start.6) | collective-permute-done | bytes 393248 | tf_op jit(solution)/shard_map/ppermute | solution.py:29
  92.1 7.2 %collective-permute-done.14 = bf16[2,2,192,256]{3,2,1,0:T(8,128)(2,1)S(1)} collective-permute-done((bf16[2,2,192,256]{3,2,1,0:T(8,128)(2,1)S(1)}, bf16[2,2,192,256]{3,2,1,0:T(8,128)(2,1)S(1)}, u32[]{:S(2)}, u32[]{:S(2)}) %collective-permute-start.14) | collective-permute-done | bytes 393248 | tf_op jit(solution)/shard_map/ppermute | solution.py:29
  99.7 0.5 collective-permute-start.3
  100.9 0.9 collective-permute-done.15
  102.2 1.8 %collective-permute-done.11 = bf16[2,2,2,192,256]{4,3,0,1,2:T(8,128)(2,1)S(1)} collective-permute-done((bf16[2,2,2,192,256]{4,3,0,1,2:T(8,128)(2,1)S(1)}, bf16[2,2,2,192,256]{4,3,0,1,2:T(8,128)(2,1)S(1)}, u32[]{:S(2)}, u32[]{:S(2)}) %collective-permute-start.11) | collective-permute-done | bytes 786464 | tf_op jit(solution)/shard_map/ppermute | solution.py:29
  104.4 1.6 fusion.6
  106.0 0.4 fusion.19
  106.7 0.3 convolution_bitcast_fusion
  107.4 1.1 fusion.16
  108.5 0.3 fusion.37
  109.0 0.4 pad_maximum_fusion
  109.8 0.7 fusion.32
  110.9 0.4 collective-permute-start.21
  111.7 0.4 collective-permute-start.27
  112.2 1.0 fusion.20
  113.2 6.9 %collective-permute-done.27 = f32[2,2,2,64,128]{4,3,2,1,0:T(8,128)S(1)} collective-permute-done((f32[2,2,2,64,128]{4,3,2,1,0:T(8,128)S(1)}, f32[2,2,2,64,128]{4,3,2,1,0:T(8,128)S(1)}, u32[]{:S(2)}, u32[]{:S(2)}) %collective-permute-start.27) | collective-permute-done | bytes 262176 | tf_op jit(solution)/shard_map/weight_grad_sum/ppermute | solution.py:29
  120.2 1.5 collective-permute-start.28
  121.9 1.0 collective-permute-start.22
  122.9 2.3 %collective-permute-done.28 = f32[2,2,64,128]{3,2,1,0:T(8,128)S(1)} collective-permute-done((f32[2,2,64,128]{3,2,1,0:T(8,128)S(1)}, f32[2,2,64,128]{3,2,1,0:T(8,128)S(1)}, u32[]{:S(2)}, u32[]{:S(2)}) %collective-permute-start.28) | collective-permute-done | bytes 131104 | tf_op jit(solution)/shard_map/weight_grad_sum/ppermute | solution.py:29
  125.3 1.0 collective-permute-start.29
  126.4 9.9 %collective-permute-done.29 = f32[2,64,128]{2,1,0:T(8,128)S(1)} collective-permute-done((f32[2,64,128]{2,1,0:T(8,128)S(1)}, f32[2,64,128]{2,1,0:T(8,128)S(1)}, u32[]{:S(2)}, u32[]{:S(2)}) %collective-permute-start.29) | collective-permute-done | bytes 65568 | tf_op jit(solution)/shard_map/weight_grad_sum/ppermute | solution.py:29
  136.3 1.0 collective-permute-start.30
  137.3 0.6 collective-permute-start.17
  137.9 3.3 %collective-permute-done.30 = f32[64,128]{1,0:T(8,128)S(1)} collective-permute-done((f32[64,128]{1,0:T(8,128)S(1)}, f32[64,128]{1,0:T(8,128)S(1)}, u32[]{:S(2)}, u32[]{:S(2)}) %collective-permute-start.30) | collective-permute-done | bytes 32800 | tf_op jit(solution)/shard_map/weight_grad_sum/ppermute | solution.py:29
  141.7 7.4 %collective-permute-done.17 = f32[2,2,2,64,192]{4,3,2,1,0:T(8,128)S(1)} collective-permute-done((f32[2,2,2,64,192]{4,3,2,1,0:T(8,128)S(1)}, f32[2,2,2,64,192]{4,3,2,1,0:T(8,128)S(1)}, u32[]{:S(2)}, u32[]{:S(2)}) %collective-permute-start.17) | collective-permute-done | bytes 393248 | tf_op jit(solution)/shard_map/weight_grad_sum/ppermute | solution.py:29
  149.1 0.9 collective-permute-start.18
  150.1 0.6 collective-permute-start.24
  150.7 4.9 %collective-permute-done.18 = f32[2,2,64,192]{3,2,1,0:T(8,128)S(1)} collective-permute-done((f32[2,2,64,192]{3,2,1,0:T(8,128)S(1)}, f32[2,2,64,192]{3,2,1,0:T(8,128)S(1)}, u32[]{:S(2)}, u32[]{:S(2)}) %collective-permute-start.18) | collective-permute-done | bytes 196640 | tf_op jit(solution)/shard_map/weight_grad_sum/ppermute | solution.py:29
  155.7 1.8 %collective-permute-start.19 = (f32[2,64,192]{2,1,0:T(8,128)S(1)}, f32[2,64,192]{2,1,0:T(8,128)S(1)}, u32[]{:S(2)}, u32[]{:S(2)}) collective-permute-start(f32[2,64,192]{2,1,0:T(8,128)S(1)} %dynamic-slice_bitcast_fusion.8), channel_id=1, source_target_pairs={{0,4},{1,5},{2,6},{3,7},{4,0},{5,1},{6,2},{7,3},{8,12},{9,13},{10,... | collective-permute-start | bytes 294920 | tf_op jit(solution)/shard_map/weight_grad_sum/ppermute | solution.py:29
  157.5 0.6 collective-permute-start.25
  158.1 3.2 %collective-permute-done.19 = f32[2,64,192]{2,1,0:T(8,128)S(1)} collective-permute-done((f32[2,64,192]{2,1,0:T(8,128)S(1)}, f32[2,64,192]{2,1,0:T(8,128)S(1)}, u32[]{:S(2)}, u32[]{:S(2)}) %collective-permute-start.19) | collective-permute-done | bytes 98336 | tf_op jit(solution)/shard_map/weight_grad_sum/ppermute | solution.py:29
  161.3 1.8 %collective-permute-start.20 = (f32[64,192]{1,0:T(8,128)S(1)}, f32[64,192]{1,0:T(8,128)S(1)}, u32[]{:S(2)}, u32[]{:S(2)}) collective-permute-start(f32[64,192]{1,0:T(8,128)S(1)} %dynamic-slice_bitcast_fusion.11), channel_id=1, source_target_pairs={{0,8},{1,9},{2,10},{3,11},{4,12},{5,13},{6,14},{7,15},{8,0},{9,1},... | collective-permute-start | bytes 147464 | tf_op jit(solution)/shard_map/weight_grad_sum/ppermute | solution.py:29
  163.1 0.3 collective-permute-done.25
  163.4 3.8 %collective-permute-done.20 = f32[64,192]{1,0:T(8,128)S(1)} collective-permute-done((f32[64,192]{1,0:T(8,128)S(1)}, f32[64,192]{1,0:T(8,128)S(1)}, u32[]{:S(2)}, u32[]{:S(2)}) %collective-permute-start.20) | collective-permute-done | bytes 49184 | tf_op jit(solution)/shard_map/weight_grad_sum/ppermute | solution.py:29
  167.3 0.8 pad_maximum_fusion.18
  (111 shorter events, 6.2 us)
Async XLA Ops:
  0.6 10.4 %copy-start = (bf16[192,512]{1,0:T(8,128)(2,1)S(1)}, bf16[192,512]{1,0:T(8,128)(2,1)}, u32[]{:S(2)}) copy-start(bf16[192,512]{1,0:T(8,128)(2,1)} %param.13) | copy-start | bytes 589828
  0.6 16.1 %copy-start.5 = (s32[3072]{0:T(1024)S(1)}, s32[3072]{0:T(1024)}, u32[]{:S(2)}) copy-start(s32[3072]{0:T(1024)} %param.12) | copy-start | bytes 36868
  0.7 16.2 %copy-start.3 = (s32[3072,8]{0,1:T(8,128)S(1)}, s32[3072,8]{0,1:T(8,128)}, u32[]{:S(2)}) copy-start(s32[3072,8]{0,1:T(8,128)} %param.11) | copy-start | bytes 294916
  0.7 16.2 %copy-start.4 = (s32[3072,8]{0,1:T(8,128)S(1)}, s32[3072,8]{0,1:T(8,128)}, u32[]{:S(2)}) copy-start(s32[3072,8]{0,1:T(8,128)} %param.10) | copy-start | bytes 294916
  2.8 40.4 %all-to-all-start = ((bf16[32,16,192]{2,0,1:T(8,128)(2,1)}), bf16[32,16,192]{2,0,1:T(8,128)(2,1)S(1)}, u32[]{:S(2)}, u32[]{:S(2)}) async-start(bf16[32,16,192]{2,0,1:T(8,128)(2,1)} %copy.31), calls=%async_computation | async-start | bytes 524288 | tf_op jit(solution)/shard_map/all_to_all | solution.py:100
  12.4 23.8 %collective-permute-start.8 = (bf16[192,256]{1,0:T(8,128)(2,1)S(1)}, bf16[192,256]{1,0:T(8,128)(2,1)S(1)}, u32[]{:S(2)}, u32[]{:S(2)}) collective-permute-start(bf16[192,256]{1,0:T(8,128)(2,1)S(1)} %get-tuple-element.42), channel_id=1, source_target_pairs={{0,8},{1,9},{2,10},{3,11},{4,12},{5,13},{6,14},{7,15},{8,0},{9,1},... | collective-permute-start | bytes 294920 | tf_op jit(solution)/shard_map/ppermute | solution.py:29
  15.3 20.9 %collective-permute-start.12 = (bf16[192,256]{1,0:T(8,128)(2,1)S(1)}, bf16[192,256]{1,0:T(8,128)(2,1)S(1)}, u32[]{:S(2)}, u32[]{:S(2)}) collective-permute-start(bf16[192,256]{1,0:T(8,128)(2,1)S(1)} %get-tuple-element.43), channel_id=1, source_target_pairs={{0,2},{1,3},{2,0},{3,1},{4,6},{5,7},{6,4},{7,5},{8,10},{9,11},{10,... | collective-permute-start | bytes 294920 | tf_op jit(solution)/shard_map/ppermute | solution.py:29
  17.7 9.7 %copy-start.2 = (bf16[32,3072]{1,0:T(8,128)(2,1)S(1)}, bf16[32,3072]{1,0:T(8,128)(2,1)}, u32[]{:S(2)}) copy-start(bf16[32,3072]{1,0:T(8,128)(2,1)} %param.7) | copy-start | bytes 589828
  36.2 6.9 %collective-permute-start.9 = (bf16[2,192,256]{2,1,0:T(8,128)(2,1)S(1)}, bf16[2,192,256]{2,1,0:T(8,128)(2,1)S(1)}, u32[]{:S(2)}, u32[]{:S(2)}) collective-permute-start(bf16[2,192,256]{2,1,0:T(8,128)(2,1)S(1)} %pad_maximum_fusion.16), channel_id=1, source_target_pairs={{0,4},{1,5},{2,6},{3,7},{4,0},{5,1},{6,2},{7,3},{8,12},{9,13},{10,... | collective-permute-start | bytes 589832 | tf_op jit(solution)/shard_map/ppermute | solution.py:29
  39.5 31.0 %collective-permute-start.13 = (bf16[2,192,256]{2,1,0:T(8,128)(2,1)S(1)}, bf16[2,192,256]{2,1,0:T(8,128)(2,1)}, u32[]{:S(2)}, u32[]{:S(2)}) collective-permute-start(bf16[2,192,256]{2,1,0:T(8,128)(2,1)S(1)} %pad_maximum_fusion.17), channel_id=1, source_target_pairs={{0,8},{1,9},{2,10},{3,11},{4,12},{5,13},{6,14},{7,15},{8,0},{9,1},... | collective-permute-start | bytes 589832 | tf_op jit(solution)/shard_map/ppermute | solution.py:29
  43.2 15.7 %all-to-all-start.1 = ((bf16[32,16,192]{2,0,1:T(8,128)(2,1)}), bf16[32,16,192]{2,0,1:T(8,128)(2,1)S(1)}, u32[]{:S(2)}, u32[]{:S(2)}) async-start(bf16[32,16,192]{2,0,1:T(8,128)(2,1)} %copy.32), calls=%async_computation.1 | async-start | bytes 524288 | tf_op jit(solution)/shard_map/all_to_all | solution.py:101
  48.9 50.7 %collective-permute-start.10 = (bf16[2,2,192,256]{3,2,0,1:T(8,128)(2,1)S(1)}, bf16[2,2,192,256]{3,2,0,1:T(8,128)(2,1)S(1)}, u32[]{:S(2)}, u32[]{:S(2)}) collective-permute-start(bf16[2,2,192,256]{3,2,0,1:T(8,128)(2,1)S(1)} %pad_maximum_fusion.12), channel_id=1, source_target_pairs={{0,2},{1,3},{2,0},{3,1},{4,6},{5,7},{6,4},{7,5},{8,10},{9,11},{10,... | collective-permute-start | bytes 1179656 | tf_op jit(solution)/shard_map/ppermute | solution.py:29
  60.3 7.8 %copy-start.1 = (bf16[1024,512]{1,0:T(8,128)(2,1)S(1)}, bf16[1024,512]{1,0:T(8,128)(2,1)}, u32[]{:S(2)}) copy-start(bf16[1024,512]{1,0:T(8,128)(2,1)} %param.9) | copy-start | bytes 3145732
  60.3 7.6 %collective-permute-start = (bf16[192,256]{1,0:T(8,128)(2,1)S(1)}, bf16[192,256]{1,0:T(8,128)(2,1)S(1)}, u32[]{:S(2)}, u32[]{:S(2)}) collective-permute-start(bf16[192,256]{1,0:T(8,128)(2,1)S(1)} %get-tuple-element.46), channel_id=1, source_target_pairs={{0,8},{1,9},{2,10},{3,11},{4,12},{5,13},{6,14},{7,15},{8,0},{9,1},... | collective-permute-start | bytes 294920 | tf_op jit(solution)/shard_map/ppermute | solution.py:29
  61.4 6.5 %collective-permute-start.4 = (bf16[192,256]{1,0:T(8,128)(2,1)S(1)}, bf16[192,256]{1,0:T(8,128)(2,1)S(1)}, u32[]{:S(2)}, u32[]{:S(2)}) collective-permute-start(bf16[192,256]{1,0:T(8,128)(2,1)S(1)} %get-tuple-element.47), channel_id=1, source_target_pairs={{0,2},{1,3},{2,0},{3,1},{4,6},{5,7},{6,4},{7,5},{8,10},{9,11},{10,... | collective-permute-start | bytes 294920 | tf_op jit(solution)/shard_map/ppermute | solution.py:29
  68.0 10.8 %collective-permute-start.5 = (bf16[2,192,256]{2,1,0:T(8,128)(2,1)S(1)}, bf16[2,192,256]{2,1,0:T(8,128)(2,1)S(1)}, u32[]{:S(2)}, u32[]{:S(2)}) collective-permute-start(bf16[2,192,256]{2,1,0:T(8,128)(2,1)S(1)} %pad_maximum_fusion.15), channel_id=1, source_target_pairs={{0,8},{1,9},{2,10},{3,11},{4,12},{5,13},{6,14},{7,15},{8,0},{9,1},... | collective-permute-start | bytes 589832 | tf_op jit(solution)/shard_map/ppermute | solution.py:29
  68.4 13.6 %collective-permute-start.1 = (bf16[2,192,256]{2,1,0:T(8,128)(2,1)S(1)}, bf16[2,192,256]{2,1,0:T(8,128)(2,1)S(1)}, u32[]{:S(2)}, u32[]{:S(2)}) collective-permute-start(bf16[2,192,256]{2,1,0:T(8,128)(2,1)S(1)} %pad_maximum_fusion.14), channel_id=1, source_target_pairs={{0,4},{1,5},{2,6},{3,7},{4,0},{5,1},{6,2},{7,3},{8,12},{9,13},{10,... | collective-permute-start | bytes 589832 | tf_op jit(solution)/shard_map/ppermute | solution.py:29
  79.8 12.1 %collective-permute-start.6 = (bf16[2,2,192,256]{3,2,1,0:T(8,128)(2,1)S(1)}, bf16[2,2,192,256]{3,2,1,0:T(8,128)(2,1)S(1)}, u32[]{:S(2)}, u32[]{:S(2)}) collective-permute-start(bf16[2,2,192,256]{3,2,1,0:T(8,128)(2,1)S(1)} %pad_maximum_fusion.11), channel_id=1, source_target_pairs={{0,4},{1,5},{2,6},{3,7},{4,0},{5,1},{6,2},{7,3},{8,12},{9,13},{10,... | collective-permute-start | bytes 1179656 | tf_op jit(solution)/shard_map/ppermute | solution.py:29
  79.9 19.3 %collective-permute-start.14 = (bf16[2,2,192,256]{3,2,1,0:T(8,128)(2,1)S(1)}, bf16[2,2,192,256]{3,2,1,0:T(8,128)(2,1)S(1)}, u32[]{:S(2)}, u32[]{:S(2)}) collective-permute-start(bf16[2,2,192,256]{3,2,1,0:T(8,128)(2,1)S(1)} %pad_maximum_fusion.13), channel_id=1, source_target_pairs={{0,4},{1,5},{2,6},{3,7},{4,0},{5,1},{6,2},{7,3},{8,12},{9,13},{10,... | collective-permute-start | bytes 1179656 | tf_op jit(solution)/shard_map/ppermute | solution.py:29
  82.1 17.4 %collective-permute-start.2 = (bf16[2,2,192,256]{3,2,0,1:T(8,128)(2,1)S(1)}, bf16[2,2,192,256]{3,2,0,1:T(8,128)(2,1)S(1)}, u32[]{:S(2)}, u32[]{:S(2)}) collective-permute-start(bf16[2,2,192,256]{3,2,0,1:T(8,128)(2,1)S(1)} %pad_maximum_fusion.10), channel_id=1, source_target_pairs={{0,2},{1,3},{2,0},{3,1},{4,6},{5,7},{6,4},{7,5},{8,10},{9,11},{10,... | collective-permute-start | bytes 1179656 | tf_op jit(solution)/shard_map/ppermute | solution.py:29
  92.0 8.4 %collective-permute-start.7 = (bf16[2,2,2,192,256]{4,3,2,0,1:T(8,128)(2,1)S(1)}, bf16[2,2,2,192,256]{4,3,2,0,1:T(8,128)(2,1)S(1)}, u32[]{:S(2)}, u32[]{:S(2)}) collective-permute-start(bf16[2,2,2,192,256]{4,3,2,0,1:T(8,128)(2,1)S(1)} %pad_maximum_fusion.7), channel_id=1, source_target_pairs={{0,1},{1,0},{2,3},{3,2},{4,5},{5,4},{6,7},{7,6},{8,9},{9,8},{10,11... | collective-permute-start | bytes 2359304 | tf_op jit(solution)/shard_map/ppermute | solution.py:29
  99.4 2.4 %collective-permute-start.15 = (bf16[2,2,2,192,256]{4,3,2,0,1:T(8,128)(2,1)S(1)}, bf16[2,2,2,192,256]{4,3,2,0,1:T(8,128)(2,1)S(1)}, u32[]{:S(2)}, u32[]{:S(2)}) collective-permute-start(bf16[2,2,2,192,256]{4,3,2,0,1:T(8,128)(2,1)S(1)} %pad_maximum_fusion.9), channel_id=1, source_target_pairs={{0,1},{1,0},{2,3},{3,2},{4,5},{5,4},{6,7},{7,6},{8,9},{9,8},{10,11... | collective-permute-start | bytes 2359304 | tf_op jit(solution)/shard_map/ppermute | solution.py:29
  99.7 7.2 %collective-permute-start.3 = (bf16[2,2,2,192,256]{4,3,0,1,2:T(8,128)(2,1)S(1)}, bf16[2,2,2,192,256]{4,3,0,1,2:T(8,128)(2,1)S(1)}, u32[]{:S(2)}, u32[]{:S(2)}) collective-permute-start(bf16[2,2,2,192,256]{4,3,0,1,2:T(8,128)(2,1)S(1)} %pad_maximum_fusion.6), channel_id=1, source_target_pairs={{0,1},{1,0},{2,3},{3,2},{4,5},{5,4},{6,7},{7,6},{8,9},{9,8},{10,11... | collective-permute-start | bytes 2359304 | tf_op jit(solution)/shard_map/ppermute | solution.py:29
  100.3 3.7 %collective-permute-start.11 = (bf16[2,2,2,192,256]{4,3,0,1,2:T(8,128)(2,1)S(1)}, bf16[2,2,2,192,256]{4,3,0,1,2:T(8,128)(2,1)S(1)}, u32[]{:S(2)}, u32[]{:S(2)}) collective-permute-start(bf16[2,2,2,192,256]{4,3,0,1,2:T(8,128)(2,1)S(1)} %pad_maximum_fusion.8), channel_id=1, source_target_pairs={{0,1},{1,0},{2,3},{3,2},{4,5},{5,4},{6,7},{7,6},{8,9},{9,8},{10,11... | collective-permute-start | bytes 2359304 | tf_op jit(solution)/shard_map/ppermute | solution.py:29
  109.6 2.0 %collective-permute-start.26 = (f32[2,2,2,2,64,128]{5,4,3,1,0,2:T(8,128)S(1)}, f32[2,2,2,2,64,128]{5,4,3,1,0,2:T(8,128)S(1)}, u32[]{:S(2)}, u32[]{:S(2)}) collective-permute-start(f32[2,2,2,2,64,128]{5,4,3,1,0,2:T(8,128)S(1)} %bitcast.178), channel_id=1, source_target_pairs={{0,1},{1,0},{2,3},{3,2},{4,5},{5,4},{6,7},{7,6},{8,9},{9,8},{10,11... | collective-permute-start | bytes 1572872 | tf_op jit(solution)/shard_map/weight_grad_sum/ppermute | solution.py:29
  110.9 10.8 %collective-permute-start.21 = (f32[2,2,2,2,64,192]{5,4,2,1,0,3:T(8,128)S(1)}, f32[2,2,2,2,64,192]{5,4,2,1,0,3:T(8,128)S(1)}, u32[]{:S(2)}, u32[]{:S(2)}) collective-permute-start(f32[2,2,2,2,64,192]{5,4,2,1,0,3:T(8,128)S(1)} %bitcast.175), channel_id=1, source_target_pairs={{0,1},{1,0},{2,3},{3,2},{4,5},{5,4},{6,7},{7,6},{8,9},{9,8},{10,11... | collective-permute-start | bytes 2359304 | tf_op jit(solution)/shard_map/weight_grad_sum/ppermute | solution.py:29
  111.7 8.4 %collective-permute-start.27 = (f32[2,2,2,64,128]{4,3,2,1,0:T(8,128)S(1)}, f32[2,2,2,64,128]{4,3,2,1,0:T(8,128)S(1)}, u32[]{:S(2)}, u32[]{:S(2)}) collective-permute-start(f32[2,2,2,64,128]{4,3,2,1,0:T(8,128)S(1)} %dynamic-slice_bitcast_fusion.3), channel_id=1, source_target_pairs={{0,4},{1,5},{2,6},{3,7},{4,0},{5,1},{6,2},{7,3},{8,12},{9,13},{10,... | collective-permute-start | bytes 786440 | tf_op jit(solution)/shard_map/weight_grad_sum/ppermute | solution.py:29
  112.2 14.1 %collective-permute-start.16 = (f32[2,2,2,2,64,192]{5,4,3,2,1,0:T(8,128)S(1)}, f32[2,2,2,2,64,192]{5,4,3,2,1,0:T(8,128)S(1)}, u32[]{:S(2)}, u32[]{:S(2)}) collective-permute-start(f32[2,2,2,2,64,192]{5,4,3,2,1,0:T(8,128)S(1)} %dynamic-slice_bitcast_fusion), channel_id=1, source_target_pairs={{0,1},{1,0},{2,3},{3,2},{4,5},{5,4},{6,7},{7,6},{8,9},{9,8},{10,11... | collective-permute-start | bytes 2359304 | tf_op jit(solution)/shard_map/weight_grad_sum/ppermute | solution.py:29
  120.2 5.0 %collective-permute-start.28 = (f32[2,2,64,128]{3,2,1,0:T(8,128)S(1)}, f32[2,2,64,128]{3,2,1,0:T(8,128)S(1)}, u32[]{:S(2)}, u32[]{:S(2)}) collective-permute-start(f32[2,2,64,128]{3,2,1,0:T(8,128)S(1)} %dynamic-slice_bitcast_fusion.6), channel_id=1, source_target_pairs={{0,16},{16,0},{1,17},{17,1},{2,18},{18,2},{3,19},{19,3},{4,20},{20... | collective-permute-start | bytes 393224 | tf_op jit(solution)/shard_map/weight_grad_sum/ppermute | solution.py:29
  121.9 19.3 %collective-permute-start.22 = (f32[2,2,2,64,192]{4,3,2,1,0:T(8,128)S(1)}, f32[2,2,2,64,192]{4,3,2,1,0:T(8,128)S(1)}, u32[]{:S(2)}, u32[]{:S(2)}) collective-permute-start(f32[2,2,2,64,192]{4,3,2,1,0:T(8,128)S(1)} %dynamic-slice_bitcast_fusion.1), channel_id=1, source_target_pairs={{0,2},{1,3},{2,0},{3,1},{4,6},{5,7},{6,4},{7,5},{8,10},{9,11},{10,... | collective-permute-start | bytes 1179656 | tf_op jit(solution)/shard_map/weight_grad_sum/ppermute | solution.py:29
  125.3 11.0 %collective-permute-start.29 = (f32[2,64,128]{2,1,0:T(8,128)S(1)}, f32[2,64,128]{2,1,0:T(8,128)S(1)}, u32[]{:S(2)}, u32[]{:S(2)}) collective-permute-start(f32[2,64,128]{2,1,0:T(8,128)S(1)} %dynamic-slice_bitcast_fusion.9), channel_id=1, source_target_pairs={{0,2},{1,3},{2,0},{3,1},{4,6},{5,7},{6,4},{7,5},{8,10},{9,11},{10,... | collective-permute-start | bytes 196616 | tf_op jit(solution)/shard_map/weight_grad_sum/ppermute | solution.py:29
  136.3 5.0 %collective-permute-start.30 = (f32[64,128]{1,0:T(8,128)S(1)}, f32[64,128]{1,0:T(8,128)S(1)}, u32[]{:S(2)}, u32[]{:S(2)}) collective-permute-start(f32[64,128]{1,0:T(8,128)S(1)} %dynamic-slice_bitcast_fusion.12), channel_id=1, source_target_pairs={{0,8},{1,9},{2,10},{3,11},{4,12},{5,13},{6,14},{7,15},{8,0},{9,1},... | collective-permute-start | bytes 98312 | tf_op jit(solution)/shard_map/weight_grad_sum/ppermute | solution.py:29
  137.3 11.7 %collective-permute-start.17 = (f32[2,2,2,64,192]{4,3,2,1,0:T(8,128)S(1)}, f32[2,2,2,64,192]{4,3,2,1,0:T(8,128)S(1)}, u32[]{:S(2)}, u32[]{:S(2)}) collective-permute-start(f32[2,2,2,64,192]{4,3,2,1,0:T(8,128)S(1)} %dynamic-slice_bitcast_fusion.2), channel_id=1, source_target_pairs={{0,16},{16,0},{1,17},{17,1},{2,18},{18,2},{3,19},{19,3},{4,20},{20... | collective-permute-start | bytes 1179656 | tf_op jit(solution)/shard_map/weight_grad_sum/ppermute | solution.py:29
  141.4 8.6 %collective-permute-start.23 = (f32[2,2,64,192]{3,2,1,0:T(8,128)S(1)}, f32[2,2,64,192]{3,2,1,0:T(8,128)S(1)}, u32[]{:S(2)}, u32[]{:S(2)}) collective-permute-start(f32[2,2,64,192]{3,2,1,0:T(8,128)S(1)} %dynamic-slice_bitcast_fusion.4), channel_id=1, source_target_pairs={{0,4},{1,5},{2,6},{3,7},{4,0},{5,1},{6,2},{7,3},{8,12},{9,13},{10,... | collective-permute-start | bytes 589832 | tf_op jit(solution)/shard_map/weight_grad_sum/ppermute | solution.py:29
  149.1 6.4 %collective-permute-start.18 = (f32[2,2,64,192]{3,2,1,0:T(8,128)S(1)}, f32[2,2,64,192]{3,2,1,0:T(8,128)S(1)}, u32[]{:S(2)}, u32[]{:S(2)}) collective-permute-start(f32[2,2,64,192]{3,2,1,0:T(8,128)S(1)} %dynamic-slice_bitcast_fusion.5), channel_id=1, source_target_pairs={{0,2},{1,3},{2,0},{3,1},{4,6},{5,7},{6,4},{7,5},{8,10},{9,11},{10,... | collective-permute-start | bytes 589832 | tf_op jit(solution)/shard_map/weight_grad_sum/ppermute | solution.py:29
  150.1 7.4 %collective-permute-start.24 = (f32[2,64,192]{2,1,0:T(8,128)S(1)}, f32[2,64,192]{2,1,0:T(8,128)S(1)}, u32[]{:S(2)}, u32[]{:S(2)}) collective-permute-start(f32[2,64,192]{2,1,0:T(8,128)S(1)} %dynamic-slice_bitcast_fusion.7), channel_id=1, source_target_pairs={{0,16},{16,0},{1,17},{17,1},{2,18},{18,2},{3,19},{19,3},{4,20},{20... | collective-permute-start | bytes 294920 | tf_op jit(solution)/shard_map/weight_grad_sum/ppermute | solution.py:29
  155.7 5.6 %collective-permute-start.19 = (f32[2,64,192]{2,1,0:T(8,128)S(1)}, f32[2,64,192]{2,1,0:T(8,128)S(1)}, u32[]{:S(2)}, u32[]{:S(2)}) collective-permute-start(f32[2,64,192]{2,1,0:T(8,128)S(1)} %dynamic-slice_bitcast_fusion.8), channel_id=1, source_target_pairs={{0,4},{1,5},{2,6},{3,7},{4,0},{5,1},{6,2},{7,3},{8,12},{9,13},{10,... | collective-permute-start | bytes 294920 | tf_op jit(solution)/shard_map/weight_grad_sum/ppermute | solution.py:29
  157.5 5.9 %collective-permute-start.25 = (f32[64,192]{1,0:T(8,128)S(1)}, f32[64,192]{1,0:T(8,128)S(1)}, u32[]{:S(2)}, u32[]{:S(2)}) collective-permute-start(f32[64,192]{1,0:T(8,128)S(1)} %dynamic-slice_bitcast_fusion.10), channel_id=1, source_target_pairs={{0,8},{1,9},{2,10},{3,11},{4,12},{5,13},{6,14},{7,15},{8,0},{9,1},... | collective-permute-start | bytes 147464 | tf_op jit(solution)/shard_map/weight_grad_sum/ppermute | solution.py:29
  161.3 5.9 %collective-permute-start.20 = (f32[64,192]{1,0:T(8,128)S(1)}, f32[64,192]{1,0:T(8,128)S(1)}, u32[]{:S(2)}, u32[]{:S(2)}) collective-permute-start(f32[64,192]{1,0:T(8,128)S(1)} %dynamic-slice_bitcast_fusion.11), channel_id=1, source_target_pairs={{0,8},{1,9},{2,10},{3,11},{4,12},{5,13},{6,14},{7,15},{8,0},{9,1},... | collective-permute-start | bytes 147464 | tf_op jit(solution)/shard_map/weight_grad_sum/ppermute | solution.py:29

commit v9 on v5

--- a/solution.py
+++ b/solution.py
@@ -47,14 +47,19 @@
     return values.reshape(rows, terms.shape[1])
 
 
+def doubling_step(current, order, step):
+    own = lax.axis_index("mp")
+    bit = order[step]
+    got = swap(current, "mp", 1 << bit)
+    low = jnp.where((own >> bit) & 1 == 0, current, got)
+    high = jnp.where((own >> bit) & 1 == 0, got, current)
+    return jnp.stack([low, high], axis=sum(1 for done in order[:step] if done > bit))
+
+
 def doubling_gather(rows, order):
-    own = lax.axis_index("mp")
     current = rows
-    for step, bit in enumerate(order):
-        got = swap(current, "mp", 1 << bit)
-        low = jnp.where((own >> bit) & 1 == 0, current, got)
-        high = jnp.where((own >> bit) & 1 == 0, got, current)
-        current = jnp.stack([low, high], axis=sum(1 for done in order[:step] if done > bit))
+    for step in range(len(order)):
+        current = doubling_step(current, order, step)
     return current.reshape(-1, rows.shape[-1])
 
 
@@ -84,27 +89,50 @@
     match = (neighbor_owner[None, :, :] == owner_ids) & live[None, :, :]
     rowsel = jnp.max(jnp.where(match, neighbor_row[None, :, :], -1), axis=2)
 
+    self_two = weights_two[:hidden]
+    neigh_two = weights_two[hidden:]
+    own_inverse = lax.dynamic_slice_in_dim(inverse_all, own_index * node_dev, node_dev, 0)
+    order = list(range(devices.bit_length() - 2, -1, -1))
+    other = [1] + [bit for bit in order if bit != 1] if devices == 16 else order
+    dense_one = all_nodes * all_nodes <= 4096 * 4096
+
+    down_neigh = (contract(cotangent, neigh_two, 1, 1) * own_inverse[:, None]).astype(jnp.bfloat16)
+    half = down_neigh.shape[1] // 2
+    parts = [down_neigh[:, :half], down_neigh[:, half:]]
+    orders = [order, other]
+    steps_done = 0
+
+    def advance(parts, steps_done):
+        if steps_done < len(order):
+            parts = [doubling_step(p, o, steps_done) for p, o in zip(parts, orders)]
+        return parts, steps_done + 1
+
+    parts, steps_done = advance(parts, steps_done)
+
     with jax.named_scope("layer_one_mean"):
-        if all_nodes * all_nodes <= 4096 * 4096:
+        if dense_one:
             row_ids = lax.broadcasted_iota(jnp.int32, (1, node_dev, 1), 1)
             adjacency = (rowsel[:, None, :] == row_ids).astype(jnp.bfloat16)
             adjacency = adjacency.reshape(devices * node_dev, all_nodes)
+            parts, adjacency = lax.optimization_barrier((parts, adjacency))
+            parts, steps_done = advance(parts, steps_done)
             summed = contract(node_features, adjacency, 1, 0)
             agg_one_cols = (summed * inverse_all[None, :]).astype(jnp.bfloat16)
         else:
             owner_slots = neighbor_owner.T
             global_ids = owner_slots * node_dev + neighbor_row.T
             agg_one_cols = column_mean(node_features, global_ids, live.T, inverse_all)
+    parts, agg_one_cols = lax.optimization_barrier((parts, agg_one_cols))
+    parts, steps_done = advance(parts, steps_done)
 
     own_feats, own_agg_one = (
         lax.all_to_all(node_features, "mp", split_axis=1, concat_axis=0, tiled=True),
         lax.all_to_all(agg_one_cols, "mp", split_axis=1, concat_axis=0, tiled=True),
     )
-    self_two = weights_two[:hidden]
-    neigh_two = weights_two[hidden:]
-    own_inverse = lax.dynamic_slice_in_dim(inverse_all, own_index * node_dev, node_dev, 0)
-    order = list(range(devices.bit_length() - 2, -1, -1))
-    other = [1] + [bit for bit in order if bit != 1] if devices == 16 else order
+    parts, own_agg_one = lax.optimization_barrier((parts, own_agg_one))
+    while steps_done < len(order):
+        parts, steps_done = advance(parts, steps_done)
+    down_all = jnp.concatenate([p.reshape(-1, half) for p in parts], axis=1)
 
     with jax.named_scope("neighbor_tables"):
         row_ids = lax.broadcasted_iota(jnp.int32, (1, node_dev, 1), 1)
@@ -113,9 +141,6 @@
         own_edges = own_edges.reshape(devices * node_dev, node_dev)
         mine_sel = lax.dynamic_index_in_dim(rowsel, own_index, 0, keepdims=False)
         named_by = (mine_sel[:, None] == row_ids.reshape(1, node_dev)).astype(jnp.bfloat16)
-
-    down_neigh = (contract(cotangent, neigh_two, 1, 1) * own_inverse[:, None]).astype(jnp.bfloat16)
-    down_all = split_gather(down_neigh, order, other)
 
     pre_one = contract(own_feats, weights_one[:feat_width], 0, 0) + contract(
         own_agg_one, weights_one[feat_width:], 0, 0

time: 150 us -> 139 us (0.927)
  other arithmetic: 19.8 us -> 14.1 us
  waiting for transfers between devices: 68.1 us -> 64.9 us
  matrix products: 17.2 us -> 14.6 us
    eq x1 -> x0, other arithmetic: 9.69 us -> none  [shards(): adjacency = (rowsel[:, None, :] == row_ids).astype(jnp.bfloat16)]
    all_to_all x1, waiting for transfers between devices: 10.6 us -> 4.99 us  [shards(): lax.all_to_all(agg_one_cols, 'mp', split_axis=1, concat_axis=0, tiled=True)]
    convert_element_type x0 -> x1, other arithmetic: none -> 3.87 us  [shards(): adjacency = (rowsel[:, None, :] == row_ids).astype(jnp.bfloat16)]
    all_to_all x1, starting transfers between devices: 7.39 us -> 3.53 us  [shards(): lax.all_to_all(node_features, 'mp', split_axis=1, concat_axis=0, tiled=True)]
    ppermute x26, starting transfers between devices: 22.5 us -> 25.7 us  [swap(): return lax.ppermute(values, axis, [(j, j ^ mask) for j in range(size)])]
    dot_general x13, matrix products: 17.2 us -> 14.6 us  [contract(): lax.dot_general(left, right, (((left_dim,), (right_dim,)), ((), ())), pre...]
    ppermute x26, waiting for transfers between devices: 57.5 us -> 59.9 us  [swap(): return lax.ppermute(values, axis, [(j, j ^ mask) for j in range(size)])]
  transfers between devices with their start and end apart: 28 -> 28, of which waited for: 16 -> 19; matrix products, arithmetic and copies ran while one was open for 25% -> 18% of each run, Pallas kernels for 0% -> 0%
where the time goes in v9:
time: 139 us; the launch traced here: 138 us
  waiting for transfers between devices  64.9 us (47%)
  starting transfers between devices  33 us (24%)
  matrix products  14.6 us (11%)
  other arithmetic  14.1 us (10%)
  local copies, waits for them, and re-layouts  9.87 us (7%)
  between operations  1.4 us (1%)
    ppermute x26, waiting for transfers between devices, swap(): return lax.ppermute(values, axis, [(j, j ^ mask) for j in range(size)])  59.9 us
    ppermute x26, starting transfers between devices, swap(): return lax.ppermute(values, axis, [(j, j ^ mask) for j in range(size)])  25.7 us
    dot_general x13, matrix products, contract(): lax.dot_general(left, right, (((left_dim,), (right_dim,)), ((), ())), pre...  14.6 us
    all_to_all x1, waiting for transfers between devices, shards(): lax.all_to_all(agg_one_cols, 'mp', split_axis=1, concat_axis=0, tiled=True)  4.99 us
    convert_element_type x1, other arithmetic, shards(): adjacency = (rowsel[:, None, :] == row_ids).astype(jnp.bfloat16)  3.87 us
    all_to_all x1, starting transfers between devices, shards(): lax.all_to_all(agg_one_cols, 'mp', split_axis=1, concat_axis=0, tiled=True)  3.77 us
    all_to_all x1, starting transfers between devices, shards(): lax.all_to_all(node_features, 'mp', split_axis=1, concat_axis=0, tiled=True)  3.53 us
    add x10, other arithmetic, halving_scatter(): values = keep + got  3.11 us
  transfers between devices with their start and end apart: 28, of which 19 were waited for; matrix products, arithmetic and copies ran while one was open for 18% of the time, Pallas kernels for 0%

profile of v9, /device:TPU:0, one launch (start us, length us, event | category | flops | bytes accessed | tf_op | source)
XLA Modules:
  0.0 137.9 jit_solution(4562864577453369239)
XLA Ops:
  0.7 0.8 convert_divide_fusion
  1.6 1.4 fusion.21
  3.0 4.1 %collective-permute-start = (bf16[192,256]{1,0:T(8,128)(2,1)S(1)}, bf16[192,256]{1,0:T(8,128)(2,1)S(1)}, u32[]{:S(2)}, u32[]{:S(2)}) collective-permute-start(bf16[192,256]{1,0:T(8,128)(2,1)S(1)} %get-tuple-element.63), channel_id=1, source_target_pairs={{0,8},{1,9},{2,10},{3,11},{4,12},{5,13},{6,14},{7,15},{8,0},{9,1},... | collective-permute-start | bytes 294920 | tf_op jit(solution)/shard_map/ppermute | solution.py:29
  7.1 1.5 %collective-permute-start.1 = (bf16[192,256]{1,0:T(8,128)(2,1)S(1)}, bf16[192,256]{1,0:T(8,128)(2,1)S(1)}, u32[]{:S(2)}, u32[]{:S(2)}) collective-permute-start(bf16[192,256]{1,0:T(8,128)(2,1)S(1)} %get-tuple-element.62), channel_id=1, source_target_pairs={{0,2},{1,3},{2,0},{3,1},{4,6},{5,7},{6,4},{7,5},{8,10},{9,11},{10,... | collective-permute-start | bytes 294920 | tf_op jit(solution)/shard_map/ppermute | solution.py:29
  8.6 1.3 all_to_all.28
  9.8 0.8 copy.29
  10.6 3.5 %all-to-all-start = ((bf16[32,16,192]{2,0,1:T(8,128)(2,1)}), bf16[32,16,192]{2,0,1:T(8,128)(2,1)S(1)}, u32[]{:S(2)}, u32[]{:S(2)}) async-start(bf16[32,16,192]{2,0,1:T(8,128)(2,1)} %copy.29), calls=%async_computation | async-start | bytes 524288 | tf_op jit(solution)/shard_map/all_to_all | solution.py:129
  14.3 0.8 select_reduce_fusion
  15.2 3.9 %fusion = bf16[3072,3072]{1,0:T(8,128)(2,1)S(1)} fusion(s32[3072]{0:T(1024)S(1)} %eq.57, s32[16,3072]{1,0:T(8,128)S(1)} %select_reduce_fusion), kind=kLoop, calls=%fused_computation.1 | loop fusion | flops 18874368 | bytes 19083264 | tf_op jit(solution)/shard_map/layer_one_mean/convert_element_type | solution.py:115
  19.1 2.8 %collective-permute-start.3 = (bf16[2,192,256]{2,1,0:T(8,128)(2,1)S(1)}, bf16[2,192,256]{2,1,0:T(8,128)(2,1)S(1)}, u32[]{:S(2)}, u32[]{:S(2)}) collective-permute-start(bf16[2,192,256]{2,1,0:T(8,128)(2,1)S(1)} %get-tuple-element.12), channel_id=1, source_target_pairs={{0,8},{1,9},{2,10},{3,11},{4,12},{5,13},{6,14},{7,15},{8,0},{9,1},... | collective-permute-start | bytes 589832 | tf_op jit(solution)/shard_map/layer_one_mean/ppermute | solution.py:29
  22.0 1.5 %collective-permute-start.2 = (bf16[2,192,256]{2,1,0:T(8,128)(2,1)S(1)}, bf16[2,192,256]{2,1,0:T(8,128)(2,1)S(1)}, u32[]{:S(2)}, u32[]{:S(2)}) collective-permute-start(bf16[2,192,256]{2,1,0:T(8,128)(2,1)S(1)} %get-tuple-element.11), channel_id=1, source_target_pairs={{0,4},{1,5},{2,6},{3,7},{4,0},{5,1},{6,2},{7,3},{8,12},{9,13},{10,... | collective-permute-start | bytes 589832 | tf_op jit(solution)/shard_map/layer_one_mean/ppermute | solution.py:29
  23.5 3.4 %fusion.2 = bf16[32,3072]{1,0:T(8,128)(2,1)S(1)} fusion(bf16[32,3072]{1,0:T(8,128)(2,1)S(1)} %copy-done.3, bf16[3072,3072]{1,0:T(8,128)(2,1)S(1)} %fusion, f32[3072]{0:T(1024)S(1)} %convert_divide_fusion), kind=kOutput, calls=%fused_computation.5 | convolution fusion | flops 604176384 | bytes 19279872 | tf_op jit(solution)/shard_map/layer_one_mean/dot_general | solution.py:22
  26.8 5.5 %collective-permute-done.3 = bf16[2,192,256]{2,1,0:T(8,128)(2,1)S(1)} collective-permute-done((bf16[2,192,256]{2,1,0:T(8,128)(2,1)S(1)}, bf16[2,192,256]{2,1,0:T(8,128)(2,1)S(1)}, u32[]{:S(2)}, u32[]{:S(2)}) %collective-permute-start.3) | collective-permute-done | bytes 196640 | tf_op jit(solution)/shard_map/layer_one_mean/ppermute | solution.py:29
  32.5 0.9 collective-permute-start.5
  33.4 1.5 %collective-permute-start.4 = (bf16[2,2,192,256]{3,2,0,1:T(8,128)(2,1)S(1)}, bf16[2,2,192,256]{3,2,0,1:T(8,128)(2,1)S(1)}, u32[]{:S(2)}, u32[]{:S(2)}) collective-permute-start(bf16[2,2,192,256]{3,2,0,1:T(8,128)(2,1)S(1)} %pad_maximum_fusion.9), channel_id=1, source_target_pairs={{0,2},{1,3},{2,0},{3,1},{4,6},{5,7},{6,4},{7,5},{8,10},{9,11},{10,... | collective-permute-start | bytes 1179656 | tf_op jit(solution)/shard_map/ppermute | solution.py:29
  35.2 0.8 copy.30
  35.9 3.8 %all-to-all-start.1 = ((bf16[32,16,192]{2,0,1:T(8,128)(2,1)}), bf16[32,16,192]{2,0,1:T(8,128)(2,1)S(1)}, u32[]{:S(2)}, u32[]{:S(2)}) async-start(bf16[32,16,192]{2,0,1:T(8,128)(2,1)} %copy.30), calls=%async_computation.1 | async-start | bytes 524288 | tf_op jit(solution)/shard_map/all_to_all | solution.py:130
  39.7 1.3 fusion.24
  41.0 2.4 %collective-permute-done.5 = bf16[2,2,192,256]{3,2,1,0:T(8,128)(2,1)} collective-permute-done((bf16[2,2,192,256]{3,2,1,0:T(8,128)(2,1)S(1)}, bf16[2,2,192,256]{3,2,1,0:T(8,128)(2,1)}, u32[]{:S(2)}, u32[]{:S(2)}) %collective-permute-start.5) | collective-permute-done | bytes 393248 | tf_op jit(solution)/shard_map/ppermute | solution.py:29
  43.5 1.1 select_bitcast_fusion.13
  44.8 5.0 %all-to-all-done.1 = bf16[32,16,192]{2,0,1:T(8,128)(2,1)S(1)} async-done(((bf16[32,16,192]{2,0,1:T(8,128)(2,1)}), bf16[32,16,192]{2,0,1:T(8,128)(2,1)S(1)}, u32[]{:S(2)}, u32[]{:S(2)}) %all-to-all-start.1) | async-done | bytes 196640 | tf_op jit(solution)/shard_map/all_to_all | solution.py:130
  49.7 2.1 %multiply_convert_fusion = (bf16[192,512]{1,0:T(8,128)(2,1)S(1)}, f32[192,512]{1,0:T(8,128)}) fusion(f32[192,512]{1,0:T(8,128)S(1)} %fusion.24, bf16[512,192]{1,0:T(8,128)(2,1)S(1)} %bitcast.154, bf16[1024,512]{1,0:T(8,128)(2,1)} %param.8), kind=kOutput, calls=%fused_computation.71 | convolution fusion | flops 101253120 | bytes 1703936 | tf_op jit(solution)/shard_map/dot_general | solution.py:22
  51.9 1.1 collective-permute-start.6
  53.1 3.4 %collective-permute-done.10 = bf16[192,256]{1,0:T(8,128)(2,1)S(1)} collective-permute-done((bf16[192,256]{1,0:T(8,128)(2,1)S(1)}, bf16[192,256]{1,0:T(8,128)(2,1)S(1)}, u32[]{:S(2)}, u32[]{:S(2)}) %collective-permute-start.10) | collective-permute-done | bytes 98336 | tf_op jit(solution)/shard_map/ppermute | solution.py:29
  56.5 3.3 %collective-permute-done.6 = bf16[192,256]{1,0:T(8,128)(2,1)S(1)} collective-permute-done((bf16[192,256]{1,0:T(8,128)(2,1)S(1)}, bf16[192,256]{1,0:T(8,128)(2,1)S(1)}, u32[]{:S(2)}, u32[]{:S(2)}) %collective-permute-start.6) | collective-permute-done | bytes 98336 | tf_op jit(solution)/shard_map/ppermute | solution.py:29
  60.1 1.4 %bitcast_compare_fusion.1 = pred[3072,192]{1,0:T(32,128)(4,1)} fusion(s32[3072]{0:T(1024)S(1)} %eq.57, s32[16,192]{1,0:T(8,128)S(1)} %constant_dynamic-slice_fusion.3), kind=kLoop, calls=%fused_computation.14 | loop fusion | flops 589824 | bytes 614400 | tf_op jit(solution)/shard_map/neighbor_tables/eq | solution.py:140
  61.5 2.1 %collective-permute-start.11 = (bf16[2,192,256]{2,1,0:T(8,128)(2,1)S(1)}, bf16[2,192,256]{2,1,0:T(8,128)(2,1)S(1)}, u32[]{:S(2)}, u32[]{:S(2)}) collective-permute-start(bf16[2,192,256]{2,1,0:T(8,128)(2,1)S(1)} %pad_maximum_fusion.16), channel_id=1, source_target_pairs={{0,8},{1,9},{2,10},{3,11},{4,12},{5,13},{6,14},{7,15},{8,0},{9,1},... | collective-permute-start | bytes 589832 | tf_op jit(solution)/shard_map/ppermute | solution.py:29
  63.6 4.4 %collective-permute-done.7 = bf16[2,192,256]{2,1,0:T(8,128)(2,1)S(1)} collective-permute-done((bf16[2,192,256]{2,1,0:T(8,128)(2,1)S(1)}, bf16[2,192,256]{2,1,0:T(8,128)(2,1)S(1)}, u32[]{:S(2)}, u32[]{:S(2)}) %collective-permute-start.7) | collective-permute-done | bytes 196640 | tf_op jit(solution)/shard_map/ppermute | solution.py:29
  68.1 1.4 collective-permute-start.8
  69.4 4.6 %collective-permute-done.11 = bf16[2,192,256]{2,1,0:T(8,128)(2,1)S(1)} collective-permute-done((bf16[2,192,256]{2,1,0:T(8,128)(2,1)S(1)}, bf16[2,192,256]{2,1,0:T(8,128)(2,1)S(1)}, u32[]{:S(2)}, u32[]{:S(2)}) %collective-permute-start.11) | collective-permute-done | bytes 196640 | tf_op jit(solution)/shard_map/ppermute | solution.py:29
  74.2 0.3 fusion.37
  74.6 1.9 %collective-permute-done.8 = bf16[2,2,192,256]{3,2,0,1:T(8,128)(2,1)S(1)} collective-permute-done((bf16[2,2,192,256]{3,2,0,1:T(8,128)(2,1)S(1)}, bf16[2,2,192,256]{3,2,0,1:T(8,128)(2,1)S(1)}, u32[]{:S(2)}, u32[]{:S(2)}) %collective-permute-start.8) | collective-permute-done | bytes 393248 | tf_op jit(solution)/shard_map/ppermute | solution.py:29
  76.7 8.2 %collective-permute-done.12 = bf16[2,2,192,256]{3,2,1,0:T(8,128)(2,1)S(1)} collective-permute-done((bf16[2,2,192,256]{3,2,1,0:T(8,128)(2,1)S(1)}, bf16[2,2,192,256]{3,2,1,0:T(8,128)(2,1)S(1)}, u32[]{:S(2)}, u32[]{:S(2)}) %collective-permute-start.12) | collective-permute-done | bytes 393248 | tf_op jit(solution)/shard_map/ppermute | solution.py:29
  86.0 1.6 %fusion.7 = f32[192,512]{1,0:T(8,128)S(1)} fusion(bf16[3072,256]{1,0:T(8,128)(2,1)S(1)} %bitcast.153, bf16[3072,256]{1,0:T(8,128)(2,1)S(1)} %bitcast.151, s32[3072]{0:T(1024)S(1)} %bitcast.156), kind=kOutput, calls=%fused_computation.10 | convolution fusion | flops 610861056 | bytes 3551232 | tf_op jit(solution)/shard_map/dot_general | solution.py:22
  87.6 0.4 fusion.20
  89.5 1.0 copy-done.6
  90.4 1.1 fusion.17
  91.6 0.7 copy-done.7
  92.2 0.3 fusion.38
  92.6 0.4 pad_maximum_fusion
  93.0 0.3 fusion.33
  93.4 1.3 copy-done.1
  94.7 1.1 dynamic-slice_bitcast_fusion
  95.8 0.5 collective-permute-start.16
  96.4 1.0 copy.43
  97.5 1.3 fusion.27
  98.9 1.4 bitcast_add_fusion.1
  100.3 1.6 %collective-permute-start.17 = (f32[2,2,2,64,256]{4,3,2,1,0:T(8,128)S(1)}, f32[2,2,2,64,256]{4,3,2,1,0:T(8,128)S(1)}, u32[]{:S(2)}, u32[]{:S(2)}) collective-permute-start(f32[2,2,2,64,256]{4,3,2,1,0:T(8,128)S(1)} %dynamic-slice_bitcast_fusion.2), channel_id=1, source_target_pairs={{0,16},{16,0},{1,17},{17,1},{2,18},{18,2},{3,19},{19,3},{4,20},{20... | collective-permute-start | bytes 1572872 | tf_op jit(solution)/shard_map/weight_grad_sum/ppermute | solution.py:29
  101.9 1.5 %bitcast_add_fusion = f32[2,2,2,2,64,256]{5,4,2,1,0,3:T(8,128)S(1)} fusion(f32[2,2,2,2,64,256]{5,4,2,1,0,3:T(8,128)} %collective-permute-done.21, f32[2,2,2,2,1,64,256]{6,5,4,3,2,1,0:T(8,128)S(1)} %get-tuple-element.22), kind=kLoop, calls=%fused_computation.35 | loop fusion | flops 262144 | bytes 3145728 | tf_op jit(solution)/shard_map/weight_grad_sum/add | solution.py:45
  103.4 1.4 %collective-permute-start.22 = (f32[2,2,2,64,256]{4,3,2,1,0:T(8,128)S(1)}, f32[2,2,2,64,256]{4,3,2,1,0:T(8,128)S(1)}, u32[]{:S(2)}, u32[]{:S(2)}) collective-permute-start(f32[2,2,2,64,256]{4,3,2,1,0:T(8,128)S(1)} %dynamic-slice_bitcast_fusion.1), channel_id=1, source_target_pairs={{0,2},{1,3},{2,0},{3,1},{4,6},{5,7},{6,4},{7,5},{8,10},{9,11},{10,... | collective-permute-start | bytes 1572872 | tf_op jit(solution)/shard_map/weight_grad_sum/ppermute | solution.py:29
  104.9 1.0 fusion.22
  105.8 8.9 %collective-permute-done.17 = f32[2,2,2,64,256]{4,3,2,1,0:T(8,128)S(1)} collective-permute-done((f32[2,2,2,64,256]{4,3,2,1,0:T(8,128)S(1)}, f32[2,2,2,64,256]{4,3,2,1,0:T(8,128)S(1)}, u32[]{:S(2)}, u32[]{:S(2)}) %collective-permute-start.17) | collective-permute-done | bytes 524320 | tf_op jit(solution)/shard_map/weight_grad_sum/ppermute | solution.py:29
  114.8 1.4 %collective-permute-start.18 = (f32[2,2,64,256]{3,2,1,0:T(8,128)S(1)}, f32[2,2,64,256]{3,2,1,0:T(8,128)S(1)}, u32[]{:S(2)}, u32[]{:S(2)}) collective-permute-start(f32[2,2,64,256]{3,2,1,0:T(8,128)S(1)} %dynamic-slice_bitcast_fusion.4), channel_id=1, source_target_pairs={{0,2},{1,3},{2,0},{3,1},{4,6},{5,7},{6,4},{7,5},{8,10},{9,11},{10,... | collective-permute-start | bytes 786440 | tf_op jit(solution)/shard_map/weight_grad_sum/ppermute | solution.py:29
  116.2 1.6 %collective-permute-done.22 = f32[2,2,2,64,256]{4,3,2,1,0:T(8,128)S(1)} collective-permute-done((f32[2,2,2,64,256]{4,3,2,1,0:T(8,128)S(1)}, f32[2,2,2,64,256]{4,3,2,1,0:T(8,128)S(1)}, u32[]{:S(2)}, u32[]{:S(2)}) %collective-permute-start.22) | collective-permute-done | bytes 524320 | tf_op jit(solution)/shard_map/weight_grad_sum/ppermute | solution.py:29
  118.2 4.9 %collective-permute-done.18 = f32[2,2,64,256]{3,2,1,0:T(8,128)S(1)} collective-permute-done((f32[2,2,64,256]{3,2,1,0:T(8,128)S(1)}, f32[2,2,64,256]{3,2,1,0:T(8,128)S(1)}, u32[]{:S(2)}, u32[]{:S(2)}) %collective-permute-start.18) | collective-permute-done | bytes 262176 | tf_op jit(solution)/shard_map/weight_grad_sum/ppermute | solution.py:29
  123.2 0.8 collective-permute-start.19
  123.9 1.3 collective-permute-done.23
  125.3 0.5 collective-permute-start.24
  125.8 5.5 %collective-permute-done.19 = f32[2,64,256]{2,1,0:T(8,128)S(1)} collective-permute-done((f32[2,64,256]{2,1,0:T(8,128)S(1)}, f32[2,64,256]{2,1,0:T(8,128)S(1)}, u32[]{:S(2)}, u32[]{:S(2)}) %collective-permute-start.19) | collective-permute-done | bytes 131104 | tf_op jit(solution)/shard_map/weight_grad_sum/ppermute | solution.py:29
  131.4 0.6 collective-permute-done.24
  132.0 1.9 %collective-permute-start.25 = (f32[64,256]{1,0:T(8,128)S(1)}, f32[64,256]{1,0:T(8,128)S(1)}, u32[]{:S(2)}, u32[]{:S(2)}) collective-permute-start(f32[64,256]{1,0:T(8,128)S(1)} %dynamic-slice_bitcast_fusion.7), channel_id=1, source_target_pairs={{0,8},{1,9},{2,10},{3,11},{4,12},{5,13},{6,14},{7,15},{8,0},{9,1},... | collective-permute-start | bytes 196616 | tf_op jit(solution)/shard_map/weight_grad_sum/ppermute | solution.py:29
  133.9 2.0 %collective-permute-done.20 = f32[64,256]{1,0:T(8,128)S(1)} collective-permute-done((f32[64,256]{1,0:T(8,128)S(1)}, f32[64,256]{1,0:T(8,128)S(1)}, u32[]{:S(2)}, u32[]{:S(2)}) %collective-permute-start.20) | collective-permute-done | bytes 65568 | tf_op jit(solution)/shard_map/weight_grad_sum/ppermute | solution.py:29
  135.9 1.3 collective-permute-done.25
  137.2 0.7 pad_maximum_fusion.17
  (104 shorter events, 5.3 us)
Async XLA Ops:
  0.6 0.9 copy-start
  0.6 13.5 %copy-start.11 = (s32[3072]{0:T(1024)S(1)}, s32[3072]{0:T(1024)}, u32[]{:S(2)}) copy-start(s32[3072]{0:T(1024)} %param.12) | copy-start | bytes 36868
  0.7 13.7 %copy-start.10 = (s32[3072,8]{0,1:T(8,128)S(1)}, s32[3072,8]{0,1:T(8,128)}, u32[]{:S(2)}) copy-start(s32[3072,8]{0,1:T(8,128)} %param.10) | copy-start | bytes 294916
  0.7 13.7 %copy-start.9 = (s32[3072,8]{0,1:T(8,128)S(1)}, s32[3072,8]{0,1:T(8,128)}, u32[]{:S(2)}) copy-start(s32[3072,8]{0,1:T(8,128)} %param.11) | copy-start | bytes 294916
  3.0 16.1 %collective-permute-start = (bf16[192,256]{1,0:T(8,128)(2,1)S(1)}, bf16[192,256]{1,0:T(8,128)(2,1)S(1)}, u32[]{:S(2)}, u32[]{:S(2)}) collective-permute-start(bf16[192,256]{1,0:T(8,128)(2,1)S(1)} %get-tuple-element.63), channel_id=1, source_target_pairs={{0,8},{1,9},{2,10},{3,11},{4,12},{5,13},{6,14},{7,15},{8,0},{9,1},... | collective-permute-start | bytes 294920 | tf_op jit(solution)/shard_map/ppermute | solution.py:29
  7.1 12.0 %collective-permute-start.1 = (bf16[192,256]{1,0:T(8,128)(2,1)S(1)}, bf16[192,256]{1,0:T(8,128)(2,1)S(1)}, u32[]{:S(2)}, u32[]{:S(2)}) collective-permute-start(bf16[192,256]{1,0:T(8,128)(2,1)S(1)} %get-tuple-element.62), channel_id=1, source_target_pairs={{0,2},{1,3},{2,0},{3,1},{4,6},{5,7},{6,4},{7,5},{8,10},{9,11},{10,... | collective-permute-start | bytes 294920 | tf_op jit(solution)/shard_map/ppermute | solution.py:29
  10.6 25.3 %all-to-all-start = ((bf16[32,16,192]{2,0,1:T(8,128)(2,1)}), bf16[32,16,192]{2,0,1:T(8,128)(2,1)S(1)}, u32[]{:S(2)}, u32[]{:S(2)}) async-start(bf16[32,16,192]{2,0,1:T(8,128)(2,1)} %copy.29), calls=%async_computation | async-start | bytes 524288 | tf_op jit(solution)/shard_map/all_to_all | solution.py:129
  15.2 8.3 %copy-start.3 = (bf16[32,3072]{1,0:T(8,128)(2,1)S(1)}, bf16[32,3072]{1,0:T(8,128)(2,1)}, u32[]{:S(2)}) copy-start(bf16[32,3072]{1,0:T(8,128)(2,1)} %param.7) | copy-start | bytes 589828
  19.1 13.1 %collective-permute-start.3 = (bf16[2,192,256]{2,1,0:T(8,128)(2,1)S(1)}, bf16[2,192,256]{2,1,0:T(8,128)(2,1)S(1)}, u32[]{:S(2)}, u32[]{:S(2)}) collective-permute-start(bf16[2,192,256]{2,1,0:T(8,128)(2,1)S(1)} %get-tuple-element.12), channel_id=1, source_target_pairs={{0,8},{1,9},{2,10},{3,11},{4,12},{5,13},{6,14},{7,15},{8,0},{9,1},... | collective-permute-start | bytes 589832 | tf_op jit(solution)/shard_map/layer_one_mean/ppermute | solution.py:29
  22.0 10.4 %collective-permute-start.2 = (bf16[2,192,256]{2,1,0:T(8,128)(2,1)S(1)}, bf16[2,192,256]{2,1,0:T(8,128)(2,1)S(1)}, u32[]{:S(2)}, u32[]{:S(2)}) collective-permute-start(bf16[2,192,256]{2,1,0:T(8,128)(2,1)S(1)} %get-tuple-element.11), channel_id=1, source_target_pairs={{0,4},{1,5},{2,6},{3,7},{4,0},{5,1},{6,2},{7,3},{8,12},{9,13},{10,... | collective-permute-start | bytes 589832 | tf_op jit(solution)/shard_map/layer_one_mean/ppermute | solution.py:29
  32.5 10.9 %collective-permute-start.5 = (bf16[2,2,192,256]{3,2,1,0:T(8,128)(2,1)S(1)}, bf16[2,2,192,256]{3,2,1,0:T(8,128)(2,1)}, u32[]{:S(2)}, u32[]{:S(2)}) collective-permute-start(bf16[2,2,192,256]{3,2,1,0:T(8,128)(2,1)S(1)} %pad_maximum_fusion.10), channel_id=1, source_target_pairs={{0,4},{1,5},{2,6},{3,7},{4,0},{5,1},{6,2},{7,3},{8,12},{9,13},{10,... | collective-permute-start | bytes 1179656 | tf_op jit(solution)/shard_map/ppermute | solution.py:29
  33.4 11.2 %collective-permute-start.4 = (bf16[2,2,192,256]{3,2,0,1:T(8,128)(2,1)S(1)}, bf16[2,2,192,256]{3,2,0,1:T(8,128)(2,1)S(1)}, u32[]{:S(2)}, u32[]{:S(2)}) collective-permute-start(bf16[2,2,192,256]{3,2,0,1:T(8,128)(2,1)S(1)} %pad_maximum_fusion.9), channel_id=1, source_target_pairs={{0,2},{1,3},{2,0},{3,1},{4,6},{5,7},{6,4},{7,5},{8,10},{9,11},{10,... | collective-permute-start | bytes 1179656 | tf_op jit(solution)/shard_map/ppermute | solution.py:29
  35.9 13.8 %all-to-all-start.1 = ((bf16[32,16,192]{2,0,1:T(8,128)(2,1)}), bf16[32,16,192]{2,0,1:T(8,128)(2,1)S(1)}, u32[]{:S(2)}, u32[]{:S(2)}) async-start(bf16[32,16,192]{2,0,1:T(8,128)(2,1)} %copy.30), calls=%async_computation.1 | async-start | bytes 524288 | tf_op jit(solution)/shard_map/all_to_all | solution.py:130
  51.8 4.7 %collective-permute-start.10 = (bf16[192,256]{1,0:T(8,128)(2,1)S(1)}, bf16[192,256]{1,0:T(8,128)(2,1)S(1)}, u32[]{:S(2)}, u32[]{:S(2)}) collective-permute-start(bf16[192,256]{1,0:T(8,128)(2,1)S(1)} %get-tuple-element.59), channel_id=1, source_target_pairs={{0,2},{1,3},{2,0},{3,1},{4,6},{5,7},{6,4},{7,5},{8,10},{9,11},{10,... | collective-permute-start | bytes 294920 | tf_op jit(solution)/shard_map/ppermute | solution.py:29
  51.9 7.9 %collective-permute-start.6 = (bf16[192,256]{1,0:T(8,128)(2,1)S(1)}, bf16[192,256]{1,0:T(8,128)(2,1)S(1)}, u32[]{:S(2)}, u32[]{:S(2)}) collective-permute-start(bf16[192,256]{1,0:T(8,128)(2,1)S(1)} %get-tuple-element.58), channel_id=1, source_target_pairs={{0,8},{1,9},{2,10},{3,11},{4,12},{5,13},{6,14},{7,15},{8,0},{9,1},... | collective-permute-start | bytes 294920 | tf_op jit(solution)/shard_map/ppermute | solution.py:29
  59.9 8.1 %collective-permute-start.7 = (bf16[2,192,256]{2,1,0:T(8,128)(2,1)S(1)}, bf16[2,192,256]{2,1,0:T(8,128)(2,1)S(1)}, u32[]{:S(2)}, u32[]{:S(2)}) collective-permute-start(bf16[2,192,256]{2,1,0:T(8,128)(2,1)S(1)} %pad_maximum_fusion.15), channel_id=1, source_target_pairs={{0,4},{1,5},{2,6},{3,7},{4,0},{5,1},{6,2},{7,3},{8,12},{9,13},{10,... | collective-permute-start | bytes 589832 | tf_op jit(solution)/shard_map/ppermute | solution.py:29
  61.5 23.7 %collective-permute-start.14 = (bf16[2,2,2,192,256]{4,3,0,1,2:T(8,128)(2,1)S(1)}, bf16[2,2,2,192,256]{4,3,0,1,2:T(8,128)(2,1)S(1)}, u32[]{:S(2)}, u32[]{:S(2)}) collective-permute-start(bf16[2,2,2,192,256]{4,3,0,1,2:T(8,128)(2,1)S(1)} %pad_maximum_fusion.5), channel_id=1, source_target_pairs={{0,1},{1,0},{2,3},{3,2},{4,5},{5,4},{6,7},{7,6},{8,9},{9,8},{10,11... | collective-permute-start | bytes 2359304 | tf_op jit(solution)/shard_map/ppermute | solution.py:29
  61.5 12.5 %collective-permute-start.11 = (bf16[2,192,256]{2,1,0:T(8,128)(2,1)S(1)}, bf16[2,192,256]{2,1,0:T(8,128)(2,1)S(1)}, u32[]{:S(2)}, u32[]{:S(2)}) collective-permute-start(bf16[2,192,256]{2,1,0:T(8,128)(2,1)S(1)} %pad_maximum_fusion.16), channel_id=1, source_target_pairs={{0,8},{1,9},{2,10},{3,11},{4,12},{5,13},{6,14},{7,15},{8,0},{9,1},... | collective-permute-start | bytes 589832 | tf_op jit(solution)/shard_map/ppermute | solution.py:29
  68.1 8.4 %collective-permute-start.8 = (bf16[2,2,192,256]{3,2,0,1:T(8,128)(2,1)S(1)}, bf16[2,2,192,256]{3,2,0,1:T(8,128)(2,1)S(1)}, u32[]{:S(2)}, u32[]{:S(2)}) collective-permute-start(bf16[2,2,192,256]{3,2,0,1:T(8,128)(2,1)S(1)} %pad_maximum_fusion.11), channel_id=1, source_target_pairs={{0,2},{1,3},{2,0},{3,1},{4,6},{5,7},{6,4},{7,5},{8,10},{9,11},{10,... | collective-permute-start | bytes 1179656 | tf_op jit(solution)/shard_map/ppermute | solution.py:29
  74.1 10.8 %collective-permute-start.12 = (bf16[2,2,192,256]{3,2,1,0:T(8,128)(2,1)S(1)}, bf16[2,2,192,256]{3,2,1,0:T(8,128)(2,1)S(1)}, u32[]{:S(2)}, u32[]{:S(2)}) collective-permute-start(bf16[2,2,192,256]{3,2,1,0:T(8,128)(2,1)S(1)} %pad_maximum_fusion.12), channel_id=1, source_target_pairs={{0,4},{1,5},{2,6},{3,7},{4,0},{5,1},{6,2},{7,3},{8,12},{9,13},{10,... | collective-permute-start | bytes 1179656 | tf_op jit(solution)/shard_map/ppermute | solution.py:29
  74.5 11.1 %collective-permute-start.15 = (bf16[2,2,2,192,256]{4,3,2,0,1:T(8,128)(2,1)S(1)}, bf16[2,2,2,192,256]{4,3,2,0,1:T(8,128)(2,1)S(1)}, u32[]{:S(2)}, u32[]{:S(2)}) collective-permute-start(bf16[2,2,2,192,256]{4,3,2,0,1:T(8,128)(2,1)S(1)} %pad_maximum_fusion.6), channel_id=1, source_target_pairs={{0,1},{1,0},{2,3},{3,2},{4,5},{5,4},{6,7},{7,6},{8,9},{9,8},{10,11... | collective-permute-start | bytes 2359304 | tf_op jit(solution)/shard_map/ppermute | solution.py:29
  76.6 12.0 %collective-permute-start.9 = (bf16[2,2,2,192,256]{4,3,0,1,2:T(8,128)(2,1)S(1)}, bf16[2,2,2,192,256]{4,3,0,1,2:T(8,128)(2,1)S(1)}, u32[]{:S(2)}, u32[]{:S(2)}) collective-permute-start(bf16[2,2,2,192,256]{4,3,0,1,2:T(8,128)(2,1)S(1)} %pad_maximum_fusion.7), channel_id=1, source_target_pairs={{0,1},{1,0},{2,3},{3,2},{4,5},{5,4},{6,7},{7,6},{8,9},{9,8},{10,11... | collective-permute-start | bytes 2359304 | tf_op jit(solution)/shard_map/ppermute | solution.py:29
  85.1 3.9 %collective-permute-start.13 = (bf16[2,2,2,192,256]{4,3,2,0,1:T(8,128)(2,1)S(1)}, bf16[2,2,2,192,256]{4,3,2,0,1:T(8,128)(2,1)S(1)}, u32[]{:S(2)}, u32[]{:S(2)}) collective-permute-start(bf16[2,2,2,192,256]{4,3,2,0,1:T(8,128)(2,1)S(1)} %pad_maximum_fusion.8), channel_id=1, source_target_pairs={{0,1},{1,0},{2,3},{3,2},{4,5},{5,4},{6,7},{7,6},{8,9},{9,8},{10,11... | collective-permute-start | bytes 2359304 | tf_op jit(solution)/shard_map/ppermute | solution.py:29
  86.0 1.6 %copy-start.4 = (bf16[1024,512]{1,0:T(8,128)(2,1)S(1)}, bf16[1024,512]{1,0:T(8,128)(2,1)}, u32[]{:S(2)}) copy-start(bf16[1024,512]{1,0:T(8,128)(2,1)} %param.9) | copy-start | bytes 3145732
  86.0 1.6 %copy-start.12 = (f32[192,512]{1,0:T(8,128)S(1)}, f32[192,512]{1,0:T(8,128)}, u32[]{:S(2)}) copy-start(f32[192,512]{1,0:T(8,128)} %get-tuple-element.65) | copy-start | bytes 1179652
  89.3 1.1 copy-start.6
  91.5 0.7 copy-start.7
  93.3 1.4 copy-start.1
  95.8 3.1 %collective-permute-start.16 = (f32[2,2,2,2,64,256]{5,4,3,2,1,0:T(8,128)}, f32[2,2,2,2,64,256]{5,4,3,2,1,0:T(8,128)}, u32[]{:S(2)}, u32[]{:S(2)}) collective-permute-start(f32[2,2,2,2,64,256]{5,4,3,2,1,0:T(8,128)} %dynamic-slice_bitcast_fusion), channel_id=1, source_target_pairs={{0,1},{1,0},{2,3},{3,2},{4,5},{5,4},{6,7},{7,6},{8,9},{9,8},{10,11... | collective-permute-start | bytes 3145736 | tf_op jit(solution)/shard_map/weight_grad_sum/ppermute | solution.py:29
  96.4 2.5 %copy-start.2 = (f32[2048,256]{1,0:T(8,128)S(1)}, f32[2048,256]{1,0:T(8,128)}, u32[]{:S(2)}) copy-start(f32[2048,256]{1,0:T(8,128)} %copy-done.1) | copy-start | bytes 6291460
  97.5 4.4 %collective-permute-start.21 = (f32[2,2,2,2,64,256]{5,4,2,1,0,3:T(8,128)}, f32[2,2,2,2,64,256]{5,4,2,1,0,3:T(8,128)}, u32[]{:S(2)}, u32[]{:S(2)}) collective-permute-start(f32[2,2,2,2,64,256]{5,4,2,1,0,3:T(8,128)} %bitcast.144), channel_id=1, source_target_pairs={{0,1},{1,0},{2,3},{3,2},{4,5},{5,4},{6,7},{7,6},{8,9},{9,8},{10,11... | collective-permute-start | bytes 3145736 | tf_op jit(solution)/shard_map/weight_grad_sum/ppermute | solution.py:29
  100.3 14.3 %collective-permute-start.17 = (f32[2,2,2,64,256]{4,3,2,1,0:T(8,128)S(1)}, f32[2,2,2,64,256]{4,3,2,1,0:T(8,128)S(1)}, u32[]{:S(2)}, u32[]{:S(2)}) collective-permute-start(f32[2,2,2,64,256]{4,3,2,1,0:T(8,128)S(1)} %dynamic-slice_bitcast_fusion.2), channel_id=1, source_target_pairs={{0,16},{16,0},{1,17},{17,1},{2,18},{18,2},{3,19},{19,3},{4,20},{20... | collective-permute-start | bytes 1572872 | tf_op jit(solution)/shard_map/weight_grad_sum/ppermute | solution.py:29
  101.9 3.0 %copy-start.5 = (bf16[1024,512]{1,0:T(8,128)(2,1)S(1)}, bf16[1024,512]{1,0:T(8,128)(2,1)}, u32[]{:S(2)}) copy-start(bf16[1024,512]{1,0:T(8,128)(2,1)} %param.9) | copy-start | bytes 3145732
  101.9 3.0 %copy-start.8 = (bf16[192,512]{1,0:T(8,128)(2,1)S(1)}, bf16[192,512]{1,0:T(8,128)(2,1)}, u32[]{:S(2)}) copy-start(bf16[192,512]{1,0:T(8,128)(2,1)} %copy-done.7) | copy-start | bytes 589828
  103.4 14.4 %collective-permute-start.22 = (f32[2,2,2,64,256]{4,3,2,1,0:T(8,128)S(1)}, f32[2,2,2,64,256]{4,3,2,1,0:T(8,128)S(1)}, u32[]{:S(2)}, u32[]{:S(2)}) collective-permute-start(f32[2,2,2,64,256]{4,3,2,1,0:T(8,128)S(1)} %dynamic-slice_bitcast_fusion.1), channel_id=1, source_target_pairs={{0,2},{1,3},{2,0},{3,1},{4,6},{5,7},{6,4},{7,5},{8,10},{9,11},{10,... | collective-permute-start | bytes 1572872 | tf_op jit(solution)/shard_map/weight_grad_sum/ppermute | solution.py:29
  114.8 8.3 %collective-permute-start.18 = (f32[2,2,64,256]{3,2,1,0:T(8,128)S(1)}, f32[2,2,64,256]{3,2,1,0:T(8,128)S(1)}, u32[]{:S(2)}, u32[]{:S(2)}) collective-permute-start(f32[2,2,64,256]{3,2,1,0:T(8,128)S(1)} %dynamic-slice_bitcast_fusion.4), channel_id=1, source_target_pairs={{0,2},{1,3},{2,0},{3,1},{4,6},{5,7},{6,4},{7,5},{8,10},{9,11},{10,... | collective-permute-start | bytes 786440 | tf_op jit(solution)/shard_map/weight_grad_sum/ppermute | solution.py:29
  117.9 7.3 %collective-permute-start.23 = (f32[2,2,64,256]{3,2,1,0:T(8,128)S(1)}, f32[2,2,64,256]{3,2,1,0:T(8,128)S(1)}, u32[]{:S(2)}, u32[]{:S(2)}) collective-permute-start(f32[2,2,64,256]{3,2,1,0:T(8,128)S(1)} %dynamic-slice_bitcast_fusion.3), channel_id=1, source_target_pairs={{0,16},{16,0},{1,17},{17,1},{2,18},{18,2},{3,19},{19,3},{4,20},{20... | collective-permute-start | bytes 786440 | tf_op jit(solution)/shard_map/weight_grad_sum/ppermute | solution.py:29
  123.2 8.1 %collective-permute-start.19 = (f32[2,64,256]{2,1,0:T(8,128)S(1)}, f32[2,64,256]{2,1,0:T(8,128)S(1)}, u32[]{:S(2)}, u32[]{:S(2)}) collective-permute-start(f32[2,64,256]{2,1,0:T(8,128)S(1)} %dynamic-slice_bitcast_fusion.6), channel_id=1, source_target_pairs={{0,8},{1,9},{2,10},{3,11},{4,12},{5,13},{6,14},{7,15},{8,0},{9,1},... | collective-permute-start | bytes 393224 | tf_op jit(solution)/shard_map/weight_grad_sum/ppermute | solution.py:29
  125.3 6.7 %collective-permute-start.24 = (f32[2,64,256]{2,1,0:T(8,128)S(1)}, f32[2,64,256]{2,1,0:T(8,128)S(1)}, u32[]{:S(2)}, u32[]{:S(2)}) collective-permute-start(f32[2,64,256]{2,1,0:T(8,128)S(1)} %dynamic-slice_bitcast_fusion.5), channel_id=1, source_target_pairs={{0,4},{1,5},{2,6},{3,7},{4,0},{5,1},{6,2},{7,3},{8,12},{9,13},{10,... | collective-permute-start | bytes 393224 | tf_op jit(solution)/shard_map/weight_grad_sum/ppermute | solution.py:29
  131.3 4.5 %collective-permute-start.20 = (f32[64,256]{1,0:T(8,128)S(1)}, f32[64,256]{1,0:T(8,128)S(1)}, u32[]{:S(2)}, u32[]{:S(2)}) collective-permute-start(f32[64,256]{1,0:T(8,128)S(1)} %dynamic-slice_bitcast_fusion.8), channel_id=1, source_target_pairs={{0,4},{1,5},{2,6},{3,7},{4,0},{5,1},{6,2},{7,3},{8,12},{9,13},{10,... | collective-permute-start | bytes 196616 | tf_op jit(solution)/shard_map/weight_grad_sum/ppermute | solution.py:29
  132.0 5.2 %collective-permute-start.25 = (f32[64,256]{1,0:T(8,128)S(1)}, f32[64,256]{1,0:T(8,128)S(1)}, u32[]{:S(2)}, u32[]{:S(2)}) collective-permute-start(f32[64,256]{1,0:T(8,128)S(1)} %dynamic-slice_bitcast_fusion.7), channel_id=1, source_target_pairs={{0,8},{1,9},{2,10},{3,11},{4,12},{5,13},{6,14},{7,15},{8,0},{9,1},... | collective-permute-start | bytes 196616 | tf_op jit(solution)/shard_map/weight_grad_sum/ppermute | solution.py:29

commit v10 on v9

--- a/solution.py
+++ b/solution.py
@@ -72,6 +72,46 @@
     )
 
 
+def halving_step(state, order, step):
+    values, bits, place = state
+    top = lax.axis_size("mp").bit_length() - 1
+    bit = order[step]
+    position = bits.index(bit)
+    mine = (place >> bit) & 1
+    keep = lax.dynamic_index_in_dim(values, mine, position, keepdims=False)
+    send = lax.dynamic_index_in_dim(values, 1 - mine, position, keepdims=False)
+    got = swap(send, "dp", 1) if bit == top else swap(send, "mp", 1 << bit)
+    return (keep + got, [b for b in bits if b != bit], place)
+
+
+def halving_start(terms):
+    n_mp = lax.axis_size("mp")
+    top = n_mp.bit_length() - 1
+    place = lax.axis_index("dp") * n_mp + lax.axis_index("mp")
+    rows = terms.shape[0] // (2 * n_mp)
+    values = terms.reshape((2,) * (top + 1) + (rows, terms.shape[1]))
+    return (values, list(range(top, -1, -1)), place)
+
+
+def last_block_sum(block):
+    mp_index = lax.axis_index("mp")
+    rows = block.shape[0] // 8
+    values = block.reshape(2, 2, 2, rows, block.shape[1])
+    bits = [2, 1, 0]
+    for bit in [0, 1, 2]:
+        position = bits.index(bit)
+        mine = (mp_index >> bit) & 1
+        keep = lax.dynamic_index_in_dim(values, mine, position, keepdims=False)
+        send = lax.dynamic_index_in_dim(values, 1 - mine, position, keepdims=False)
+        values = keep + swap(send, "mp", 1 << bit)
+        bits.pop(position)
+    values = values.reshape(rows, block.shape[1])
+    values = values + swap(values, "mp", 8)
+    values = values + swap(values, "dp", 1)
+    lands = (lax.axis_index("dp") == 1) & (mp_index >= 8)
+    return jnp.where(lands, values, jnp.zeros_like(values))
+
+
 def shards(
     node_features, weights_one, weights_two, neighbor_owner, neighbor_row, neighbor_count, cotangent
 ):
@@ -146,36 +186,45 @@
         own_agg_one, weights_one[feat_width:], 0, 0
     )
     hidden_one = jax.nn.silu(pre_one).astype(jnp.bfloat16)
-    hidden_all = split_gather(hidden_one, order, other)
+    down_self = contract(cotangent, self_two, 1, 1)
+    neighbor_sum = contract(named_by, down_all, 0, 0)
+    grad_hidden = down_self + neighbor_sum
+    grad_pre = (grad_hidden * silu_slope(pre_one)).astype(jnp.bfloat16)
+    early_terms = [
+        contract(own_feats, grad_pre, 1, 0),
+        contract(own_agg_one, grad_pre, 1, 0),
+        contract(hidden_one, cotangent, 0, 0),
+    ]
+    paced = lax.axis_size("dp") == 2 and devices == 16
+    if paced:
+        early = jnp.concatenate(early_terms + [jnp.zeros_like(early_terms[0])], axis=0)
+        cols = early.shape[1] // 2
+        sum_orders = [[0, 4, 1, 3, 2], [0, 1, 4, 2, 3]]
+        sums = [halving_start(early[:, :cols]), halving_start(early[:, cols:])]
+        hparts = [hidden_one[:, :half], hidden_one[:, half:]]
+        for step in range(len(order)):
+            hparts = [doubling_step(p, o, step) for p, o in zip(hparts, orders)]
+            sums = [halving_step(t, o, step) for t, o in zip(sums, sum_orders)]
+            hparts, sum_values = lax.optimization_barrier((hparts, [t[0] for t in sums]))
+            sums = [(v, t[1], t[2]) for v, t in zip(sum_values, sums)]
+        hidden_all = jnp.concatenate([p.reshape(-1, half) for p in hparts], axis=1)
+    else:
+        hidden_all = split_gather(hidden_one, order, other)
     total = contract(own_edges, hidden_all, 0, 0)
     agg_two = (total * own_inverse[:, None]).astype(jnp.bfloat16)
     node_output = (
         contract(hidden_one, self_two, 1, 0) + contract(agg_two, neigh_two, 1, 0)
     ).astype(jnp.bfloat16)
-    down_self = contract(cotangent, self_two, 1, 1)
-    neighbor_sum = contract(named_by, down_all, 0, 0)
-    grad_hidden = down_self + neighbor_sum
-    grad_pre = (grad_hidden * silu_slope(pre_one)).astype(jnp.bfloat16)
-    terms = jnp.concatenate(
-        [
-            contract(own_feats, grad_pre, 1, 0),
-            contract(own_agg_one, grad_pre, 1, 0),
-            contract(hidden_one, cotangent, 0, 0),
-            contract(agg_two, cotangent, 0, 0),
-        ],
-        axis=0,
-    )
+    last_term = contract(agg_two, cotangent, 0, 0)
     with jax.named_scope("weight_grad_sum"):
-        if lax.axis_size("dp") == 2 and devices == 16:
-            half = terms.shape[1] // 2
-            weight_grads = jnp.concatenate(
-                [
-                    halving_scatter(terms[:, :half], [0, 4, 1, 3, 2]),
-                    halving_scatter(terms[:, half:], [0, 1, 4, 2, 3]),
-                ],
-                axis=1,
-            )
+        if paced:
+            for step in range(len(order), len(sum_orders[0])):
+                sums = [halving_step(t, o, step) for t, o in zip(sums, sum_orders)]
+            rows = sums[0][0].shape[-2]
+            weight_grads = jnp.concatenate([t[0].reshape(rows, cols) for t in sums], axis=1)
+            weight_grads = weight_grads + last_block_sum(last_term)
         else:
+            terms = jnp.concatenate(early_terms + [last_term], axis=0)
             weight_grads = lax.psum_scatter(terms, ("dp", "mp"), scatter_dimension=0, tiled=True)
     return (node_output, weight_grads)
 

time: 139 us -> 163 us (1.17)
  waiting for transfers between devices: 64.9 us -> 81.1 us
  starting transfers between devices: 33 us -> 37.4 us
  other arithmetic: 14.1 us -> 18.3 us
    all_to_all x1, waiting for transfers between devices: 0.01 us -> 9.51 us  [shards(): lax.all_to_all(node_features, 'mp', split_axis=1, concat_axis=0, tiled=True)]
    ppermute x26 -> x31, waiting for transfers between devices: 59.9 us -> 64.5 us  [swap(): return lax.ppermute(values, axis, [(j, j ^ mask) for j in range(size)])]
    ppermute x26 -> x31, starting transfers between devices: 25.7 us -> 28.3 us  [swap(): return lax.ppermute(values, axis, [(j, j ^ mask) for j in range(size)])]
    add x10 -> x15, other arithmetic: 3.11 us -> 5.58 us  [the longest x10 4.75 us: halving_step(): return (keep + got, [b for b in bits if b != bit], place)]
    all_to_all x1, waiting for transfers between devices: 4.99 us -> 7.02 us  [shards(): lax.all_to_all(agg_one_cols, 'mp', split_axis=1, concat_axis=0, tiled=True)]
    dot_general x13, matrix products: 14.6 us -> 13 us  [contract(): lax.dot_general(left, right, (((left_dim,), (right_dim,)), ((), ())), pre...]
    all_to_all x1, starting transfers between devices: 3.77 us -> 5.4 us  [shards(): lax.all_to_all(agg_one_cols, 'mp', split_axis=1, concat_axis=0, tiled=True)]
  transfers between devices with their start and end apart: 28 -> 33, of which waited for: 19 -> 22; matrix products, arithmetic and copies ran while one was open for 18% -> 17% of each run, Pallas kernels for 0% -> 0%
where the time goes in v10:
time: 163 us; the launch traced here: 162 us
  waiting for transfers between devices  81.1 us (50%)
  starting transfers between devices  37.4 us (23%)
  other arithmetic  18.3 us (11%)
  matrix products  13 us (8%)
  local copies, waits for them, and re-layouts  10.9 us (7%)
    ppermute x31, waiting for transfers between devices, swap(): return lax.ppermute(values, axis, [(j, j ^ mask) for j in range(size)])  64.5 us
    ppermute x31, starting transfers between devices, swap(): return lax.ppermute(values, axis, [(j, j ^ mask) for j in range(size)])  28.3 us
    dot_general x13, matrix products, contract(): lax.dot_general(left, right, (((left_dim,), (right_dim,)), ((), ())), pre...  13 us
    all_to_all x1, waiting for transfers between devices, shards(): lax.all_to_all(node_features, 'mp', split_axis=1, concat_axis=0, tiled=True)  9.51 us
    all_to_all x1, waiting for transfers between devices, shards(): lax.all_to_all(agg_one_cols, 'mp', split_axis=1, concat_axis=0, tiled=True)  7.02 us
    all_to_all x1, starting transfers between devices, shards(): lax.all_to_all(agg_one_cols, 'mp', split_axis=1, concat_axis=0, tiled=True)  5.4 us
    add x10, other arithmetic, halving_step(): return (keep + got, [b for b in bits if b != bit], place)  4.75 us
    another operation x29, other arithmetic, doubling_step(): jnp.stack([low, high], axis=sum((1 for done in order[:step] if done > bit)))  4.07 us
  transfers between devices with their start and end apart: 33, of which 22 were waited for; matrix products, arithmetic and copies ran while one was open for 17% of the time, Pallas kernels for 0%

profile of v10, /device:TPU:0, one launch (start us, length us, event | category | flops | bytes accessed | tf_op | source)
XLA Modules:
  0.0 162.0 jit_solution(13158928862282404704)
XLA Ops:
  0.6 0.8 convert_divide_fusion
  1.6 1.4 fusion.21
  3.0 4.1 %collective-permute-start = (bf16[192,256]{1,0:T(8,128)(2,1)S(1)}, bf16[192,256]{1,0:T(8,128)(2,1)S(1)}, u32[]{:S(2)}, u32[]{:S(2)}) collective-permute-start(bf16[192,256]{1,0:T(8,128)(2,1)S(1)} %get-tuple-element.95), channel_id=1, source_target_pairs={{0,8},{1,9},{2,10},{3,11},{4,12},{5,13},{6,14},{7,15},{8,0},{9,1},... | collective-permute-start | bytes 294920 | tf_op jit(solution)/shard_map/ppermute | solution.py:29
  7.1 1.5 collective-permute-start.1
  8.6 0.7 iota_compare_fusion.3
  9.4 1.8 %select_reduce_fusion = s32[16,3072]{1,0:T(8,128)S(1)} fusion(s32[3072,8]{0,1:T(8,128)} %param.11, s32[3072,8]{0,1:T(8,128)} %param.10, pred[3072,8]{0,1:T(8,128)(4,1)S(1)} %iota_compare_fusion.3), kind=kLoop, calls=%fused_computation.21 | loop fusion | flops 1523712 | bytes 417792 | tf_op jit(solution)/shard_map/reduce_max | solution.py:130
  11.2 3.9 %fusion = bf16[3072,3072]{1,0:T(8,128)(2,1)S(1)} fusion(s32[3072]{0:T(1024)S(1)} %eq.59, s32[16,3072]{1,0:T(8,128)S(1)} %select_reduce_fusion), kind=kLoop, calls=%fused_computation.1 | loop fusion | flops 18874368 | bytes 19083264 | tf_op jit(solution)/shard_map/layer_one_mean/convert_element_type | solution.py:155
  15.6 1.6 collective-permute-start.2
  17.2 3.4 %fusion.2 = bf16[32,3072]{1,0:T(8,128)(2,1)S(1)} fusion(bf16[32,3072]{1,0:T(8,128)(2,1)S(1)} %copy-done.3, bf16[3072,3072]{1,0:T(8,128)(2,1)S(1)} %fusion, f32[3072]{0:T(1024)S(1)} %convert_divide_fusion), kind=kOutput, calls=%fused_computation.5 | convolution fusion | flops 604176384 | bytes 19279872 | tf_op jit(solution)/shard_map/layer_one_mean/dot_general | solution.py:22
  20.6 6.0 %collective-permute-done.3 = bf16[2,192,256]{2,1,0:T(8,128)(2,1)S(1)} collective-permute-done((bf16[2,192,256]{2,1,0:T(8,128)(2,1)S(1)}, bf16[2,192,256]{2,1,0:T(8,128)(2,1)S(1)}, u32[]{:S(2)}, u32[]{:S(2)}) %collective-permute-start.3) | collective-permute-done | bytes 196640 | tf_op jit(solution)/shard_map/layer_one_mean/ppermute | solution.py:29
  27.1 0.8 copy.27
  28.7 0.8 copy.28
  29.5 5.4 %all-to-all-start.1 = ((bf16[32,16,192]{2,0,1:T(8,128)(2,1)}), bf16[32,16,192]{2,0,1:T(8,128)(2,1)S(1)}, u32[]{:S(2)}, u32[]{:S(2)}) async-start(bf16[32,16,192]{2,0,1:T(8,128)(2,1)} %copy.28), calls=%async_computation.1 | async-start | bytes 524288 | tf_op jit(solution)/shard_map/all_to_all | solution.py:170
  34.9 1.8 %collective-permute-done.5 = bf16[2,2,192,256]{3,2,1,0:T(8,128)(2,1)S(1)} collective-permute-done((bf16[2,2,192,256]{3,2,1,0:T(8,128)(2,1)S(1)}, bf16[2,2,192,256]{3,2,1,0:T(8,128)(2,1)S(1)}, u32[]{:S(2)}, u32[]{:S(2)}) %collective-permute-start.5) | collective-permute-done | bytes 393248 | tf_op jit(solution)/shard_map/ppermute | solution.py:29
  36.9 1.0 collective-permute-done.4
  38.0 7.0 %all-to-all-done.1 = bf16[32,16,192]{2,0,1:T(8,128)(2,1)S(1)} async-done(((bf16[32,16,192]{2,0,1:T(8,128)(2,1)}), bf16[32,16,192]{2,0,1:T(8,128)(2,1)S(1)}, u32[]{:S(2)}, u32[]{:S(2)}) %all-to-all-start.1) | async-done | bytes 196640 | tf_op jit(solution)/shard_map/all_to_all | solution.py:170
  45.0 3.7 %all-to-all-start = ((bf16[32,16,192]{2,0,1:T(8,128)(2,1)}), bf16[32,16,192]{2,0,1:T(8,128)(2,1)S(1)}, u32[]{:S(2)}, u32[]{:S(2)}) async-start(bf16[32,16,192]{2,0,1:T(8,128)(2,1)} %copy.27), calls=%async_computation | async-start | bytes 524288 | tf_op jit(solution)/shard_map/all_to_all | solution.py:169
  49.0 9.5 %all-to-all-done = bf16[32,16,192]{2,0,1:T(8,128)(2,1)S(1)} async-done(((bf16[32,16,192]{2,0,1:T(8,128)(2,1)}), bf16[32,16,192]{2,0,1:T(8,128)(2,1)S(1)}, u32[]{:S(2)}, u32[]{:S(2)}) %all-to-all-start) | async-done | bytes 196640 | tf_op jit(solution)/shard_map/all_to_all | solution.py:169
  58.5 1.3 fusion.24
  59.9 1.4 multiply_convert_fusion
  62.6 1.6 fusion.3
  65.8 1.3 copy-done.1
  67.2 1.1 dynamic-slice_bitcast_fusion
  68.9 1.0 copy.40
  70.0 0.7 fusion.34
  70.7 1.0 collective-permute-start.6
  71.7 7.1 %collective-permute-done.6 = bf16[192,256]{1,0:T(8,128)(2,1)} collective-permute-done((bf16[192,256]{1,0:T(8,128)(2,1)}, bf16[192,256]{1,0:T(8,128)(2,1)}, u32[]{:S(2)}, u32[]{:S(2)}) %collective-permute-start.6) | collective-permute-done | bytes 98336 | tf_op jit(solution)/shard_map/ppermute | solution.py:29
  78.8 1.0 select_bitcast_fusion.25
  79.9 1.4 bitcast_add_fusion.1
  81.3 1.4 bitcast_add_fusion
  83.4 1.6 collective-permute-start.14
  84.9 2.0 %collective-permute-start.12 = (bf16[2,192,256]{2,1,0:T(8,128)(2,1)S(1)}, bf16[2,192,256]{2,1,0:T(8,128)(2,1)S(1)}, u32[]{:S(2)}, u32[]{:S(2)}) collective-permute-start(bf16[2,192,256]{2,1,0:T(8,128)(2,1)S(1)} %pad_maximum_fusion.14), channel_id=1, source_target_pairs={{0,4},{1,5},{2,6},{3,7},{4,0},{5,1},{6,2},{7,3},{8,12},{9,13},{10,... | collective-permute-start | bytes 589832 | tf_op jit(solution)/shard_map/ppermute | solution.py:29
  86.9 5.9 %collective-permute-done.13 = bf16[2,192,256]{2,1,0:T(8,128)(2,1)S(1)} collective-permute-done((bf16[2,192,256]{2,1,0:T(8,128)(2,1)S(1)}, bf16[2,192,256]{2,1,0:T(8,128)(2,1)S(1)}, u32[]{:S(2)}, u32[]{:S(2)}) %collective-permute-start.13) | collective-permute-done | bytes 196640 | tf_op jit(solution)/shard_map/ppermute | solution.py:29
  92.9 2.5 %collective-permute-done.12 = bf16[2,192,256]{2,1,0:T(8,128)(2,1)S(1)} collective-permute-done((bf16[2,192,256]{2,1,0:T(8,128)(2,1)S(1)}, bf16[2,192,256]{2,1,0:T(8,128)(2,1)S(1)}, u32[]{:S(2)}, u32[]{:S(2)}) %collective-permute-start.12) | collective-permute-done | bytes 196640 | tf_op jit(solution)/shard_map/ppermute | solution.py:29
  95.5 1.4 collective-permute-done.15
  97.1 1.6 collective-permute-start.19
  98.7 1.8 %collective-permute-start.18 = (f32[2,2,64,256]{3,2,1,0:T(8,128)S(1)}, f32[2,2,64,256]{3,2,1,0:T(8,128)S(1)}, u32[]{:S(2)}, u32[]{:S(2)}) collective-permute-start(f32[2,2,64,256]{3,2,1,0:T(8,128)S(1)} %dynamic-slice_bitcast_fusion.6), channel_id=1, source_target_pairs={{0,2},{1,3},{2,0},{3,1},{4,6},{5,7},{6,4},{7,5},{8,10},{9,11},{10,... | collective-permute-start | bytes 786440 | tf_op jit(solution)/shard_map/ppermute | solution.py:29
  100.5 0.8 collective-permute-start.17
  101.2 1.3 collective-permute-start.16
  102.5 2.1 %collective-permute-done.19 = f32[2,2,64,256]{3,2,1,0:T(8,128)} collective-permute-done((f32[2,2,64,256]{3,2,1,0:T(8,128)S(1)}, f32[2,2,64,256]{3,2,1,0:T(8,128)}, u32[]{:S(2)}, u32[]{:S(2)}) %collective-permute-start.19) | collective-permute-done | bytes 262176 | tf_op jit(solution)/shard_map/ppermute | solution.py:29
  104.7 1.0 bitcast_add_fusion.6
  105.7 2.3 %collective-permute-done.18 = f32[2,2,64,256]{3,2,1,0:T(8,128)S(1)} collective-permute-done((f32[2,2,64,256]{3,2,1,0:T(8,128)S(1)}, f32[2,2,64,256]{3,2,1,0:T(8,128)S(1)}, u32[]{:S(2)}, u32[]{:S(2)}) %collective-permute-start.18) | collective-permute-done | bytes 262176 | tf_op jit(solution)/shard_map/ppermute | solution.py:29
  108.0 1.8 %collective-permute-done.17 = bf16[2,2,192,256]{3,2,1,0:T(8,128)(2,1)S(1)} collective-permute-done((bf16[2,2,192,256]{3,2,1,0:T(8,128)(2,1)S(1)}, bf16[2,2,192,256]{3,2,1,0:T(8,128)(2,1)S(1)}, u32[]{:S(2)}, u32[]{:S(2)}) %collective-permute-start.17) | collective-permute-done | bytes 393248 | tf_op jit(solution)/shard_map/ppermute | solution.py:29
  110.0 4.3 %collective-permute-done.16 = bf16[2,2,192,256]{3,2,0,1:T(8,128)(2,1)S(1)} collective-permute-done((bf16[2,2,192,256]{3,2,0,1:T(8,128)(2,1)S(1)}, bf16[2,2,192,256]{3,2,0,1:T(8,128)(2,1)S(1)}, u32[]{:S(2)}, u32[]{:S(2)}) %collective-permute-start.16) | collective-permute-done | bytes 393248 | tf_op jit(solution)/shard_map/ppermute | solution.py:29
  114.5 1.2 collective-permute-start.23
  115.8 1.4 constant_dynamic-slice_fusion.3
  117.2 1.2 bitcast_compare_fusion.1
  118.4 1.2 collective-permute-start.22
  120.5 7.3 %collective-permute-done.22 = f32[2,64,256]{2,1,0:T(8,128)S(1)} collective-permute-done((f32[2,64,256]{2,1,0:T(8,128)S(1)}, f32[2,64,256]{2,1,0:T(8,128)S(1)}, u32[]{:S(2)}, u32[]{:S(2)}) %collective-permute-start.22) | collective-permute-done | bytes 131104 | tf_op jit(solution)/shard_map/ppermute | solution.py:29
  127.8 0.7 bitcast_add_fusion.10
  128.5 1.2 select_bitcast_fusion.1
  130.4 1.1 fusion.17
  131.5 0.7 copy-done.7
  132.6 0.8 dynamic-slice_bitcast_fusion.1
  133.4 2.1 %collective-permute-done.26 = f32[2,2,64,512]{3,2,1,0:T(8,128)S(1)} collective-permute-done((f32[2,2,64,512]{3,2,1,0:T(8,128)}, f32[2,2,64,512]{3,2,1,0:T(8,128)S(1)}, u32[]{:S(2)}, u32[]{:S(2)}) %collective-permute-start.26) | collective-permute-done | bytes 524320 | tf_op jit(solution)/shard_map/weight_grad_sum/ppermute | solution.py:29
  135.7 0.7 collective-permute-start.27
  137.1 3.4 %collective-permute-start.25 = (f32[64,256]{1,0:T(8,128)S(1)}, f32[64,256]{1,0:T(8,128)S(1)}, u32[]{:S(2)}, u32[]{:S(2)}) collective-permute-start(f32[64,256]{1,0:T(8,128)S(1)} %dynamic-slice_bitcast_fusion.10), channel_id=1, source_target_pairs={{0,8},{1,9},{2,10},{3,11},{4,12},{5,13},{6,14},{7,15},{8,0},{9,1},... | collective-permute-start | bytes 196616 | tf_op jit(solution)/shard_map/weight_grad_sum/ppermute | solution.py:29
  140.5 3.6 %collective-permute-done.27 = f32[2,64,512]{2,1,0:T(8,128)S(1)} collective-permute-done((f32[2,64,512]{2,1,0:T(8,128)S(1)}, f32[2,64,512]{2,1,0:T(8,128)S(1)}, u32[]{:S(2)}, u32[]{:S(2)}) %collective-permute-start.27) | collective-permute-done | bytes 262176 | tf_op jit(solution)/shard_map/weight_grad_sum/ppermute | solution.py:29
  144.2 1.0 fusion.22
  145.2 4.0 %collective-permute-done.28 = f32[64,512]{1,0:T(8,128)S(1)} collective-permute-done((f32[64,512]{1,0:T(8,128)S(1)}, f32[64,512]{1,0:T(8,128)S(1)}, u32[]{:S(2)}, u32[]{:S(2)}) %collective-permute-start.28) | collective-permute-done | bytes 131104 | tf_op jit(solution)/shard_map/weight_grad_sum/ppermute | solution.py:29
  149.2 1.0 collective-permute-start.29
  150.2 6.1 %collective-permute-done.29 = f32[64,512]{1,0:T(8,128)S(1)} collective-permute-done((f32[64,512]{1,0:T(8,128)S(1)}, f32[64,512]{1,0:T(8,128)S(1)}, u32[]{:S(2)}, u32[]{:S(2)}) %collective-permute-start.29) | collective-permute-done | bytes 131104 | tf_op jit(solution)/shard_map/weight_grad_sum/ppermute | solution.py:29
  156.9 4.4 %collective-permute-done.30 = f32[64,512]{1,0:T(8,128)S(1)} collective-permute-done((f32[64,512]{1,0:T(8,128)S(1)}, f32[64,512]{1,0:T(8,128)S(1)}, u32[]{:S(2)}, u32[]{:S(2)}) %collective-permute-start.30) | collective-permute-done | bytes 131104 | tf_op jit(solution)/shard_map/weight_grad_sum/ppermute | solution.py:29
  161.3 0.7 maximum_add_fusion
  (117 shorter events, 11.1 us)
Async XLA Ops:
  0.6 0.9 copy-start
  3.0 12.2 %collective-permute-start = (bf16[192,256]{1,0:T(8,128)(2,1)S(1)}, bf16[192,256]{1,0:T(8,128)(2,1)S(1)}, u32[]{:S(2)}, u32[]{:S(2)}) collective-permute-start(bf16[192,256]{1,0:T(8,128)(2,1)S(1)} %get-tuple-element.95), channel_id=1, source_target_pairs={{0,8},{1,9},{2,10},{3,11},{4,12},{5,13},{6,14},{7,15},{8,0},{9,1},... | collective-permute-start | bytes 294920 | tf_op jit(solution)/shard_map/ppermute | solution.py:29
  7.1 8.1 %collective-permute-start.1 = (bf16[192,256]{1,0:T(8,128)(2,1)S(1)}, bf16[192,256]{1,0:T(8,128)(2,1)S(1)}, u32[]{:S(2)}, u32[]{:S(2)}) collective-permute-start(bf16[192,256]{1,0:T(8,128)(2,1)S(1)} %get-tuple-element.94), channel_id=1, source_target_pairs={{0,2},{1,3},{2,0},{3,1},{4,6},{5,7},{6,4},{7,5},{8,10},{9,11},{10,... | collective-permute-start | bytes 294920 | tf_op jit(solution)/shard_map/ppermute | solution.py:29
  11.2 37.7 %copy-start.6 = (s32[16,3072]{1,0:T(8,128)}, s32[16,3072]{1,0:T(8,128)S(1)}, u32[]{:S(2)}) copy-start(s32[16,3072]{1,0:T(8,128)S(1)} %select_reduce_fusion) | copy-start | bytes 589828
  11.2 6.0 %copy-start.3 = (bf16[32,3072]{1,0:T(8,128)(2,1)S(1)}, bf16[32,3072]{1,0:T(8,128)(2,1)}, u32[]{:S(2)}) copy-start(bf16[32,3072]{1,0:T(8,128)(2,1)} %param.7) | copy-start | bytes 589828
  15.2 11.3 %collective-permute-start.3 = (bf16[2,192,256]{2,1,0:T(8,128)(2,1)S(1)}, bf16[2,192,256]{2,1,0:T(8,128)(2,1)S(1)}, u32[]{:S(2)}, u32[]{:S(2)}) collective-permute-start(bf16[2,192,256]{2,1,0:T(8,128)(2,1)S(1)} %get-tuple-element.28), channel_id=1, source_target_pairs={{0,8},{1,9},{2,10},{3,11},{4,12},{5,13},{6,14},{7,15},{8,0},{9,1},... | collective-permute-start | bytes 589832 | tf_op jit(solution)/shard_map/layer_one_mean/ppermute | solution.py:29
  15.6 11.0 %collective-permute-start.2 = (bf16[2,192,256]{2,1,0:T(8,128)(2,1)S(1)}, bf16[2,192,256]{2,1,0:T(8,128)(2,1)S(1)}, u32[]{:S(2)}, u32[]{:S(2)}) collective-permute-start(bf16[2,192,256]{2,1,0:T(8,128)(2,1)S(1)} %get-tuple-element.27), channel_id=1, source_target_pairs={{0,4},{1,5},{2,6},{3,7},{4,0},{5,1},{6,2},{7,3},{8,12},{9,13},{10,... | collective-permute-start | bytes 589832 | tf_op jit(solution)/shard_map/layer_one_mean/ppermute | solution.py:29
  26.7 10.1 %collective-permute-start.5 = (bf16[2,2,192,256]{3,2,1,0:T(8,128)(2,1)S(1)}, bf16[2,2,192,256]{3,2,1,0:T(8,128)(2,1)S(1)}, u32[]{:S(2)}, u32[]{:S(2)}) collective-permute-start(bf16[2,2,192,256]{3,2,1,0:T(8,128)(2,1)S(1)} %pad_maximum_fusion.9), channel_id=1, source_target_pairs={{0,4},{1,5},{2,6},{3,7},{4,0},{5,1},{6,2},{7,3},{8,12},{9,13},{10,... | collective-permute-start | bytes 1179656 | tf_op jit(solution)/shard_map/ppermute | solution.py:29
  27.9 10.0 %collective-permute-start.4 = (bf16[2,2,192,256]{3,2,0,1:T(8,128)(2,1)S(1)}, bf16[2,2,192,256]{3,2,0,1:T(8,128)(2,1)S(1)}, u32[]{:S(2)}, u32[]{:S(2)}) collective-permute-start(bf16[2,2,192,256]{3,2,0,1:T(8,128)(2,1)S(1)} %pad_maximum_fusion.8), channel_id=1, source_target_pairs={{0,2},{1,3},{2,0},{3,1},{4,6},{5,7},{6,4},{7,5},{8,10},{9,11},{10,... | collective-permute-start | bytes 1179656 | tf_op jit(solution)/shard_map/ppermute | solution.py:29
  29.5 15.5 %all-to-all-start.1 = ((bf16[32,16,192]{2,0,1:T(8,128)(2,1)}), bf16[32,16,192]{2,0,1:T(8,128)(2,1)S(1)}, u32[]{:S(2)}, u32[]{:S(2)}) async-start(bf16[32,16,192]{2,0,1:T(8,128)(2,1)} %copy.28), calls=%async_computation.1 | async-start | bytes 524288 | tf_op jit(solution)/shard_map/all_to_all | solution.py:170
  45.0 13.5 %all-to-all-start = ((bf16[32,16,192]{2,0,1:T(8,128)(2,1)}), bf16[32,16,192]{2,0,1:T(8,128)(2,1)S(1)}, u32[]{:S(2)}, u32[]{:S(2)}) async-start(bf16[32,16,192]{2,0,1:T(8,128)(2,1)} %copy.27), calls=%async_computation | async-start | bytes 524288 | tf_op jit(solution)/shard_map/all_to_all | solution.py:169
  48.8 12.9 %collective-permute-start.8 = (bf16[2,2,2,192,256]{4,3,0,1,2:T(8,128)(2,1)S(1)}, bf16[2,2,2,192,256]{4,3,0,1,2:T(8,128)(2,1)S(1)}, u32[]{:S(2)}, u32[]{:S(2)}) collective-permute-start(bf16[2,2,2,192,256]{4,3,0,1,2:T(8,128)(2,1)S(1)} %pad_maximum_fusion.4), channel_id=1, source_target_pairs={{0,1},{1,0},{2,3},{3,2},{4,5},{5,4},{6,7},{7,6},{8,9},{9,8},{10,11... | collective-permute-start | bytes 2359304 | tf_op jit(solution)/shard_map/ppermute | solution.py:29
  59.9 2.4 %collective-permute-start.9 = (bf16[2,2,2,192,256]{4,3,2,0,1:T(8,128)(2,1)S(1)}, bf16[2,2,2,192,256]{4,3,2,0,1:T(8,128)(2,1)S(1)}, u32[]{:S(2)}, u32[]{:S(2)}) collective-permute-start(bf16[2,2,2,192,256]{4,3,2,0,1:T(8,128)(2,1)S(1)} %pad_maximum_fusion.5), channel_id=1, source_target_pairs={{0,1},{1,0},{2,3},{3,2},{4,5},{5,4},{6,7},{7,6},{8,9},{9,8},{10,11... | collective-permute-start | bytes 2359304 | tf_op jit(solution)/shard_map/ppermute | solution.py:29
  62.6 1.6 copy-start.4
  65.8 1.4 copy-start.1
  68.3 11.6 %collective-permute-start.10 = (f32[2,2,2,2,64,256]{5,4,3,2,1,0:T(8,128)}, f32[2,2,2,2,64,256]{5,4,3,2,1,0:T(8,128)}, u32[]{:S(2)}, u32[]{:S(2)}) collective-permute-start(f32[2,2,2,2,64,256]{5,4,3,2,1,0:T(8,128)} %dynamic-slice_bitcast_fusion), channel_id=1, source_target_pairs={{0,1},{1,0},{2,3},{3,2},{4,5},{5,4},{6,7},{7,6},{8,9},{9,8},{10,11... | collective-permute-start | bytes 3145736 | tf_op jit(solution)/shard_map/ppermute | solution.py:29
  68.9 11.0 %copy-start.2 = (f32[2048,256]{1,0:T(8,128)S(1)}, f32[2048,256]{1,0:T(8,128)}, u32[]{:S(2)}) copy-start(f32[2048,256]{1,0:T(8,128)} %copy-done.1) | copy-start | bytes 6291460
  69.9 11.4 %collective-permute-start.11 = (f32[2,2,2,2,64,256]{5,4,2,1,0,3:T(8,128)}, f32[2,2,2,2,64,256]{5,4,2,1,0,3:T(8,128)}, u32[]{:S(2)}, u32[]{:S(2)}) collective-permute-start(f32[2,2,2,2,64,256]{5,4,2,1,0,3:T(8,128)} %bitcast.159), channel_id=1, source_target_pairs={{0,1},{1,0},{2,3},{3,2},{4,5},{5,4},{6,7},{7,6},{8,9},{9,8},{10,11... | collective-permute-start | bytes 3145736 | tf_op jit(solution)/shard_map/ppermute | solution.py:29
  70.7 8.1 %collective-permute-start.6 = (bf16[192,256]{1,0:T(8,128)(2,1)}, bf16[192,256]{1,0:T(8,128)(2,1)}, u32[]{:S(2)}, u32[]{:S(2)}) collective-permute-start(bf16[192,256]{1,0:T(8,128)(2,1)} %get-tuple-element.91), channel_id=1, source_target_pairs={{0,8},{1,9},{2,10},{3,11},{4,12},{5,13},{6,14},{7,15},{8,0},{9,1},... | collective-permute-start | bytes 294920 | tf_op jit(solution)/shard_map/ppermute | solution.py:29
  71.7 7.1 %collective-permute-start.7 = (bf16[192,256]{1,0:T(8,128)(2,1)}, bf16[192,256]{1,0:T(8,128)(2,1)}, u32[]{:S(2)}, u32[]{:S(2)}) collective-permute-start(bf16[192,256]{1,0:T(8,128)(2,1)} %get-tuple-element.90), channel_id=1, source_target_pairs={{0,2},{1,3},{2,0},{3,1},{4,6},{5,7},{6,4},{7,5},{8,10},{9,11},{10,... | collective-permute-start | bytes 294920 | tf_op jit(solution)/shard_map/ppermute | solution.py:29
  82.8 10.1 %collective-permute-start.13 = (bf16[2,192,256]{2,1,0:T(8,128)(2,1)S(1)}, bf16[2,192,256]{2,1,0:T(8,128)(2,1)S(1)}, u32[]{:S(2)}, u32[]{:S(2)}) collective-permute-start(bf16[2,192,256]{2,1,0:T(8,128)(2,1)S(1)} %pad_maximum_fusion.15), channel_id=1, source_target_pairs={{0,8},{1,9},{2,10},{3,11},{4,12},{5,13},{6,14},{7,15},{8,0},{9,1},... | collective-permute-start | bytes 589832 | tf_op jit(solution)/shard_map/ppermute | solution.py:29
  82.9 14.0 %collective-permute-start.15 = (f32[2,2,2,64,256]{4,3,2,1,0:T(8,128)S(1)}, f32[2,2,2,64,256]{4,3,2,1,0:T(8,128)S(1)}, u32[]{:S(2)}, u32[]{:S(2)}) collective-permute-start(f32[2,2,2,64,256]{4,3,2,1,0:T(8,128)S(1)} %dynamic-slice_bitcast_fusion.2), channel_id=1, source_target_pairs={{0,2},{1,3},{2,0},{3,1},{4,6},{5,7},{6,4},{7,5},{8,10},{9,11},{10,... | collective-permute-start | bytes 1572872 | tf_op jit(solution)/shard_map/ppermute | solution.py:29
  83.4 13.6 %collective-permute-start.14 = (f32[2,2,2,64,256]{4,3,2,1,0:T(8,128)S(1)}, f32[2,2,2,64,256]{4,3,2,1,0:T(8,128)S(1)}, u32[]{:S(2)}, u32[]{:S(2)}) collective-permute-start(f32[2,2,2,64,256]{4,3,2,1,0:T(8,128)S(1)} %dynamic-slice_bitcast_fusion.3), channel_id=1, source_target_pairs={{0,16},{16,0},{1,17},{17,1},{2,18},{18,2},{3,19},{19,3},{4,20},{20... | collective-permute-start | bytes 1572872 | tf_op jit(solution)/shard_map/ppermute | solution.py:29
  84.9 10.4 %collective-permute-start.12 = (bf16[2,192,256]{2,1,0:T(8,128)(2,1)S(1)}, bf16[2,192,256]{2,1,0:T(8,128)(2,1)S(1)}, u32[]{:S(2)}, u32[]{:S(2)}) collective-permute-start(bf16[2,192,256]{2,1,0:T(8,128)(2,1)S(1)} %pad_maximum_fusion.14), channel_id=1, source_target_pairs={{0,4},{1,5},{2,6},{3,7},{4,0},{5,1},{6,2},{7,3},{8,12},{9,13},{10,... | collective-permute-start | bytes 589832 | tf_op jit(solution)/shard_map/ppermute | solution.py:29
  97.1 7.6 %collective-permute-start.19 = (f32[2,2,64,256]{3,2,1,0:T(8,128)S(1)}, f32[2,2,64,256]{3,2,1,0:T(8,128)}, u32[]{:S(2)}, u32[]{:S(2)}) collective-permute-start(f32[2,2,64,256]{3,2,1,0:T(8,128)S(1)} %dynamic-slice_bitcast_fusion.5), channel_id=1, source_target_pairs={{0,16},{16,0},{1,17},{17,1},{2,18},{18,2},{3,19},{19,3},{4,20},{20... | collective-permute-start | bytes 786440 | tf_op jit(solution)/shard_map/ppermute | solution.py:29
  98.7 9.3 %collective-permute-start.18 = (f32[2,2,64,256]{3,2,1,0:T(8,128)S(1)}, f32[2,2,64,256]{3,2,1,0:T(8,128)S(1)}, u32[]{:S(2)}, u32[]{:S(2)}) collective-permute-start(f32[2,2,64,256]{3,2,1,0:T(8,128)S(1)} %dynamic-slice_bitcast_fusion.6), channel_id=1, source_target_pairs={{0,2},{1,3},{2,0},{3,1},{4,6},{5,7},{6,4},{7,5},{8,10},{9,11},{10,... | collective-permute-start | bytes 786440 | tf_op jit(solution)/shard_map/ppermute | solution.py:29
  100.5 9.4 %collective-permute-start.17 = (bf16[2,2,192,256]{3,2,1,0:T(8,128)(2,1)S(1)}, bf16[2,2,192,256]{3,2,1,0:T(8,128)(2,1)S(1)}, u32[]{:S(2)}, u32[]{:S(2)}) collective-permute-start(bf16[2,2,192,256]{3,2,1,0:T(8,128)(2,1)S(1)} %pad_maximum_fusion.11), channel_id=1, source_target_pairs={{0,4},{1,5},{2,6},{3,7},{4,0},{5,1},{6,2},{7,3},{8,12},{9,13},{10,... | collective-permute-start | bytes 1179656 | tf_op jit(solution)/shard_map/ppermute | solution.py:29
  101.2 13.0 %collective-permute-start.16 = (bf16[2,2,192,256]{3,2,0,1:T(8,128)(2,1)S(1)}, bf16[2,2,192,256]{3,2,0,1:T(8,128)(2,1)S(1)}, u32[]{:S(2)}, u32[]{:S(2)}) collective-permute-start(bf16[2,2,192,256]{3,2,0,1:T(8,128)(2,1)S(1)} %pad_maximum_fusion.10), channel_id=1, source_target_pairs={{0,2},{1,3},{2,0},{3,1},{4,6},{5,7},{6,4},{7,5},{8,10},{9,11},{10,... | collective-permute-start | bytes 1179656 | tf_op jit(solution)/shard_map/ppermute | solution.py:29
  114.4 14.0 %collective-permute-start.21 = (bf16[2,2,2,192,256]{4,3,2,0,1:T(8,128)(2,1)S(1)}, bf16[2,2,2,192,256]{4,3,2,0,1:T(8,128)(2,1)}, u32[]{:S(2)}, u32[]{:S(2)}) collective-permute-start(bf16[2,2,2,192,256]{4,3,2,0,1:T(8,128)(2,1)S(1)} %pad_maximum_fusion.7), channel_id=1, source_target_pairs={{0,1},{1,0},{2,3},{3,2},{4,5},{5,4},{6,7},{7,6},{8,9},{9,8},{10,11... | collective-permute-start | bytes 2359304 | tf_op jit(solution)/shard_map/ppermute | solution.py:29
  114.5 5.9 %collective-permute-start.23 = (f32[2,64,256]{2,1,0:T(8,128)S(1)}, f32[2,64,256]{2,1,0:T(8,128)S(1)}, u32[]{:S(2)}, u32[]{:S(2)}) collective-permute-start(f32[2,64,256]{2,1,0:T(8,128)S(1)} %dynamic-slice_bitcast_fusion.8), channel_id=1, source_target_pairs={{0,4},{1,5},{2,6},{3,7},{4,0},{5,1},{6,2},{7,3},{8,12},{9,13},{10,... | collective-permute-start | bytes 393224 | tf_op jit(solution)/shard_map/ppermute | solution.py:29
  118.4 9.4 %collective-permute-start.22 = (f32[2,64,256]{2,1,0:T(8,128)S(1)}, f32[2,64,256]{2,1,0:T(8,128)S(1)}, u32[]{:S(2)}, u32[]{:S(2)}) collective-permute-start(f32[2,64,256]{2,1,0:T(8,128)S(1)} %dynamic-slice_bitcast_fusion.9), channel_id=1, source_target_pairs={{0,8},{1,9},{2,10},{3,11},{4,12},{5,13},{6,14},{7,15},{8,0},{9,1},... | collective-permute-start | bytes 393224 | tf_op jit(solution)/shard_map/ppermute | solution.py:29
  119.6 10.2 %collective-permute-start.20 = (bf16[2,2,2,192,256]{4,3,2,0,1:T(8,128)(2,1)S(1)}, bf16[2,2,2,192,256]{4,3,2,0,1:T(8,128)(2,1)S(1)}, u32[]{:S(2)}, u32[]{:S(2)}) collective-permute-start(bf16[2,2,2,192,256]{4,3,2,0,1:T(8,128)(2,1)S(1)} %pad_maximum_fusion.6), channel_id=1, source_target_pairs={{0,1},{1,0},{2,3},{3,2},{4,5},{5,4},{6,7},{7,6},{8,9},{9,8},{10,11... | collective-permute-start | bytes 2359304 | tf_op jit(solution)/shard_map/ppermute | solution.py:29
  131.5 0.7 copy-start.7
  132.2 4.1 %copy-start.5 = (bf16[1024,512]{1,0:T(8,128)(2,1)S(1)}, bf16[1024,512]{1,0:T(8,128)(2,1)}, u32[]{:S(2)}) copy-start(bf16[1024,512]{1,0:T(8,128)(2,1)} %param.9) | copy-start | bytes 3145732
  132.6 4.0 %copy-start.9 = (f32[2,64,256]{2,1,0:T(8,128)S(1)}, f32[2,64,256]{2,1,0:T(8,128)}, u32[]{:S(2)}) copy-start(f32[2,64,256]{2,1,0:T(8,128)} %bitcast_add_fusion.10) | copy-start | bytes 393220
  133.4 2.1 %collective-permute-start.26 = (f32[2,2,64,512]{3,2,1,0:T(8,128)}, f32[2,2,64,512]{3,2,1,0:T(8,128)S(1)}, u32[]{:S(2)}, u32[]{:S(2)}) collective-permute-start(f32[2,2,64,512]{3,2,1,0:T(8,128)} %dynamic-slice_bitcast_fusion.1), channel_id=1, source_target_pairs={{0,1},{1,0},{2,3},{3,2},{4,5},{5,4},{6,7},{7,6},{8,9},{9,8},{10,11... | collective-permute-start | bytes 1572872 | tf_op jit(solution)/shard_map/weight_grad_sum/ppermute | solution.py:29
  133.4 10.8 %copy-start.8 = (bf16[192,512]{1,0:T(8,128)(2,1)S(1)}, bf16[192,512]{1,0:T(8,128)(2,1)}, u32[]{:S(2)}) copy-start(bf16[192,512]{1,0:T(8,128)(2,1)} %copy-done.7) | copy-start | bytes 589828
  135.7 8.4 %collective-permute-start.27 = (f32[2,64,512]{2,1,0:T(8,128)S(1)}, f32[2,64,512]{2,1,0:T(8,128)S(1)}, u32[]{:S(2)}, u32[]{:S(2)}) collective-permute-start(f32[2,64,512]{2,1,0:T(8,128)S(1)} %dynamic-slice_bitcast_fusion.4), channel_id=1, source_target_pairs={{0,2},{1,3},{2,0},{3,1},{4,6},{5,7},{6,4},{7,5},{8,10},{9,11},{10,... | collective-permute-start | bytes 786440 | tf_op jit(solution)/shard_map/weight_grad_sum/ppermute | solution.py:29
  136.6 13.6 %collective-permute-start.24 = (f32[64,256]{1,0:T(8,128)S(1)}, f32[64,256]{1,0:T(8,128)S(1)}, u32[]{:S(2)}, u32[]{:S(2)}) collective-permute-start(f32[64,256]{1,0:T(8,128)S(1)} %dynamic-slice_bitcast_fusion.11), channel_id=1, source_target_pairs={{0,4},{1,5},{2,6},{3,7},{4,0},{5,1},{6,2},{7,3},{8,12},{9,13},{10,... | collective-permute-start | bytes 196616 | tf_op jit(solution)/shard_map/weight_grad_sum/ppermute | solution.py:29
  137.1 19.8 %collective-permute-start.25 = (f32[64,256]{1,0:T(8,128)S(1)}, f32[64,256]{1,0:T(8,128)S(1)}, u32[]{:S(2)}, u32[]{:S(2)}) collective-permute-start(f32[64,256]{1,0:T(8,128)S(1)} %dynamic-slice_bitcast_fusion.10), channel_id=1, source_target_pairs={{0,8},{1,9},{2,10},{3,11},{4,12},{5,13},{6,14},{7,15},{8,0},{9,1},... | collective-permute-start | bytes 196616 | tf_op jit(solution)/shard_map/weight_grad_sum/ppermute | solution.py:29
  144.1 5.0 %collective-permute-start.28 = (f32[64,512]{1,0:T(8,128)S(1)}, f32[64,512]{1,0:T(8,128)S(1)}, u32[]{:S(2)}, u32[]{:S(2)}) collective-permute-start(f32[64,512]{1,0:T(8,128)S(1)} %dynamic-slice_bitcast_fusion.7), channel_id=1, source_target_pairs={{0,4},{1,5},{2,6},{3,7},{4,0},{5,1},{6,2},{7,3},{8,12},{9,13},{10,... | collective-permute-start | bytes 393224 | tf_op jit(solution)/shard_map/weight_grad_sum/ppermute | solution.py:29
  149.2 7.1 %collective-permute-start.29 = (f32[64,512]{1,0:T(8,128)S(1)}, f32[64,512]{1,0:T(8,128)S(1)}, u32[]{:S(2)}, u32[]{:S(2)}) collective-permute-start(f32[64,512]{1,0:T(8,128)S(1)} %bitcast_add_fusion.8), channel_id=1, source_target_pairs={{0,8},{1,9},{2,10},{3,11},{4,12},{5,13},{6,14},{7,15},{8,0},{9,1},... | collective-permute-start | bytes 393224 | tf_op jit(solution)/shard_map/weight_grad_sum/ppermute | solution.py:29
  156.3 5.0 %collective-permute-start.30 = (f32[64,512]{1,0:T(8,128)S(1)}, f32[64,512]{1,0:T(8,128)S(1)}, u32[]{:S(2)}, u32[]{:S(2)}) collective-permute-start(f32[64,512]{1,0:T(8,128)S(1)} %add.191), channel_id=1, source_target_pairs={{0,16},{16,0},{1,17},{17,1},{2,18},{18,2},{3,19},{19,3},{4,20},{20... | collective-permute-start | bytes 393224 | tf_op jit(solution)/shard_map/weight_grad_sum/ppermute | solution.py:29

commit v11 on v9

--- a/solution.py
+++ b/solution.py
@@ -122,14 +122,12 @@
             owner_slots = neighbor_owner.T
             global_ids = owner_slots * node_dev + neighbor_row.T
             agg_one_cols = column_mean(node_features, global_ids, live.T, inverse_all)
-    parts, agg_one_cols = lax.optimization_barrier((parts, agg_one_cols))
-    parts, steps_done = advance(parts, steps_done)
-
     own_feats, own_agg_one = (
         lax.all_to_all(node_features, "mp", split_axis=1, concat_axis=0, tiled=True),
         lax.all_to_all(agg_one_cols, "mp", split_axis=1, concat_axis=0, tiled=True),
     )
     parts, own_agg_one = lax.optimization_barrier((parts, own_agg_one))
+    parts, steps_done = advance(parts, steps_done)
     while steps_done < len(order):
         parts, steps_done = advance(parts, steps_done)
     down_all = jnp.concatenate([p.reshape(-1, half) for p in parts], axis=1)

time: 139 us -> 141 us (1.014)
  waiting for transfers between devices: 64.9 us -> 59.5 us
  matrix products: 14.6 us -> 18.9 us
  starting transfers between devices: 33 us -> 36.1 us
    ppermute x26, waiting for transfers between devices: 59.9 us -> 50 us  [swap(): return lax.ppermute(values, axis, [(j, j ^ mask) for j in range(size)])]
    all_to_all x1, waiting for transfers between devices: 4.99 us -> 9.48 us  [shards(): lax.all_to_all(agg_one_cols, 'mp', split_axis=1, concat_axis=0, tiled=True)]
    dot_general x13, matrix products: 14.6 us -> 18.9 us  [contract(): lax.dot_general(left, right, (((left_dim,), (right_dim,)), ((), ())), pre...]
    convert_element_type x1, other arithmetic: 3.87 us -> 7.2 us  [shards(): adjacency = (rowsel[:, None, :] == row_ids).astype(jnp.bfloat16)]
    ppermute x26, starting transfers between devices: 25.7 us -> 28.8 us  [swap(): return lax.ppermute(values, axis, [(j, j ^ mask) for j in range(size)])]
  transfers between devices with their start and end apart: 28 -> 28, of which waited for: 19 -> 12; matrix products, arithmetic and copies ran while one was open for 18% -> 23% of each run, Pallas kernels for 0% -> 0%
where the time goes in v11:
time: 141 us; the launch traced here: 140 us
  waiting for transfers between devices  59.5 us (42%)
  starting transfers between devices  36.1 us (26%)
  matrix products  18.9 us (13%)
  other arithmetic  15.5 us (11%)
  local copies, waits for them, and re-layouts  8.93 us (6%)
    ppermute x26, waiting for transfers between devices, swap(): return lax.ppermute(values, axis, [(j, j ^ mask) for j in range(size)])  50 us
    ppermute x26, starting transfers between devices, swap(): return lax.ppermute(values, axis, [(j, j ^ mask) for j in range(size)])  28.8 us
    dot_general x13, matrix products, contract(): lax.dot_general(left, right, (((left_dim,), (right_dim,)), ((), ())), pre...  18.9 us
    all_to_all x1, waiting for transfers between devices, shards(): lax.all_to_all(agg_one_cols, 'mp', split_axis=1, concat_axis=0, tiled=True)  9.48 us
    convert_element_type x1, other arithmetic, shards(): adjacency = (rowsel[:, None, :] == row_ids).astype(jnp.bfloat16)  7.2 us
    all_to_all x1, starting transfers between devices, shards(): lax.all_to_all(agg_one_cols, 'mp', split_axis=1, concat_axis=0, tiled=True)  3.72 us
    all_to_all x1, starting transfers between devices, shards(): lax.all_to_all(node_features, 'mp', split_axis=1, concat_axis=0, tiled=True)  3.53 us
    add x10, other arithmetic, halving_scatter(): values = keep + got  3.09 us
  transfers between devices with their start and end apart: 28, of which 12 were waited for; matrix products, arithmetic and copies ran while one was open for 23% of the time, Pallas kernels for 0%

profile of v11, /device:TPU:0, one launch (start us, length us, event | category | flops | bytes accessed | tf_op | source)
XLA Modules:
  0.0 140.3 jit_solution(1497347171281526752)
XLA Ops:
  0.7 0.8 convert_divide_fusion
  1.6 1.4 fusion.21
  3.0 4.1 %collective-permute-start = (bf16[192,256]{1,0:T(8,128)(2,1)S(1)}, bf16[192,256]{1,0:T(8,128)(2,1)S(1)}, u32[]{:S(2)}, u32[]{:S(2)}) collective-permute-start(bf16[192,256]{1,0:T(8,128)(2,1)S(1)} %get-tuple-element.57), channel_id=1, source_target_pairs={{0,8},{1,9},{2,10},{3,11},{4,12},{5,13},{6,14},{7,15},{8,0},{9,1},... | collective-permute-start | bytes 294920 | tf_op jit(solution)/shard_map/ppermute | solution.py:29
  7.1 1.5 %collective-permute-start.1 = (bf16[192,256]{1,0:T(8,128)(2,1)S(1)}, bf16[192,256]{1,0:T(8,128)(2,1)S(1)}, u32[]{:S(2)}, u32[]{:S(2)}) collective-permute-start(bf16[192,256]{1,0:T(8,128)(2,1)S(1)} %get-tuple-element.56), channel_id=1, source_target_pairs={{0,2},{1,3},{2,0},{3,1},{4,6},{5,7},{6,4},{7,5},{8,10},{9,11},{10,... | collective-permute-start | bytes 294920 | tf_op jit(solution)/shard_map/ppermute | solution.py:29
  8.6 1.2 all_to_all.28
  9.8 0.8 copy.29
  10.7 3.5 %all-to-all-start = ((bf16[32,16,192]{2,0,1:T(8,128)(2,1)}), bf16[32,16,192]{2,0,1:T(8,128)(2,1)S(1)}, u32[]{:S(2)}, u32[]{:S(2)}) async-start(bf16[32,16,192]{2,0,1:T(8,128)(2,1)} %copy.29), calls=%async_computation | async-start | bytes 524288 | tf_op jit(solution)/shard_map/all_to_all | solution.py:126
  14.2 0.8 select_reduce_fusion
  15.2 7.2 %fusion = bf16[3072,3072]{1,0:T(8,128)(2,1)} fusion(s32[3072]{0:T(1024)S(1)} %eq.57, s32[16,3072]{1,0:T(8,128)S(1)} %select_reduce_fusion), kind=kLoop, calls=%fused_computation.1 | loop fusion | flops 18874368 | bytes 19083264 | tf_op jit(solution)/shard_map/layer_one_mean/convert_element_type | solution.py:115
  22.5 2.8 %collective-permute-start.3 = (bf16[2,192,256]{2,1,0:T(8,128)(2,1)S(1)}, bf16[2,192,256]{2,1,0:T(8,128)(2,1)S(1)}, u32[]{:S(2)}, u32[]{:S(2)}) collective-permute-start(bf16[2,192,256]{2,1,0:T(8,128)(2,1)S(1)} %get-tuple-element.9), channel_id=1, source_target_pairs={{0,8},{1,9},{2,10},{3,11},{4,12},{5,13},{6,14},{7,15},{8,0},{9,1},... | collective-permute-start | bytes 589832 | tf_op jit(solution)/shard_map/layer_one_mean/ppermute | solution.py:29
  25.3 1.5 %collective-permute-start.2 = (bf16[2,192,256]{2,1,0:T(8,128)(2,1)S(1)}, bf16[2,192,256]{2,1,0:T(8,128)(2,1)S(1)}, u32[]{:S(2)}, u32[]{:S(2)}) collective-permute-start(bf16[2,192,256]{2,1,0:T(8,128)(2,1)S(1)} %get-tuple-element.8), channel_id=1, source_target_pairs={{0,4},{1,5},{2,6},{3,7},{4,0},{5,1},{6,2},{7,3},{8,12},{9,13},{10,... | collective-permute-start | bytes 589832 | tf_op jit(solution)/shard_map/layer_one_mean/ppermute | solution.py:29
  26.8 9.7 %fusion.2 = bf16[32,3072]{1,0:T(8,128)(2,1)S(1)} fusion(bf16[32,3072]{1,0:T(8,128)(2,1)S(1)} %copy-done.3, bf16[3072,3072]{1,0:T(8,128)(2,1)} %fusion, f32[3072]{0:T(1024)S(1)} %convert_divide_fusion), kind=kOutput, calls=%fused_computation.5 | convolution fusion | flops 604176384 | bytes 19279872 | tf_op jit(solution)/shard_map/layer_one_mean/dot_general | solution.py:22
  36.5 0.3 all_to_all.32
  36.8 0.8 copy.30
  37.8 3.7 %all-to-all-start.1 = ((bf16[32,16,192]{2,0,1:T(8,128)(2,1)}), bf16[32,16,192]{2,0,1:T(8,128)(2,1)S(1)}, u32[]{:S(2)}, u32[]{:S(2)}) async-start(bf16[32,16,192]{2,0,1:T(8,128)(2,1)} %copy.30), calls=%async_computation.1 | async-start | bytes 524288 | tf_op jit(solution)/shard_map/all_to_all | solution.py:127
  41.6 0.3 fusion.24
  41.9 9.5 %all-to-all-done.1 = bf16[32,16,192]{2,0,1:T(8,128)(2,1)S(1)} async-done(((bf16[32,16,192]{2,0,1:T(8,128)(2,1)}), bf16[32,16,192]{2,0,1:T(8,128)(2,1)S(1)}, u32[]{:S(2)}, u32[]{:S(2)}) %all-to-all-start.1) | async-done | bytes 196640 | tf_op jit(solution)/shard_map/all_to_all | solution.py:127
  51.3 1.0 multiply_convert_fusion
  52.4 1.1 collective-permute-start.4
  53.6 0.5 bitcast_compare_fusion.1
  54.1 6.0 %collective-permute-done.4 = bf16[192,256]{1,0:T(8,128)(2,1)S(1)} collective-permute-done((bf16[192,256]{1,0:T(8,128)(2,1)S(1)}, bf16[192,256]{1,0:T(8,128)(2,1)S(1)}, u32[]{:S(2)}, u32[]{:S(2)}) %collective-permute-start.4) | collective-permute-done | bytes 98336 | tf_op jit(solution)/shard_map/ppermute | solution.py:29
  60.2 0.3 fusion.37
  60.6 2.1 %collective-permute-start.14 = (bf16[2,2,192,256]{3,2,1,0:T(8,128)(2,1)S(1)}, bf16[2,2,192,256]{3,2,1,0:T(8,128)(2,1)S(1)}, u32[]{:S(2)}, u32[]{:S(2)}) collective-permute-start(bf16[2,2,192,256]{3,2,1,0:T(8,128)(2,1)S(1)} %pad_maximum_fusion.10), channel_id=1, source_target_pairs={{0,4},{1,5},{2,6},{3,7},{4,0},{5,1},{6,2},{7,3},{8,12},{9,13},{10,... | collective-permute-start | bytes 1179656 | tf_op jit(solution)/shard_map/ppermute | solution.py:29
  62.7 0.7 collective-permute-start.9
  63.3 8.8 %collective-permute-done.5 = bf16[2,192,256]{2,1,0:T(8,128)(2,1)S(1)} collective-permute-done((bf16[2,192,256]{2,1,0:T(8,128)(2,1)S(1)}, bf16[2,192,256]{2,1,0:T(8,128)(2,1)S(1)}, u32[]{:S(2)}, u32[]{:S(2)}) %collective-permute-start.5) | collective-permute-done | bytes 196640 | tf_op jit(solution)/shard_map/ppermute | solution.py:29
  72.3 4.8 %collective-permute-done.9 = bf16[2,192,256]{2,1,0:T(8,128)(2,1)S(1)} collective-permute-done((bf16[2,192,256]{2,1,0:T(8,128)(2,1)S(1)}, bf16[2,192,256]{2,1,0:T(8,128)(2,1)S(1)}, u32[]{:S(2)}, u32[]{:S(2)}) %collective-permute-start.9) | collective-permute-done | bytes 196640 | tf_op jit(solution)/shard_map/ppermute | solution.py:29
  77.2 2.6 %collective-permute-start.10 = (bf16[2,2,192,256]{3,2,1,0:T(8,128)(2,1)S(1)}, bf16[2,2,192,256]{3,2,1,0:T(8,128)(2,1)S(1)}, u32[]{:S(2)}, u32[]{:S(2)}) collective-permute-start(bf16[2,2,192,256]{3,2,1,0:T(8,128)(2,1)S(1)} %pad_maximum_fusion.12), channel_id=1, source_target_pairs={{0,4},{1,5},{2,6},{3,7},{4,0},{5,1},{6,2},{7,3},{8,12},{9,13},{10,... | collective-permute-start | bytes 1179656 | tf_op jit(solution)/shard_map/ppermute | solution.py:29
  80.2 0.5 collective-permute-start.15
  81.0 7.3 %collective-permute-done.10 = bf16[2,2,192,256]{3,2,1,0:T(8,128)(2,1)S(1)} collective-permute-done((bf16[2,2,192,256]{3,2,1,0:T(8,128)(2,1)S(1)}, bf16[2,2,192,256]{3,2,1,0:T(8,128)(2,1)S(1)}, u32[]{:S(2)}, u32[]{:S(2)}) %collective-permute-start.10) | collective-permute-done | bytes 393248 | tf_op jit(solution)/shard_map/ppermute | solution.py:29
  88.7 0.1 pad_maximum_fusion.3
  89.4 1.6 %fusion.7 = f32[192,512]{1,0:T(8,128)S(1)} fusion(bf16[3072,256]{1,0:T(8,128)(2,1)S(1)} %bitcast.153, bf16[3072,256]{1,0:T(8,128)(2,1)S(1)} %bitcast.151, s32[3072]{0:T(1024)S(1)} %bitcast.156), kind=kOutput, calls=%fused_computation.10 | convolution fusion | flops 610861056 | bytes 3551232 | tf_op jit(solution)/shard_map/dot_general | solution.py:22
  91.0 0.4 fusion.20
  91.4 0.3 convolution_bitcast_fusion
  91.7 0.3 fusion.36
  92.5 0.1 pad_maximum_fusion.2
  92.8 1.1 fusion.17
  94.0 0.7 copy-done.6
  94.7 0.3 fusion.38
  95.0 0.4 pad_maximum_fusion
  95.4 0.3 fusion.33
  95.8 1.3 copy-done.1
  97.1 1.1 dynamic-slice_bitcast_fusion
  98.2 0.5 collective-permute-start.16
  98.7 0.2 constant_dynamic-slice_fusion.1
  98.9 1.0 copy.43
  100.0 1.3 fusion.27
  101.3 1.4 bitcast_add_fusion.1
  102.8 1.5 %collective-permute-start.17 = (f32[2,2,2,64,256]{4,3,2,1,0:T(8,128)S(1)}, f32[2,2,2,64,256]{4,3,2,1,0:T(8,128)S(1)}, u32[]{:S(2)}, u32[]{:S(2)}) collective-permute-start(f32[2,2,2,64,256]{4,3,2,1,0:T(8,128)S(1)} %dynamic-slice_bitcast_fusion.2), channel_id=1, source_target_pairs={{0,16},{16,0},{1,17},{17,1},{2,18},{18,2},{3,19},{19,3},{4,20},{20... | collective-permute-start | bytes 1572872 | tf_op jit(solution)/shard_map/weight_grad_sum/ppermute | solution.py:29
  104.3 1.5 %bitcast_add_fusion = f32[2,2,2,2,64,256]{5,4,2,1,0,3:T(8,128)S(1)} fusion(f32[2,2,2,2,64,256]{5,4,2,1,0,3:T(8,128)} %collective-permute-done.21, f32[2,2,2,2,1,64,256]{6,5,4,3,2,1,0:T(8,128)S(1)} %get-tuple-element.16), kind=kLoop, calls=%fused_computation.35 | loop fusion | flops 262144 | bytes 3145728 | tf_op jit(solution)/shard_map/weight_grad_sum/add | solution.py:45
  105.8 1.3 collective-permute-start.22
  107.1 0.9 fusion.22
  108.1 9.0 %collective-permute-done.17 = f32[2,2,2,64,256]{4,3,2,1,0:T(8,128)S(1)} collective-permute-done((f32[2,2,2,64,256]{4,3,2,1,0:T(8,128)S(1)}, f32[2,2,2,64,256]{4,3,2,1,0:T(8,128)S(1)}, u32[]{:S(2)}, u32[]{:S(2)}) %collective-permute-start.17) | collective-permute-done | bytes 524320 | tf_op jit(solution)/shard_map/weight_grad_sum/ppermute | solution.py:29
  117.2 1.3 collective-permute-start.18
  118.5 1.8 %collective-permute-done.22 = f32[2,2,2,64,256]{4,3,2,1,0:T(8,128)S(1)} collective-permute-done((f32[2,2,2,64,256]{4,3,2,1,0:T(8,128)S(1)}, f32[2,2,2,64,256]{4,3,2,1,0:T(8,128)S(1)}, u32[]{:S(2)}, u32[]{:S(2)}) %collective-permute-start.22) | collective-permute-done | bytes 524320 | tf_op jit(solution)/shard_map/weight_grad_sum/ppermute | solution.py:29
  120.3 0.3 collective-permute-start.23
  120.6 4.9 %collective-permute-done.18 = f32[2,2,64,256]{3,2,1,0:T(8,128)S(1)} collective-permute-done((f32[2,2,64,256]{3,2,1,0:T(8,128)S(1)}, f32[2,2,64,256]{3,2,1,0:T(8,128)S(1)}, u32[]{:S(2)}, u32[]{:S(2)}) %collective-permute-start.18) | collective-permute-done | bytes 262176 | tf_op jit(solution)/shard_map/weight_grad_sum/ppermute | solution.py:29
  125.6 2.5 %collective-permute-start.19 = (f32[2,64,256]{2,1,0:T(8,128)S(1)}, f32[2,64,256]{2,1,0:T(8,128)S(1)}, u32[]{:S(2)}, u32[]{:S(2)}) collective-permute-start(f32[2,64,256]{2,1,0:T(8,128)S(1)} %dynamic-slice_bitcast_fusion.6), channel_id=1, source_target_pairs={{0,8},{1,9},{2,10},{3,11},{4,12},{5,13},{6,14},{7,15},{8,0},{9,1},... | collective-permute-start | bytes 393224 | tf_op jit(solution)/shard_map/weight_grad_sum/ppermute | solution.py:29
  128.2 1.3 collective-permute-start.24
  129.5 4.5 %collective-permute-done.19 = f32[2,64,256]{2,1,0:T(8,128)S(1)} collective-permute-done((f32[2,64,256]{2,1,0:T(8,128)S(1)}, f32[2,64,256]{2,1,0:T(8,128)S(1)}, u32[]{:S(2)}, u32[]{:S(2)}) %collective-permute-start.19) | collective-permute-done | bytes 131104 | tf_op jit(solution)/shard_map/weight_grad_sum/ppermute | solution.py:29
  134.0 0.3 collective-permute-start.20
  134.4 2.4 %collective-permute-start.25 = (f32[64,256]{1,0:T(8,128)S(1)}, f32[64,256]{1,0:T(8,128)S(1)}, u32[]{:S(2)}, u32[]{:S(2)}) collective-permute-start(f32[64,256]{1,0:T(8,128)S(1)} %dynamic-slice_bitcast_fusion.7), channel_id=1, source_target_pairs={{0,8},{1,9},{2,10},{3,11},{4,12},{5,13},{6,14},{7,15},{8,0},{9,1},... | collective-permute-start | bytes 196616 | tf_op jit(solution)/shard_map/weight_grad_sum/ppermute | solution.py:29
  136.9 1.5 %collective-permute-done.20 = f32[64,256]{1,0:T(8,128)S(1)} collective-permute-done((f32[64,256]{1,0:T(8,128)S(1)}, f32[64,256]{1,0:T(8,128)S(1)}, u32[]{:S(2)}, u32[]{:S(2)}) %collective-permute-start.20) | collective-permute-done | bytes 65568 | tf_op jit(solution)/shard_map/weight_grad_sum/ppermute | solution.py:29
  138.4 1.3 collective-permute-done.25
  139.7 0.7 pad_maximum_fusion.17
  (104 shorter events, 3.7 us)
Async XLA Ops:
  0.6 0.9 copy-start
  0.6 13.5 %copy-start.11 = (s32[3072]{0:T(1024)S(1)}, s32[3072]{0:T(1024)}, u32[]{:S(2)}) copy-start(s32[3072]{0:T(1024)} %param.12) | copy-start | bytes 36868
  0.7 13.6 %copy-start.10 = (s32[3072,8]{0,1:T(8,128)S(1)}, s32[3072,8]{0,1:T(8,128)}, u32[]{:S(2)}) copy-start(s32[3072,8]{0,1:T(8,128)} %param.10) | copy-start | bytes 294916
  0.7 13.6 %copy-start.9 = (s32[3072,8]{0,1:T(8,128)S(1)}, s32[3072,8]{0,1:T(8,128)}, u32[]{:S(2)}) copy-start(s32[3072,8]{0,1:T(8,128)} %param.11) | copy-start | bytes 294916
  3.0 19.5 %collective-permute-start = (bf16[192,256]{1,0:T(8,128)(2,1)S(1)}, bf16[192,256]{1,0:T(8,128)(2,1)S(1)}, u32[]{:S(2)}, u32[]{:S(2)}) collective-permute-start(bf16[192,256]{1,0:T(8,128)(2,1)S(1)} %get-tuple-element.57), channel_id=1, source_target_pairs={{0,8},{1,9},{2,10},{3,11},{4,12},{5,13},{6,14},{7,15},{8,0},{9,1},... | collective-permute-start | bytes 294920 | tf_op jit(solution)/shard_map/ppermute | solution.py:29
  7.1 15.4 %collective-permute-start.1 = (bf16[192,256]{1,0:T(8,128)(2,1)S(1)}, bf16[192,256]{1,0:T(8,128)(2,1)S(1)}, u32[]{:S(2)}, u32[]{:S(2)}) collective-permute-start(bf16[192,256]{1,0:T(8,128)(2,1)S(1)} %get-tuple-element.56), channel_id=1, source_target_pairs={{0,2},{1,3},{2,0},{3,1},{4,6},{5,7},{6,4},{7,5},{8,10},{9,11},{10,... | collective-permute-start | bytes 294920 | tf_op jit(solution)/shard_map/ppermute | solution.py:29
  10.7 27.1 %all-to-all-start = ((bf16[32,16,192]{2,0,1:T(8,128)(2,1)}), bf16[32,16,192]{2,0,1:T(8,128)(2,1)S(1)}, u32[]{:S(2)}, u32[]{:S(2)}) async-start(bf16[32,16,192]{2,0,1:T(8,128)(2,1)} %copy.29), calls=%async_computation | async-start | bytes 524288 | tf_op jit(solution)/shard_map/all_to_all | solution.py:126
  15.2 11.6 %copy-start.3 = (bf16[32,3072]{1,0:T(8,128)(2,1)S(1)}, bf16[32,3072]{1,0:T(8,128)(2,1)}, u32[]{:S(2)}) copy-start(bf16[32,3072]{1,0:T(8,128)(2,1)} %param.7) | copy-start | bytes 589828
  22.5 15.1 %collective-permute-start.3 = (bf16[2,192,256]{2,1,0:T(8,128)(2,1)S(1)}, bf16[2,192,256]{2,1,0:T(8,128)(2,1)S(1)}, u32[]{:S(2)}, u32[]{:S(2)}) collective-permute-start(bf16[2,192,256]{2,1,0:T(8,128)(2,1)S(1)} %get-tuple-element.9), channel_id=1, source_target_pairs={{0,8},{1,9},{2,10},{3,11},{4,12},{5,13},{6,14},{7,15},{8,0},{9,1},... | collective-permute-start | bytes 589832 | tf_op jit(solution)/shard_map/layer_one_mean/ppermute | solution.py:29
  25.3 12.4 %collective-permute-start.2 = (bf16[2,192,256]{2,1,0:T(8,128)(2,1)S(1)}, bf16[2,192,256]{2,1,0:T(8,128)(2,1)S(1)}, u32[]{:S(2)}, u32[]{:S(2)}) collective-permute-start(bf16[2,192,256]{2,1,0:T(8,128)(2,1)S(1)} %get-tuple-element.8), channel_id=1, source_target_pairs={{0,4},{1,5},{2,6},{3,7},{4,0},{5,1},{6,2},{7,3},{8,12},{9,13},{10,... | collective-permute-start | bytes 589832 | tf_op jit(solution)/shard_map/layer_one_mean/ppermute | solution.py:29
  36.8 4.7 %copy-start.8 = (bf16[1024,512]{1,0:T(8,128)(2,1)S(1)}, bf16[1024,512]{1,0:T(8,128)(2,1)}, u32[]{:S(2)}) copy-start(bf16[1024,512]{1,0:T(8,128)(2,1)} %param.8) | copy-start | bytes 3145732
  37.8 13.6 %all-to-all-start.1 = ((bf16[32,16,192]{2,0,1:T(8,128)(2,1)}), bf16[32,16,192]{2,0,1:T(8,128)(2,1)S(1)}, u32[]{:S(2)}, u32[]{:S(2)}) async-start(bf16[32,16,192]{2,0,1:T(8,128)(2,1)} %copy.30), calls=%async_computation.1 | async-start | bytes 524288 | tf_op jit(solution)/shard_map/all_to_all | solution.py:127
  52.4 7.6 %collective-permute-start.4 = (bf16[192,256]{1,0:T(8,128)(2,1)S(1)}, bf16[192,256]{1,0:T(8,128)(2,1)S(1)}, u32[]{:S(2)}, u32[]{:S(2)}) collective-permute-start(bf16[192,256]{1,0:T(8,128)(2,1)S(1)} %get-tuple-element.52), channel_id=1, source_target_pairs={{0,8},{1,9},{2,10},{3,11},{4,12},{5,13},{6,14},{7,15},{8,0},{9,1},... | collective-permute-start | bytes 294920 | tf_op jit(solution)/shard_map/ppermute | solution.py:29
  53.5 6.5 %collective-permute-start.8 = (bf16[192,256]{1,0:T(8,128)(2,1)S(1)}, bf16[192,256]{1,0:T(8,128)(2,1)S(1)}, u32[]{:S(2)}, u32[]{:S(2)}) collective-permute-start(bf16[192,256]{1,0:T(8,128)(2,1)S(1)} %get-tuple-element.53), channel_id=1, source_target_pairs={{0,2},{1,3},{2,0},{3,1},{4,6},{5,7},{6,4},{7,5},{8,10},{9,11},{10,... | collective-permute-start | bytes 294920 | tf_op jit(solution)/shard_map/ppermute | solution.py:29
  60.1 12.1 %collective-permute-start.5 = (bf16[2,192,256]{2,1,0:T(8,128)(2,1)S(1)}, bf16[2,192,256]{2,1,0:T(8,128)(2,1)S(1)}, u32[]{:S(2)}, u32[]{:S(2)}) collective-permute-start(bf16[2,192,256]{2,1,0:T(8,128)(2,1)S(1)} %pad_maximum_fusion.15), channel_id=1, source_target_pairs={{0,4},{1,5},{2,6},{3,7},{4,0},{5,1},{6,2},{7,3},{8,12},{9,13},{10,... | collective-permute-start | bytes 589832 | tf_op jit(solution)/shard_map/ppermute | solution.py:29
  60.5 19.3 %collective-permute-start.12 = (bf16[2,2,192,256]{3,2,0,1:T(8,128)(2,1)S(1)}, bf16[2,2,192,256]{3,2,0,1:T(8,128)(2,1)S(1)}, u32[]{:S(2)}, u32[]{:S(2)}) collective-permute-start(bf16[2,2,192,256]{3,2,0,1:T(8,128)(2,1)S(1)} %pad_maximum_fusion.9), channel_id=1, source_target_pairs={{0,2},{1,3},{2,0},{3,1},{4,6},{5,7},{6,4},{7,5},{8,10},{9,11},{10,... | collective-permute-start | bytes 1179656 | tf_op jit(solution)/shard_map/ppermute | solution.py:29
  60.6 19.5 %collective-permute-start.14 = (bf16[2,2,192,256]{3,2,1,0:T(8,128)(2,1)S(1)}, bf16[2,2,192,256]{3,2,1,0:T(8,128)(2,1)S(1)}, u32[]{:S(2)}, u32[]{:S(2)}) collective-permute-start(bf16[2,2,192,256]{3,2,1,0:T(8,128)(2,1)S(1)} %pad_maximum_fusion.10), channel_id=1, source_target_pairs={{0,4},{1,5},{2,6},{3,7},{4,0},{5,1},{6,2},{7,3},{8,12},{9,13},{10,... | collective-permute-start | bytes 1179656 | tf_op jit(solution)/shard_map/ppermute | solution.py:29
  62.7 14.4 %collective-permute-start.9 = (bf16[2,192,256]{2,1,0:T(8,128)(2,1)S(1)}, bf16[2,192,256]{2,1,0:T(8,128)(2,1)S(1)}, u32[]{:S(2)}, u32[]{:S(2)}) collective-permute-start(bf16[2,192,256]{2,1,0:T(8,128)(2,1)S(1)} %pad_maximum_fusion.16), channel_id=1, source_target_pairs={{0,8},{1,9},{2,10},{3,11},{4,12},{5,13},{6,14},{7,15},{8,0},{9,1},... | collective-permute-start | bytes 589832 | tf_op jit(solution)/shard_map/ppermute | solution.py:29
  72.2 8.5 %collective-permute-start.6 = (bf16[2,2,192,256]{3,2,0,1:T(8,128)(2,1)S(1)}, bf16[2,2,192,256]{3,2,0,1:T(8,128)(2,1)S(1)}, u32[]{:S(2)}, u32[]{:S(2)}) collective-permute-start(bf16[2,2,192,256]{3,2,0,1:T(8,128)(2,1)S(1)} %pad_maximum_fusion.11), channel_id=1, source_target_pairs={{0,2},{1,3},{2,0},{3,1},{4,6},{5,7},{6,4},{7,5},{8,10},{9,11},{10,... | collective-permute-start | bytes 1179656 | tf_op jit(solution)/shard_map/ppermute | solution.py:29
  77.2 11.1 %collective-permute-start.10 = (bf16[2,2,192,256]{3,2,1,0:T(8,128)(2,1)S(1)}, bf16[2,2,192,256]{3,2,1,0:T(8,128)(2,1)S(1)}, u32[]{:S(2)}, u32[]{:S(2)}) collective-permute-start(bf16[2,2,192,256]{3,2,1,0:T(8,128)(2,1)S(1)} %pad_maximum_fusion.12), channel_id=1, source_target_pairs={{0,4},{1,5},{2,6},{3,7},{4,0},{5,1},{6,2},{7,3},{8,12},{9,13},{10,... | collective-permute-start | bytes 1179656 | tf_op jit(solution)/shard_map/ppermute | solution.py:29
  80.0 8.6 %collective-permute-start.13 = (bf16[2,2,2,192,256]{4,3,0,1,2:T(8,128)(2,1)S(1)}, bf16[2,2,2,192,256]{4,3,0,1,2:T(8,128)(2,1)S(1)}, u32[]{:S(2)}, u32[]{:S(2)}) collective-permute-start(bf16[2,2,2,192,256]{4,3,0,1,2:T(8,128)(2,1)S(1)} %pad_maximum_fusion.7), channel_id=1, source_target_pairs={{0,1},{1,0},{2,3},{3,2},{4,5},{5,4},{6,7},{7,6},{8,9},{9,8},{10,11... | collective-permute-start | bytes 2359304 | tf_op jit(solution)/shard_map/ppermute | solution.py:29
  80.2 8.8 %collective-permute-start.15 = (bf16[2,2,2,192,256]{4,3,2,0,1:T(8,128)(2,1)S(1)}, bf16[2,2,2,192,256]{4,3,2,0,1:T(8,128)(2,1)S(1)}, u32[]{:S(2)}, u32[]{:S(2)}) collective-permute-start(bf16[2,2,2,192,256]{4,3,2,0,1:T(8,128)(2,1)S(1)} %pad_maximum_fusion.8), channel_id=1, source_target_pairs={{0,1},{1,0},{2,3},{3,2},{4,5},{5,4},{6,7},{7,6},{8,9},{9,8},{10,11... | collective-permute-start | bytes 2359304 | tf_op jit(solution)/shard_map/ppermute | solution.py:29
  80.9 11.1 %collective-permute-start.7 = (bf16[2,2,2,192,256]{4,3,0,1,2:T(8,128)(2,1)S(1)}, bf16[2,2,2,192,256]{4,3,0,1,2:T(8,128)(2,1)S(1)}, u32[]{:S(2)}, u32[]{:S(2)}) collective-permute-start(bf16[2,2,2,192,256]{4,3,0,1,2:T(8,128)(2,1)S(1)} %pad_maximum_fusion.5), channel_id=1, source_target_pairs={{0,1},{1,0},{2,3},{3,2},{4,5},{5,4},{6,7},{7,6},{8,9},{9,8},{10,11... | collective-permute-start | bytes 2359304 | tf_op jit(solution)/shard_map/ppermute | solution.py:29
  88.5 3.9 %collective-permute-start.11 = (bf16[2,2,2,192,256]{4,3,2,0,1:T(8,128)(2,1)S(1)}, bf16[2,2,2,192,256]{4,3,2,0,1:T(8,128)(2,1)S(1)}, u32[]{:S(2)}, u32[]{:S(2)}) collective-permute-start(bf16[2,2,2,192,256]{4,3,2,0,1:T(8,128)(2,1)S(1)} %pad_maximum_fusion.6), channel_id=1, source_target_pairs={{0,1},{1,0},{2,3},{3,2},{4,5},{5,4},{6,7},{7,6},{8,9},{9,8},{10,11... | collective-permute-start | bytes 2359304 | tf_op jit(solution)/shard_map/ppermute | solution.py:29
  89.4 1.6 %copy-start.4 = (bf16[1024,512]{1,0:T(8,128)(2,1)S(1)}, bf16[1024,512]{1,0:T(8,128)(2,1)}, u32[]{:S(2)}) copy-start(bf16[1024,512]{1,0:T(8,128)(2,1)} %param.9) | copy-start | bytes 3145732
  89.4 1.6 %copy-start.12 = (f32[192,512]{1,0:T(8,128)S(1)}, f32[192,512]{1,0:T(8,128)}, u32[]{:S(2)}) copy-start(f32[192,512]{1,0:T(8,128)} %get-tuple-element.59) | copy-start | bytes 1179652
  94.0 0.7 copy-start.6
  95.8 1.4 copy-start.1
  98.2 3.1 %collective-permute-start.16 = (f32[2,2,2,2,64,256]{5,4,3,2,1,0:T(8,128)}, f32[2,2,2,2,64,256]{5,4,3,2,1,0:T(8,128)}, u32[]{:S(2)}, u32[]{:S(2)}) collective-permute-start(f32[2,2,2,2,64,256]{5,4,3,2,1,0:T(8,128)} %dynamic-slice_bitcast_fusion), channel_id=1, source_target_pairs={{0,1},{1,0},{2,3},{3,2},{4,5},{5,4},{6,7},{7,6},{8,9},{9,8},{10,11... | collective-permute-start | bytes 3145736 | tf_op jit(solution)/shard_map/weight_grad_sum/ppermute | solution.py:29
  98.9 2.5 %copy-start.2 = (f32[2048,256]{1,0:T(8,128)S(1)}, f32[2048,256]{1,0:T(8,128)}, u32[]{:S(2)}) copy-start(f32[2048,256]{1,0:T(8,128)} %copy-done.1) | copy-start | bytes 6291460
  99.9 4.4 %collective-permute-start.21 = (f32[2,2,2,2,64,256]{5,4,2,1,0,3:T(8,128)}, f32[2,2,2,2,64,256]{5,4,2,1,0,3:T(8,128)}, u32[]{:S(2)}, u32[]{:S(2)}) collective-permute-start(f32[2,2,2,2,64,256]{5,4,2,1,0,3:T(8,128)} %bitcast.144), channel_id=1, source_target_pairs={{0,1},{1,0},{2,3},{3,2},{4,5},{5,4},{6,7},{7,6},{8,9},{9,8},{10,11... | collective-permute-start | bytes 3145736 | tf_op jit(solution)/shard_map/weight_grad_sum/ppermute | solution.py:29
  102.8 14.3 %collective-permute-start.17 = (f32[2,2,2,64,256]{4,3,2,1,0:T(8,128)S(1)}, f32[2,2,2,64,256]{4,3,2,1,0:T(8,128)S(1)}, u32[]{:S(2)}, u32[]{:S(2)}) collective-permute-start(f32[2,2,2,64,256]{4,3,2,1,0:T(8,128)S(1)} %dynamic-slice_bitcast_fusion.2), channel_id=1, source_target_pairs={{0,16},{16,0},{1,17},{17,1},{2,18},{18,2},{3,19},{19,3},{4,20},{20... | collective-permute-start | bytes 1572872 | tf_op jit(solution)/shard_map/weight_grad_sum/ppermute | solution.py:29
  104.3 2.8 %copy-start.5 = (bf16[1024,512]{1,0:T(8,128)(2,1)S(1)}, bf16[1024,512]{1,0:T(8,128)(2,1)}, u32[]{:S(2)}) copy-start(bf16[1024,512]{1,0:T(8,128)(2,1)} %param.9) | copy-start | bytes 3145732
  104.3 2.8 %copy-start.7 = (bf16[192,512]{1,0:T(8,128)(2,1)S(1)}, bf16[192,512]{1,0:T(8,128)(2,1)}, u32[]{:S(2)}) copy-start(bf16[192,512]{1,0:T(8,128)(2,1)} %copy-done.6) | copy-start | bytes 589828
  105.8 14.4 %collective-permute-start.22 = (f32[2,2,2,64,256]{4,3,2,1,0:T(8,128)S(1)}, f32[2,2,2,64,256]{4,3,2,1,0:T(8,128)S(1)}, u32[]{:S(2)}, u32[]{:S(2)}) collective-permute-start(f32[2,2,2,64,256]{4,3,2,1,0:T(8,128)S(1)} %dynamic-slice_bitcast_fusion.1), channel_id=1, source_target_pairs={{0,2},{1,3},{2,0},{3,1},{4,6},{5,7},{6,4},{7,5},{8,10},{9,11},{10,... | collective-permute-start | bytes 1572872 | tf_op jit(solution)/shard_map/weight_grad_sum/ppermute | solution.py:29
  117.2 8.3 %collective-permute-start.18 = (f32[2,2,64,256]{3,2,1,0:T(8,128)S(1)}, f32[2,2,64,256]{3,2,1,0:T(8,128)S(1)}, u32[]{:S(2)}, u32[]{:S(2)}) collective-permute-start(f32[2,2,64,256]{3,2,1,0:T(8,128)S(1)} %dynamic-slice_bitcast_fusion.4), channel_id=1, source_target_pairs={{0,2},{1,3},{2,0},{3,1},{4,6},{5,7},{6,4},{7,5},{8,10},{9,11},{10,... | collective-permute-start | bytes 786440 | tf_op jit(solution)/shard_map/weight_grad_sum/ppermute | solution.py:29
  120.3 7.8 %collective-permute-start.23 = (f32[2,2,64,256]{3,2,1,0:T(8,128)S(1)}, f32[2,2,64,256]{3,2,1,0:T(8,128)S(1)}, u32[]{:S(2)}, u32[]{:S(2)}) collective-permute-start(f32[2,2,64,256]{3,2,1,0:T(8,128)S(1)} %dynamic-slice_bitcast_fusion.3), channel_id=1, source_target_pairs={{0,16},{16,0},{1,17},{17,1},{2,18},{18,2},{3,19},{19,3},{4,20},{20... | collective-permute-start | bytes 786440 | tf_op jit(solution)/shard_map/weight_grad_sum/ppermute | solution.py:29
  125.6 8.4 %collective-permute-start.19 = (f32[2,64,256]{2,1,0:T(8,128)S(1)}, f32[2,64,256]{2,1,0:T(8,128)S(1)}, u32[]{:S(2)}, u32[]{:S(2)}) collective-permute-start(f32[2,64,256]{2,1,0:T(8,128)S(1)} %dynamic-slice_bitcast_fusion.6), channel_id=1, source_target_pairs={{0,8},{1,9},{2,10},{3,11},{4,12},{5,13},{6,14},{7,15},{8,0},{9,1},... | collective-permute-start | bytes 393224 | tf_op jit(solution)/shard_map/weight_grad_sum/ppermute | solution.py:29
  128.2 6.2 %collective-permute-start.24 = (f32[2,64,256]{2,1,0:T(8,128)S(1)}, f32[2,64,256]{2,1,0:T(8,128)S(1)}, u32[]{:S(2)}, u32[]{:S(2)}) collective-permute-start(f32[2,64,256]{2,1,0:T(8,128)S(1)} %dynamic-slice_bitcast_fusion.5), channel_id=1, source_target_pairs={{0,4},{1,5},{2,6},{3,7},{4,0},{5,1},{6,2},{7,3},{8,12},{9,13},{10,... | collective-permute-start | bytes 393224 | tf_op jit(solution)/shard_map/weight_grad_sum/ppermute | solution.py:29
  134.0 4.3 %collective-permute-start.20 = (f32[64,256]{1,0:T(8,128)S(1)}, f32[64,256]{1,0:T(8,128)S(1)}, u32[]{:S(2)}, u32[]{:S(2)}) collective-permute-start(f32[64,256]{1,0:T(8,128)S(1)} %dynamic-slice_bitcast_fusion.8), channel_id=1, source_target_pairs={{0,4},{1,5},{2,6},{3,7},{4,0},{5,1},{6,2},{7,3},{8,12},{9,13},{10,... | collective-permute-start | bytes 196616 | tf_op jit(solution)/shard_map/weight_grad_sum/ppermute | solution.py:29
  134.4 5.2 %collective-permute-start.25 = (f32[64,256]{1,0:T(8,128)S(1)}, f32[64,256]{1,0:T(8,128)S(1)}, u32[]{:S(2)}, u32[]{:S(2)}) collective-permute-start(f32[64,256]{1,0:T(8,128)S(1)} %dynamic-slice_bitcast_fusion.7), channel_id=1, source_target_pairs={{0,8},{1,9},{2,10},{3,11},{4,12},{5,13},{6,14},{7,15},{8,0},{9,1},... | collective-permute-start | bytes 196616 | tf_op jit(solution)/shard_map/weight_grad_sum/ppermute | solution.py:29

commit v12 on v9

--- a/solution.py
+++ b/solution.py
@@ -130,9 +130,6 @@
         lax.all_to_all(agg_one_cols, "mp", split_axis=1, concat_axis=0, tiled=True),
     )
     parts, own_agg_one = lax.optimization_barrier((parts, own_agg_one))
-    while steps_done < len(order):
-        parts, steps_done = advance(parts, steps_done)
-    down_all = jnp.concatenate([p.reshape(-1, half) for p in parts], axis=1)
 
     with jax.named_scope("neighbor_tables"):
         row_ids = lax.broadcasted_iota(jnp.int32, (1, node_dev, 1), 1)
@@ -146,7 +143,15 @@
         own_agg_one, weights_one[feat_width:], 0, 0
     )
     hidden_one = jax.nn.silu(pre_one).astype(jnp.bfloat16)
-    hidden_all = split_gather(hidden_one, order, other)
+    hparts = [hidden_one[:, :half], hidden_one[:, half:]]
+    hparts = [doubling_step(p, o, 0) for p, o in zip(hparts, orders)]
+    hparts, parts = lax.optimization_barrier((hparts, parts))
+    while steps_done < len(order):
+        parts, steps_done = advance(parts, steps_done)
+    for step in range(1, len(order)):
+        hparts = [doubling_step(p, o, step) for p, o in zip(hparts, orders)]
+    hidden_all = jnp.concatenate([p.reshape(-1, half) for p in hparts], axis=1)
+    down_all = jnp.concatenate([p.reshape(-1, half) for p in parts], axis=1)
     total = contract(own_edges, hidden_all, 0, 0)
     agg_two = (total * own_inverse[:, None]).astype(jnp.bfloat16)
     node_output = (

time: 139 us -> 136 us (0.978)
  starting transfers between devices: 33 us -> 30.6 us
    ppermute x26, starting transfers between devices: 25.7 us -> 23.3 us  [swap(): return lax.ppermute(values, axis, [(j, j ^ mask) for j in range(size)])]
    unnamed x26 -> x28, local copies, waits for them, and re-layouts: 3.07 us -> 2.42 us
where the time goes in v12:
time: 136 us; the launch traced here: 135 us
  waiting for transfers between devices  65.7 us (48%)
  starting transfers between devices  30.6 us (22%)
  matrix products  15.4 us (11%)
  other arithmetic  13.1 us (10%)
  local copies, waits for them, and re-layouts  9.17 us (7%)
  between operations  1.38 us (1%)
    ppermute x26, waiting for transfers between devices, swap(): return lax.ppermute(values, axis, [(j, j ^ mask) for j in range(size)])  59.9 us
    ppermute x26, starting transfers between devices, swap(): return lax.ppermute(values, axis, [(j, j ^ mask) for j in range(size)])  23.3 us
    dot_general x13, matrix products, contract(): lax.dot_general(left, right, (((left_dim,), (right_dim,)), ((), ())), pre...  15.4 us
    all_to_all x1, waiting for transfers between devices, shards(): lax.all_to_all(agg_one_cols, 'mp', split_axis=1, concat_axis=0, tiled=True)  5.82 us
    convert_element_type x1, other arithmetic, shards(): adjacency = (rowsel[:, None, :] == row_ids).astype(jnp.bfloat16)  3.87 us
    all_to_all x1, starting transfers between devices, shards(): lax.all_to_all(agg_one_cols, 'mp', split_axis=1, concat_axis=0, tiled=True)  3.77 us
    all_to_all x1, starting transfers between devices, shards(): lax.all_to_all(node_features, 'mp', split_axis=1, concat_axis=0, tiled=True)  3.53 us
    add x10, other arithmetic, halving_scatter(): values = keep + got  3.09 us
  transfers between devices with their start and end apart: 28, of which 19 were waited for; matrix products, arithmetic and copies ran while one was open for 18% of the time, Pallas kernels for 0%

profile of v12, /device:TPU:0, one launch (start us, length us, event | category | flops | bytes accessed | tf_op | source)
XLA Modules:
  0.0 135.3 jit_solution(17648339066246796679)
XLA Ops:
  0.7 0.8 convert_divide_fusion
  1.6 1.4 %fusion.21 = bf16[192,512]{1,0:T(8,128)(2,1)S(1)} fusion(bf16[192,512]{1,0:T(8,128)(2,1)S(1)} %copy-done, bf16[1024,512]{1,0:T(8,128)(2,1)} %param.9, f32[192]{0:T(256)S(1)} %dynamic_slice.78), kind=kOutput, calls=%fused_computation.33 | convolution fusion | flops 100859904 | bytes 918272 | tf_op jit(solution)/shard_map/dot_general | solution.py:22
  3.0 4.1 %collective-permute-start = (bf16[192,256]{1,0:T(8,128)(2,1)S(1)}, bf16[192,256]{1,0:T(8,128)(2,1)S(1)}, u32[]{:S(2)}, u32[]{:S(2)}) collective-permute-start(bf16[192,256]{1,0:T(8,128)(2,1)S(1)} %get-tuple-element.71), channel_id=1, source_target_pairs={{0,8},{1,9},{2,10},{3,11},{4,12},{5,13},{6,14},{7,15},{8,0},{9,1},... | collective-permute-start | bytes 294920 | tf_op jit(solution)/shard_map/ppermute | solution.py:29
  7.1 1.5 %collective-permute-start.1 = (bf16[192,256]{1,0:T(8,128)(2,1)S(1)}, bf16[192,256]{1,0:T(8,128)(2,1)S(1)}, u32[]{:S(2)}, u32[]{:S(2)}) collective-permute-start(bf16[192,256]{1,0:T(8,128)(2,1)S(1)} %get-tuple-element.70), channel_id=1, source_target_pairs={{0,2},{1,3},{2,0},{3,1},{4,6},{5,7},{6,4},{7,5},{8,10},{9,11},{10,... | collective-permute-start | bytes 294920 | tf_op jit(solution)/shard_map/ppermute | solution.py:29
  8.6 1.2 all_to_all.28
  9.8 0.8 copy.29
  10.6 3.5 %all-to-all-start = ((bf16[32,16,192]{2,0,1:T(8,128)(2,1)}), bf16[32,16,192]{2,0,1:T(8,128)(2,1)S(1)}, u32[]{:S(2)}, u32[]{:S(2)}) async-start(bf16[32,16,192]{2,0,1:T(8,128)(2,1)} %copy.29), calls=%async_computation | async-start | bytes 524288 | tf_op jit(solution)/shard_map/all_to_all | solution.py:129
  14.3 0.8 select_reduce_fusion
  15.2 3.9 %fusion = bf16[3072,3072]{1,0:T(8,128)(2,1)S(1)} fusion(s32[3072]{0:T(1024)S(1)} %eq.57, s32[16,3072]{1,0:T(8,128)S(1)} %select_reduce_fusion), kind=kLoop, calls=%fused_computation.1 | loop fusion | flops 18874368 | bytes 19083264 | tf_op jit(solution)/shard_map/layer_one_mean/convert_element_type | solution.py:115
  19.1 2.8 %collective-permute-start.3 = (bf16[2,192,256]{2,1,0:T(8,128)(2,1)S(1)}, bf16[2,192,256]{2,1,0:T(8,128)(2,1)S(1)}, u32[]{:S(2)}, u32[]{:S(2)}) collective-permute-start(bf16[2,192,256]{2,1,0:T(8,128)(2,1)S(1)} %get-tuple-element.16), channel_id=1, source_target_pairs={{0,8},{1,9},{2,10},{3,11},{4,12},{5,13},{6,14},{7,15},{8,0},{9,1},... | collective-permute-start | bytes 589832 | tf_op jit(solution)/shard_map/layer_one_mean/ppermute | solution.py:29
  22.0 1.5 %collective-permute-start.2 = (bf16[2,192,256]{2,1,0:T(8,128)(2,1)S(1)}, bf16[2,192,256]{2,1,0:T(8,128)(2,1)S(1)}, u32[]{:S(2)}, u32[]{:S(2)}) collective-permute-start(bf16[2,192,256]{2,1,0:T(8,128)(2,1)S(1)} %get-tuple-element.15), channel_id=1, source_target_pairs={{0,4},{1,5},{2,6},{3,7},{4,0},{5,1},{6,2},{7,3},{8,12},{9,13},{10,... | collective-permute-start | bytes 589832 | tf_op jit(solution)/shard_map/layer_one_mean/ppermute | solution.py:29
  23.4 3.4 %fusion.2 = bf16[32,3072]{1,0:T(8,128)(2,1)S(1)} fusion(bf16[32,3072]{1,0:T(8,128)(2,1)S(1)} %copy-done.3, bf16[3072,3072]{1,0:T(8,128)(2,1)S(1)} %fusion, f32[3072]{0:T(1024)S(1)} %convert_divide_fusion), kind=kOutput, calls=%fused_computation.5 | convolution fusion | flops 604176384 | bytes 19279872 | tf_op jit(solution)/shard_map/layer_one_mean/dot_general | solution.py:22
  26.8 5.5 %collective-permute-done.3 = bf16[2,192,256]{2,1,0:T(8,128)(2,1)S(1)} collective-permute-done((bf16[2,192,256]{2,1,0:T(8,128)(2,1)S(1)}, bf16[2,192,256]{2,1,0:T(8,128)(2,1)S(1)}, u32[]{:S(2)}, u32[]{:S(2)}) %collective-permute-start.3) | collective-permute-done | bytes 196640 | tf_op jit(solution)/shard_map/layer_one_mean/ppermute | solution.py:29
  32.5 0.9 collective-permute-start.5
  33.4 1.5 %collective-permute-start.4 = (bf16[2,2,192,256]{3,2,0,1:T(8,128)(2,1)S(1)}, bf16[2,2,192,256]{3,2,0,1:T(8,128)(2,1)S(1)}, u32[]{:S(2)}, u32[]{:S(2)}) collective-permute-start(bf16[2,2,192,256]{3,2,0,1:T(8,128)(2,1)S(1)} %pad_maximum_fusion.9), channel_id=1, source_target_pairs={{0,2},{1,3},{2,0},{3,1},{4,6},{5,7},{6,4},{7,5},{8,10},{9,11},{10,... | collective-permute-start | bytes 1179656 | tf_op jit(solution)/shard_map/ppermute | solution.py:29
  34.8 0.3 all_to_all.32
  35.1 0.8 copy.30
  35.9 3.8 %all-to-all-start.1 = ((bf16[32,16,192]{2,0,1:T(8,128)(2,1)}), bf16[32,16,192]{2,0,1:T(8,128)(2,1)S(1)}, u32[]{:S(2)}, u32[]{:S(2)}) async-start(bf16[32,16,192]{2,0,1:T(8,128)(2,1)} %copy.30), calls=%async_computation.1 | async-start | bytes 524288 | tf_op jit(solution)/shard_map/all_to_all | solution.py:130
  39.7 2.1 %fusion.24 = f32[192,512]{1,0:T(8,128)} fusion(bf16[512,192]{1,0:T(8,128)(2,1)S(1)} %bitcast.148, bf16[1024,512]{1,0:T(8,128)(2,1)} %param.8), kind=kOutput, calls=%fused_computation.56 | convolution fusion | flops 100663296 | bytes 1114112 | tf_op jit(solution)/shard_map/dot_general | solution.py:22
  41.8 1.6 %collective-permute-done.5 = bf16[2,2,192,256]{3,2,1,0:T(8,128)(2,1)S(1)} collective-permute-done((bf16[2,2,192,256]{3,2,1,0:T(8,128)(2,1)S(1)}, bf16[2,2,192,256]{3,2,1,0:T(8,128)(2,1)S(1)}, u32[]{:S(2)}, u32[]{:S(2)}) %collective-permute-start.5) | collective-permute-done | bytes 393248 | tf_op jit(solution)/shard_map/ppermute | solution.py:29
  43.9 5.8 %all-to-all-done.1 = bf16[32,16,192]{2,0,1:T(8,128)(2,1)S(1)} async-done(((bf16[32,16,192]{2,0,1:T(8,128)(2,1)}), bf16[32,16,192]{2,0,1:T(8,128)(2,1)S(1)}, u32[]{:S(2)}, u32[]{:S(2)}) %all-to-all-start.1) | async-done | bytes 196640 | tf_op jit(solution)/shard_map/all_to_all | solution.py:130
  49.7 2.1 %multiply_convert_fusion = (bf16[192,512]{1,0:T(8,128)(2,1)S(1)}, f32[192,512]{1,0:T(8,128)}) fusion(f32[192,512]{1,0:T(8,128)S(1)} %copy-done.9, bf16[512,192]{1,0:T(8,128)(2,1)S(1)} %bitcast.154, bf16[1024,512]{1,0:T(8,128)(2,1)} %param.8), kind=kOutput, calls=%fused_computation.71 | convolution fusion | flops 101253120 | bytes 1703936 | tf_op jit(solution)/shard_map/dot_general | solution.py:22
  51.8 1.1 collective-permute-start.6
  53.0 1.4 %bitcast_compare_fusion.1 = pred[3072,192]{1,0:T(32,128)(4,1)} fusion(s32[3072]{0:T(1024)S(1)} %eq.57, s32[16,192]{1,0:T(8,128)S(1)} %constant_dynamic-slice_fusion.3), kind=kLoop, calls=%fused_computation.14 | loop fusion | flops 589824 | bytes 614400 | tf_op jit(solution)/shard_map/neighbor_tables/eq | solution.py:137
  54.4 5.0 %collective-permute-done.6 = bf16[192,256]{1,0:T(8,128)(2,1)S(1)} collective-permute-done((bf16[192,256]{1,0:T(8,128)(2,1)S(1)}, bf16[192,256]{1,0:T(8,128)(2,1)S(1)}, u32[]{:S(2)}, u32[]{:S(2)}) %collective-permute-start.6) | collective-permute-done | bytes 98336 | tf_op jit(solution)/shard_map/ppermute | solution.py:29
  59.7 2.1 %collective-permute-start.11 = (bf16[2,192,256]{2,1,0:T(8,128)(2,1)S(1)}, bf16[2,192,256]{2,1,0:T(8,128)(2,1)S(1)}, u32[]{:S(2)}, u32[]{:S(2)}) collective-permute-start(bf16[2,192,256]{2,1,0:T(8,128)(2,1)S(1)} %pad_maximum_fusion.16), channel_id=1, source_target_pairs={{0,8},{1,9},{2,10},{3,11},{4,12},{5,13},{6,14},{7,15},{8,0},{9,1},... | collective-permute-start | bytes 589832 | tf_op jit(solution)/shard_map/ppermute | solution.py:29
  61.9 6.8 %collective-permute-done.8 = bf16[2,192,256]{2,1,0:T(8,128)(2,1)S(1)} collective-permute-done((bf16[2,192,256]{2,1,0:T(8,128)(2,1)S(1)}, bf16[2,192,256]{2,1,0:T(8,128)(2,1)S(1)}, u32[]{:S(2)}, u32[]{:S(2)}) %collective-permute-start.8) | collective-permute-done | bytes 196640 | tf_op jit(solution)/shard_map/ppermute | solution.py:29
  68.8 1.2 collective-permute-start.9
  69.9 2.3 %collective-permute-done.11 = bf16[2,192,256]{2,1,0:T(8,128)(2,1)S(1)} collective-permute-done((bf16[2,192,256]{2,1,0:T(8,128)(2,1)S(1)}, bf16[2,192,256]{2,1,0:T(8,128)(2,1)S(1)}, u32[]{:S(2)}, u32[]{:S(2)}) %collective-permute-start.11) | collective-permute-done | bytes 196640 | tf_op jit(solution)/shard_map/ppermute | solution.py:29
  72.4 0.3 fusion.37
  72.8 5.9 %collective-permute-done.9 = bf16[2,2,192,256]{3,2,0,1:T(8,128)(2,1)S(1)} collective-permute-done((bf16[2,2,192,256]{3,2,0,1:T(8,128)(2,1)S(1)}, bf16[2,2,192,256]{3,2,0,1:T(8,128)(2,1)S(1)}, u32[]{:S(2)}, u32[]{:S(2)}) %collective-permute-start.9) | collective-permute-done | bytes 393248 | tf_op jit(solution)/shard_map/ppermute | solution.py:29
  78.9 4.1 %collective-permute-done.12 = bf16[2,2,192,256]{3,2,1,0:T(8,128)(2,1)S(1)} collective-permute-done((bf16[2,2,192,256]{3,2,1,0:T(8,128)(2,1)S(1)}, bf16[2,2,192,256]{3,2,1,0:T(8,128)(2,1)S(1)}, u32[]{:S(2)}, u32[]{:S(2)}) %collective-permute-start.12) | collective-permute-done | bytes 393248 | tf_op jit(solution)/shard_map/ppermute | solution.py:29
  84.1 1.6 %fusion.7 = f32[192,512]{1,0:T(8,128)S(1)} fusion(bf16[3072,256]{1,0:T(8,128)(2,1)S(1)} %bitcast.153, bf16[3072,256]{1,0:T(8,128)(2,1)S(1)} %bitcast.151, s32[3072]{0:T(1024)S(1)} %bitcast.156), kind=kOutput, calls=%fused_computation.10 | convolution fusion | flops 610861056 | bytes 3551232 | tf_op jit(solution)/shard_map/dot_general | solution.py:22
  85.7 0.4 fusion.20
  86.1 0.3 convolution_bitcast_fusion
  86.4 0.3 fusion.36
  87.5 1.0 copy-done.6
  88.5 1.1 fusion.17
  89.6 0.3 fusion.38
  90.0 0.4 pad_maximum_fusion
  90.4 0.3 fusion.33
  90.8 1.4 %copy-done.1 = f32[2048,256]{1,0:T(8,128)} copy-done((f32[2048,256]{1,0:T(8,128)}, f32[2048,256]{1,0:T(8,128)S(1)}, u32[]{:S(2)}) %copy-start.1) | copy-done | bytes 2097176
  92.1 1.1 dynamic-slice_bitcast_fusion
  93.2 0.5 collective-permute-start.16
  93.9 1.0 copy.43
  95.0 1.3 fusion.27
  96.3 1.4 %bitcast_add_fusion.1 = f32[2,2,2,2,64,256]{5,4,3,2,1,0:T(8,128)S(1)} fusion(f32[2,2,2,2,64,256]{5,4,3,2,1,0:T(8,128)} %collective-permute-done.16, f32[2,2,2,2,2,64,256]{6,5,4,3,2,1,0:T(8,128)S(1)} %bitcast.147, s32[]{:T(128)S(6)} %select_n.252), kind=kLoop, calls=%fused_computation.36 | loop fusion | flops 262144 | bytes 3145732 | tf_op jit(solution)/shard_map/weight_grad_sum/add | solution.py:45
  97.8 1.6 %collective-permute-start.17 = (f32[2,2,2,64,256]{4,3,2,1,0:T(8,128)S(1)}, f32[2,2,2,64,256]{4,3,2,1,0:T(8,128)S(1)}, u32[]{:S(2)}, u32[]{:S(2)}) collective-permute-start(f32[2,2,2,64,256]{4,3,2,1,0:T(8,128)S(1)} %dynamic-slice_bitcast_fusion.2), channel_id=1, source_target_pairs={{0,16},{16,0},{1,17},{17,1},{2,18},{18,2},{3,19},{19,3},{4,20},{20... | collective-permute-start | bytes 1572872 | tf_op jit(solution)/shard_map/weight_grad_sum/ppermute | solution.py:29
  99.3 1.5 %bitcast_add_fusion = f32[2,2,2,2,64,256]{5,4,2,1,0,3:T(8,128)S(1)} fusion(f32[2,2,2,2,64,256]{5,4,2,1,0,3:T(8,128)} %collective-permute-done.21, f32[2,2,2,2,1,64,256]{6,5,4,3,2,1,0:T(8,128)S(1)} %get-tuple-element.30), kind=kLoop, calls=%fused_computation.35 | loop fusion | flops 262144 | bytes 3145728 | tf_op jit(solution)/shard_map/weight_grad_sum/add | solution.py:45
  100.8 0.3 collective-permute-start.22
  101.2 1.0 fusion.22
  102.1 9.9 %collective-permute-done.17 = f32[2,2,2,64,256]{4,3,2,1,0:T(8,128)S(1)} collective-permute-done((f32[2,2,2,64,256]{4,3,2,1,0:T(8,128)S(1)}, f32[2,2,2,64,256]{4,3,2,1,0:T(8,128)S(1)}, u32[]{:S(2)}, u32[]{:S(2)}) %collective-permute-start.17) | collective-permute-done | bytes 524320 | tf_op jit(solution)/shard_map/weight_grad_sum/ppermute | solution.py:29
  112.2 0.3 collective-permute-start.18
  112.5 2.7 %collective-permute-done.22 = f32[2,2,2,64,256]{4,3,2,1,0:T(8,128)S(1)} collective-permute-done((f32[2,2,2,64,256]{4,3,2,1,0:T(8,128)S(1)}, f32[2,2,2,64,256]{4,3,2,1,0:T(8,128)S(1)}, u32[]{:S(2)}, u32[]{:S(2)}) %collective-permute-start.22) | collective-permute-done | bytes 524320 | tf_op jit(solution)/shard_map/weight_grad_sum/ppermute | solution.py:29
  115.6 4.9 %collective-permute-done.18 = f32[2,2,64,256]{3,2,1,0:T(8,128)S(1)} collective-permute-done((f32[2,2,64,256]{3,2,1,0:T(8,128)S(1)}, f32[2,2,64,256]{3,2,1,0:T(8,128)S(1)}, u32[]{:S(2)}, u32[]{:S(2)}) %collective-permute-start.18) | collective-permute-done | bytes 262176 | tf_op jit(solution)/shard_map/weight_grad_sum/ppermute | solution.py:29
  120.6 0.7 collective-permute-start.19
  121.3 1.3 collective-permute-done.23
  122.7 0.5 collective-permute-start.24
  123.2 5.5 %collective-permute-done.19 = f32[2,64,256]{2,1,0:T(8,128)S(1)} collective-permute-done((f32[2,64,256]{2,1,0:T(8,128)S(1)}, f32[2,64,256]{2,1,0:T(8,128)S(1)}, u32[]{:S(2)}, u32[]{:S(2)}) %collective-permute-start.19) | collective-permute-done | bytes 131104 | tf_op jit(solution)/shard_map/weight_grad_sum/ppermute | solution.py:29
  128.8 0.6 collective-permute-done.24
  129.4 1.9 %collective-permute-start.25 = (f32[64,256]{1,0:T(8,128)S(1)}, f32[64,256]{1,0:T(8,128)S(1)}, u32[]{:S(2)}, u32[]{:S(2)}) collective-permute-start(f32[64,256]{1,0:T(8,128)S(1)} %dynamic-slice_bitcast_fusion.7), channel_id=1, source_target_pairs={{0,8},{1,9},{2,10},{3,11},{4,12},{5,13},{6,14},{7,15},{8,0},{9,1},... | collective-permute-start | bytes 196616 | tf_op jit(solution)/shard_map/weight_grad_sum/ppermute | solution.py:29
  131.2 2.0 %collective-permute-done.20 = f32[64,256]{1,0:T(8,128)S(1)} collective-permute-done((f32[64,256]{1,0:T(8,128)S(1)}, f32[64,256]{1,0:T(8,128)S(1)}, u32[]{:S(2)}, u32[]{:S(2)}) %collective-permute-start.20) | collective-permute-done | bytes 65568 | tf_op jit(solution)/shard_map/weight_grad_sum/ppermute | solution.py:29
  133.3 1.4 %collective-permute-done.25 = f32[64,256]{1,0:T(8,128)S(1)} collective-permute-done((f32[64,256]{1,0:T(8,128)S(1)}, f32[64,256]{1,0:T(8,128)S(1)}, u32[]{:S(2)}, u32[]{:S(2)}) %collective-permute-start.25) | collective-permute-done | bytes 65568 | tf_op jit(solution)/shard_map/weight_grad_sum/ppermute | solution.py:29
  134.6 0.7 pad_maximum_fusion.17
  (106 shorter events, 4.7 us)
Async XLA Ops:
  0.6 0.9 copy-start
  0.6 13.5 %copy-start.12 = (s32[3072]{0:T(1024)S(1)}, s32[3072]{0:T(1024)}, u32[]{:S(2)}) copy-start(s32[3072]{0:T(1024)} %param.12) | copy-start | bytes 36868
  0.7 13.6 %copy-start.11 = (s32[3072,8]{0,1:T(8,128)S(1)}, s32[3072,8]{0,1:T(8,128)}, u32[]{:S(2)}) copy-start(s32[3072,8]{0,1:T(8,128)} %param.10) | copy-start | bytes 294916
  0.7 13.6 %copy-start.10 = (s32[3072,8]{0,1:T(8,128)S(1)}, s32[3072,8]{0,1:T(8,128)}, u32[]{:S(2)}) copy-start(s32[3072,8]{0,1:T(8,128)} %param.11) | copy-start | bytes 294916
  3.0 16.1 %collective-permute-start = (bf16[192,256]{1,0:T(8,128)(2,1)S(1)}, bf16[192,256]{1,0:T(8,128)(2,1)S(1)}, u32[]{:S(2)}, u32[]{:S(2)}) collective-permute-start(bf16[192,256]{1,0:T(8,128)(2,1)S(1)} %get-tuple-element.71), channel_id=1, source_target_pairs={{0,8},{1,9},{2,10},{3,11},{4,12},{5,13},{6,14},{7,15},{8,0},{9,1},... | collective-permute-start | bytes 294920 | tf_op jit(solution)/shard_map/ppermute | solution.py:29
  7.1 12.0 %collective-permute-start.1 = (bf16[192,256]{1,0:T(8,128)(2,1)S(1)}, bf16[192,256]{1,0:T(8,128)(2,1)S(1)}, u32[]{:S(2)}, u32[]{:S(2)}) collective-permute-start(bf16[192,256]{1,0:T(8,128)(2,1)S(1)} %get-tuple-element.70), channel_id=1, source_target_pairs={{0,2},{1,3},{2,0},{3,1},{4,6},{5,7},{6,4},{7,5},{8,10},{9,11},{10,... | collective-permute-start | bytes 294920 | tf_op jit(solution)/shard_map/ppermute | solution.py:29
  10.6 25.3 %all-to-all-start = ((bf16[32,16,192]{2,0,1:T(8,128)(2,1)}), bf16[32,16,192]{2,0,1:T(8,128)(2,1)S(1)}, u32[]{:S(2)}, u32[]{:S(2)}) async-start(bf16[32,16,192]{2,0,1:T(8,128)(2,1)} %copy.29), calls=%async_computation | async-start | bytes 524288 | tf_op jit(solution)/shard_map/all_to_all | solution.py:129
  15.1 8.3 %copy-start.3 = (bf16[32,3072]{1,0:T(8,128)(2,1)S(1)}, bf16[32,3072]{1,0:T(8,128)(2,1)}, u32[]{:S(2)}) copy-start(bf16[32,3072]{1,0:T(8,128)(2,1)} %param.7) | copy-start | bytes 589828
  19.1 13.1 %collective-permute-start.3 = (bf16[2,192,256]{2,1,0:T(8,128)(2,1)S(1)}, bf16[2,192,256]{2,1,0:T(8,128)(2,1)S(1)}, u32[]{:S(2)}, u32[]{:S(2)}) collective-permute-start(bf16[2,192,256]{2,1,0:T(8,128)(2,1)S(1)} %get-tuple-element.16), channel_id=1, source_target_pairs={{0,8},{1,9},{2,10},{3,11},{4,12},{5,13},{6,14},{7,15},{8,0},{9,1},... | collective-permute-start | bytes 589832 | tf_op jit(solution)/shard_map/layer_one_mean/ppermute | solution.py:29
  22.0 10.4 %collective-permute-start.2 = (bf16[2,192,256]{2,1,0:T(8,128)(2,1)S(1)}, bf16[2,192,256]{2,1,0:T(8,128)(2,1)S(1)}, u32[]{:S(2)}, u32[]{:S(2)}) collective-permute-start(bf16[2,192,256]{2,1,0:T(8,128)(2,1)S(1)} %get-tuple-element.15), channel_id=1, source_target_pairs={{0,4},{1,5},{2,6},{3,7},{4,0},{5,1},{6,2},{7,3},{8,12},{9,13},{10,... | collective-permute-start | bytes 589832 | tf_op jit(solution)/shard_map/layer_one_mean/ppermute | solution.py:29
  32.5 10.8 %collective-permute-start.5 = (bf16[2,2,192,256]{3,2,1,0:T(8,128)(2,1)S(1)}, bf16[2,2,192,256]{3,2,1,0:T(8,128)(2,1)S(1)}, u32[]{:S(2)}, u32[]{:S(2)}) collective-permute-start(bf16[2,2,192,256]{3,2,1,0:T(8,128)(2,1)S(1)} %pad_maximum_fusion.10), channel_id=1, source_target_pairs={{0,4},{1,5},{2,6},{3,7},{4,0},{5,1},{6,2},{7,3},{8,12},{9,13},{10,... | collective-permute-start | bytes 1179656 | tf_op jit(solution)/shard_map/ppermute | solution.py:29
  33.4 10.4 %collective-permute-start.4 = (bf16[2,2,192,256]{3,2,0,1:T(8,128)(2,1)S(1)}, bf16[2,2,192,256]{3,2,0,1:T(8,128)(2,1)S(1)}, u32[]{:S(2)}, u32[]{:S(2)}) collective-permute-start(bf16[2,2,192,256]{3,2,0,1:T(8,128)(2,1)S(1)} %pad_maximum_fusion.9), channel_id=1, source_target_pairs={{0,2},{1,3},{2,0},{3,1},{4,6},{5,7},{6,4},{7,5},{8,10},{9,11},{10,... | collective-permute-start | bytes 1179656 | tf_op jit(solution)/shard_map/ppermute | solution.py:29
  35.9 13.8 %all-to-all-start.1 = ((bf16[32,16,192]{2,0,1:T(8,128)(2,1)}), bf16[32,16,192]{2,0,1:T(8,128)(2,1)S(1)}, u32[]{:S(2)}, u32[]{:S(2)}) async-start(bf16[32,16,192]{2,0,1:T(8,128)(2,1)} %copy.30), calls=%async_computation.1 | async-start | bytes 524288 | tf_op jit(solution)/shard_map/all_to_all | solution.py:130
  43.4 6.3 %copy-start.9 = (f32[192,512]{1,0:T(8,128)S(1)}, f32[192,512]{1,0:T(8,128)}, u32[]{:S(2)}) copy-start(f32[192,512]{1,0:T(8,128)} %fusion.24) | copy-start | bytes 1179652
  51.8 7.6 %collective-permute-start.6 = (bf16[192,256]{1,0:T(8,128)(2,1)S(1)}, bf16[192,256]{1,0:T(8,128)(2,1)S(1)}, u32[]{:S(2)}, u32[]{:S(2)}) collective-permute-start(bf16[192,256]{1,0:T(8,128)(2,1)S(1)} %get-tuple-element.67), channel_id=1, source_target_pairs={{0,8},{1,9},{2,10},{3,11},{4,12},{5,13},{6,14},{7,15},{8,0},{9,1},... | collective-permute-start | bytes 294920 | tf_op jit(solution)/shard_map/ppermute | solution.py:29
  53.0 6.5 %collective-permute-start.7 = (bf16[192,256]{1,0:T(8,128)(2,1)S(1)}, bf16[192,256]{1,0:T(8,128)(2,1)S(1)}, u32[]{:S(2)}, u32[]{:S(2)}) collective-permute-start(bf16[192,256]{1,0:T(8,128)(2,1)S(1)} %get-tuple-element.66), channel_id=1, source_target_pairs={{0,2},{1,3},{2,0},{3,1},{4,6},{5,7},{6,4},{7,5},{8,10},{9,11},{10,... | collective-permute-start | bytes 294920 | tf_op jit(solution)/shard_map/ppermute | solution.py:29
  59.6 9.1 %collective-permute-start.8 = (bf16[2,192,256]{2,1,0:T(8,128)(2,1)S(1)}, bf16[2,192,256]{2,1,0:T(8,128)(2,1)S(1)}, u32[]{:S(2)}, u32[]{:S(2)}) collective-permute-start(bf16[2,192,256]{2,1,0:T(8,128)(2,1)S(1)} %pad_maximum_fusion.15), channel_id=1, source_target_pairs={{0,4},{1,5},{2,6},{3,7},{4,0},{5,1},{6,2},{7,3},{8,12},{9,13},{10,... | collective-permute-start | bytes 589832 | tf_op jit(solution)/shard_map/ppermute | solution.py:29
  59.7 23.6 %collective-permute-start.14 = (bf16[2,2,2,192,256]{4,3,0,1,2:T(8,128)(2,1)S(1)}, bf16[2,2,2,192,256]{4,3,0,1,2:T(8,128)(2,1)S(1)}, u32[]{:S(2)}, u32[]{:S(2)}) collective-permute-start(bf16[2,2,2,192,256]{4,3,0,1,2:T(8,128)(2,1)S(1)} %pad_maximum_fusion.5), channel_id=1, source_target_pairs={{0,1},{1,0},{2,3},{3,2},{4,5},{5,4},{6,7},{7,6},{8,9},{9,8},{10,11... | collective-permute-start | bytes 2359304 | tf_op jit(solution)/shard_map/ppermute | solution.py:29
  59.7 12.5 %collective-permute-start.11 = (bf16[2,192,256]{2,1,0:T(8,128)(2,1)S(1)}, bf16[2,192,256]{2,1,0:T(8,128)(2,1)S(1)}, u32[]{:S(2)}, u32[]{:S(2)}) collective-permute-start(bf16[2,192,256]{2,1,0:T(8,128)(2,1)S(1)} %pad_maximum_fusion.16), channel_id=1, source_target_pairs={{0,8},{1,9},{2,10},{3,11},{4,12},{5,13},{6,14},{7,15},{8,0},{9,1},... | collective-permute-start | bytes 589832 | tf_op jit(solution)/shard_map/ppermute | solution.py:29
  68.8 9.9 %collective-permute-start.9 = (bf16[2,2,192,256]{3,2,0,1:T(8,128)(2,1)S(1)}, bf16[2,2,192,256]{3,2,0,1:T(8,128)(2,1)S(1)}, u32[]{:S(2)}, u32[]{:S(2)}) collective-permute-start(bf16[2,2,192,256]{3,2,0,1:T(8,128)(2,1)S(1)} %pad_maximum_fusion.11), channel_id=1, source_target_pairs={{0,2},{1,3},{2,0},{3,1},{4,6},{5,7},{6,4},{7,5},{8,10},{9,11},{10,... | collective-permute-start | bytes 1179656 | tf_op jit(solution)/shard_map/ppermute | solution.py:29
  72.3 10.7 %collective-permute-start.12 = (bf16[2,2,192,256]{3,2,1,0:T(8,128)(2,1)S(1)}, bf16[2,2,192,256]{3,2,1,0:T(8,128)(2,1)S(1)}, u32[]{:S(2)}, u32[]{:S(2)}) collective-permute-start(bf16[2,2,192,256]{3,2,1,0:T(8,128)(2,1)S(1)} %pad_maximum_fusion.12), channel_id=1, source_target_pairs={{0,4},{1,5},{2,6},{3,7},{4,0},{5,1},{6,2},{7,3},{8,12},{9,13},{10,... | collective-permute-start | bytes 1179656 | tf_op jit(solution)/shard_map/ppermute | solution.py:29
  72.7 11.0 %collective-permute-start.15 = (bf16[2,2,2,192,256]{4,3,2,0,1:T(8,128)(2,1)S(1)}, bf16[2,2,2,192,256]{4,3,2,0,1:T(8,128)(2,1)S(1)}, u32[]{:S(2)}, u32[]{:S(2)}) collective-permute-start(bf16[2,2,2,192,256]{4,3,2,0,1:T(8,128)(2,1)S(1)} %pad_maximum_fusion.6), channel_id=1, source_target_pairs={{0,1},{1,0},{2,3},{3,2},{4,5},{5,4},{6,7},{7,6},{8,9},{9,8},{10,11... | collective-permute-start | bytes 2359304 | tf_op jit(solution)/shard_map/ppermute | solution.py:29
  78.8 7.8 %collective-permute-start.10 = (bf16[2,2,2,192,256]{4,3,0,1,2:T(8,128)(2,1)S(1)}, bf16[2,2,2,192,256]{4,3,0,1,2:T(8,128)(2,1)S(1)}, u32[]{:S(2)}, u32[]{:S(2)}) collective-permute-start(bf16[2,2,2,192,256]{4,3,0,1,2:T(8,128)(2,1)S(1)} %pad_maximum_fusion.7), channel_id=1, source_target_pairs={{0,1},{1,0},{2,3},{3,2},{4,5},{5,4},{6,7},{7,6},{8,9},{9,8},{10,11... | collective-permute-start | bytes 2359304 | tf_op jit(solution)/shard_map/ppermute | solution.py:29
  83.2 3.9 %collective-permute-start.13 = (bf16[2,2,2,192,256]{4,3,2,0,1:T(8,128)(2,1)S(1)}, bf16[2,2,2,192,256]{4,3,2,0,1:T(8,128)(2,1)S(1)}, u32[]{:S(2)}, u32[]{:S(2)}) collective-permute-start(bf16[2,2,2,192,256]{4,3,2,0,1:T(8,128)(2,1)S(1)} %pad_maximum_fusion.8), channel_id=1, source_target_pairs={{0,1},{1,0},{2,3},{3,2},{4,5},{5,4},{6,7},{7,6},{8,9},{9,8},{10,11... | collective-permute-start | bytes 2359304 | tf_op jit(solution)/shard_map/ppermute | solution.py:29
  84.1 1.6 %copy-start.4 = (bf16[1024,512]{1,0:T(8,128)(2,1)S(1)}, bf16[1024,512]{1,0:T(8,128)(2,1)}, u32[]{:S(2)}) copy-start(bf16[1024,512]{1,0:T(8,128)(2,1)} %param.9) | copy-start | bytes 3145732
  84.1 1.6 %copy-start.13 = (f32[192,512]{1,0:T(8,128)S(1)}, f32[192,512]{1,0:T(8,128)}, u32[]{:S(2)}) copy-start(f32[192,512]{1,0:T(8,128)} %get-tuple-element.73) | copy-start | bytes 1179652
  87.4 1.1 copy-start.6
  89.6 0.8 copy-start.7
  90.8 1.4 %copy-start.1 = (f32[2048,256]{1,0:T(8,128)}, f32[2048,256]{1,0:T(8,128)S(1)}, u32[]{:S(2)}) copy-start(f32[2048,256]{1,0:T(8,128)S(1)} %get-tuple-element.28) | copy-start | bytes 6291460
  93.2 3.1 %collective-permute-start.16 = (f32[2,2,2,2,64,256]{5,4,3,2,1,0:T(8,128)}, f32[2,2,2,2,64,256]{5,4,3,2,1,0:T(8,128)}, u32[]{:S(2)}, u32[]{:S(2)}) collective-permute-start(f32[2,2,2,2,64,256]{5,4,3,2,1,0:T(8,128)} %dynamic-slice_bitcast_fusion), channel_id=1, source_target_pairs={{0,1},{1,0},{2,3},{3,2},{4,5},{5,4},{6,7},{7,6},{8,9},{9,8},{10,11... | collective-permute-start | bytes 3145736 | tf_op jit(solution)/shard_map/weight_grad_sum/ppermute | solution.py:29
  93.9 2.5 %copy-start.2 = (f32[2048,256]{1,0:T(8,128)S(1)}, f32[2048,256]{1,0:T(8,128)}, u32[]{:S(2)}) copy-start(f32[2048,256]{1,0:T(8,128)} %copy-done.1) | copy-start | bytes 6291460
  94.9 4.4 %collective-permute-start.21 = (f32[2,2,2,2,64,256]{5,4,2,1,0,3:T(8,128)}, f32[2,2,2,2,64,256]{5,4,2,1,0,3:T(8,128)}, u32[]{:S(2)}, u32[]{:S(2)}) collective-permute-start(f32[2,2,2,2,64,256]{5,4,2,1,0,3:T(8,128)} %bitcast.144), channel_id=1, source_target_pairs={{0,1},{1,0},{2,3},{3,2},{4,5},{5,4},{6,7},{7,6},{8,9},{9,8},{10,11... | collective-permute-start | bytes 3145736 | tf_op jit(solution)/shard_map/weight_grad_sum/ppermute | solution.py:29
  97.8 14.3 %collective-permute-start.17 = (f32[2,2,2,64,256]{4,3,2,1,0:T(8,128)S(1)}, f32[2,2,2,64,256]{4,3,2,1,0:T(8,128)S(1)}, u32[]{:S(2)}, u32[]{:S(2)}) collective-permute-start(f32[2,2,2,64,256]{4,3,2,1,0:T(8,128)S(1)} %dynamic-slice_bitcast_fusion.2), channel_id=1, source_target_pairs={{0,16},{16,0},{1,17},{17,1},{2,18},{18,2},{3,19},{19,3},{4,20},{20... | collective-permute-start | bytes 1572872 | tf_op jit(solution)/shard_map/weight_grad_sum/ppermute | solution.py:29
  99.3 1.9 %copy-start.5 = (bf16[1024,512]{1,0:T(8,128)(2,1)S(1)}, bf16[1024,512]{1,0:T(8,128)(2,1)}, u32[]{:S(2)}) copy-start(bf16[1024,512]{1,0:T(8,128)(2,1)} %param.9) | copy-start | bytes 3145732
  99.3 1.9 %copy-start.8 = (bf16[192,512]{1,0:T(8,128)(2,1)S(1)}, bf16[192,512]{1,0:T(8,128)(2,1)}, u32[]{:S(2)}) copy-start(bf16[192,512]{1,0:T(8,128)(2,1)} %copy-done.7) | copy-start | bytes 589828
  100.8 14.4 %collective-permute-start.22 = (f32[2,2,2,64,256]{4,3,2,1,0:T(8,128)S(1)}, f32[2,2,2,64,256]{4,3,2,1,0:T(8,128)S(1)}, u32[]{:S(2)}, u32[]{:S(2)}) collective-permute-start(f32[2,2,2,64,256]{4,3,2,1,0:T(8,128)S(1)} %dynamic-slice_bitcast_fusion.1), channel_id=1, source_target_pairs={{0,2},{1,3},{2,0},{3,1},{4,6},{5,7},{6,4},{7,5},{8,10},{9,11},{10,... | collective-permute-start | bytes 1572872 | tf_op jit(solution)/shard_map/weight_grad_sum/ppermute | solution.py:29
  112.2 8.3 %collective-permute-start.18 = (f32[2,2,64,256]{3,2,1,0:T(8,128)S(1)}, f32[2,2,64,256]{3,2,1,0:T(8,128)S(1)}, u32[]{:S(2)}, u32[]{:S(2)}) collective-permute-start(f32[2,2,64,256]{3,2,1,0:T(8,128)S(1)} %dynamic-slice_bitcast_fusion.4), channel_id=1, source_target_pairs={{0,2},{1,3},{2,0},{3,1},{4,6},{5,7},{6,4},{7,5},{8,10},{9,11},{10,... | collective-permute-start | bytes 786440 | tf_op jit(solution)/shard_map/weight_grad_sum/ppermute | solution.py:29
  115.3 7.3 %collective-permute-start.23 = (f32[2,2,64,256]{3,2,1,0:T(8,128)S(1)}, f32[2,2,64,256]{3,2,1,0:T(8,128)S(1)}, u32[]{:S(2)}, u32[]{:S(2)}) collective-permute-start(f32[2,2,64,256]{3,2,1,0:T(8,128)S(1)} %dynamic-slice_bitcast_fusion.3), channel_id=1, source_target_pairs={{0,16},{16,0},{1,17},{17,1},{2,18},{18,2},{3,19},{19,3},{4,20},{20... | collective-permute-start | bytes 786440 | tf_op jit(solution)/shard_map/weight_grad_sum/ppermute | solution.py:29
  120.6 8.1 %collective-permute-start.19 = (f32[2,64,256]{2,1,0:T(8,128)S(1)}, f32[2,64,256]{2,1,0:T(8,128)S(1)}, u32[]{:S(2)}, u32[]{:S(2)}) collective-permute-start(f32[2,64,256]{2,1,0:T(8,128)S(1)} %dynamic-slice_bitcast_fusion.6), channel_id=1, source_target_pairs={{0,8},{1,9},{2,10},{3,11},{4,12},{5,13},{6,14},{7,15},{8,0},{9,1},... | collective-permute-start | bytes 393224 | tf_op jit(solution)/shard_map/weight_grad_sum/ppermute | solution.py:29
  122.7 6.7 %collective-permute-start.24 = (f32[2,64,256]{2,1,0:T(8,128)S(1)}, f32[2,64,256]{2,1,0:T(8,128)S(1)}, u32[]{:S(2)}, u32[]{:S(2)}) collective-permute-start(f32[2,64,256]{2,1,0:T(8,128)S(1)} %dynamic-slice_bitcast_fusion.5), channel_id=1, source_target_pairs={{0,4},{1,5},{2,6},{3,7},{4,0},{5,1},{6,2},{7,3},{8,12},{9,13},{10,... | collective-permute-start | bytes 393224 | tf_op jit(solution)/shard_map/weight_grad_sum/ppermute | solution.py:29
  128.7 4.5 %collective-permute-start.20 = (f32[64,256]{1,0:T(8,128)S(1)}, f32[64,256]{1,0:T(8,128)S(1)}, u32[]{:S(2)}, u32[]{:S(2)}) collective-permute-start(f32[64,256]{1,0:T(8,128)S(1)} %dynamic-slice_bitcast_fusion.8), channel_id=1, source_target_pairs={{0,4},{1,5},{2,6},{3,7},{4,0},{5,1},{6,2},{7,3},{8,12},{9,13},{10,... | collective-permute-start | bytes 196616 | tf_op jit(solution)/shard_map/weight_grad_sum/ppermute | solution.py:29
  129.4 5.2 %collective-permute-start.25 = (f32[64,256]{1,0:T(8,128)S(1)}, f32[64,256]{1,0:T(8,128)S(1)}, u32[]{:S(2)}, u32[]{:S(2)}) collective-permute-start(f32[64,256]{1,0:T(8,128)S(1)} %dynamic-slice_bitcast_fusion.7), channel_id=1, source_target_pairs={{0,8},{1,9},{2,10},{3,11},{4,12},{5,13},{6,14},{7,15},{8,0},{9,1},... | collective-permute-start | bytes 196616 | tf_op jit(solution)/shard_map/weight_grad_sum/ppermute | solution.py:29

commit v13 on v12

--- a/solution.py
+++ b/solution.py
@@ -144,11 +144,13 @@
     )
     hidden_one = jax.nn.silu(pre_one).astype(jnp.bfloat16)
     hparts = [hidden_one[:, :half], hidden_one[:, half:]]
-    hparts = [doubling_step(p, o, 0) for p, o in zip(hparts, orders)]
+    lead = 2 if devices == 16 else 1
+    for step in range(lead):
+        hparts = [doubling_step(p, o, step) for p, o in zip(hparts, orders)]
     hparts, parts = lax.optimization_barrier((hparts, parts))
     while steps_done < len(order):
         parts, steps_done = advance(parts, steps_done)
-    for step in range(1, len(order)):
+    for step in range(lead, len(order)):
         hparts = [doubling_step(p, o, step) for p, o in zip(hparts, orders)]
     hidden_all = jnp.concatenate([p.reshape(-1, half) for p in hparts], axis=1)
     down_all = jnp.concatenate([p.reshape(-1, half) for p in parts], axis=1)

time: 136 us -> 139 us (1.022)
  starting transfers between devices: 30.6 us -> 33.4 us
  waiting for transfers between devices: 65.7 us -> 63.7 us
  other arithmetic: 13.1 us -> 15 us
    ppermute x26, starting transfers between devices: 23.3 us -> 26.1 us  [swap(): return lax.ppermute(values, axis, [(j, j ^ mask) for j in range(size)])]
    another operation x29, other arithmetic: 1.97 us -> 3.96 us  [doubling_step(): jnp.stack([low, high], axis=sum((1 for done in order[:step] if done > bit)))]
    unnamed x28 -> x26, local copies, waits for them, and re-layouts: 2.42 us -> 3.07 us
  transfers between devices with their start and end apart: 28 -> 28, of which waited for: 19 -> 18; matrix products, arithmetic and copies ran while one was open for 18% -> 19% of each run, Pallas kernels for 0% -> 0%
where the time goes in v13:
time: 139 us; the launch traced here: 138 us
  waiting for transfers between devices  63.7 us (46%)
  starting transfers between devices  33.4 us (24%)
  other arithmetic  15 us (11%)
  matrix products  14.6 us (11%)
  local copies, waits for them, and re-layouts  9.87 us (7%)
    ppermute x26, waiting for transfers between devices, swap(): return lax.ppermute(values, axis, [(j, j ^ mask) for j in range(size)])  58.7 us
    ppermute x26, starting transfers between devices, swap(): return lax.ppermute(values, axis, [(j, j ^ mask) for j in range(size)])  26.1 us
    dot_general x13, matrix products, contract(): lax.dot_general(left, right, (((left_dim,), (right_dim,)), ((), ())), pre...  14.6 us
    all_to_all x1, waiting for transfers between devices, shards(): lax.all_to_all(agg_one_cols, 'mp', split_axis=1, concat_axis=0, tiled=True)  4.99 us
    another operation x29, other arithmetic, doubling_step(): jnp.stack([low, high], axis=sum((1 for done in order[:step] if done > bit)))  3.96 us
    convert_element_type x1, other arithmetic, shards(): adjacency = (rowsel[:, None, :] == row_ids).astype(jnp.bfloat16)  3.87 us
    all_to_all x1, starting transfers between devices, shards(): lax.all_to_all(agg_one_cols, 'mp', split_axis=1, concat_axis=0, tiled=True)  3.77 us
    all_to_all x1, starting transfers between devices, shards(): lax.all_to_all(node_features, 'mp', split_axis=1, concat_axis=0, tiled=True)  3.53 us
  transfers between devices with their start and end apart: 28, of which 18 were waited for; matrix products, arithmetic and copies ran while one was open for 19% of the time, Pallas kernels for 0%

profile of v13, /device:TPU:0, one launch (start us, length us, event | category | flops | bytes accessed | tf_op | source)
XLA Modules:
  0.0 138.1 jit_solution(15681957392453213100)
XLA Ops:
  0.7 0.8 convert_divide_fusion
  1.6 1.4 fusion.21
  3.0 4.1 %collective-permute-start = (bf16[192,256]{1,0:T(8,128)(2,1)S(1)}, bf16[192,256]{1,0:T(8,128)(2,1)S(1)}, u32[]{:S(2)}, u32[]{:S(2)}) collective-permute-start(bf16[192,256]{1,0:T(8,128)(2,1)S(1)} %get-tuple-element.71), channel_id=1, source_target_pairs={{0,8},{1,9},{2,10},{3,11},{4,12},{5,13},{6,14},{7,15},{8,0},{9,1},... | collective-permute-start | bytes 294920 | tf_op jit(solution)/shard_map/ppermute | solution.py:29
  7.1 1.5 %collective-permute-start.1 = (bf16[192,256]{1,0:T(8,128)(2,1)S(1)}, bf16[192,256]{1,0:T(8,128)(2,1)S(1)}, u32[]{:S(2)}, u32[]{:S(2)}) collective-permute-start(bf16[192,256]{1,0:T(8,128)(2,1)S(1)} %get-tuple-element.70), channel_id=1, source_target_pairs={{0,2},{1,3},{2,0},{3,1},{4,6},{5,7},{6,4},{7,5},{8,10},{9,11},{10,... | collective-permute-start | bytes 294920 | tf_op jit(solution)/shard_map/ppermute | solution.py:29
  8.6 1.2 all_to_all.28
  9.8 0.8 copy.29
  10.6 3.5 %all-to-all-start = ((bf16[32,16,192]{2,0,1:T(8,128)(2,1)}), bf16[32,16,192]{2,0,1:T(8,128)(2,1)S(1)}, u32[]{:S(2)}, u32[]{:S(2)}) async-start(bf16[32,16,192]{2,0,1:T(8,128)(2,1)} %copy.29), calls=%async_computation | async-start | bytes 524288 | tf_op jit(solution)/shard_map/all_to_all | solution.py:129
  14.3 0.8 select_reduce_fusion
  15.2 3.9 %fusion = bf16[3072,3072]{1,0:T(8,128)(2,1)S(1)} fusion(s32[3072]{0:T(1024)S(1)} %eq.57, s32[16,3072]{1,0:T(8,128)S(1)} %select_reduce_fusion), kind=kLoop, calls=%fused_computation.1 | loop fusion | flops 18874368 | bytes 19083264 | tf_op jit(solution)/shard_map/layer_one_mean/convert_element_type | solution.py:115
  19.1 2.8 %collective-permute-start.3 = (bf16[2,192,256]{2,1,0:T(8,128)(2,1)S(1)}, bf16[2,192,256]{2,1,0:T(8,128)(2,1)S(1)}, u32[]{:S(2)}, u32[]{:S(2)}) collective-permute-start(bf16[2,192,256]{2,1,0:T(8,128)(2,1)S(1)} %get-tuple-element.16), channel_id=1, source_target_pairs={{0,8},{1,9},{2,10},{3,11},{4,12},{5,13},{6,14},{7,15},{8,0},{9,1},... | collective-permute-start | bytes 589832 | tf_op jit(solution)/shard_map/layer_one_mean/ppermute | solution.py:29
  22.0 1.5 %collective-permute-start.2 = (bf16[2,192,256]{2,1,0:T(8,128)(2,1)S(1)}, bf16[2,192,256]{2,1,0:T(8,128)(2,1)S(1)}, u32[]{:S(2)}, u32[]{:S(2)}) collective-permute-start(bf16[2,192,256]{2,1,0:T(8,128)(2,1)S(1)} %get-tuple-element.15), channel_id=1, source_target_pairs={{0,4},{1,5},{2,6},{3,7},{4,0},{5,1},{6,2},{7,3},{8,12},{9,13},{10,... | collective-permute-start | bytes 589832 | tf_op jit(solution)/shard_map/layer_one_mean/ppermute | solution.py:29
  23.5 3.4 %fusion.2 = bf16[32,3072]{1,0:T(8,128)(2,1)S(1)} fusion(bf16[32,3072]{1,0:T(8,128)(2,1)S(1)} %copy-done.3, bf16[3072,3072]{1,0:T(8,128)(2,1)S(1)} %fusion, f32[3072]{0:T(1024)S(1)} %convert_divide_fusion), kind=kOutput, calls=%fused_computation.5 | convolution fusion | flops 604176384 | bytes 19279872 | tf_op jit(solution)/shard_map/layer_one_mean/dot_general | solution.py:22
  26.8 5.5 %collective-permute-done.3 = bf16[2,192,256]{2,1,0:T(8,128)(2,1)S(1)} collective-permute-done((bf16[2,192,256]{2,1,0:T(8,128)(2,1)S(1)}, bf16[2,192,256]{2,1,0:T(8,128)(2,1)S(1)}, u32[]{:S(2)}, u32[]{:S(2)}) %collective-permute-start.3) | collective-permute-done | bytes 196640 | tf_op jit(solution)/shard_map/layer_one_mean/ppermute | solution.py:29
  32.5 0.9 collective-permute-start.5
  33.4 1.5 %collective-permute-start.4 = (bf16[2,2,192,256]{3,2,0,1:T(8,128)(2,1)S(1)}, bf16[2,2,192,256]{3,2,0,1:T(8,128)(2,1)S(1)}, u32[]{:S(2)}, u32[]{:S(2)}) collective-permute-start(bf16[2,2,192,256]{3,2,0,1:T(8,128)(2,1)S(1)} %pad_maximum_fusion.9), channel_id=1, source_target_pairs={{0,2},{1,3},{2,0},{3,1},{4,6},{5,7},{6,4},{7,5},{8,10},{9,11},{10,... | collective-permute-start | bytes 1179656 | tf_op jit(solution)/shard_map/ppermute | solution.py:29
  35.1 0.8 copy.30
  35.9 3.8 %all-to-all-start.1 = ((bf16[32,16,192]{2,0,1:T(8,128)(2,1)}), bf16[32,16,192]{2,0,1:T(8,128)(2,1)S(1)}, u32[]{:S(2)}, u32[]{:S(2)}) async-start(bf16[32,16,192]{2,0,1:T(8,128)(2,1)} %copy.30), calls=%async_computation.1 | async-start | bytes 524288 | tf_op jit(solution)/shard_map/all_to_all | solution.py:130
  39.7 1.3 fusion.24
  41.0 2.4 %collective-permute-done.5 = bf16[2,2,192,256]{3,2,1,0:T(8,128)(2,1)} collective-permute-done((bf16[2,2,192,256]{3,2,1,0:T(8,128)(2,1)S(1)}, bf16[2,2,192,256]{3,2,1,0:T(8,128)(2,1)}, u32[]{:S(2)}, u32[]{:S(2)}) %collective-permute-start.5) | collective-permute-done | bytes 393248 | tf_op jit(solution)/shard_map/ppermute | solution.py:29
  43.5 1.1 select_bitcast_fusion.13
  44.8 5.0 %all-to-all-done.1 = bf16[32,16,192]{2,0,1:T(8,128)(2,1)S(1)} async-done(((bf16[32,16,192]{2,0,1:T(8,128)(2,1)}), bf16[32,16,192]{2,0,1:T(8,128)(2,1)S(1)}, u32[]{:S(2)}, u32[]{:S(2)}) %all-to-all-start.1) | async-done | bytes 196640 | tf_op jit(solution)/shard_map/all_to_all | solution.py:130
  49.7 2.1 %multiply_convert_fusion = (bf16[192,512]{1,0:T(8,128)(2,1)S(1)}, f32[192,512]{1,0:T(8,128)}) fusion(f32[192,512]{1,0:T(8,128)S(1)} %fusion.24, bf16[512,192]{1,0:T(8,128)(2,1)S(1)} %bitcast.154, bf16[1024,512]{1,0:T(8,128)(2,1)} %param.8), kind=kOutput, calls=%fused_computation.71 | convolution fusion | flops 101253120 | bytes 1703936 | tf_op jit(solution)/shard_map/dot_general | solution.py:22
  51.8 1.1 collective-permute-start.6
  53.0 6.5 %collective-permute-done.6 = bf16[192,256]{1,0:T(8,128)(2,1)S(1)} collective-permute-done((bf16[192,256]{1,0:T(8,128)(2,1)S(1)}, bf16[192,256]{1,0:T(8,128)(2,1)S(1)}, u32[]{:S(2)}, u32[]{:S(2)}) %collective-permute-start.6) | collective-permute-done | bytes 98336 | tf_op jit(solution)/shard_map/ppermute | solution.py:29
  59.6 2.1 %collective-permute-start.7 = (bf16[2,192,256]{2,1,0:T(8,128)(2,1)S(1)}, bf16[2,192,256]{2,1,0:T(8,128)(2,1)S(1)}, u32[]{:S(2)}, u32[]{:S(2)}) collective-permute-start(bf16[2,192,256]{2,1,0:T(8,128)(2,1)S(1)} %pad_maximum_fusion.15), channel_id=1, source_target_pairs={{0,4},{1,5},{2,6},{3,7},{4,0},{5,1},{6,2},{7,3},{8,12},{9,13},{10,... | collective-permute-start | bytes 589832 | tf_op jit(solution)/shard_map/ppermute | solution.py:29
  61.8 8.8 %collective-permute-done.9 = bf16[2,192,256]{2,1,0:T(8,128)(2,1)S(1)} collective-permute-done((bf16[2,192,256]{2,1,0:T(8,128)(2,1)S(1)}, bf16[2,192,256]{2,1,0:T(8,128)(2,1)S(1)}, u32[]{:S(2)}, u32[]{:S(2)}) %collective-permute-start.9) | collective-permute-done | bytes 196640 | tf_op jit(solution)/shard_map/ppermute | solution.py:29
  70.9 0.8 collective-permute-start.10
  71.7 1.4 %bitcast_compare_fusion.1 = pred[3072,192]{1,0:T(32,128)(4,1)} fusion(s32[3072]{0:T(1024)S(1)} %eq.57, s32[16,192]{1,0:T(8,128)S(1)} %constant_dynamic-slice_fusion.3), kind=kLoop, calls=%fused_computation.14 | loop fusion | flops 589824 | bytes 614400 | tf_op jit(solution)/shard_map/neighbor_tables/eq | solution.py:137
  73.1 0.3 fusion.37
  73.5 0.5 collective-permute-start.15
  74.0 7.8 %collective-permute-done.10 = bf16[2,2,192,256]{3,2,0,1:T(8,128)(2,1)} collective-permute-done((bf16[2,2,192,256]{3,2,0,1:T(8,128)(2,1)S(1)}, bf16[2,2,192,256]{3,2,0,1:T(8,128)(2,1)}, u32[]{:S(2)}, u32[]{:S(2)}) %collective-permute-start.10) | collective-permute-done | bytes 393248 | tf_op jit(solution)/shard_map/ppermute | solution.py:29
  81.9 1.1 select_bitcast_fusion.11
  83.1 2.1 %collective-permute-done.12 = bf16[2,2,192,256]{3,2,1,0:T(8,128)(2,1)S(1)} collective-permute-done((bf16[2,2,192,256]{3,2,1,0:T(8,128)(2,1)S(1)}, bf16[2,2,192,256]{3,2,1,0:T(8,128)(2,1)S(1)}, u32[]{:S(2)}, u32[]{:S(2)}) %collective-permute-start.12) | collective-permute-done | bytes 393248 | tf_op jit(solution)/shard_map/ppermute | solution.py:29
  86.2 1.6 %fusion.7 = f32[192,512]{1,0:T(8,128)S(1)} fusion(bf16[3072,256]{1,0:T(8,128)(2,1)S(1)} %bitcast.153, bf16[3072,256]{1,0:T(8,128)(2,1)S(1)} %bitcast.151, s32[3072]{0:T(1024)S(1)} %bitcast.156), kind=kOutput, calls=%fused_computation.10 | convolution fusion | flops 610861056 | bytes 3551232 | tf_op jit(solution)/shard_map/dot_general | solution.py:22
  87.8 0.4 fusion.20
  89.6 1.0 copy-done.6
  90.6 1.1 fusion.17
  91.7 0.7 copy-done.7
  92.4 0.3 fusion.38
  92.7 0.4 pad_maximum_fusion
  93.2 0.3 fusion.33
  93.5 1.3 copy-done.1
  94.9 1.1 dynamic-slice_bitcast_fusion
  96.0 0.5 collective-permute-start.16
  96.7 1.0 copy.43
  97.7 1.3 fusion.27
  99.1 1.4 bitcast_add_fusion.1
  100.5 1.6 %collective-permute-start.17 = (f32[2,2,2,64,256]{4,3,2,1,0:T(8,128)S(1)}, f32[2,2,2,64,256]{4,3,2,1,0:T(8,128)S(1)}, u32[]{:S(2)}, u32[]{:S(2)}) collective-permute-start(f32[2,2,2,64,256]{4,3,2,1,0:T(8,128)S(1)} %dynamic-slice_bitcast_fusion.2), channel_id=1, source_target_pairs={{0,16},{16,0},{1,17},{17,1},{2,18},{18,2},{3,19},{19,3},{4,20},{20... | collective-permute-start | bytes 1572872 | tf_op jit(solution)/shard_map/weight_grad_sum/ppermute | solution.py:29
  102.1 1.5 %bitcast_add_fusion = f32[2,2,2,2,64,256]{5,4,2,1,0,3:T(8,128)S(1)} fusion(f32[2,2,2,2,64,256]{5,4,2,1,0,3:T(8,128)} %collective-permute-done.21, f32[2,2,2,2,1,64,256]{6,5,4,3,2,1,0:T(8,128)S(1)} %get-tuple-element.30), kind=kLoop, calls=%fused_computation.35 | loop fusion | flops 262144 | bytes 3145728 | tf_op jit(solution)/shard_map/weight_grad_sum/add | solution.py:45
  103.6 1.4 %collective-permute-start.22 = (f32[2,2,2,64,256]{4,3,2,1,0:T(8,128)S(1)}, f32[2,2,2,64,256]{4,3,2,1,0:T(8,128)S(1)}, u32[]{:S(2)}, u32[]{:S(2)}) collective-permute-start(f32[2,2,2,64,256]{4,3,2,1,0:T(8,128)S(1)} %dynamic-slice_bitcast_fusion.1), channel_id=1, source_target_pairs={{0,2},{1,3},{2,0},{3,1},{4,6},{5,7},{6,4},{7,5},{8,10},{9,11},{10,... | collective-permute-start | bytes 1572872 | tf_op jit(solution)/shard_map/weight_grad_sum/ppermute | solution.py:29
  105.0 0.9 fusion.22
  106.0 8.9 %collective-permute-done.17 = f32[2,2,2,64,256]{4,3,2,1,0:T(8,128)S(1)} collective-permute-done((f32[2,2,2,64,256]{4,3,2,1,0:T(8,128)S(1)}, f32[2,2,2,64,256]{4,3,2,1,0:T(8,128)S(1)}, u32[]{:S(2)}, u32[]{:S(2)}) %collective-permute-start.17) | collective-permute-done | bytes 524320 | tf_op jit(solution)/shard_map/weight_grad_sum/ppermute | solution.py:29
  115.0 1.4 %collective-permute-start.18 = (f32[2,2,64,256]{3,2,1,0:T(8,128)S(1)}, f32[2,2,64,256]{3,2,1,0:T(8,128)S(1)}, u32[]{:S(2)}, u32[]{:S(2)}) collective-permute-start(f32[2,2,64,256]{3,2,1,0:T(8,128)S(1)} %dynamic-slice_bitcast_fusion.4), channel_id=1, source_target_pairs={{0,2},{1,3},{2,0},{3,1},{4,6},{5,7},{6,4},{7,5},{8,10},{9,11},{10,... | collective-permute-start | bytes 786440 | tf_op jit(solution)/shard_map/weight_grad_sum/ppermute | solution.py:29
  116.4 1.6 %collective-permute-done.22 = f32[2,2,2,64,256]{4,3,2,1,0:T(8,128)S(1)} collective-permute-done((f32[2,2,2,64,256]{4,3,2,1,0:T(8,128)S(1)}, f32[2,2,2,64,256]{4,3,2,1,0:T(8,128)S(1)}, u32[]{:S(2)}, u32[]{:S(2)}) %collective-permute-start.22) | collective-permute-done | bytes 524320 | tf_op jit(solution)/shard_map/weight_grad_sum/ppermute | solution.py:29
  118.4 4.9 %collective-permute-done.18 = f32[2,2,64,256]{3,2,1,0:T(8,128)S(1)} collective-permute-done((f32[2,2,64,256]{3,2,1,0:T(8,128)S(1)}, f32[2,2,64,256]{3,2,1,0:T(8,128)S(1)}, u32[]{:S(2)}, u32[]{:S(2)}) %collective-permute-start.18) | collective-permute-done | bytes 262176 | tf_op jit(solution)/shard_map/weight_grad_sum/ppermute | solution.py:29
  123.4 1.0 collective-permute-start.19
  124.3 1.1 collective-permute-done.23
  125.5 0.8 collective-permute-start.24
  126.2 5.2 %collective-permute-done.19 = f32[2,64,256]{2,1,0:T(8,128)S(1)} collective-permute-done((f32[2,64,256]{2,1,0:T(8,128)S(1)}, f32[2,64,256]{2,1,0:T(8,128)S(1)}, u32[]{:S(2)}, u32[]{:S(2)}) %collective-permute-start.19) | collective-permute-done | bytes 131104 | tf_op jit(solution)/shard_map/weight_grad_sum/ppermute | solution.py:29
  131.6 0.6 collective-permute-done.24
  132.2 2.2 %collective-permute-start.25 = (f32[64,256]{1,0:T(8,128)S(1)}, f32[64,256]{1,0:T(8,128)S(1)}, u32[]{:S(2)}, u32[]{:S(2)}) collective-permute-start(f32[64,256]{1,0:T(8,128)S(1)} %dynamic-slice_bitcast_fusion.7), channel_id=1, source_target_pairs={{0,8},{1,9},{2,10},{3,11},{4,12},{5,13},{6,14},{7,15},{8,0},{9,1},... | collective-permute-start | bytes 196616 | tf_op jit(solution)/shard_map/weight_grad_sum/ppermute | solution.py:29
  134.3 1.7 %collective-permute-done.20 = f32[64,256]{1,0:T(8,128)S(1)} collective-permute-done((f32[64,256]{1,0:T(8,128)S(1)}, f32[64,256]{1,0:T(8,128)S(1)}, u32[]{:S(2)}, u32[]{:S(2)}) %collective-permute-start.20) | collective-permute-done | bytes 65568 | tf_op jit(solution)/shard_map/weight_grad_sum/ppermute | solution.py:29
  136.0 1.4 collective-permute-done.25
  137.4 0.7 pad_maximum_fusion.17
  (104 shorter events, 5.3 us)
Async XLA Ops:
  0.6 0.9 copy-start
  0.6 13.5 %copy-start.11 = (s32[3072]{0:T(1024)S(1)}, s32[3072]{0:T(1024)}, u32[]{:S(2)}) copy-start(s32[3072]{0:T(1024)} %param.12) | copy-start | bytes 36868
  0.7 13.7 %copy-start.10 = (s32[3072,8]{0,1:T(8,128)S(1)}, s32[3072,8]{0,1:T(8,128)}, u32[]{:S(2)}) copy-start(s32[3072,8]{0,1:T(8,128)} %param.10) | copy-start | bytes 294916
  0.7 13.6 %copy-start.9 = (s32[3072,8]{0,1:T(8,128)S(1)}, s32[3072,8]{0,1:T(8,128)}, u32[]{:S(2)}) copy-start(s32[3072,8]{0,1:T(8,128)} %param.11) | copy-start | bytes 294916
  3.0 16.1 %collective-permute-start = (bf16[192,256]{1,0:T(8,128)(2,1)S(1)}, bf16[192,256]{1,0:T(8,128)(2,1)S(1)}, u32[]{:S(2)}, u32[]{:S(2)}) collective-permute-start(bf16[192,256]{1,0:T(8,128)(2,1)S(1)} %get-tuple-element.71), channel_id=1, source_target_pairs={{0,8},{1,9},{2,10},{3,11},{4,12},{5,13},{6,14},{7,15},{8,0},{9,1},... | collective-permute-start | bytes 294920 | tf_op jit(solution)/shard_map/ppermute | solution.py:29
  7.1 12.0 %collective-permute-start.1 = (bf16[192,256]{1,0:T(8,128)(2,1)S(1)}, bf16[192,256]{1,0:T(8,128)(2,1)S(1)}, u32[]{:S(2)}, u32[]{:S(2)}) collective-permute-start(bf16[192,256]{1,0:T(8,128)(2,1)S(1)} %get-tuple-element.70), channel_id=1, source_target_pairs={{0,2},{1,3},{2,0},{3,1},{4,6},{5,7},{6,4},{7,5},{8,10},{9,11},{10,... | collective-permute-start | bytes 294920 | tf_op jit(solution)/shard_map/ppermute | solution.py:29
  10.6 25.3 %all-to-all-start = ((bf16[32,16,192]{2,0,1:T(8,128)(2,1)}), bf16[32,16,192]{2,0,1:T(8,128)(2,1)S(1)}, u32[]{:S(2)}, u32[]{:S(2)}) async-start(bf16[32,16,192]{2,0,1:T(8,128)(2,1)} %copy.29), calls=%async_computation | async-start | bytes 524288 | tf_op jit(solution)/shard_map/all_to_all | solution.py:129
  15.1 8.3 %copy-start.3 = (bf16[32,3072]{1,0:T(8,128)(2,1)S(1)}, bf16[32,3072]{1,0:T(8,128)(2,1)}, u32[]{:S(2)}) copy-start(bf16[32,3072]{1,0:T(8,128)(2,1)} %param.7) | copy-start | bytes 589828
  19.1 13.1 %collective-permute-start.3 = (bf16[2,192,256]{2,1,0:T(8,128)(2,1)S(1)}, bf16[2,192,256]{2,1,0:T(8,128)(2,1)S(1)}, u32[]{:S(2)}, u32[]{:S(2)}) collective-permute-start(bf16[2,192,256]{2,1,0:T(8,128)(2,1)S(1)} %get-tuple-element.16), channel_id=1, source_target_pairs={{0,8},{1,9},{2,10},{3,11},{4,12},{5,13},{6,14},{7,15},{8,0},{9,1},... | collective-permute-start | bytes 589832 | tf_op jit(solution)/shard_map/layer_one_mean/ppermute | solution.py:29
  22.0 10.4 %collective-permute-start.2 = (bf16[2,192,256]{2,1,0:T(8,128)(2,1)S(1)}, bf16[2,192,256]{2,1,0:T(8,128)(2,1)S(1)}, u32[]{:S(2)}, u32[]{:S(2)}) collective-permute-start(bf16[2,192,256]{2,1,0:T(8,128)(2,1)S(1)} %get-tuple-element.15), channel_id=1, source_target_pairs={{0,4},{1,5},{2,6},{3,7},{4,0},{5,1},{6,2},{7,3},{8,12},{9,13},{10,... | collective-permute-start | bytes 589832 | tf_op jit(solution)/shard_map/layer_one_mean/ppermute | solution.py:29
  32.5 10.9 %collective-permute-start.5 = (bf16[2,2,192,256]{3,2,1,0:T(8,128)(2,1)S(1)}, bf16[2,2,192,256]{3,2,1,0:T(8,128)(2,1)}, u32[]{:S(2)}, u32[]{:S(2)}) collective-permute-start(bf16[2,2,192,256]{3,2,1,0:T(8,128)(2,1)S(1)} %pad_maximum_fusion.10), channel_id=1, source_target_pairs={{0,4},{1,5},{2,6},{3,7},{4,0},{5,1},{6,2},{7,3},{8,12},{9,13},{10,... | collective-permute-start | bytes 1179656 | tf_op jit(solution)/shard_map/ppermute | solution.py:29
  33.4 11.2 %collective-permute-start.4 = (bf16[2,2,192,256]{3,2,0,1:T(8,128)(2,1)S(1)}, bf16[2,2,192,256]{3,2,0,1:T(8,128)(2,1)S(1)}, u32[]{:S(2)}, u32[]{:S(2)}) collective-permute-start(bf16[2,2,192,256]{3,2,0,1:T(8,128)(2,1)S(1)} %pad_maximum_fusion.9), channel_id=1, source_target_pairs={{0,2},{1,3},{2,0},{3,1},{4,6},{5,7},{6,4},{7,5},{8,10},{9,11},{10,... | collective-permute-start | bytes 1179656 | tf_op jit(solution)/shard_map/ppermute | solution.py:29
  35.9 13.8 %all-to-all-start.1 = ((bf16[32,16,192]{2,0,1:T(8,128)(2,1)}), bf16[32,16,192]{2,0,1:T(8,128)(2,1)S(1)}, u32[]{:S(2)}, u32[]{:S(2)}) async-start(bf16[32,16,192]{2,0,1:T(8,128)(2,1)} %copy.30), calls=%async_computation.1 | async-start | bytes 524288 | tf_op jit(solution)/shard_map/all_to_all | solution.py:130
  51.8 7.6 %collective-permute-start.6 = (bf16[192,256]{1,0:T(8,128)(2,1)S(1)}, bf16[192,256]{1,0:T(8,128)(2,1)S(1)}, u32[]{:S(2)}, u32[]{:S(2)}) collective-permute-start(bf16[192,256]{1,0:T(8,128)(2,1)S(1)} %get-tuple-element.67), channel_id=1, source_target_pairs={{0,8},{1,9},{2,10},{3,11},{4,12},{5,13},{6,14},{7,15},{8,0},{9,1},... | collective-permute-start | bytes 294920 | tf_op jit(solution)/shard_map/ppermute | solution.py:29
  53.0 6.5 %collective-permute-start.8 = (bf16[192,256]{1,0:T(8,128)(2,1)S(1)}, bf16[192,256]{1,0:T(8,128)(2,1)S(1)}, u32[]{:S(2)}, u32[]{:S(2)}) collective-permute-start(bf16[192,256]{1,0:T(8,128)(2,1)S(1)} %get-tuple-element.66), channel_id=1, source_target_pairs={{0,2},{1,3},{2,0},{3,1},{4,6},{5,7},{6,4},{7,5},{8,10},{9,11},{10,... | collective-permute-start | bytes 294920 | tf_op jit(solution)/shard_map/ppermute | solution.py:29
  59.5 11.0 %collective-permute-start.9 = (bf16[2,192,256]{2,1,0:T(8,128)(2,1)S(1)}, bf16[2,192,256]{2,1,0:T(8,128)(2,1)S(1)}, u32[]{:S(2)}, u32[]{:S(2)}) collective-permute-start(bf16[2,192,256]{2,1,0:T(8,128)(2,1)S(1)} %pad_maximum_fusion.16), channel_id=1, source_target_pairs={{0,8},{1,9},{2,10},{3,11},{4,12},{5,13},{6,14},{7,15},{8,0},{9,1},... | collective-permute-start | bytes 589832 | tf_op jit(solution)/shard_map/ppermute | solution.py:29
  59.6 11.2 %collective-permute-start.7 = (bf16[2,192,256]{2,1,0:T(8,128)(2,1)S(1)}, bf16[2,192,256]{2,1,0:T(8,128)(2,1)S(1)}, u32[]{:S(2)}, u32[]{:S(2)}) collective-permute-start(bf16[2,192,256]{2,1,0:T(8,128)(2,1)S(1)} %pad_maximum_fusion.15), channel_id=1, source_target_pairs={{0,4},{1,5},{2,6},{3,7},{4,0},{5,1},{6,2},{7,3},{8,12},{9,13},{10,... | collective-permute-start | bytes 589832 | tf_op jit(solution)/shard_map/ppermute | solution.py:29
  70.9 11.0 %collective-permute-start.10 = (bf16[2,2,192,256]{3,2,0,1:T(8,128)(2,1)S(1)}, bf16[2,2,192,256]{3,2,0,1:T(8,128)(2,1)}, u32[]{:S(2)}, u32[]{:S(2)}) collective-permute-start(bf16[2,2,192,256]{3,2,0,1:T(8,128)(2,1)S(1)} %pad_maximum_fusion.11), channel_id=1, source_target_pairs={{0,2},{1,3},{2,0},{3,1},{4,6},{5,7},{6,4},{7,5},{8,10},{9,11},{10,... | collective-permute-start | bytes 1179656 | tf_op jit(solution)/shard_map/ppermute | solution.py:29
  73.5 11.9 %collective-permute-start.14 = (bf16[2,2,2,192,256]{4,3,0,1,2:T(8,128)(2,1)S(1)}, bf16[2,2,2,192,256]{4,3,0,1,2:T(8,128)(2,1)S(1)}, u32[]{:S(2)}, u32[]{:S(2)}) collective-permute-start(bf16[2,2,2,192,256]{4,3,0,1,2:T(8,128)(2,1)S(1)} %pad_maximum_fusion.5), channel_id=1, source_target_pairs={{0,1},{1,0},{2,3},{3,2},{4,5},{5,4},{6,7},{7,6},{8,9},{9,8},{10,11... | collective-permute-start | bytes 2359304 | tf_op jit(solution)/shard_map/ppermute | solution.py:29
  73.5 12.2 %collective-permute-start.15 = (bf16[2,2,2,192,256]{4,3,2,0,1:T(8,128)(2,1)S(1)}, bf16[2,2,2,192,256]{4,3,2,0,1:T(8,128)(2,1)S(1)}, u32[]{:S(2)}, u32[]{:S(2)}) collective-permute-start(bf16[2,2,2,192,256]{4,3,2,0,1:T(8,128)(2,1)S(1)} %pad_maximum_fusion.6), channel_id=1, source_target_pairs={{0,1},{1,0},{2,3},{3,2},{4,5},{5,4},{6,7},{7,6},{8,9},{9,8},{10,11... | collective-permute-start | bytes 2359304 | tf_op jit(solution)/shard_map/ppermute | solution.py:29
  74.0 11.1 %collective-permute-start.12 = (bf16[2,2,192,256]{3,2,1,0:T(8,128)(2,1)S(1)}, bf16[2,2,192,256]{3,2,1,0:T(8,128)(2,1)S(1)}, u32[]{:S(2)}, u32[]{:S(2)}) collective-permute-start(bf16[2,2,192,256]{3,2,1,0:T(8,128)(2,1)S(1)} %pad_maximum_fusion.12), channel_id=1, source_target_pairs={{0,4},{1,5},{2,6},{3,7},{4,0},{5,1},{6,2},{7,3},{8,12},{9,13},{10,... | collective-permute-start | bytes 1179656 | tf_op jit(solution)/shard_map/ppermute | solution.py:29
  83.0 5.8 %collective-permute-start.11 = (bf16[2,2,2,192,256]{4,3,0,1,2:T(8,128)(2,1)S(1)}, bf16[2,2,2,192,256]{4,3,0,1,2:T(8,128)(2,1)S(1)}, u32[]{:S(2)}, u32[]{:S(2)}) collective-permute-start(bf16[2,2,2,192,256]{4,3,0,1,2:T(8,128)(2,1)S(1)} %pad_maximum_fusion.7), channel_id=1, source_target_pairs={{0,1},{1,0},{2,3},{3,2},{4,5},{5,4},{6,7},{7,6},{8,9},{9,8},{10,11... | collective-permute-start | bytes 2359304 | tf_op jit(solution)/shard_map/ppermute | solution.py:29
  85.3 3.9 %collective-permute-start.13 = (bf16[2,2,2,192,256]{4,3,2,0,1:T(8,128)(2,1)S(1)}, bf16[2,2,2,192,256]{4,3,2,0,1:T(8,128)(2,1)S(1)}, u32[]{:S(2)}, u32[]{:S(2)}) collective-permute-start(bf16[2,2,2,192,256]{4,3,2,0,1:T(8,128)(2,1)S(1)} %pad_maximum_fusion.8), channel_id=1, source_target_pairs={{0,1},{1,0},{2,3},{3,2},{4,5},{5,4},{6,7},{7,6},{8,9},{9,8},{10,11... | collective-permute-start | bytes 2359304 | tf_op jit(solution)/shard_map/ppermute | solution.py:29
  86.2 1.6 %copy-start.4 = (bf16[1024,512]{1,0:T(8,128)(2,1)S(1)}, bf16[1024,512]{1,0:T(8,128)(2,1)}, u32[]{:S(2)}) copy-start(bf16[1024,512]{1,0:T(8,128)(2,1)} %param.9) | copy-start | bytes 3145732
  86.2 1.6 %copy-start.12 = (f32[192,512]{1,0:T(8,128)S(1)}, f32[192,512]{1,0:T(8,128)}, u32[]{:S(2)}) copy-start(f32[192,512]{1,0:T(8,128)} %get-tuple-element.73) | copy-start | bytes 1179652
  89.5 1.1 copy-start.6
  91.7 0.7 copy-start.7
  93.5 1.4 copy-start.1
  96.0 3.1 %collective-permute-start.16 = (f32[2,2,2,2,64,256]{5,4,3,2,1,0:T(8,128)}, f32[2,2,2,2,64,256]{5,4,3,2,1,0:T(8,128)}, u32[]{:S(2)}, u32[]{:S(2)}) collective-permute-start(f32[2,2,2,2,64,256]{5,4,3,2,1,0:T(8,128)} %dynamic-slice_bitcast_fusion), channel_id=1, source_target_pairs={{0,1},{1,0},{2,3},{3,2},{4,5},{5,4},{6,7},{7,6},{8,9},{9,8},{10,11... | collective-permute-start | bytes 3145736 | tf_op jit(solution)/shard_map/weight_grad_sum/ppermute | solution.py:29
  96.6 2.5 %copy-start.2 = (f32[2048,256]{1,0:T(8,128)S(1)}, f32[2048,256]{1,0:T(8,128)}, u32[]{:S(2)}) copy-start(f32[2048,256]{1,0:T(8,128)} %copy-done.1) | copy-start | bytes 6291460
  97.7 4.4 %collective-permute-start.21 = (f32[2,2,2,2,64,256]{5,4,2,1,0,3:T(8,128)}, f32[2,2,2,2,64,256]{5,4,2,1,0,3:T(8,128)}, u32[]{:S(2)}, u32[]{:S(2)}) collective-permute-start(f32[2,2,2,2,64,256]{5,4,2,1,0,3:T(8,128)} %bitcast.144), channel_id=1, source_target_pairs={{0,1},{1,0},{2,3},{3,2},{4,5},{5,4},{6,7},{7,6},{8,9},{9,8},{10,11... | collective-permute-start | bytes 3145736 | tf_op jit(solution)/shard_map/weight_grad_sum/ppermute | solution.py:29
  100.5 14.3 %collective-permute-start.17 = (f32[2,2,2,64,256]{4,3,2,1,0:T(8,128)S(1)}, f32[2,2,2,64,256]{4,3,2,1,0:T(8,128)S(1)}, u32[]{:S(2)}, u32[]{:S(2)}) collective-permute-start(f32[2,2,2,64,256]{4,3,2,1,0:T(8,128)S(1)} %dynamic-slice_bitcast_fusion.2), channel_id=1, source_target_pairs={{0,16},{16,0},{1,17},{17,1},{2,18},{18,2},{3,19},{19,3},{4,20},{20... | collective-permute-start | bytes 1572872 | tf_op jit(solution)/shard_map/weight_grad_sum/ppermute | solution.py:29
  102.1 2.9 %copy-start.5 = (bf16[1024,512]{1,0:T(8,128)(2,1)S(1)}, bf16[1024,512]{1,0:T(8,128)(2,1)}, u32[]{:S(2)}) copy-start(bf16[1024,512]{1,0:T(8,128)(2,1)} %param.9) | copy-start | bytes 3145732
  102.1 2.9 %copy-start.8 = (bf16[192,512]{1,0:T(8,128)(2,1)S(1)}, bf16[192,512]{1,0:T(8,128)(2,1)}, u32[]{:S(2)}) copy-start(bf16[192,512]{1,0:T(8,128)(2,1)} %copy-done.7) | copy-start | bytes 589828
  103.6 14.4 %collective-permute-start.22 = (f32[2,2,2,64,256]{4,3,2,1,0:T(8,128)S(1)}, f32[2,2,2,64,256]{4,3,2,1,0:T(8,128)S(1)}, u32[]{:S(2)}, u32[]{:S(2)}) collective-permute-start(f32[2,2,2,64,256]{4,3,2,1,0:T(8,128)S(1)} %dynamic-slice_bitcast_fusion.1), channel_id=1, source_target_pairs={{0,2},{1,3},{2,0},{3,1},{4,6},{5,7},{6,4},{7,5},{8,10},{9,11},{10,... | collective-permute-start | bytes 1572872 | tf_op jit(solution)/shard_map/weight_grad_sum/ppermute | solution.py:29
  115.0 8.3 %collective-permute-start.18 = (f32[2,2,64,256]{3,2,1,0:T(8,128)S(1)}, f32[2,2,64,256]{3,2,1,0:T(8,128)S(1)}, u32[]{:S(2)}, u32[]{:S(2)}) collective-permute-start(f32[2,2,64,256]{3,2,1,0:T(8,128)S(1)} %dynamic-slice_bitcast_fusion.4), channel_id=1, source_target_pairs={{0,2},{1,3},{2,0},{3,1},{4,6},{5,7},{6,4},{7,5},{8,10},{9,11},{10,... | collective-permute-start | bytes 786440 | tf_op jit(solution)/shard_map/weight_grad_sum/ppermute | solution.py:29
  118.1 7.3 %collective-permute-start.23 = (f32[2,2,64,256]{3,2,1,0:T(8,128)S(1)}, f32[2,2,64,256]{3,2,1,0:T(8,128)S(1)}, u32[]{:S(2)}, u32[]{:S(2)}) collective-permute-start(f32[2,2,64,256]{3,2,1,0:T(8,128)S(1)} %dynamic-slice_bitcast_fusion.3), channel_id=1, source_target_pairs={{0,16},{16,0},{1,17},{17,1},{2,18},{18,2},{3,19},{19,3},{4,20},{20... | collective-permute-start | bytes 786440 | tf_op jit(solution)/shard_map/weight_grad_sum/ppermute | solution.py:29
  123.4 8.1 %collective-permute-start.19 = (f32[2,64,256]{2,1,0:T(8,128)S(1)}, f32[2,64,256]{2,1,0:T(8,128)S(1)}, u32[]{:S(2)}, u32[]{:S(2)}) collective-permute-start(f32[2,64,256]{2,1,0:T(8,128)S(1)} %dynamic-slice_bitcast_fusion.6), channel_id=1, source_target_pairs={{0,8},{1,9},{2,10},{3,11},{4,12},{5,13},{6,14},{7,15},{8,0},{9,1},... | collective-permute-start | bytes 393224 | tf_op jit(solution)/shard_map/weight_grad_sum/ppermute | solution.py:29
  125.5 6.7 %collective-permute-start.24 = (f32[2,64,256]{2,1,0:T(8,128)S(1)}, f32[2,64,256]{2,1,0:T(8,128)S(1)}, u32[]{:S(2)}, u32[]{:S(2)}) collective-permute-start(f32[2,64,256]{2,1,0:T(8,128)S(1)} %dynamic-slice_bitcast_fusion.5), channel_id=1, source_target_pairs={{0,4},{1,5},{2,6},{3,7},{4,0},{5,1},{6,2},{7,3},{8,12},{9,13},{10,... | collective-permute-start | bytes 393224 | tf_op jit(solution)/shard_map/weight_grad_sum/ppermute | solution.py:29
  131.5 4.5 %collective-permute-start.20 = (f32[64,256]{1,0:T(8,128)S(1)}, f32[64,256]{1,0:T(8,128)S(1)}, u32[]{:S(2)}, u32[]{:S(2)}) collective-permute-start(f32[64,256]{1,0:T(8,128)S(1)} %dynamic-slice_bitcast_fusion.8), channel_id=1, source_target_pairs={{0,4},{1,5},{2,6},{3,7},{4,0},{5,1},{6,2},{7,3},{8,12},{9,13},{10,... | collective-permute-start | bytes 196616 | tf_op jit(solution)/shard_map/weight_grad_sum/ppermute | solution.py:29
  132.2 5.2 %collective-permute-start.25 = (f32[64,256]{1,0:T(8,128)S(1)}, f32[64,256]{1,0:T(8,128)S(1)}, u32[]{:S(2)}, u32[]{:S(2)}) collective-permute-start(f32[64,256]{1,0:T(8,128)S(1)} %dynamic-slice_bitcast_fusion.7), channel_id=1, source_target_pairs={{0,8},{1,9},{2,10},{3,11},{4,12},{5,13},{6,14},{7,15},{8,0},{9,1},... | collective-permute-start | bytes 196616 | tf_op jit(solution)/shard_map/weight_grad_sum/ppermute | solution.py:29

commit v14 on v12

--- a/solution.py
+++ b/solution.py
@@ -123,7 +123,8 @@
             global_ids = owner_slots * node_dev + neighbor_row.T
             agg_one_cols = column_mean(node_features, global_ids, live.T, inverse_all)
     parts, agg_one_cols = lax.optimization_barrier((parts, agg_one_cols))
-    parts, steps_done = advance(parts, steps_done)
+    if devices != 16:
+        parts, steps_done = advance(parts, steps_done)
 
     own_feats, own_agg_one = (
         lax.all_to_all(node_features, "mp", split_axis=1, concat_axis=0, tiled=True),

time: 136 us -> 142 us (1.044)
  waiting for transfers between devices: 65.7 us -> 59.9 us
  starting transfers between devices: 30.6 us -> 36.4 us
  matrix products: 15.4 us -> 18.9 us
  other arithmetic: 13.1 us -> 15.5 us
    ppermute x26, waiting for transfers between devices: 59.9 us -> 50.2 us  [swap(): return lax.ppermute(values, axis, [(j, j ^ mask) for j in range(size)])]
    ppermute x26, starting transfers between devices: 23.3 us -> 28.9 us  [swap(): return lax.ppermute(values, axis, [(j, j ^ mask) for j in range(size)])]
    all_to_all x1, waiting for transfers between devices: 5.82 us -> 9.7 us  [shards(): lax.all_to_all(agg_one_cols, 'mp', split_axis=1, concat_axis=0, tiled=True)]
    dot_general x13, matrix products: 15.4 us -> 18.9 us  [contract(): lax.dot_general(left, right, (((left_dim,), (right_dim,)), ((), ())), pre...]
    convert_element_type x1, other arithmetic: 3.87 us -> 7.24 us  [shards(): adjacency = (rowsel[:, None, :] == row_ids).astype(jnp.bfloat16)]
  transfers between devices with their start and end apart: 28 -> 28, of which waited for: 19 -> 12; matrix products, arithmetic and copies ran while one was open for 18% -> 23% of each run, Pallas kernels for 0% -> 0%
where the time goes in v14:
time: 142 us; the launch traced here: 141 us
  waiting for transfers between devices  59.9 us (42%)
  starting transfers between devices  36.4 us (26%)
  matrix products  18.9 us (13%)
  other arithmetic  15.5 us (11%)
  local copies, waits for them, and re-layouts  8.93 us (6%)
    ppermute x26, waiting for transfers between devices, swap(): return lax.ppermute(values, axis, [(j, j ^ mask) for j in range(size)])  50.2 us
    ppermute x26, starting transfers between devices, swap(): return lax.ppermute(values, axis, [(j, j ^ mask) for j in range(size)])  28.9 us
    dot_general x13, matrix products, contract(): lax.dot_general(left, right, (((left_dim,), (right_dim,)), ((), ())), pre...  18.9 us
    all_to_all x1, waiting for transfers between devices, shards(): lax.all_to_all(agg_one_cols, 'mp', split_axis=1, concat_axis=0, tiled=True)  9.7 us
    convert_element_type x1, other arithmetic, shards(): adjacency = (rowsel[:, None, :] == row_ids).astype(jnp.bfloat16)  7.24 us
    all_to_all x1, starting transfers between devices, shards(): lax.all_to_all(agg_one_cols, 'mp', split_axis=1, concat_axis=0, tiled=True)  4.04 us
    all_to_all x1, starting transfers between devices, shards(): lax.all_to_all(node_features, 'mp', split_axis=1, concat_axis=0, tiled=True)  3.53 us
    add x10, other arithmetic, halving_scatter(): values = keep + got  3.09 us
  transfers between devices with their start and end apart: 28, of which 12 were waited for; matrix products, arithmetic and copies ran while one was open for 23% of the time, Pallas kernels for 0%

profile of v14, /device:TPU:0, one launch (start us, length us, event | category | flops | bytes accessed | tf_op | source)
XLA Modules:
  0.0 141.2 jit_solution(4003903431999423856)
XLA Ops:
  0.7 0.8 convert_divide_fusion
  1.6 1.4 fusion.21
  3.0 4.1 %collective-permute-start = (bf16[192,256]{1,0:T(8,128)(2,1)S(1)}, bf16[192,256]{1,0:T(8,128)(2,1)S(1)}, u32[]{:S(2)}, u32[]{:S(2)}) collective-permute-start(bf16[192,256]{1,0:T(8,128)(2,1)S(1)} %get-tuple-element.71), channel_id=1, source_target_pairs={{0,8},{1,9},{2,10},{3,11},{4,12},{5,13},{6,14},{7,15},{8,0},{9,1},... | collective-permute-start | bytes 294920 | tf_op jit(solution)/shard_map/ppermute | solution.py:29
  7.1 1.5 %collective-permute-start.1 = (bf16[192,256]{1,0:T(8,128)(2,1)S(1)}, bf16[192,256]{1,0:T(8,128)(2,1)S(1)}, u32[]{:S(2)}, u32[]{:S(2)}) collective-permute-start(bf16[192,256]{1,0:T(8,128)(2,1)S(1)} %get-tuple-element.70), channel_id=1, source_target_pairs={{0,2},{1,3},{2,0},{3,1},{4,6},{5,7},{6,4},{7,5},{8,10},{9,11},{10,... | collective-permute-start | bytes 294920 | tf_op jit(solution)/shard_map/ppermute | solution.py:29
  8.6 1.2 all_to_all.28
  9.8 0.8 copy.29
  10.7 3.5 %all-to-all-start = ((bf16[32,16,192]{2,0,1:T(8,128)(2,1)}), bf16[32,16,192]{2,0,1:T(8,128)(2,1)S(1)}, u32[]{:S(2)}, u32[]{:S(2)}) async-start(bf16[32,16,192]{2,0,1:T(8,128)(2,1)} %copy.29), calls=%async_computation | async-start | bytes 524288 | tf_op jit(solution)/shard_map/all_to_all | solution.py:130
  14.3 0.8 select_reduce_fusion
  15.2 7.2 %fusion = bf16[3072,3072]{1,0:T(8,128)(2,1)} fusion(s32[3072]{0:T(1024)S(1)} %eq.57, s32[16,3072]{1,0:T(8,128)S(1)} %select_reduce_fusion), kind=kLoop, calls=%fused_computation.1 | loop fusion | flops 18874368 | bytes 19083264 | tf_op jit(solution)/shard_map/layer_one_mean/convert_element_type | solution.py:115
  22.5 2.8 %collective-permute-start.3 = (bf16[2,192,256]{2,1,0:T(8,128)(2,1)S(1)}, bf16[2,192,256]{2,1,0:T(8,128)(2,1)S(1)}, u32[]{:S(2)}, u32[]{:S(2)}) collective-permute-start(bf16[2,192,256]{2,1,0:T(8,128)(2,1)S(1)} %get-tuple-element.16), channel_id=1, source_target_pairs={{0,8},{1,9},{2,10},{3,11},{4,12},{5,13},{6,14},{7,15},{8,0},{9,1},... | collective-permute-start | bytes 589832 | tf_op jit(solution)/shard_map/layer_one_mean/ppermute | solution.py:29
  25.3 1.5 %collective-permute-start.2 = (bf16[2,192,256]{2,1,0:T(8,128)(2,1)S(1)}, bf16[2,192,256]{2,1,0:T(8,128)(2,1)S(1)}, u32[]{:S(2)}, u32[]{:S(2)}) collective-permute-start(bf16[2,192,256]{2,1,0:T(8,128)(2,1)S(1)} %get-tuple-element.15), channel_id=1, source_target_pairs={{0,4},{1,5},{2,6},{3,7},{4,0},{5,1},{6,2},{7,3},{8,12},{9,13},{10,... | collective-permute-start | bytes 589832 | tf_op jit(solution)/shard_map/layer_one_mean/ppermute | solution.py:29
  26.8 9.7 %fusion.2 = bf16[32,3072]{1,0:T(8,128)(2,1)S(1)} fusion(bf16[32,3072]{1,0:T(8,128)(2,1)S(1)} %copy-done.3, bf16[3072,3072]{1,0:T(8,128)(2,1)} %fusion, f32[3072]{0:T(1024)S(1)} %convert_divide_fusion), kind=kOutput, calls=%fused_computation.5 | convolution fusion | flops 604176384 | bytes 19279872 | tf_op jit(solution)/shard_map/layer_one_mean/dot_general | solution.py:22
  36.7 0.3 all_to_all.32
  37.0 0.8 copy.30
  37.8 4.0 %all-to-all-start.1 = ((bf16[32,16,192]{2,0,1:T(8,128)(2,1)}), bf16[32,16,192]{2,0,1:T(8,128)(2,1)S(1)}, u32[]{:S(2)}, u32[]{:S(2)}) async-start(bf16[32,16,192]{2,0,1:T(8,128)(2,1)} %copy.30), calls=%async_computation.1 | async-start | bytes 524288 | tf_op jit(solution)/shard_map/all_to_all | solution.py:131
  41.9 0.3 fusion.24
  42.2 9.7 %all-to-all-done.1 = bf16[32,16,192]{2,0,1:T(8,128)(2,1)S(1)} async-done(((bf16[32,16,192]{2,0,1:T(8,128)(2,1)}), bf16[32,16,192]{2,0,1:T(8,128)(2,1)S(1)}, u32[]{:S(2)}, u32[]{:S(2)}) %all-to-all-start.1) | async-done | bytes 196640 | tf_op jit(solution)/shard_map/all_to_all | solution.py:131
  51.9 1.0 multiply_convert_fusion
  53.0 1.1 collective-permute-start.4
  54.2 0.5 bitcast_compare_fusion.1
  54.7 5.9 %collective-permute-done.4 = bf16[192,256]{1,0:T(8,128)(2,1)S(1)} collective-permute-done((bf16[192,256]{1,0:T(8,128)(2,1)S(1)}, bf16[192,256]{1,0:T(8,128)(2,1)S(1)}, u32[]{:S(2)}, u32[]{:S(2)}) %collective-permute-start.4) | collective-permute-done | bytes 98336 | tf_op jit(solution)/shard_map/ppermute | solution.py:29
  60.8 0.3 fusion.37
  61.1 0.5 collective-permute-start.12
  61.6 2.0 %collective-permute-start.14 = (bf16[2,2,192,256]{3,2,1,0:T(8,128)(2,1)S(1)}, bf16[2,2,192,256]{3,2,1,0:T(8,128)(2,1)S(1)}, u32[]{:S(2)}, u32[]{:S(2)}) collective-permute-start(bf16[2,2,192,256]{3,2,1,0:T(8,128)(2,1)S(1)} %pad_maximum_fusion.10), channel_id=1, source_target_pairs={{0,4},{1,5},{2,6},{3,7},{4,0},{5,1},{6,2},{7,3},{8,12},{9,13},{10,... | collective-permute-start | bytes 1179656 | tf_op jit(solution)/shard_map/ppermute | solution.py:29
  63.6 0.3 collective-permute-start.9
  63.9 8.9 %collective-permute-done.6 = bf16[2,192,256]{2,1,0:T(8,128)(2,1)S(1)} collective-permute-done((bf16[2,192,256]{2,1,0:T(8,128)(2,1)S(1)}, bf16[2,192,256]{2,1,0:T(8,128)(2,1)S(1)}, u32[]{:S(2)}, u32[]{:S(2)}) %collective-permute-start.6) | collective-permute-done | bytes 196640 | tf_op jit(solution)/shard_map/ppermute | solution.py:29
  72.9 0.4 collective-permute-start.7
  73.3 4.5 %collective-permute-done.9 = bf16[2,192,256]{2,1,0:T(8,128)(2,1)S(1)} collective-permute-done((bf16[2,192,256]{2,1,0:T(8,128)(2,1)S(1)}, bf16[2,192,256]{2,1,0:T(8,128)(2,1)S(1)}, u32[]{:S(2)}, u32[]{:S(2)}) %collective-permute-start.9) | collective-permute-done | bytes 196640 | tf_op jit(solution)/shard_map/ppermute | solution.py:29
  77.8 2.7 %collective-permute-start.10 = (bf16[2,2,192,256]{3,2,1,0:T(8,128)(2,1)S(1)}, bf16[2,2,192,256]{3,2,1,0:T(8,128)(2,1)S(1)}, u32[]{:S(2)}, u32[]{:S(2)}) collective-permute-start(bf16[2,2,192,256]{3,2,1,0:T(8,128)(2,1)S(1)} %pad_maximum_fusion.12), channel_id=1, source_target_pairs={{0,4},{1,5},{2,6},{3,7},{4,0},{5,1},{6,2},{7,3},{8,12},{9,13},{10,... | collective-permute-start | bytes 1179656 | tf_op jit(solution)/shard_map/ppermute | solution.py:29
  80.9 0.5 collective-permute-start.15
  81.7 7.4 %collective-permute-done.10 = bf16[2,2,192,256]{3,2,1,0:T(8,128)(2,1)S(1)} collective-permute-done((bf16[2,2,192,256]{3,2,1,0:T(8,128)(2,1)S(1)}, bf16[2,2,192,256]{3,2,1,0:T(8,128)(2,1)S(1)}, u32[]{:S(2)}, u32[]{:S(2)}) %collective-permute-start.10) | collective-permute-done | bytes 393248 | tf_op jit(solution)/shard_map/ppermute | solution.py:29
  90.2 1.6 %fusion.7 = f32[192,512]{1,0:T(8,128)S(1)} fusion(bf16[3072,256]{1,0:T(8,128)(2,1)S(1)} %bitcast.153, bf16[3072,256]{1,0:T(8,128)(2,1)S(1)} %bitcast.151, s32[3072]{0:T(1024)S(1)} %bitcast.156), kind=kOutput, calls=%fused_computation.10 | convolution fusion | flops 610861056 | bytes 3551232 | tf_op jit(solution)/shard_map/dot_general | solution.py:22
  91.8 0.4 fusion.20
  92.2 0.3 convolution_bitcast_fusion
  92.5 0.3 fusion.36
  93.6 1.1 fusion.17
  94.8 0.7 copy-done.6
  95.5 0.3 fusion.38
  95.8 0.4 pad_maximum_fusion
  96.2 0.3 fusion.33
  96.6 1.3 copy-done.1
  97.9 1.1 dynamic-slice_bitcast_fusion
  99.0 0.5 collective-permute-start.16
  99.5 0.2 constant_dynamic-slice_fusion.1
  99.7 1.0 copy.43
  100.8 1.3 fusion.27
  102.2 1.4 bitcast_add_fusion.1
  103.6 1.6 %collective-permute-start.17 = (f32[2,2,2,64,256]{4,3,2,1,0:T(8,128)S(1)}, f32[2,2,2,64,256]{4,3,2,1,0:T(8,128)S(1)}, u32[]{:S(2)}, u32[]{:S(2)}) collective-permute-start(f32[2,2,2,64,256]{4,3,2,1,0:T(8,128)S(1)} %dynamic-slice_bitcast_fusion.2), channel_id=1, source_target_pairs={{0,16},{16,0},{1,17},{17,1},{2,18},{18,2},{3,19},{19,3},{4,20},{20... | collective-permute-start | bytes 1572872 | tf_op jit(solution)/shard_map/weight_grad_sum/ppermute | solution.py:29
  105.1 1.5 %bitcast_add_fusion = f32[2,2,2,2,64,256]{5,4,2,1,0,3:T(8,128)S(1)} fusion(f32[2,2,2,2,64,256]{5,4,2,1,0,3:T(8,128)} %collective-permute-done.21, f32[2,2,2,2,1,64,256]{6,5,4,3,2,1,0:T(8,128)S(1)} %get-tuple-element.30), kind=kLoop, calls=%fused_computation.35 | loop fusion | flops 262144 | bytes 3145728 | tf_op jit(solution)/shard_map/weight_grad_sum/add | solution.py:45
  106.7 1.1 collective-permute-start.22
  107.8 0.9 fusion.22
  108.7 9.2 %collective-permute-done.17 = f32[2,2,2,64,256]{4,3,2,1,0:T(8,128)S(1)} collective-permute-done((f32[2,2,2,64,256]{4,3,2,1,0:T(8,128)S(1)}, f32[2,2,2,64,256]{4,3,2,1,0:T(8,128)S(1)}, u32[]{:S(2)}, u32[]{:S(2)}) %collective-permute-start.17) | collective-permute-done | bytes 524320 | tf_op jit(solution)/shard_map/weight_grad_sum/ppermute | solution.py:29
  118.0 1.1 collective-permute-start.18
  119.1 1.9 %collective-permute-done.22 = f32[2,2,2,64,256]{4,3,2,1,0:T(8,128)S(1)} collective-permute-done((f32[2,2,2,64,256]{4,3,2,1,0:T(8,128)S(1)}, f32[2,2,2,64,256]{4,3,2,1,0:T(8,128)S(1)}, u32[]{:S(2)}, u32[]{:S(2)}) %collective-permute-start.22) | collective-permute-done | bytes 524320 | tf_op jit(solution)/shard_map/weight_grad_sum/ppermute | solution.py:29
  121.1 0.3 collective-permute-start.23
  121.4 4.9 %collective-permute-done.18 = f32[2,2,64,256]{3,2,1,0:T(8,128)S(1)} collective-permute-done((f32[2,2,64,256]{3,2,1,0:T(8,128)S(1)}, f32[2,2,64,256]{3,2,1,0:T(8,128)S(1)}, u32[]{:S(2)}, u32[]{:S(2)}) %collective-permute-start.18) | collective-permute-done | bytes 262176 | tf_op jit(solution)/shard_map/weight_grad_sum/ppermute | solution.py:29
  126.4 2.4 %collective-permute-start.19 = (f32[2,64,256]{2,1,0:T(8,128)S(1)}, f32[2,64,256]{2,1,0:T(8,128)S(1)}, u32[]{:S(2)}, u32[]{:S(2)}) collective-permute-start(f32[2,64,256]{2,1,0:T(8,128)S(1)} %dynamic-slice_bitcast_fusion.6), channel_id=1, source_target_pairs={{0,8},{1,9},{2,10},{3,11},{4,12},{5,13},{6,14},{7,15},{8,0},{9,1},... | collective-permute-start | bytes 393224 | tf_op jit(solution)/shard_map/weight_grad_sum/ppermute | solution.py:29
  128.8 1.5 %collective-permute-start.24 = (f32[2,64,256]{2,1,0:T(8,128)S(1)}, f32[2,64,256]{2,1,0:T(8,128)S(1)}, u32[]{:S(2)}, u32[]{:S(2)}) collective-permute-start(f32[2,64,256]{2,1,0:T(8,128)S(1)} %dynamic-slice_bitcast_fusion.5), channel_id=1, source_target_pairs={{0,4},{1,5},{2,6},{3,7},{4,0},{5,1},{6,2},{7,3},{8,12},{9,13},{10,... | collective-permute-start | bytes 393224 | tf_op jit(solution)/shard_map/weight_grad_sum/ppermute | solution.py:29
  130.3 4.5 %collective-permute-done.19 = f32[2,64,256]{2,1,0:T(8,128)S(1)} collective-permute-done((f32[2,64,256]{2,1,0:T(8,128)S(1)}, f32[2,64,256]{2,1,0:T(8,128)S(1)}, u32[]{:S(2)}, u32[]{:S(2)}) %collective-permute-start.19) | collective-permute-done | bytes 131104 | tf_op jit(solution)/shard_map/weight_grad_sum/ppermute | solution.py:29
  134.8 0.4 collective-permute-start.20
  135.2 2.3 %collective-permute-start.25 = (f32[64,256]{1,0:T(8,128)S(1)}, f32[64,256]{1,0:T(8,128)S(1)}, u32[]{:S(2)}, u32[]{:S(2)}) collective-permute-start(f32[64,256]{1,0:T(8,128)S(1)} %dynamic-slice_bitcast_fusion.7), channel_id=1, source_target_pairs={{0,8},{1,9},{2,10},{3,11},{4,12},{5,13},{6,14},{7,15},{8,0},{9,1},... | collective-permute-start | bytes 196616 | tf_op jit(solution)/shard_map/weight_grad_sum/ppermute | solution.py:29
  137.5 1.6 %collective-permute-done.20 = f32[64,256]{1,0:T(8,128)S(1)} collective-permute-done((f32[64,256]{1,0:T(8,128)S(1)}, f32[64,256]{1,0:T(8,128)S(1)}, u32[]{:S(2)}, u32[]{:S(2)}) %collective-permute-start.20) | collective-permute-done | bytes 65568 | tf_op jit(solution)/shard_map/weight_grad_sum/ppermute | solution.py:29
  139.2 1.3 collective-permute-done.25
  140.5 0.7 pad_maximum_fusion.17
  (104 shorter events, 3.8 us)
Async XLA Ops:
  0.6 0.9 copy-start
  0.6 13.5 %copy-start.11 = (s32[3072]{0:T(1024)S(1)}, s32[3072]{0:T(1024)}, u32[]{:S(2)}) copy-start(s32[3072]{0:T(1024)} %param.12) | copy-start | bytes 36868
  0.7 13.7 %copy-start.10 = (s32[3072,8]{0,1:T(8,128)S(1)}, s32[3072,8]{0,1:T(8,128)}, u32[]{:S(2)}) copy-start(s32[3072,8]{0,1:T(8,128)} %param.10) | copy-start | bytes 294916
  0.7 13.7 %copy-start.9 = (s32[3072,8]{0,1:T(8,128)S(1)}, s32[3072,8]{0,1:T(8,128)}, u32[]{:S(2)}) copy-start(s32[3072,8]{0,1:T(8,128)} %param.11) | copy-start | bytes 294916
  3.0 19.5 %collective-permute-start = (bf16[192,256]{1,0:T(8,128)(2,1)S(1)}, bf16[192,256]{1,0:T(8,128)(2,1)S(1)}, u32[]{:S(2)}, u32[]{:S(2)}) collective-permute-start(bf16[192,256]{1,0:T(8,128)(2,1)S(1)} %get-tuple-element.71), channel_id=1, source_target_pairs={{0,8},{1,9},{2,10},{3,11},{4,12},{5,13},{6,14},{7,15},{8,0},{9,1},... | collective-permute-start | bytes 294920 | tf_op jit(solution)/shard_map/ppermute | solution.py:29
  7.1 15.4 %collective-permute-start.1 = (bf16[192,256]{1,0:T(8,128)(2,1)S(1)}, bf16[192,256]{1,0:T(8,128)(2,1)S(1)}, u32[]{:S(2)}, u32[]{:S(2)}) collective-permute-start(bf16[192,256]{1,0:T(8,128)(2,1)S(1)} %get-tuple-element.70), channel_id=1, source_target_pairs={{0,2},{1,3},{2,0},{3,1},{4,6},{5,7},{6,4},{7,5},{8,10},{9,11},{10,... | collective-permute-start | bytes 294920 | tf_op jit(solution)/shard_map/ppermute | solution.py:29
  10.7 27.2 %all-to-all-start = ((bf16[32,16,192]{2,0,1:T(8,128)(2,1)}), bf16[32,16,192]{2,0,1:T(8,128)(2,1)S(1)}, u32[]{:S(2)}, u32[]{:S(2)}) async-start(bf16[32,16,192]{2,0,1:T(8,128)(2,1)} %copy.29), calls=%async_computation | async-start | bytes 524288 | tf_op jit(solution)/shard_map/all_to_all | solution.py:130
  15.2 11.6 %copy-start.3 = (bf16[32,3072]{1,0:T(8,128)(2,1)S(1)}, bf16[32,3072]{1,0:T(8,128)(2,1)}, u32[]{:S(2)}) copy-start(bf16[32,3072]{1,0:T(8,128)(2,1)} %param.7) | copy-start | bytes 589828
  22.5 14.0 %collective-permute-start.3 = (bf16[2,192,256]{2,1,0:T(8,128)(2,1)S(1)}, bf16[2,192,256]{2,1,0:T(8,128)(2,1)S(1)}, u32[]{:S(2)}, u32[]{:S(2)}) collective-permute-start(bf16[2,192,256]{2,1,0:T(8,128)(2,1)S(1)} %get-tuple-element.16), channel_id=1, source_target_pairs={{0,8},{1,9},{2,10},{3,11},{4,12},{5,13},{6,14},{7,15},{8,0},{9,1},... | collective-permute-start | bytes 589832 | tf_op jit(solution)/shard_map/layer_one_mean/ppermute | solution.py:29
  25.3 11.3 %collective-permute-start.2 = (bf16[2,192,256]{2,1,0:T(8,128)(2,1)S(1)}, bf16[2,192,256]{2,1,0:T(8,128)(2,1)S(1)}, u32[]{:S(2)}, u32[]{:S(2)}) collective-permute-start(bf16[2,192,256]{2,1,0:T(8,128)(2,1)S(1)} %get-tuple-element.15), channel_id=1, source_target_pairs={{0,4},{1,5},{2,6},{3,7},{4,0},{5,1},{6,2},{7,3},{8,12},{9,13},{10,... | collective-permute-start | bytes 589832 | tf_op jit(solution)/shard_map/layer_one_mean/ppermute | solution.py:29
  36.6 5.4 %copy-start.8 = (bf16[1024,512]{1,0:T(8,128)(2,1)S(1)}, bf16[1024,512]{1,0:T(8,128)(2,1)}, u32[]{:S(2)}) copy-start(bf16[1024,512]{1,0:T(8,128)(2,1)} %param.8) | copy-start | bytes 3145732
  37.8 14.1 %all-to-all-start.1 = ((bf16[32,16,192]{2,0,1:T(8,128)(2,1)}), bf16[32,16,192]{2,0,1:T(8,128)(2,1)S(1)}, u32[]{:S(2)}, u32[]{:S(2)}) async-start(bf16[32,16,192]{2,0,1:T(8,128)(2,1)} %copy.30), calls=%async_computation.1 | async-start | bytes 524288 | tf_op jit(solution)/shard_map/all_to_all | solution.py:131
  53.0 7.6 %collective-permute-start.4 = (bf16[192,256]{1,0:T(8,128)(2,1)S(1)}, bf16[192,256]{1,0:T(8,128)(2,1)S(1)}, u32[]{:S(2)}, u32[]{:S(2)}) collective-permute-start(bf16[192,256]{1,0:T(8,128)(2,1)S(1)} %get-tuple-element.67), channel_id=1, source_target_pairs={{0,8},{1,9},{2,10},{3,11},{4,12},{5,13},{6,14},{7,15},{8,0},{9,1},... | collective-permute-start | bytes 294920 | tf_op jit(solution)/shard_map/ppermute | solution.py:29
  54.1 6.5 %collective-permute-start.5 = (bf16[192,256]{1,0:T(8,128)(2,1)S(1)}, bf16[192,256]{1,0:T(8,128)(2,1)S(1)}, u32[]{:S(2)}, u32[]{:S(2)}) collective-permute-start(bf16[192,256]{1,0:T(8,128)(2,1)S(1)} %get-tuple-element.66), channel_id=1, source_target_pairs={{0,2},{1,3},{2,0},{3,1},{4,6},{5,7},{6,4},{7,5},{8,10},{9,11},{10,... | collective-permute-start | bytes 294920 | tf_op jit(solution)/shard_map/ppermute | solution.py:29
  60.7 12.1 %collective-permute-start.6 = (bf16[2,192,256]{2,1,0:T(8,128)(2,1)S(1)}, bf16[2,192,256]{2,1,0:T(8,128)(2,1)S(1)}, u32[]{:S(2)}, u32[]{:S(2)}) collective-permute-start(bf16[2,192,256]{2,1,0:T(8,128)(2,1)S(1)} %pad_maximum_fusion.15), channel_id=1, source_target_pairs={{0,4},{1,5},{2,6},{3,7},{4,0},{5,1},{6,2},{7,3},{8,12},{9,13},{10,... | collective-permute-start | bytes 589832 | tf_op jit(solution)/shard_map/ppermute | solution.py:29
  61.1 19.4 %collective-permute-start.12 = (bf16[2,2,192,256]{3,2,0,1:T(8,128)(2,1)S(1)}, bf16[2,2,192,256]{3,2,0,1:T(8,128)(2,1)S(1)}, u32[]{:S(2)}, u32[]{:S(2)}) collective-permute-start(bf16[2,2,192,256]{3,2,0,1:T(8,128)(2,1)S(1)} %pad_maximum_fusion.9), channel_id=1, source_target_pairs={{0,2},{1,3},{2,0},{3,1},{4,6},{5,7},{6,4},{7,5},{8,10},{9,11},{10,... | collective-permute-start | bytes 1179656 | tf_op jit(solution)/shard_map/ppermute | solution.py:29
  61.6 19.2 %collective-permute-start.14 = (bf16[2,2,192,256]{3,2,1,0:T(8,128)(2,1)S(1)}, bf16[2,2,192,256]{3,2,1,0:T(8,128)(2,1)S(1)}, u32[]{:S(2)}, u32[]{:S(2)}) collective-permute-start(bf16[2,2,192,256]{3,2,1,0:T(8,128)(2,1)S(1)} %pad_maximum_fusion.10), channel_id=1, source_target_pairs={{0,4},{1,5},{2,6},{3,7},{4,0},{5,1},{6,2},{7,3},{8,12},{9,13},{10,... | collective-permute-start | bytes 1179656 | tf_op jit(solution)/shard_map/ppermute | solution.py:29
  63.6 14.2 %collective-permute-start.9 = (bf16[2,192,256]{2,1,0:T(8,128)(2,1)S(1)}, bf16[2,192,256]{2,1,0:T(8,128)(2,1)S(1)}, u32[]{:S(2)}, u32[]{:S(2)}) collective-permute-start(bf16[2,192,256]{2,1,0:T(8,128)(2,1)S(1)} %pad_maximum_fusion.16), channel_id=1, source_target_pairs={{0,8},{1,9},{2,10},{3,11},{4,12},{5,13},{6,14},{7,15},{8,0},{9,1},... | collective-permute-start | bytes 589832 | tf_op jit(solution)/shard_map/ppermute | solution.py:29
  72.9 8.6 %collective-permute-start.7 = (bf16[2,2,192,256]{3,2,0,1:T(8,128)(2,1)S(1)}, bf16[2,2,192,256]{3,2,0,1:T(8,128)(2,1)S(1)}, u32[]{:S(2)}, u32[]{:S(2)}) collective-permute-start(bf16[2,2,192,256]{3,2,0,1:T(8,128)(2,1)S(1)} %pad_maximum_fusion.11), channel_id=1, source_target_pairs={{0,2},{1,3},{2,0},{3,1},{4,6},{5,7},{6,4},{7,5},{8,10},{9,11},{10,... | collective-permute-start | bytes 1179656 | tf_op jit(solution)/shard_map/ppermute | solution.py:29
  77.8 11.3 %collective-permute-start.10 = (bf16[2,2,192,256]{3,2,1,0:T(8,128)(2,1)S(1)}, bf16[2,2,192,256]{3,2,1,0:T(8,128)(2,1)S(1)}, u32[]{:S(2)}, u32[]{:S(2)}) collective-permute-start(bf16[2,2,192,256]{3,2,1,0:T(8,128)(2,1)S(1)} %pad_maximum_fusion.12), channel_id=1, source_target_pairs={{0,4},{1,5},{2,6},{3,7},{4,0},{5,1},{6,2},{7,3},{8,12},{9,13},{10,... | collective-permute-start | bytes 1179656 | tf_op jit(solution)/shard_map/ppermute | solution.py:29
  80.7 8.7 %collective-permute-start.13 = (bf16[2,2,2,192,256]{4,3,0,1,2:T(8,128)(2,1)S(1)}, bf16[2,2,2,192,256]{4,3,0,1,2:T(8,128)(2,1)S(1)}, u32[]{:S(2)}, u32[]{:S(2)}) collective-permute-start(bf16[2,2,2,192,256]{4,3,0,1,2:T(8,128)(2,1)S(1)} %pad_maximum_fusion.7), channel_id=1, source_target_pairs={{0,1},{1,0},{2,3},{3,2},{4,5},{5,4},{6,7},{7,6},{8,9},{9,8},{10,11... | collective-permute-start | bytes 2359304 | tf_op jit(solution)/shard_map/ppermute | solution.py:29
  80.9 8.9 %collective-permute-start.15 = (bf16[2,2,2,192,256]{4,3,2,0,1:T(8,128)(2,1)S(1)}, bf16[2,2,2,192,256]{4,3,2,0,1:T(8,128)(2,1)S(1)}, u32[]{:S(2)}, u32[]{:S(2)}) collective-permute-start(bf16[2,2,2,192,256]{4,3,2,0,1:T(8,128)(2,1)S(1)} %pad_maximum_fusion.8), channel_id=1, source_target_pairs={{0,1},{1,0},{2,3},{3,2},{4,5},{5,4},{6,7},{7,6},{8,9},{9,8},{10,11... | collective-permute-start | bytes 2359304 | tf_op jit(solution)/shard_map/ppermute | solution.py:29
  81.6 11.2 %collective-permute-start.8 = (bf16[2,2,2,192,256]{4,3,0,1,2:T(8,128)(2,1)S(1)}, bf16[2,2,2,192,256]{4,3,0,1,2:T(8,128)(2,1)S(1)}, u32[]{:S(2)}, u32[]{:S(2)}) collective-permute-start(bf16[2,2,2,192,256]{4,3,0,1,2:T(8,128)(2,1)S(1)} %pad_maximum_fusion.5), channel_id=1, source_target_pairs={{0,1},{1,0},{2,3},{3,2},{4,5},{5,4},{6,7},{7,6},{8,9},{9,8},{10,11... | collective-permute-start | bytes 2359304 | tf_op jit(solution)/shard_map/ppermute | solution.py:29
  89.3 3.9 %collective-permute-start.11 = (bf16[2,2,2,192,256]{4,3,2,0,1:T(8,128)(2,1)S(1)}, bf16[2,2,2,192,256]{4,3,2,0,1:T(8,128)(2,1)S(1)}, u32[]{:S(2)}, u32[]{:S(2)}) collective-permute-start(bf16[2,2,2,192,256]{4,3,2,0,1:T(8,128)(2,1)S(1)} %pad_maximum_fusion.6), channel_id=1, source_target_pairs={{0,1},{1,0},{2,3},{3,2},{4,5},{5,4},{6,7},{7,6},{8,9},{9,8},{10,11... | collective-permute-start | bytes 2359304 | tf_op jit(solution)/shard_map/ppermute | solution.py:29
  90.2 1.6 %copy-start.4 = (bf16[1024,512]{1,0:T(8,128)(2,1)S(1)}, bf16[1024,512]{1,0:T(8,128)(2,1)}, u32[]{:S(2)}) copy-start(bf16[1024,512]{1,0:T(8,128)(2,1)} %param.9) | copy-start | bytes 3145732
  90.2 1.6 %copy-start.12 = (f32[192,512]{1,0:T(8,128)S(1)}, f32[192,512]{1,0:T(8,128)}, u32[]{:S(2)}) copy-start(f32[192,512]{1,0:T(8,128)} %get-tuple-element.73) | copy-start | bytes 1179652
  94.8 0.7 copy-start.6
  96.6 1.4 copy-start.1
  99.0 3.1 %collective-permute-start.16 = (f32[2,2,2,2,64,256]{5,4,3,2,1,0:T(8,128)}, f32[2,2,2,2,64,256]{5,4,3,2,1,0:T(8,128)}, u32[]{:S(2)}, u32[]{:S(2)}) collective-permute-start(f32[2,2,2,2,64,256]{5,4,3,2,1,0:T(8,128)} %dynamic-slice_bitcast_fusion), channel_id=1, source_target_pairs={{0,1},{1,0},{2,3},{3,2},{4,5},{5,4},{6,7},{7,6},{8,9},{9,8},{10,11... | collective-permute-start | bytes 3145736 | tf_op jit(solution)/shard_map/weight_grad_sum/ppermute | solution.py:29
  99.7 2.5 %copy-start.2 = (f32[2048,256]{1,0:T(8,128)S(1)}, f32[2048,256]{1,0:T(8,128)}, u32[]{:S(2)}) copy-start(f32[2048,256]{1,0:T(8,128)} %copy-done.1) | copy-start | bytes 6291460
  100.7 4.4 %collective-permute-start.21 = (f32[2,2,2,2,64,256]{5,4,2,1,0,3:T(8,128)}, f32[2,2,2,2,64,256]{5,4,2,1,0,3:T(8,128)}, u32[]{:S(2)}, u32[]{:S(2)}) collective-permute-start(f32[2,2,2,2,64,256]{5,4,2,1,0,3:T(8,128)} %bitcast.144), channel_id=1, source_target_pairs={{0,1},{1,0},{2,3},{3,2},{4,5},{5,4},{6,7},{7,6},{8,9},{9,8},{10,11... | collective-permute-start | bytes 3145736 | tf_op jit(solution)/shard_map/weight_grad_sum/ppermute | solution.py:29
  103.6 14.3 %collective-permute-start.17 = (f32[2,2,2,64,256]{4,3,2,1,0:T(8,128)S(1)}, f32[2,2,2,64,256]{4,3,2,1,0:T(8,128)S(1)}, u32[]{:S(2)}, u32[]{:S(2)}) collective-permute-start(f32[2,2,2,64,256]{4,3,2,1,0:T(8,128)S(1)} %dynamic-slice_bitcast_fusion.2), channel_id=1, source_target_pairs={{0,16},{16,0},{1,17},{17,1},{2,18},{18,2},{3,19},{19,3},{4,20},{20... | collective-permute-start | bytes 1572872 | tf_op jit(solution)/shard_map/weight_grad_sum/ppermute | solution.py:29
  105.1 2.6 %copy-start.5 = (bf16[1024,512]{1,0:T(8,128)(2,1)S(1)}, bf16[1024,512]{1,0:T(8,128)(2,1)}, u32[]{:S(2)}) copy-start(bf16[1024,512]{1,0:T(8,128)(2,1)} %param.9) | copy-start | bytes 3145732
  105.1 2.6 %copy-start.7 = (bf16[192,512]{1,0:T(8,128)(2,1)S(1)}, bf16[192,512]{1,0:T(8,128)(2,1)}, u32[]{:S(2)}) copy-start(bf16[192,512]{1,0:T(8,128)(2,1)} %copy-done.6) | copy-start | bytes 589828
  106.7 14.4 %collective-permute-start.22 = (f32[2,2,2,64,256]{4,3,2,1,0:T(8,128)S(1)}, f32[2,2,2,64,256]{4,3,2,1,0:T(8,128)S(1)}, u32[]{:S(2)}, u32[]{:S(2)}) collective-permute-start(f32[2,2,2,64,256]{4,3,2,1,0:T(8,128)S(1)} %dynamic-slice_bitcast_fusion.1), channel_id=1, source_target_pairs={{0,2},{1,3},{2,0},{3,1},{4,6},{5,7},{6,4},{7,5},{8,10},{9,11},{10,... | collective-permute-start | bytes 1572872 | tf_op jit(solution)/shard_map/weight_grad_sum/ppermute | solution.py:29
  118.0 8.3 %collective-permute-start.18 = (f32[2,2,64,256]{3,2,1,0:T(8,128)S(1)}, f32[2,2,64,256]{3,2,1,0:T(8,128)S(1)}, u32[]{:S(2)}, u32[]{:S(2)}) collective-permute-start(f32[2,2,64,256]{3,2,1,0:T(8,128)S(1)} %dynamic-slice_bitcast_fusion.4), channel_id=1, source_target_pairs={{0,2},{1,3},{2,0},{3,1},{4,6},{5,7},{6,4},{7,5},{8,10},{9,11},{10,... | collective-permute-start | bytes 786440 | tf_op jit(solution)/shard_map/weight_grad_sum/ppermute | solution.py:29
  121.1 7.6 %collective-permute-start.23 = (f32[2,2,64,256]{3,2,1,0:T(8,128)S(1)}, f32[2,2,64,256]{3,2,1,0:T(8,128)S(1)}, u32[]{:S(2)}, u32[]{:S(2)}) collective-permute-start(f32[2,2,64,256]{3,2,1,0:T(8,128)S(1)} %dynamic-slice_bitcast_fusion.3), channel_id=1, source_target_pairs={{0,16},{16,0},{1,17},{17,1},{2,18},{18,2},{3,19},{19,3},{4,20},{20... | collective-permute-start | bytes 786440 | tf_op jit(solution)/shard_map/weight_grad_sum/ppermute | solution.py:29
  126.4 8.4 %collective-permute-start.19 = (f32[2,64,256]{2,1,0:T(8,128)S(1)}, f32[2,64,256]{2,1,0:T(8,128)S(1)}, u32[]{:S(2)}, u32[]{:S(2)}) collective-permute-start(f32[2,64,256]{2,1,0:T(8,128)S(1)} %dynamic-slice_bitcast_fusion.6), channel_id=1, source_target_pairs={{0,8},{1,9},{2,10},{3,11},{4,12},{5,13},{6,14},{7,15},{8,0},{9,1},... | collective-permute-start | bytes 393224 | tf_op jit(solution)/shard_map/weight_grad_sum/ppermute | solution.py:29
  128.8 6.4 %collective-permute-start.24 = (f32[2,64,256]{2,1,0:T(8,128)S(1)}, f32[2,64,256]{2,1,0:T(8,128)S(1)}, u32[]{:S(2)}, u32[]{:S(2)}) collective-permute-start(f32[2,64,256]{2,1,0:T(8,128)S(1)} %dynamic-slice_bitcast_fusion.5), channel_id=1, source_target_pairs={{0,4},{1,5},{2,6},{3,7},{4,0},{5,1},{6,2},{7,3},{8,12},{9,13},{10,... | collective-permute-start | bytes 393224 | tf_op jit(solution)/shard_map/weight_grad_sum/ppermute | solution.py:29
  134.8 4.3 %collective-permute-start.20 = (f32[64,256]{1,0:T(8,128)S(1)}, f32[64,256]{1,0:T(8,128)S(1)}, u32[]{:S(2)}, u32[]{:S(2)}) collective-permute-start(f32[64,256]{1,0:T(8,128)S(1)} %dynamic-slice_bitcast_fusion.8), channel_id=1, source_target_pairs={{0,4},{1,5},{2,6},{3,7},{4,0},{5,1},{6,2},{7,3},{8,12},{9,13},{10,... | collective-permute-start | bytes 196616 | tf_op jit(solution)/shard_map/weight_grad_sum/ppermute | solution.py:29
  135.2 5.2 %collective-permute-start.25 = (f32[64,256]{1,0:T(8,128)S(1)}, f32[64,256]{1,0:T(8,128)S(1)}, u32[]{:S(2)}, u32[]{:S(2)}) collective-permute-start(f32[64,256]{1,0:T(8,128)S(1)} %dynamic-slice_bitcast_fusion.7), channel_id=1, source_target_pairs={{0,8},{1,9},{2,10},{3,11},{4,12},{5,13},{6,14},{7,15},{8,0},{9,1},... | collective-permute-start | bytes 196616 | tf_op jit(solution)/shard_map/weight_grad_sum/ppermute | solution.py:29
